TPU v7x, 32 devices: a whole 2x2x4 slice. The times are simulated.
32 devices in a mesh: ctx: 4 (over y, core), row: 8 (over z, x).
Axes of the slice: x: 2, y: 2, z: 4, core: 2. Of those that a mesh axis runs over, the one named last changes fastest.
Arguments:
- queries: bfloat16 [16, 2, 4096], P('row'), may hold values from -400 to 400
- prefix_id: int32 [16], P('row'), may hold values from 0 to 7
- prefix_keys: bfloat16 [8, 1024, 512], P(None, ('ctx', 'row')), may hold values from -8 to 8
- prefix_values: bfloat16 [8, 1024, 512], P(None, ('ctx', 'row')), may hold values from -6 to 6
- pool_keys: bfloat16 [512, 64, 512], P(('ctx', 'row')), may hold values from -5 to 5
- pool_values: bfloat16 [512, 64, 512], P(('ctx', 'row')), may hold values from -6 to 6
- page_table: int32 [16, 32], P('row'), may hold values from 0 to 511, as said below
- suffix_len: int32 [16], P('row'), may hold values from 256 to 2048
- new_keys: bfloat16 [16, 2, 512], P('row'), may hold values from -6.25 to 6.25
- new_values: bfloat16 [16, 2, 512], P('row'), may hold values from -6 to 6
Outputs:
- attended: bfloat16 [16, 2, 4096], P('row')
Inputs may be any that keep to these rules, and one draw needn't show every extreme that they name: `page_table`: the 64 entries of the rows i with one value of i // 2 name different pool pages p with (p // 16) % (8) == i // 2, and together they name all such pages.
All inputs are finite; a program needn't handle non-finite values.
Results may differ from a plain program's by a relative error of at most 0.003.
Values may be sent and summed in bfloat16 or wider, within the bound.
No kernel may reach another device: no remote copies, remote signals or barrier semaphores. Data moves between devices by JAX's collectives and lax.ppermute only.
A program may use at most 64 MiB of HBM per device.

v0:
```python
import math

import jax
import jax.numpy as jnp
from jax import lax
from jax.sharding import PartitionSpec as P

H = 32
KVH = 4
HD = 128


MASKED_SCORE = -1e30


def joined(value, axis, join):
    pieces = jax.tree.map(lambda part: lax.all_gather(part, axis), value)
    head = jax.tree.map(lambda part: part[0], pieces)
    tail = jax.tree.map(lambda part: part[1:], pieces)
    running, _ = lax.scan(lambda running, share: (join(running, share), None), head, tail)
    return running


def combine_pair(earlier, later):
    highest = jnp.maximum(earlier[0], later[0])
    left_factor = jnp.exp(earlier[0] - highest)
    right_factor = jnp.exp(later[0] - highest)
    totals = left_factor * earlier[1] + right_factor * later[1]
    sums = left_factor[..., None] * earlier[2] + right_factor[..., None] * later[2]
    return (highest, totals, sums)


def fold_stack(stacked):
    peak_stack, total_stack, sum_stack = stacked
    highest = jnp.max(peak_stack, axis=0)
    factor = jnp.exp(peak_stack - highest[None])
    return (
        highest,
        jnp.sum(factor * total_stack, axis=0),
        jnp.sum(factor[..., None] * sum_stack, axis=0),
    )


def block_stats(scores, valid_mask, values, einsum_form):
    block_peak = jnp.max(jnp.where(valid_mask, scores, MASKED_SCORE), axis=-1)
    weights = jnp.where(valid_mask, jnp.exp(scores - block_peak[..., None]), 0.0).astype(
        jnp.bfloat16
    )
    block_total = jnp.sum(weights.astype(jnp.float32), axis=-1)
    block_sum = jnp.einsum(einsum_form, weights, values, preferred_element_type=jnp.float32)
    return (block_peak, block_total, block_sum)


def heads_merged(stats):
    lead = stats[0].shape[:2]
    return (
        stats[0].reshape(lead + (H,)),
        stats[1].reshape(lead + (H,)),
        stats[2].reshape(lead + (H, HD)),
    )


def per_device(
    queries,
    prefix_id,
    prefix_keys,
    prefix_values,
    pool_keys,
    pool_values,
    page_table,
    suffix_len,
    new_keys,
    new_values,
):
    rows_dev, step_count, feature_width = queries.shape
    groups = H // KVH
    score_scale = 1.0 / math.sqrt(HD)
    row_count = lax.axis_size("row")
    row_index = lax.axis_index("row")
    flat_index = lax.axis_index("ctx") * row_count + row_index
    own_query = queries.reshape(rows_dev, step_count, KVH, groups, HD)
    slot_count, page_len, kv_width = pool_keys.shape
    slot_ids = flat_index * slot_count + jnp.arange(slot_count, dtype=jnp.int32)
    slot_match = page_table[:, :, None] == slot_ids[None, None, :]
    entry_pos = jnp.arange(page_table.shape[1], dtype=jnp.int32)
    page_of = jnp.sum(jnp.where(slot_match, entry_pos[None, :, None], 0), axis=1)
    owned = jnp.any(slot_match, axis=1)
    token_pos = (
        page_of[:, :, None] * page_len + jnp.arange(page_len, dtype=jnp.int32)[None, None, :]
    )
    live_mask = owned[:, :, None] & (token_pos < suffix_len[:, None, None])
    live_mask = live_mask.reshape(rows_dev, 1, 1, 1, slot_count * page_len)
    flat_keys = pool_keys.reshape(slot_count * page_len, KVH, HD)
    flat_values = pool_values.reshape(slot_count * page_len, KVH, HD)
    suffix_scores = (
        jnp.einsum("rskgd,tkd->rskgt", own_query, flat_keys, preferred_element_type=jnp.float32)
        * score_scale
    )
    suffix_stats = block_stats(suffix_scores, live_mask, flat_values, "rskgt,tkd->rskgd")
    fresh_keys = new_keys.reshape(rows_dev, step_count, KVH, HD)
    fresh_values = new_values.reshape(rows_dev, step_count, KVH, HD)
    fresh_scores = (
        jnp.einsum("rskgd,rtkd->rskgt", own_query, fresh_keys, preferred_element_type=jnp.float32)
        * score_scale
    )
    causal = jnp.arange(step_count)[None, :] <= jnp.arange(step_count)[:, None]
    causal = causal.reshape(1, step_count, 1, 1, step_count)
    fresh_stats = heads_merged(block_stats(fresh_scores, causal, fresh_values, "rskgt,rtkd->rskgd"))
    every_query, every_prefix = (
        lax.all_gather(queries, "row", axis=0, tiled=True),
        lax.all_gather(prefix_id, "row", axis=0, tiled=True),
    )
    total_rows = every_query.shape[0]
    span_len = prefix_keys.shape[1]
    row_keys = jnp.take(prefix_keys, every_prefix, axis=0).reshape(total_rows, span_len, KVH, HD)
    row_values = jnp.take(prefix_values, every_prefix, axis=0).reshape(
        total_rows, span_len, KVH, HD
    )
    every_row = every_query.reshape(total_rows, step_count, KVH, groups, HD)
    prefix_scores = (
        jnp.einsum("rskgd,rtkd->rskgt", every_row, row_keys, preferred_element_type=jnp.float32)
        * score_scale
    )
    always = jnp.ones((1, 1, 1, 1, span_len), dtype=bool)
    prefix_stats = block_stats(prefix_scores, always, row_values, "rskgt,rtkd->rskgd")
    row_start = row_index * rows_dev
    own_prefix = tuple(
        (lax.dynamic_slice_in_dim(member, row_start, rows_dev, 0) for member in prefix_stats)
    )
    own_merged = combine_pair(own_prefix, suffix_stats)
    whole_stats = tuple(
        (
            lax.dynamic_update_slice_in_dim(whole_arr, piece_arr, row_start, 0)
            for whole_arr, piece_arr in zip(prefix_stats, own_merged)
        )
    )
    block_peak, block_total, block_sum = heads_merged(whole_stats)
    stacked = (
        lax.all_to_all(block_peak[None], "row", split_axis=1, concat_axis=0, tiled=True),
        lax.all_to_all(block_total[None], "row", split_axis=1, concat_axis=0, tiled=True),
        lax.all_to_all(block_sum[None], "row", split_axis=1, concat_axis=0, tiled=True),
    )
    local_stats = fold_stack(stacked)
    merged = joined(local_stats, "ctx", combine_pair)
    final_stats = combine_pair(merged, fresh_stats)
    result = (final_stats[2] / final_stats[1][..., None]).astype(jnp.bfloat16)
    return result.reshape(rows_dev, step_count, H * HD)


def solution(mesh):
    in_specs = (
        P("row", None, None),
        P("row"),
        P(None, ("ctx", "row"), None),
        P(None, ("ctx", "row"), None),
        P(("ctx", "row"), None, None),
        P(("ctx", "row"), None, None),
        P("row", None),
        P("row"),
        P("row", None, None),
        P("row", None, None),
    )
    out_specs = P("row", None, None)
    return jax.shard_map(
        per_device, mesh=mesh, in_specs=in_specs, out_specs=out_specs, check_vma=False
    )
```

profile of v0, /device:TPU:0, one launch (start us, length us, event | category | flops | bytes accessed | tf_op | source)
XLA Modules:
  0.0 102.8 jit_solution(12264209918332326410)
XLA Ops:
  0.0 0.9 compare_reduce_fusion
  0.9 0.9 fusion.21
  1.8 0.6 copy-done.11
  2.4 0.6 dynamic-slice.4
  3.7 0.6 copy-done.10
  4.3 0.2 dynamic-update-slice
  4.5 13.1 %all-reduce = s32[16]{0:T(128)S(1)} all-reduce(s32[16]{0:T(128)S(1)} %dynamic-update-slice), channel_id=1, replica_groups=mesh['ctx'=4,'row'=8] {'row'}, use_global_device_ids=true, to_apply=%add | all-reduce | flops 16 | bytes 128
  17.6 30.8 %all_gather.25 = bf16[16,2,4096]{2,1,0:T(2,128)(2,1)S(1)} all-gather(bf16[2,2,4096]{2,1,0:T(2,128)(2,1)S(1)} %copy-done.4), channel_id=1, replica_groups=mesh['ctx'=4,'row'=8] {'row'}, dimensions={0}, use_global_device_ids=true | all-gather | bytes 294912 | tf_op jit(solution)/shard_map/all_gather | solution.py:110
  48.5 0.1 and.21
  48.8 0.1 add.73
  48.8 0.2 reshape.182
  49.1 0.6 gather_fusion.1
  49.7 0.4 copy-done.3
  50.0 0.6 gather_fusion
  50.6 0.2 broadcast_select_fusion
  50.8 0.1 reshape.129
  50.9 0.1 reshape.125
  51.0 0.5 fusion.31
  51.5 0.5 convert_reduce_fusion.1
  52.0 0.3 fusion.11
  52.3 0.9 copy-done.1
  53.2 0.3 reshape.127
  53.5 0.6 copy-done.8
  54.2 0.1 compare_and_fusion
  54.2 0.5 select_reduce_fusion
  54.8 0.9 convert_reduce_fusion
  55.7 0.1 copy.104
  55.8 0.1 copy.105
  55.8 0.7 reshape.185
  56.5 3.3 %all-to-all-start.1 = ((f32[8,1,128]{2,1,0:T(1,128)}), f32[8,1,128]{2,1,0:T(1,128)S(1)}, u32[]{:S(2)}, u32[]{:S(2)}) async-start(f32[8,1,128]{2,1,0:T(1,128)} %reshape.185), calls=%async_computation.1 | async-start | bytes 8192 | tf_op jit(solution)/shard_map/all_to_all | solution.py:140
  59.9 0.1 copy.98
  60.0 0.1 copy.99
  60.1 0.7 reshape.183
  60.8 0.3 reshape.130
  61.1 5.2 %all-to-all-done.1 = f32[8,1,128]{2,1,0:T(1,128)S(1)} async-done(((f32[8,1,128]{2,1,0:T(1,128)}), f32[8,1,128]{2,1,0:T(1,128)S(1)}, u32[]{:S(2)}, u32[]{:S(2)}) %all-to-all-start.1) | async-done | bytes 4128 | tf_op jit(solution)/shard_map/all_to_all | solution.py:140
  66.3 3.3 %all-to-all-start = ((f32[8,1,128]{2,1,0:T(1,128)}), f32[8,1,128]{2,1,0:T(1,128)S(1)}, u32[]{:S(2)}, u32[]{:S(2)}) async-start(f32[8,1,128]{2,1,0:T(1,128)} %reshape.183), calls=%async_computation | async-start | bytes 8192 | tf_op jit(solution)/shard_map/all_to_all | solution.py:139
  69.6 1.2 %fusion.7 = f32[16,2,4,8,128]{4,3,1,2,0:T(8,128)S(1)} fusion(f32[16,2,4,8,128]{4,3,1,2,0:T(8,128)S(1)} %copy.183, s32[]{:T(128)S(6)} %select_n.36, bf16[1024,4,128,1,1]{2,1,0,4,3:T(4,128)(2,1)S(1)} %bitcast.92, bf16[2,2,4,8,1024]{4,3,1,0,2:T(8,128)(2,1)} %get-tuple-element.77, f32[16,4,128,2,8]{2,4,3,1,0:T(8,128)S(1)} %fusion.11, ...), kind=kOutput, calls=%fused_computation.18 | convolution fusion | flops 33603584 | bytes 1458180 | tf_op jit(solution)/shard_map/rskgt,tkd->rskgd/dot_general | solution.py:50
  70.8 0.9 copy.179
  71.7 4.4 %all-to-all-done = f32[8,1,128]{2,1,0:T(1,128)S(1)} async-done(((f32[8,1,128]{2,1,0:T(1,128)}), f32[8,1,128]{2,1,0:T(1,128)S(1)}, u32[]{:S(2)}, u32[]{:S(2)}) %all-to-all-start) | async-done | bytes 4128 | tf_op jit(solution)/shard_map/all_to_all | solution.py:139
  76.1 3.6 %all-to-all-start.2 = ((f32[1,16,2,32,128]{4,3,2,0,1:T(8,128)}), f32[1,16,2,32,128]{4,3,2,0,1:T(8,128)S(1)}, u32[]{:S(2)}, u32[]{:S(2)}) async-start(f32[1,16,2,32,128]{4,3,2,0,1:T(8,128)} %bitcast.84), calls=%async_computation.2 | async-start | bytes 1048576 | tf_op jit(solution)/shard_map/all_to_all | solution.py:141
  79.8 0.3 select_reduce_fusion.1
  80.0 0.1 reshape.132
  80.1 0.1 convert_reduce_fusion.2
  80.3 0.1 reshape.135
  80.3 0.6 copy-done.7
  80.9 0.2 convolution_bitcast_fusion
  81.1 0.5 broadcast.101
  81.6 0.7 reduce.1
  82.3 0.1 reshape.186
  82.4 0.7 reduce
  83.1 0.1 reshape.184
  83.2 5.2 %all-gather.1 = f32[8,2,32]{2,1,0:T(2,128)S(1)} all-gather(f32[2,2,32]{2,1,0:T(2,128)S(1)} %copy.107), channel_id=3, replica_groups=mesh['ctx'=4,'row'=8] {'ctx'}, dimensions={0}, use_global_device_ids=true | all-gather | bytes 2560 | tf_op jit(solution)/shard_map/all_gather | solution.py:17
  88.4 0.6 copy-done.5
  89.0 5.1 %all-gather = f32[8,2,32]{2,1,0:T(2,128)S(1)} all-gather(f32[2,2,32]{2,1,0:T(2,128)S(1)} %copy.101), channel_id=2, replica_groups=mesh['ctx'=4,'row'=8] {'ctx'}, dimensions={0}, use_global_device_ids=true | all-gather | bytes 2560 | tf_op jit(solution)/shard_map/all_gather | solution.py:17
  94.1 0.6 copy-done.6
  94.8 0.2 multiply_reduce_fusion
  95.0 5.8 %all-gather.2 = f32[8,2,32,128]{3,2,1,0:T(8,128)S(1)} all-gather(f32[2,2,32,128]{3,2,1,0:T(8,128)S(1)} %multiply_reduce_fusion), channel_id=4, replica_groups=mesh['ctx'=4,'row'=8] {'ctx'}, dimensions={0}, use_global_device_ids=true | all-gather | bytes 327680 | tf_op jit(solution)/shard_map/all_gather | solution.py:17
  100.8 0.7 slice-done
  101.5 0.5 while.14
  101.5 0.1 fusion.36
  101.7 0.1 fusion.36
  101.9 0.1 fusion.36
  102.0 0.1 fusion.18
  102.1 0.6 reshape.136
  (51 shorter events, 0.6 us)
Async XLA Ops:
  0.0 49.0 %copy-start = (bf16[8,32,512]{2,1,0:T(8,128)(2,1)S(1)}, bf16[8,32,512]{2,1,0:T(8,128)(2,1)}, u32[]{:S(2)}) copy-start(bf16[8,32,512]{2,1,0:T(8,128)(2,1)} %param.17) | copy-start | bytes 786436
  0.0 17.6 %copy-start.4 = (bf16[2,2,4096]{2,1,0:T(2,128)(2,1)S(1)}, bf16[2,2,4096]{2,1,0:T(2,128)(2,1)}, u32[]{:S(2)}) copy-start(bf16[2,2,4096]{2,1,0:T(2,128)(2,1)} %param.14) | copy-start | bytes 98308
  1.8 0.7 copy-start.11
  3.7 0.7 copy-start.10
  49.1 1.0 copy-start.3
  52.0 1.2 %copy-start.1 = (bf16[16,64,512]{2,1,0:T(8,128)(2,1)S(1)}, bf16[16,64,512]{2,1,0:T(8,128)(2,1)}, u32[]{:S(2)}) copy-start(bf16[16,64,512]{2,1,0:T(8,128)(2,1)} %param.18) | copy-start | bytes 3145732
  53.5 0.7 copy-start.8
  54.8 6.0 %copy-start.2 = (bf16[16,64,512]{2,1,0:T(8,128)(2,1)S(1)}, bf16[16,64,512]{2,1,0:T(8,128)(2,1)}, u32[]{:S(2)}) copy-start(bf16[16,64,512]{2,1,0:T(8,128)(2,1)} %param.19) | copy-start | bytes 3145732
  56.5 9.7 %all-to-all-start.1 = ((f32[8,1,128]{2,1,0:T(1,128)}), f32[8,1,128]{2,1,0:T(1,128)S(1)}, u32[]{:S(2)}, u32[]{:S(2)}) async-start(f32[8,1,128]{2,1,0:T(1,128)} %reshape.185), calls=%async_computation.1 | async-start | bytes 8192 | tf_op jit(solution)/shard_map/all_to_all | solution.py:140
  66.3 9.8 %all-to-all-start = ((f32[8,1,128]{2,1,0:T(1,128)}), f32[8,1,128]{2,1,0:T(1,128)S(1)}, u32[]{:S(2)}, u32[]{:S(2)}) async-start(f32[8,1,128]{2,1,0:T(1,128)} %reshape.183), calls=%async_computation | async-start | bytes 8192 | tf_op jit(solution)/shard_map/all_to_all | solution.py:139
  76.1 3.6 %copy-start.9 = (bf16[2,2,512]{2,1,0:T(2,128)(2,1)S(1)}, bf16[2,2,512]{2,1,0:T(2,128)(2,1)}, u32[]{:S(2)}) copy-start(bf16[2,2,512]{2,1,0:T(2,128)(2,1)} %param.22) | copy-start | bytes 12292
  76.1 18.7 %all-to-all-start.2 = ((f32[1,16,2,32,128]{4,3,2,0,1:T(8,128)}), f32[1,16,2,32,128]{4,3,2,0,1:T(8,128)S(1)}, u32[]{:S(2)}, u32[]{:S(2)}) async-start(f32[1,16,2,32,128]{4,3,2,0,1:T(8,128)} %bitcast.84), calls=%async_computation.2 | async-start | bytes 1048576 | tf_op jit(solution)/shard_map/all_to_all | solution.py:141
  80.2 0.7 copy-start.7
  88.4 0.6 copy-start.5
  94.1 0.6 copy-start.6
  100.8 0.7 slice-start
  100.8 0.7 slice-start.1
where the time goes:
time: 103 us
  blocking collectives  60 us (58%)
  local copies, waits for them, and re-layouts  13.1 us (13%)
  starting transfers between devices  10.3 us (10%)
  waiting for transfers between devices  9.62 us (9%)
  other arithmetic  5.62 us (5%)
  matrix products  3.1 us (3%)
    all_gather x1, blocking collectives, per_device(): lax.all_gather(queries, 'row', axis=0, tiled=True)  30.8 us
    all_gather x3, blocking collectives, joined(): pieces = jax.tree.map(lambda part: lax.all_gather(part, axis), value)  16.1 us
    unnamed x1, blocking collectives  13.1 us
    unnamed x32, local copies, waits for them, and re-layouts  7.34 us
    all_to_all x1, waiting for transfers between devices, per_device(): lax.all_to_all(block_total[None], 'row', split_axis=1, concat_axis=0, til...  5.21 us
    all_to_all x1, waiting for transfers between devices, per_device(): lax.all_to_all(block_peak[None], 'row', split_axis=1, concat_axis=0, tile...  4.41 us
    all_to_all x1, starting transfers between devices, per_device(): lax.all_to_all(block_sum[None], 'row', split_axis=1, concat_axis=0, tiled...  3.62 us
    all_to_all x1, starting transfers between devices, per_device(): lax.all_to_all(block_total[None], 'row', split_axis=1, concat_axis=0, til...  3.32 us
  transfers between devices with their start and end apart: 3, of which 2 were waited for; matrix products, arithmetic and copies ran while one was open for 6% of the time, Pallas kernels for 0%

commit v1 on v0

v1 whole, which is shorter than its diff:
```python
import math

import jax
import jax.numpy as jnp
from jax import lax
from jax.sharding import PartitionSpec as P

H = 32
KVH = 4
HD = 128
LANES = 128


MASKED_SCORE = -1e30


def block_stats(scores, valid_mask, values, einsum_form):
    block_peak = jnp.max(jnp.where(valid_mask, scores, MASKED_SCORE), axis=-1)
    weights = jnp.where(valid_mask, jnp.exp(scores - block_peak[..., None]), 0.0).astype(
        jnp.bfloat16
    )
    block_total = jnp.sum(weights.astype(jnp.float32), axis=-1)
    block_sum = jnp.einsum(einsum_form, weights, values, preferred_element_type=jnp.float32)
    return (block_peak, block_total, block_sum)


def combine_pair(earlier, later):
    highest = jnp.maximum(earlier[0], later[0])
    left_factor = jnp.exp(earlier[0] - highest)
    right_factor = jnp.exp(later[0] - highest)
    totals = left_factor * earlier[1] + right_factor * later[1]
    sums = left_factor[..., None] * earlier[2] + right_factor[..., None] * later[2]
    return (highest, totals, sums)


def per_device(
    queries,
    prefix_id,
    prefix_keys,
    prefix_values,
    pool_keys,
    pool_values,
    page_table,
    suffix_len,
    new_keys,
    new_values,
):
    rows_dev, step_count, feature_width = queries.shape
    groups = H // KVH
    score_scale = 1.0 / math.sqrt(HD)
    row_count = lax.axis_size("row")
    ctx_count = lax.axis_size("ctx")
    row_index = lax.axis_index("row")
    ctx_index = lax.axis_index("ctx")
    flat_index = ctx_index * row_count + row_index
    own_query = queries.reshape(rows_dev, step_count, KVH, groups, HD)

    slot_count, page_len, kv_width = pool_keys.shape
    slot_ids = flat_index * slot_count + jnp.arange(slot_count, dtype=jnp.int32)
    slot_match = page_table[:, :, None] == slot_ids[None, None, :]
    entry_pos = jnp.arange(page_table.shape[1], dtype=jnp.int32)
    page_of = jnp.sum(jnp.where(slot_match, entry_pos[None, :, None], 0), axis=1)
    owned = jnp.any(slot_match, axis=1)
    token_pos = (
        page_of[:, :, None] * page_len + jnp.arange(page_len, dtype=jnp.int32)[None, None, :]
    )
    live_mask = owned[:, :, None] & (token_pos < suffix_len[:, None, None])
    live_mask = live_mask.reshape(rows_dev, 1, 1, 1, slot_count * page_len)
    flat_keys = pool_keys.reshape(slot_count * page_len, KVH, HD)
    flat_values = pool_values.reshape(slot_count * page_len, KVH, HD)
    suffix_scores = (
        jnp.einsum("rskgd,tkd->rskgt", own_query, flat_keys, preferred_element_type=jnp.float32)
        * score_scale
    )
    suffix_stats = block_stats(suffix_scores, live_mask, flat_values, "rskgt,tkd->rskgd")

    fresh_keys = new_keys.reshape(rows_dev, step_count, KVH, HD)
    fresh_values = new_values.reshape(rows_dev, step_count, KVH, HD)
    fresh_scores = (
        jnp.einsum("rskgd,rtkd->rskgt", own_query, fresh_keys, preferred_element_type=jnp.float32)
        * score_scale
    )
    causal = jnp.arange(step_count)[None, :] <= jnp.arange(step_count)[:, None]
    causal = causal.reshape(1, step_count, 1, 1, step_count)
    fresh_stats = block_stats(fresh_scores, causal, fresh_values, "rskgt,rtkd->rskgd")

    query_cols = step_count * feature_width
    id_cols = jnp.broadcast_to(prefix_id.astype(jnp.bfloat16)[:, None], (rows_dev, LANES))
    packed = jnp.concatenate([queries.reshape(rows_dev, query_cols), id_cols], axis=1)
    gathered = lax.all_gather(packed, "row", axis=0, tiled=True)
    total_rows = gathered.shape[0]
    every_query = gathered[:, :query_cols].reshape(total_rows, step_count, KVH, groups, HD)
    every_prefix = gathered[:, query_cols].astype(jnp.int32)

    span_len = prefix_keys.shape[1]
    row_keys = jnp.take(prefix_keys, every_prefix, axis=0).reshape(total_rows, span_len, KVH, HD)
    row_values = jnp.take(prefix_values, every_prefix, axis=0).reshape(
        total_rows, span_len, KVH, HD
    )
    prefix_scores = (
        jnp.einsum("rskgd,rtkd->rskgt", every_query, row_keys, preferred_element_type=jnp.float32)
        * score_scale
    )
    always = jnp.ones((1, 1, 1, 1, span_len), dtype=bool)
    prefix_stats = block_stats(prefix_scores, always, row_values, "rskgt,rtkd->rskgd")

    row_start = row_index * rows_dev
    own_prefix = tuple(
        lax.dynamic_slice_in_dim(member, row_start, rows_dev, 0) for member in prefix_stats
    )
    own_merged = combine_pair(own_prefix, suffix_stats)
    peak_all, total_all, sum_all = tuple(
        lax.dynamic_update_slice_in_dim(whole_arr, piece_arr, row_start, 0)
        for whole_arr, piece_arr in zip(prefix_stats, own_merged)
    )

    units = rows_dev * step_count * H
    share = units // ctx_count
    pt_rows = -(-2 * share // LANES)
    peak_u = peak_all.reshape(row_count, ctx_count, share)
    total_u = total_all.reshape(row_count, ctx_count, share)
    sum_u = sum_all.reshape(row_count, ctx_count, share, HD)
    pt = jnp.concatenate([peak_u, total_u], axis=-1)
    pt = jnp.pad(pt, ((0, 0), (0, 0), (0, pt_rows * LANES - 2 * share)))
    pt = pt.reshape(row_count, ctx_count, pt_rows, LANES)
    outgoing = jnp.concatenate([sum_u, pt], axis=2)
    outgoing = jnp.swapaxes(outgoing, 0, 1).reshape(ctx_count * row_count, share + pt_rows, LANES)
    incoming = lax.all_to_all(
        outgoing, ("ctx", "row"), split_axis=0, concat_axis=0, tiled=True
    )
    sources = incoming.shape[0]
    got_sum = incoming[:, :share, :]
    got_pt = incoming[:, share:, :].reshape(sources, pt_rows * LANES)
    got_peak = got_pt[:, :share]
    got_total = got_pt[:, share : 2 * share]

    unit_start = ctx_index * share
    fresh_peak = lax.dynamic_slice_in_dim(fresh_stats[0].reshape(units), unit_start, share)
    fresh_total = lax.dynamic_slice_in_dim(fresh_stats[1].reshape(units), unit_start, share)
    fresh_sum = lax.dynamic_slice_in_dim(fresh_stats[2].reshape(units, HD), unit_start, share)

    top = jnp.maximum(jnp.max(got_peak, axis=0), fresh_peak)
    factor = jnp.exp(got_peak - top[None])
    fresh_factor = jnp.exp(fresh_peak - top)
    denom = jnp.sum(factor * got_total, axis=0) + fresh_factor * fresh_total
    numer = jnp.sum(factor[..., None] * got_sum, axis=0) + fresh_factor[..., None] * fresh_sum
    result = (numer / denom[..., None]).astype(jnp.bfloat16)
    whole = lax.all_gather(result, "ctx", axis=0, tiled=True)
    return whole.reshape(rows_dev, step_count, H * HD)


def solution(mesh):
    in_specs = (
        P("row", None, None),
        P("row"),
        P(None, ("ctx", "row"), None),
        P(None, ("ctx", "row"), None),
        P(("ctx", "row"), None, None),
        P(("ctx", "row"), None, None),
        P("row", None),
        P("row"),
        P("row", None, None),
        P("row", None, None),
    )
    out_specs = P("row", None, None)
    return jax.shard_map(
        per_device, mesh=mesh, in_specs=in_specs, out_specs=out_specs, check_vma=False
    )
```

time: 103 us -> 78.4 us (0.76)
  blocking collectives: 60 us -> 37.7 us
  waiting for transfers between devices: 9.62 us -> 18.3 us
  starting transfers between devices: 10.3 us -> 5.54 us
  local copies, waits for them, and re-layouts: 13.1 us -> 8.64 us
  other arithmetic: 5.62 us -> 4.24 us
    unnamed x1 -> x0, blocking collectives: 13.1 us -> none
    all_gather x4 -> x2, blocking collectives: 46.9 us -> 37.7 us  [the longest x1 32.5 us: per_device(): gathered = lax.all_gather(packed, 'row', axis=0, tiled=True)]
    all_to_all x3 -> x1, waiting for transfers between devices: 9.62 us -> 18.3 us  [per_device(): lax.all_to_all(outgoing, ('ctx', 'row'), split_axis=0, concat_axis=0, til...]
    all_to_all x3 -> x1, starting transfers between devices: 10.3 us -> 5.54 us  [per_device(): lax.all_to_all(outgoing, ('ctx', 'row'), split_axis=0, concat_axis=0, til...]
    unnamed x32 -> x31, local copies, waits for them, and re-layouts: 7.34 us -> 3.59 us
    all_to_all x2 -> x0, other arithmetic: 1.32 us -> none  [the longest x1 0.66 us: per_device(): lax.all_to_all(block_peak[None], 'row', split_axis=1, concat_axis=0, tile...]
    reshape x4 -> x6, local copies, waits for them, and re-layouts: 1.01 us -> 2.16 us  [the longest x1 1.15 us: per_device(): jnp.swapaxes(outgoing, 0, 1)]
  transfers between devices with their start and end apart: 3 -> 1, of which waited for: 2 -> 1; matrix products, arithmetic and copies ran while one was open for 6% -> 1% of each run, Pallas kernels for 0% -> 0%
where the time goes in v1:
time: 78.4 us; the launch traced here: 77.9 us
  blocking collectives  37.7 us (48%)
  waiting for transfers between devices  18.3 us (23%)
  local copies, waits for them, and re-layouts  8.64 us (11%)
  starting transfers between devices  5.54 us (7%)
  other arithmetic  4.24 us (5%)
  matrix products  3.09 us (4%)
    all_gather x1, blocking collectives, per_device(): gathered = lax.all_gather(packed, 'row', axis=0, tiled=True)  32.5 us
    all_to_all x1, waiting for transfers between devices, per_device(): lax.all_to_all(outgoing, ('ctx', 'row'), split_axis=0, concat_axis=0, til...  18.3 us
    all_to_all x1, starting transfers between devices, per_device(): lax.all_to_all(outgoing, ('ctx', 'row'), split_axis=0, concat_axis=0, til...  5.54 us
    all_gather x1, blocking collectives, per_device(): whole = lax.all_gather(result, 'ctx', axis=0, tiled=True)  5.18 us
    unnamed x31, local copies, waits for them, and re-layouts  3.59 us
    dot_general x3, matrix products, block_stats(): jnp.einsum(einsum_form, weights, values, preferred_element_type=jnp.float32)  1.75 us
  transfers between devices with their start and end apart: 1, of which 1 were waited for; matrix products, arithmetic and copies ran while one was open for 1% of the time, Pallas kernels for 0%

profile of v1, /device:TPU:0, one launch (start us, length us, event | category | flops | bytes accessed | tf_op | source)
XLA Modules:
  0.0 77.9 jit_solution(5196668622109800049)
XLA Ops:
  0.0 0.7 convert_element_type.32
  0.7 0.8 %copy.117 = bf16[1,2,2,4096]{3,1,2,0:T(2,128)(2,1)S(1)} copy(bf16[1,2,2,4096]{3,2,1,0:T(2,128)(2,1)} %bitcast.69) | data formatting | bytes 65536
  1.5 0.1 broadcast_in_dim.96
  1.6 32.5 %all-gather = bf16[8,2,8320]{2,1,0:T(2,128)(2,1)S(1)} all-gather(bf16[1,2,8320]{2,1,0:T(2,128)(2,1)S(1)} %maximum_bitcast_fusion.1), channel_id=1, replica_groups=mesh['ctx'=4,'row'=8] {'row'}, dimensions={0}, use_global_device_ids=true | all-gather | bytes 299520 | tf_op jit(solution)/shard_map/all_gather | solution.py:90
  34.2 0.1 reshape.165
  34.3 0.1 convert_reduce_fusion.3
  34.4 0.0 copy-start.4
  34.4 0.0 copy-start.10
  34.5 0.7 copy-done.10
  35.1 0.2 compare_reduce_fusion
  35.3 0.2 fusion.16
  35.5 0.0 copy-start.5
  35.6 0.0 copy-start.3
  35.6 0.6 gather_fusion
  36.2 0.4 copy-done.3
  36.5 0.6 gather_fusion.1
  37.1 0.2 broadcast_select_fusion.1
  37.3 0.1 reshape.127
  37.5 0.1 reshape.128
  37.6 0.5 fusion.22
  38.1 0.5 convert_reduce_fusion.1
  38.6 0.0 copy-start.1
  38.6 0.3 fusion.10
  38.9 0.1 and.20
  39.0 0.1 and.21
  39.1 0.1 add.70
  39.2 0.1 add.71
  39.2 0.1 add.73
  39.3 0.5 copy-done.1
  39.8 0.3 reshape.130
  40.1 0.0 copy-start.11
  40.1 0.6 copy-done.11
  40.7 0.1 compare_and_fusion
  40.8 0.0 copy-done.5
  40.8 0.5 select_reduce_fusion
  41.4 0.9 %convert_reduce_fusion = (f32[2,2,4,8]{3,1,0,2:T(2,128)S(1)}, bf16[2,2,4,8,1024]{4,3,1,0,2:T(8,128)(2,1)}) fusion(f32[2,2,4,8,1024]{4,3,1,0,2:T(8,128)S(1)} %get-tuple-element.23, f32[2,2,4,8]{3,1,0,2:T(2,128)S(1)} %get-tuple-element.22, pred[2,1024]{1,0:T(4,128)(4,1)S(1)} %compare_and_fusion), kind=kLoop, calls=%fused_computation.22 | loop fusion | flops 655232 | bytes 789504 | tf_op jit(solution)/shard_map/reduce_sum | solution.py:22
  42.2 0.6 fusion.19
  42.9 0.1 reshape.135
  43.0 0.1 reshape.134
  43.1 0.0 copy-done.2
  43.2 0.0 copy-start.7
  43.2 0.3 reshape.132
  43.5 0.4 copy-done.7
  43.9 0.0 copy-done.8
  43.9 1.2 %fusion.4 = f32[16,2,4,8,128]{4,3,1,2,0:T(8,128)S(1)} fusion(f32[16,2,4,8,128]{4,3,1,2,0:T(8,128)S(1)} %copy.164, s32[]{:T(128)S(6)} %select_n.41, bf16[1024,4,128,1,1]{2,1,0,4,3:T(4,128)(2,1)S(1)} %bitcast.63, bf16[2,2,4,8,1024]{4,3,1,0,2:T(8,128)(2,1)} %get-tuple-element.16, f32[16,4,128,2,8]{2,4,3,1,0:T(8,128)S(1)} %fusion.10, ...), kind=kOutput, calls=%fused_computation.10 | convolution fusion | flops 33603584 | bytes 1458180 | tf_op jit(solution)/shard_map/rskgt,tkd->rskgd/dot_general | solution.py:23
  45.1 0.1 copy.91
  45.2 0.1 select_maximum_fusion
  45.3 0.1 maximum_bitcast_fusion
  45.3 0.3 copy.161
  45.7 1.2 %copy.96 = f32[32,33,128]{2,1,0:T(8,128)} copy(f32[32,33,128]{2,0,1:T(8,128)S(1)} %bitcast.59) | data formatting | bytes 1081344 | tf_op jit(solution)/shard_map/reshape | solution.py:127
  46.8 5.5 %all-to-all-start = ((f32[32,33,128]{2,1,0:T(8,128)}), f32[32,33,128]{2,1,0:T(8,128)S(1)}, u32[]{:S(2)}, u32[]{:S(2)}) async-start(f32[32,33,128]{2,1,0:T(8,128)} %copy.96), calls=%async_computation | async-start | bytes 1310720 | tf_op jit(solution)/shard_map/all_to_all | solution.py:128
  52.4 0.3 select_reduce_fusion.1
  52.7 0.1 reshape.140
  52.8 0.1 convert_reduce_fusion.2
  52.9 0.2 convolution_bitcast_fusion
  53.1 0.1 reshape.143
  53.2 18.3 %all-to-all-done = f32[32,33,128]{2,1,0:T(8,128)S(1)} async-done(((f32[32,33,128]{2,1,0:T(8,128)}), f32[32,33,128]{2,1,0:T(8,128)S(1)}, u32[]{:S(2)}, u32[]{:S(2)}) %all-to-all-start) | async-done | bytes 540704 | tf_op jit(solution)/shard_map/all_to_all | solution.py:128
  71.6 0.1 dynamic-slice_maximum_fusion
  71.6 0.1 fusion.17
  71.7 0.1 multiply_add_fusion
  71.8 0.2 fusion.8
  72.0 0.1 divide_convert_fusion
  72.1 5.2 %all_gather.7 = bf16[128,128]{1,0:T(8,128)(2,1)S(1)} all-gather(bf16[32,128]{1,0:T(8,128)(2,1)S(1)} %divide_convert_fusion), channel_id=1, replica_groups=mesh['ctx'=4,'row'=8] {'ctx'}, dimensions={0}, use_global_device_ids=true | all-gather | bytes 40960 | tf_op jit(solution)/shard_map/all_gather | solution.py:148
  77.3 0.6 reshape.144
  (30 shorter events, 0.3 us)
Async XLA Ops:
  0.0 35.6 %copy-start = (bf16[8,32,512]{2,1,0:T(8,128)(2,1)S(1)}, bf16[8,32,512]{2,1,0:T(8,128)(2,1)}, u32[]{:S(2)}) copy-start(bf16[8,32,512]{2,1,0:T(8,128)(2,1)} %param.15) | copy-start | bytes 786436
  34.4 1.1 %copy-start.4 = (bf16[2,2,4096]{2,1,0:T(2,128)(2,1)S(1)}, bf16[2,2,4096]{2,1,0:T(2,128)(2,1)}, u32[]{:S(2)}) copy-start(bf16[2,2,4096]{2,1,0:T(2,128)(2,1)} %param.12) | copy-start | bytes 98308
  34.4 0.7 copy-start.10
  35.5 5.3 %copy-start.5 = (bf16[2,2,4,8,128]{4,3,2,1,0:T(8,128)(2,1)}, bf16[2,2,4,8,128]{4,3,2,1,0:T(8,128)(2,1)S(1)}, u32[]{:S(2)}) copy-start(bf16[2,2,4,8,128]{4,3,2,1,0:T(8,128)(2,1)S(1)} %reshape.131) | copy-start | bytes 98308
  35.6 1.0 %copy-start.3 = (bf16[8,32,512]{2,1,0:T(8,128)(2,1)S(1)}, bf16[8,32,512]{2,1,0:T(8,128)(2,1)}, u32[]{:S(2)}) copy-start(bf16[8,32,512]{2,1,0:T(8,128)(2,1)} %param.14) | copy-start | bytes 786436
  38.6 1.2 %copy-start.1 = (bf16[16,64,512]{2,1,0:T(8,128)(2,1)S(1)}, bf16[16,64,512]{2,1,0:T(8,128)(2,1)}, u32[]{:S(2)}) copy-start(bf16[16,64,512]{2,1,0:T(8,128)(2,1)} %param.16) | copy-start | bytes 3145732
  40.1 0.7 copy-start.11
  41.4 1.8 %copy-start.2 = (bf16[16,64,512]{2,1,0:T(8,128)(2,1)S(1)}, bf16[16,64,512]{2,1,0:T(8,128)(2,1)}, u32[]{:S(2)}) copy-start(bf16[16,64,512]{2,1,0:T(8,128)(2,1)} %param.17) | copy-start | bytes 3145732
  43.2 0.7 copy-start.7
  43.2 0.7 copy-start.8
  46.8 5.6 %copy-start.6 = (bf16[2,2,4,8,128]{4,3,2,1,0:T(8,128)(2,1)S(1)}, bf16[2,2,4,8,128]{4,3,2,1,0:T(8,128)(2,1)}, u32[]{:S(2)}) copy-start(bf16[2,2,4,8,128]{4,3,2,1,0:T(8,128)(2,1)} %copy-done.5) | copy-start | bytes 98308
  46.8 5.6 %copy-start.12 = (bf16[2,2,512]{2,1,0:T(2,128)(2,1)S(1)}, bf16[2,2,512]{2,1,0:T(2,128)(2,1)}, u32[]{:S(2)}) copy-start(bf16[2,2,512]{2,1,0:T(2,128)(2,1)} %param.20) | copy-start | bytes 12292
  46.8 6.1 %copy-start.9 = (bf16[2,2,512]{2,1,0:T(2,128)(2,1)S(1)}, bf16[2,2,512]{2,1,0:T(2,128)(2,1)}, u32[]{:S(2)}) copy-start(bf16[2,2,512]{2,1,0:T(2,128)(2,1)} %param.21) | copy-start | bytes 12292
  46.8 24.7 %all-to-all-start = ((f32[32,33,128]{2,1,0:T(8,128)}), f32[32,33,128]{2,1,0:T(8,128)S(1)}, u32[]{:S(2)}, u32[]{:S(2)}) async-start(f32[32,33,128]{2,1,0:T(8,128)} %copy.96), calls=%async_computation | async-start | bytes 1310720 | tf_op jit(solution)/shard_map/all_to_all | solution.py:128

commit v2 on v1

--- a/solution.py
+++ b/solution.py
@@ -87,7 +87,9 @@
     query_cols = step_count * feature_width
     id_cols = jnp.broadcast_to(prefix_id.astype(jnp.bfloat16)[:, None], (rows_dev, LANES))
     packed = jnp.concatenate([queries.reshape(rows_dev, query_cols), id_cols], axis=1)
-    gathered = lax.all_gather(packed, "row", axis=0, tiled=True)
+    fanned = jnp.broadcast_to(packed[None], (row_count,) + packed.shape)
+    gathered = lax.all_to_all(fanned, "row", split_axis=0, concat_axis=0, tiled=True)
+    gathered = gathered.reshape(row_count * rows_dev, packed.shape[1])
     total_rows = gathered.shape[0]
     every_query = gathered[:, :query_cols].reshape(total_rows, step_count, KVH, groups, HD)
     every_prefix = gathered[:, query_cols].astype(jnp.int32)

time: 78.4 us -> 56 us (0.71)
  blocking collectives: 37.7 us -> 5.18 us
  starting transfers between devices: 5.54 us -> 11.5 us
  local copies, waits for them, and re-layouts: 8.64 us -> 11.8 us
  waiting for transfers between devices: 18.3 us -> 20.1 us
  matrix products: 3.09 us -> 2.15 us
    all_gather x1 -> x0, blocking collectives: 32.5 us -> none  [per_device(): gathered = lax.all_gather(packed, 'row', axis=0, tiled=True)]
    all_to_all x0 -> x1, starting transfers between devices: none -> 7.25 us  [per_device(): lax.all_to_all(fanned, 'row', split_axis=0, concat_axis=0, tiled=True)]
    all_to_all x0 -> x1, waiting for transfers between devices: none -> 1.81 us  [per_device(): lax.all_to_all(fanned, 'row', split_axis=0, concat_axis=0, tiled=True)]
    all_to_all x1, starting transfers between devices: 5.54 us -> 4.23 us  [per_device(): lax.all_to_all(outgoing, ('ctx', 'row'), split_axis=0, concat_axis=0, til...]
    dot_general x3, matrix products: 1.75 us -> 0.81 us  [block_stats(): jnp.einsum(einsum_form, weights, values, preferred_element_type=jnp.float32)]
    reshape x1, local copies, waits for them, and re-layouts: 0.27 us -> 1.16 us  [per_device(): flat_keys = pool_keys.reshape(slot_count * page_len, KVH, HD)]
    broadcast_in_dim x0 -> x1, local copies, waits for them, and re-layouts: none -> 0.88 us  [per_device(): fanned = jnp.broadcast_to(packed[None], (row_count,) + packed.shape)]
    reshape x1, local copies, waits for them, and re-layouts: 0.29 us -> 1.11 us  [per_device(): flat_values = pool_values.reshape(slot_count * page_len, KVH, HD)]
  transfers between devices with their start and end apart: 1 -> 2, of which waited for: 1 -> 2; matrix products, arithmetic and copies ran while one was open for 1% -> 12% of each run, Pallas kernels for 0% -> 0%
where the time goes in v2:
time: 56 us; the launch traced here: 55.4 us
  waiting for transfers between devices  20.1 us (36%)
  local copies, waits for them, and re-layouts  11.8 us (21%)
  starting transfers between devices  11.5 us (21%)
  blocking collectives  5.18 us (9%)
  other arithmetic  4.47 us (8%)
  matrix products  2.15 us (4%)
    all_to_all x1, waiting for transfers between devices, per_device(): lax.all_to_all(outgoing, ('ctx', 'row'), split_axis=0, concat_axis=0, til...  18.3 us
    all_to_all x1, starting transfers between devices, per_device(): lax.all_to_all(fanned, 'row', split_axis=0, concat_axis=0, tiled=True)  7.25 us
    all_gather x1, blocking collectives, per_device(): whole = lax.all_gather(result, 'ctx', axis=0, tiled=True)  5.18 us
    all_to_all x1, starting transfers between devices, per_device(): lax.all_to_all(outgoing, ('ctx', 'row'), split_axis=0, concat_axis=0, til...  4.23 us
    unnamed x22, local copies, waits for them, and re-layouts  3.25 us
    all_to_all x1, waiting for transfers between devices, per_device(): lax.all_to_all(fanned, 'row', split_axis=0, concat_axis=0, tiled=True)  1.81 us
    reshape x1, local copies, waits for them, and re-layouts, per_device(): flat_keys = pool_keys.reshape(slot_count * page_len, KVH, HD)  1.16 us
    reshape x1, local copies, waits for them, and re-layouts, per_device(): jnp.swapaxes(outgoing, 0, 1)  1.15 us
  transfers between devices with their start and end apart: 2, of which 2 were waited for; matrix products, arithmetic and copies ran while one was open for 12% of the time, Pallas kernels for 0%

profile of v2, /device:TPU:0, one launch (start us, length us, event | category | flops | bytes accessed | tf_op | source)
XLA Modules:
  0.0 55.4 jit_solution(486517339519004090)
XLA Ops:
  0.0 0.0 copy-start
  0.0 0.0 copy-start.1
  0.0 0.8 %convert_element_type.32 = bf16[2]{0:T(256)(128)(2,1)S(1)} convert(s32[2]{0:T(128)} %param.13) | non-fusion elementwise | flops 2 | bytes 12 | tf_op jit(solution)/shard_map/convert_element_type | solution.py:88
  0.8 0.8 %copy.117 = bf16[1,2,2,4096]{3,1,2,0:T(2,128)(2,1)S(1)} copy(bf16[1,2,2,4096]{3,2,1,0:T(2,128)(2,1)} %bitcast.67) | data formatting | bytes 65536
  1.6 0.1 broadcast_in_dim.102
  1.7 0.9 %broadcast_in_dim.103 = bf16[8,2,8320]{2,1,0:T(2,128)(2,1)} broadcast(bf16[2,8320]{1,0:T(2,128)(2,1)S(1)} %pad_maximum_fusion), dimensions={1,2} | broadcast | bytes 299520 | tf_op jit(solution)/shard_map/broadcast_in_dim | solution.py:90
  2.6 7.3 %all-to-all-start = ((bf16[8,2,8320]{2,1,0:T(2,128)(2,1)}), bf16[8,2,8320]{2,1,0:T(2,128)(2,1)S(1)}, u32[]{:S(2)}, u32[]{:S(2)}) async-start(bf16[8,2,8320]{2,1,0:T(2,128)(2,1)} %broadcast_in_dim.103), calls=%async_computation | async-start | bytes 532480 | tf_op jit(solution)/shard_map/all_to_all | solution.py:91
  9.8 0.9 %compare_reduce_fusion = pred[2,16]{1,0:T(4,128)(4,1)S(1)} fusion(s32[2,32]{1,0:T(2,128)} %param.18, s32[16]{0:T(128)S(1)} %iota_add_fusion), kind=kLoop, calls=%fused_computation.37 | loop fusion | flops 2016 | bytes 352 | tf_op jit(solution)/shard_map/reduce_or | solution.py:63
  10.7 0.9 %fusion.16 = s32[2,16]{1,0:T(2,128)S(1)} fusion(s32[2,32]{1,0:T(2,128)} %param.18, s32[16]{0:T(128)S(1)} %iota_add_fusion), kind=kLoop, calls=%fused_computation.38 | loop fusion | flops 3040 | bytes 448 | tf_op jit(solution)/shard_map/reduce_sum | solution.py:62
  11.5 0.8 %reshape.136 = bf16[2,2,4,8,128]{4,3,2,1,0:T(8,128)(2,1)S(1)} reshape(bf16[2,2,4096]{2,1,0:T(2,128)(2,1)} %param.12) | data formatting | bytes 65536 | tf_op jit(solution)/shard_map/reshape | solution.py:56
  12.3 0.1 and.20
  12.4 0.1 and.21
  12.5 0.1 add.70
  12.6 0.1 add.71
  12.7 0.1 add.73
  12.7 0.0 copy-done.1
  12.7 0.0 copy-start.2
  12.7 1.2 %reshape.135 = bf16[1024,4,128]{2,1,0:T(4,128)(2,1)} reshape(bf16[16,64,512]{2,1,0:T(8,128)(2,1)S(1)} %copy-done.1) | data formatting | bytes 2097152 | tf_op jit(solution)/shard_map/reshape | solution.py:69
  13.9 0.4 copy-done.2
  14.3 1.1 %reshape.137 = bf16[1024,4,128]{2,1,0:T(4,128)(2,1)} reshape(bf16[16,64,512]{2,1,0:T(8,128)(2,1)S(1)} %copy-done.2) | data formatting | bytes 2097152 | tf_op jit(solution)/shard_map/reshape | solution.py:70
  15.5 0.7 %copy-done.7 = s32[2]{0:T(128)S(1)} copy-done((s32[2]{0:T(128)S(1)}, s32[2]{0:T(128)}, u32[]{:S(2)}) %copy-start.7) | copy-done | bytes 32
  16.1 0.1 compare_and_fusion
  16.2 0.0 copy-done.4
  16.2 0.5 select_reduce_fusion
  16.7 0.3 convert_reduce_fusion
  17.0 1.8 %all-to-all-done = bf16[8,2,8320]{2,1,0:T(2,128)(2,1)S(1)} async-done(((bf16[8,2,8320]{2,1,0:T(2,128)(2,1)}), bf16[8,2,8320]{2,1,0:T(2,128)(2,1)S(1)}, u32[]{:S(2)}, u32[]{:S(2)}) %all-to-all-start) | async-done | bytes 266272 | tf_op jit(solution)/shard_map/all_to_all | solution.py:91
  18.8 0.1 reshape.131
  18.9 0.1 convert_reduce_fusion.3
  19.1 0.0 copy-done
  19.1 0.0 copy-start.5
  19.1 0.6 %gather_fusion = bf16[16,32,512]{2,1,0:T(8,128)(2,1)S(1)} fusion(bf16[8,32,512]{2,1,0:T(8,128)(2,1)S(1)} %copy-done, s32[1024]{0:T(1024)S(1)} %pad_clamp_fusion), kind=kCustom, calls=%fused_computation.clone | custom fusion | bytes 1048640 | tf_op jit(solution)/shard_map/jit(_take)/gather | solution.py:99
  19.7 0.4 copy-done.5
  20.1 0.6 %gather_fusion.1 = bf16[16,32,512]{2,1,0:T(8,128)(2,1)S(1)} fusion(bf16[8,32,512]{2,1,0:T(8,128)(2,1)S(1)} %copy-done.5, s32[1024]{0:T(1024)S(1)} %pad_clamp_fusion), kind=kCustom, calls=%fused_computation.1.clone | custom fusion | bytes 1048640 | tf_op jit(solution)/shard_map/jit(_take)/gather | solution.py:98
  20.6 0.2 broadcast_select_fusion.1
  20.8 0.1 reshape.132
  21.0 0.1 reshape.133
  21.1 0.5 fusion.22
  21.6 0.5 convert_reduce_fusion.1
  22.1 0.3 fusion.10
  22.5 0.1 reshape.140
  22.6 0.1 reshape.139
  22.8 0.9 %copy-done.3 = bf16[1024,4,128]{2,1,0:T(4,128)(2,1)S(1)} copy-done((bf16[1024,4,128]{2,1,0:T(4,128)(2,1)S(1)}, bf16[1024,4,128]{2,1,0:T(4,128)(2,1)}, u32[]{:S(2)}) %copy-start.3) | copy-done | bytes 1048600
  23.7 0.3 fusion.4
  24.0 0.1 copy.91
  24.0 0.1 select_maximum_fusion
  24.1 0.1 maximum_bitcast_fusion
  24.2 0.3 copy.161
  24.5 1.2 %copy.96 = f32[32,33,128]{2,1,0:T(8,128)} copy(f32[32,33,128]{2,0,1:T(8,128)S(1)} %bitcast.57) | data formatting | bytes 1081344 | tf_op jit(solution)/shard_map/reshape | solution.py:129
  25.6 4.2 %all-to-all-start.1 = ((f32[32,33,128]{2,1,0:T(8,128)}), f32[32,33,128]{2,1,0:T(8,128)S(1)}, u32[]{:S(2)}, u32[]{:S(2)}) async-start(f32[32,33,128]{2,1,0:T(8,128)} %copy.96), calls=%async_computation.1 | async-start | bytes 1310720 | tf_op jit(solution)/shard_map/all_to_all | solution.py:130
  29.9 0.0 copy-done.8
  29.9 0.3 select_reduce_fusion.1
  30.2 0.1 reshape.145
  30.3 0.1 convert_reduce_fusion.2
  30.4 0.0 copy-done.6
  30.4 0.2 convolution_bitcast_fusion
  30.6 0.1 reshape.148
  30.7 18.3 %all-to-all-done.1 = f32[32,33,128]{2,1,0:T(8,128)S(1)} async-done(((f32[32,33,128]{2,1,0:T(8,128)}), f32[32,33,128]{2,1,0:T(8,128)S(1)}, u32[]{:S(2)}, u32[]{:S(2)}) %all-to-all-start.1) | async-done | bytes 540704 | tf_op jit(solution)/shard_map/all_to_all | solution.py:130
  49.1 0.1 dynamic-slice_maximum_fusion
  49.2 0.1 fusion.17
  49.3 0.1 multiply_add_fusion
  49.3 0.2 fusion.8
  49.6 0.1 divide_convert_fusion
  49.6 5.2 %all_gather.3 = bf16[128,128]{1,0:T(8,128)(2,1)S(1)} all-gather(bf16[32,128]{1,0:T(8,128)(2,1)S(1)} %divide_convert_fusion), channel_id=1, replica_groups=mesh['ctx'=4,'row'=8] {'ctx'}, dimensions={0}, use_global_device_ids=true | all-gather | bytes 40960 | tf_op jit(solution)/shard_map/all_gather | solution.py:150
  54.8 0.6 %reshape.149 = bf16[2,2,4096]{2,1,0:T(2,128)(2,1)} reshape(bf16[128,128]{1,0:T(8,128)(2,1)S(1)} %all_gather.3) | data formatting | bytes 65536 | tf_op jit(solution)/shard_map/reshape | solution.py:151
  (24 shorter events, 0.3 us)
Async XLA Ops:
  0.0 19.1 %copy-start = (bf16[8,32,512]{2,1,0:T(8,128)(2,1)S(1)}, bf16[8,32,512]{2,1,0:T(8,128)(2,1)}, u32[]{:S(2)}) copy-start(bf16[8,32,512]{2,1,0:T(8,128)(2,1)} %param.15) | copy-start | bytes 786436
  0.0 12.7 %copy-start.1 = (bf16[16,64,512]{2,1,0:T(8,128)(2,1)S(1)}, bf16[16,64,512]{2,1,0:T(8,128)(2,1)}, u32[]{:S(2)}) copy-start(bf16[16,64,512]{2,1,0:T(8,128)(2,1)} %param.16) | copy-start | bytes 3145732
  2.6 16.3 %all-to-all-start = ((bf16[8,2,8320]{2,1,0:T(2,128)(2,1)}), bf16[8,2,8320]{2,1,0:T(2,128)(2,1)S(1)}, u32[]{:S(2)}, u32[]{:S(2)}) async-start(bf16[8,2,8320]{2,1,0:T(2,128)(2,1)} %broadcast_in_dim.103), calls=%async_computation | async-start | bytes 532480 | tf_op jit(solution)/shard_map/all_to_all | solution.py:91
  12.7 1.6 %copy-start.2 = (bf16[16,64,512]{2,1,0:T(8,128)(2,1)S(1)}, bf16[16,64,512]{2,1,0:T(8,128)(2,1)}, u32[]{:S(2)}) copy-start(bf16[16,64,512]{2,1,0:T(8,128)(2,1)} %param.17) | copy-start | bytes 3145732
  14.3 1.9 %copy-start.4 = (bf16[1024,4,128]{2,1,0:T(4,128)(2,1)S(1)}, bf16[1024,4,128]{2,1,0:T(4,128)(2,1)}, u32[]{:S(2)}) copy-start(bf16[1024,4,128]{2,1,0:T(4,128)(2,1)} %reshape.135) | copy-start | bytes 3145732
  15.5 0.7 %copy-start.7 = (s32[2]{0:T(128)S(1)}, s32[2]{0:T(128)}, u32[]{:S(2)}) copy-start(s32[2]{0:T(128)} %param.19) | copy-start | bytes 28
  19.1 1.0 %copy-start.5 = (bf16[8,32,512]{2,1,0:T(8,128)(2,1)S(1)}, bf16[8,32,512]{2,1,0:T(8,128)(2,1)}, u32[]{:S(2)}) copy-start(bf16[8,32,512]{2,1,0:T(8,128)(2,1)} %param.14) | copy-start | bytes 786436
  22.4 1.2 %copy-start.3 = (bf16[1024,4,128]{2,1,0:T(4,128)(2,1)S(1)}, bf16[1024,4,128]{2,1,0:T(4,128)(2,1)}, u32[]{:S(2)}) copy-start(bf16[1024,4,128]{2,1,0:T(4,128)(2,1)} %reshape.137) | copy-start | bytes 3145732
  25.6 4.3 %copy-start.8 = (bf16[2,2,512]{2,1,0:T(2,128)(2,1)S(1)}, bf16[2,2,512]{2,1,0:T(2,128)(2,1)}, u32[]{:S(2)}) copy-start(bf16[2,2,512]{2,1,0:T(2,128)(2,1)} %param.20) | copy-start | bytes 12292
  25.6 4.8 %copy-start.6 = (bf16[2,2,512]{2,1,0:T(2,128)(2,1)S(1)}, bf16[2,2,512]{2,1,0:T(2,128)(2,1)}, u32[]{:S(2)}) copy-start(bf16[2,2,512]{2,1,0:T(2,128)(2,1)} %param.21) | copy-start | bytes 12292
  25.6 23.4 %all-to-all-start.1 = ((f32[32,33,128]{2,1,0:T(8,128)}), f32[32,33,128]{2,1,0:T(8,128)S(1)}, u32[]{:S(2)}, u32[]{:S(2)}) async-start(f32[32,33,128]{2,1,0:T(8,128)} %copy.96), calls=%async_computation.1 | async-start | bytes 1310720 | tf_op jit(solution)/shard_map/all_to_all | solution.py:130

commit v3 on v2

--- a/solution.py
+++ b/solution.py
@@ -118,23 +118,46 @@
 
     units = rows_dev * step_count * H
     share = units // ctx_count
-    pt_rows = -(-2 * share // LANES)
-    peak_u = peak_all.reshape(row_count, ctx_count, share)
-    total_u = total_all.reshape(row_count, ctx_count, share)
-    sum_u = sum_all.reshape(row_count, ctx_count, share, HD)
-    pt = jnp.concatenate([peak_u, total_u], axis=-1)
-    pt = jnp.pad(pt, ((0, 0), (0, 0), (0, pt_rows * LANES - 2 * share)))
-    pt = pt.reshape(row_count, ctx_count, pt_rows, LANES)
-    outgoing = jnp.concatenate([sum_u, pt], axis=2)
-    outgoing = jnp.swapaxes(outgoing, 0, 1).reshape(ctx_count * row_count, share + pt_rows, LANES)
+    half = share // 2
+    pt_rows = -(-2 * half // LANES)
+    dests = ctx_count * row_count
+
+    def by_dest(member, tail=()):
+        shaped = member.reshape((row_count, ctx_count, share) + tail)
+        return jnp.swapaxes(shaped, 0, 1).reshape((dests, share) + tail)
+
+    def pack(peak, total, sums):
+        pt = jnp.concatenate([peak, total], axis=-1)
+        pt = jnp.pad(pt, ((0, 0), (0, pt_rows * LANES - 2 * half)))
+        return jnp.concatenate([sums, pt.reshape(dests, pt_rows, LANES)], axis=1)
+
+    def unpack(packed):
+        pt = packed[:, half:, :].reshape(packed.shape[0], pt_rows * LANES)
+        return (pt[:, :half], pt[:, half : 2 * half], packed[:, :half, :])
+
+    core_bit = ctx_index % 2
+    peak_d, total_d, sum_d = by_dest(peak_all), by_dest(total_all), by_dest(sum_all, (HD,))
+    keep_at = core_bit * half
+    give_at = (1 - core_bit) * half
+    kept = tuple(
+        lax.dynamic_slice_in_dim(member, keep_at, half, 1) for member in (peak_d, total_d, sum_d)
+    )
+    given = pack(
+        *(lax.dynamic_slice_in_dim(member, give_at, half, 1) for member in (peak_d, total_d, sum_d))
+    )
+    partner = lax.ppermute(given, "ctx", [(c, c ^ 1) for c in range(ctx_count)])
+    chip_stats = combine_pair(kept, unpack(partner))
+    outgoing = pack(*chip_stats)
     incoming = lax.all_to_all(
         outgoing, ("ctx", "row"), split_axis=0, concat_axis=0, tiled=True
     )
-    sources = incoming.shape[0]
-    got_sum = incoming[:, :share, :]
-    got_pt = incoming[:, share:, :].reshape(sources, pt_rows * LANES)
-    got_peak = got_pt[:, :share]
-    got_total = got_pt[:, share : 2 * share]
+    got_peak, got_total, got_sum = unpack(incoming)
+    got_peak = got_peak.reshape(ctx_count // 2, 2, row_count, half)
+    got_total = got_total.reshape(ctx_count // 2, 2, row_count, half)
+    got_sum = got_sum.reshape(ctx_count // 2, 2, row_count, half, HD)
+    got_peak = jnp.swapaxes(got_peak, 1, 2).reshape(dests // 2, share)
+    got_total = jnp.swapaxes(got_total, 1, 2).reshape(dests // 2, share)
+    got_sum = jnp.swapaxes(got_sum, 1, 2).reshape(dests // 2, share, HD)
 
     unit_start = ctx_index * share
     fresh_peak = lax.dynamic_slice_in_dim(fresh_stats[0].reshape(units), unit_start, share)

time: 56 us -> 52.8 us (0.943)
  waiting for transfers between devices: 20.1 us -> 16.1 us
    all_to_all x1, waiting for transfers between devices: 18.3 us -> 12.7 us  [per_device(): lax.all_to_all(outgoing, ('ctx', 'row'), split_axis=0, concat_axis=0, til...]
    ppermute x0 -> x1, waiting for transfers between devices: none -> 1.52 us  [per_device(): partner = lax.ppermute(given, 'ctx', [(c, c ^ 1) for c in range(ctx_count)])]
    reshape x3, local copies, waits for them, and re-layouts: 1.36 us -> 0.21 us  [the longest x2 0.2 us: by_dest(): shaped = member.reshape((row_count, ctx_count, share) + tail)]
    concatenate x0 -> x1, local copies, waits for them, and re-layouts: none -> 0.9 us  [pack(): return jnp.concatenate([sums, pt.reshape(dests, pt_rows, LANES)], axis=1)]
  transfers between devices with their start and end apart: 2 -> 3, of which waited for: 2 -> 3; matrix products, arithmetic and copies ran while one was open for 12% -> 13% of each run, Pallas kernels for 0% -> 0%
where the time goes in v3:
time: 52.8 us; the launch traced here: 52.2 us
  waiting for transfers between devices  16.1 us (30%)
  local copies, waits for them, and re-layouts  12.2 us (23%)
  starting transfers between devices  11.6 us (22%)
  blocking collectives  5.19 us (10%)
  other arithmetic  4.7 us (9%)
  matrix products  2.14 us (4%)
    all_to_all x1, waiting for transfers between devices, per_device(): lax.all_to_all(outgoing, ('ctx', 'row'), split_axis=0, concat_axis=0, til...  12.7 us
    all_to_all x1, starting transfers between devices, per_device(): lax.all_to_all(fanned, 'row', split_axis=0, concat_axis=0, tiled=True)  7.25 us
    all_gather x1, blocking collectives, per_device(): whole = lax.all_gather(result, 'ctx', axis=0, tiled=True)  5.19 us
    all_to_all x1, starting transfers between devices, per_device(): lax.all_to_all(outgoing, ('ctx', 'row'), split_axis=0, concat_axis=0, til...  4.24 us
    unnamed x22, local copies, waits for them, and re-layouts  3.23 us
    all_to_all x1, waiting for transfers between devices, per_device(): lax.all_to_all(fanned, 'row', split_axis=0, concat_axis=0, tiled=True)  1.81 us
    ppermute x1, waiting for transfers between devices, per_device(): partner = lax.ppermute(given, 'ctx', [(c, c ^ 1) for c in range(ctx_count)])  1.52 us
    reshape x1, local copies, waits for them, and re-layouts, per_device(): flat_keys = pool_keys.reshape(slot_count * page_len, KVH, HD)  1.16 us
  transfers between devices with their start and end apart: 3, of which 3 were waited for; matrix products, arithmetic and copies ran while one was open for 13% of the time, Pallas kernels for 0%

profile of v3, /device:TPU:0, one launch (start us, length us, event | category | flops | bytes accessed | tf_op | source)
XLA Modules:
  0.0 52.2 jit_solution(6146757262423353453)
XLA Ops:
  0.0 0.8 %convert_element_type.33 = bf16[2]{0:T(256)(128)(2,1)S(1)} convert(s32[2]{0:T(128)} %param.13) | non-fusion elementwise | flops 2 | bytes 12 | tf_op jit(solution)/shard_map/convert_element_type | solution.py:88
  0.8 0.8 %copy.169 = bf16[1,2,2,4096]{3,1,2,0:T(2,128)(2,1)S(1)} copy(bf16[1,2,2,4096]{3,2,1,0:T(2,128)(2,1)} %bitcast.104) | data formatting | bytes 65536
  1.6 0.1 broadcast_in_dim.104
  1.7 0.9 %broadcast_in_dim.105 = bf16[8,2,8320]{2,1,0:T(2,128)(2,1)} broadcast(bf16[2,8320]{1,0:T(2,128)(2,1)S(1)} %pad_maximum_fusion.2), dimensions={1,2} | broadcast | bytes 299520 | tf_op jit(solution)/shard_map/broadcast_in_dim | solution.py:90
  2.6 7.3 %all-to-all-start = ((bf16[8,2,8320]{2,1,0:T(2,128)(2,1)}), bf16[8,2,8320]{2,1,0:T(2,128)(2,1)S(1)}, u32[]{:S(2)}, u32[]{:S(2)}) async-start(bf16[8,2,8320]{2,1,0:T(2,128)(2,1)} %broadcast_in_dim.105), calls=%async_computation | async-start | bytes 532480 | tf_op jit(solution)/shard_map/all_to_all | solution.py:91
  9.8 0.9 %compare_reduce_fusion = pred[2,16]{1,0:T(4,128)(4,1)S(1)} fusion(s32[2,32]{1,0:T(2,128)} %param.18, s32[16]{0:T(128)S(1)} %iota_add_fusion), kind=kLoop, calls=%fused_computation.40 | loop fusion | flops 2016 | bytes 352 | tf_op jit(solution)/shard_map/reduce_or | solution.py:63
  10.7 0.9 %fusion.17 = s32[2,16]{1,0:T(2,128)S(1)} fusion(s32[2,32]{1,0:T(2,128)} %param.18, s32[16]{0:T(128)S(1)} %iota_add_fusion), kind=kLoop, calls=%fused_computation.41 | loop fusion | flops 3040 | bytes 448 | tf_op jit(solution)/shard_map/reduce_sum | solution.py:62
  11.5 0.8 %reshape.184 = bf16[2,2,4,8,128]{4,3,2,1,0:T(8,128)(2,1)S(1)} reshape(bf16[2,2,4096]{2,1,0:T(2,128)(2,1)} %param.12) | data formatting | bytes 65536 | tf_op jit(solution)/shard_map/reshape | solution.py:56
  12.3 0.1 and.25
  12.4 0.1 and.26
  12.5 0.1 add.92
  12.6 0.1 add.93
  12.7 0.1 add.95
  12.7 1.2 %reshape.183 = bf16[1024,4,128]{2,1,0:T(4,128)(2,1)} reshape(bf16[16,64,512]{2,1,0:T(8,128)(2,1)S(1)} %copy-done.1) | data formatting | bytes 2097152 | tf_op jit(solution)/shard_map/reshape | solution.py:69
  13.9 0.4 copy-done.2
  14.4 1.1 %reshape.188 = bf16[1024,4,128]{2,1,0:T(4,128)(2,1)} reshape(bf16[16,64,512]{2,1,0:T(8,128)(2,1)S(1)} %copy-done.2) | data formatting | bytes 2097152 | tf_op jit(solution)/shard_map/reshape | solution.py:70
  15.5 0.7 %copy-done.7 = s32[2]{0:T(128)S(1)} copy-done((s32[2]{0:T(128)S(1)}, s32[2]{0:T(128)}, u32[]{:S(2)}) %copy-start.7) | copy-done | bytes 32
  16.1 0.1 compare_and_fusion
  16.2 0.5 %select_reduce_fusion = (f32[2,2,4,8]{3,1,0,2:T(2,128)S(1)}, f32[2,2,4,8,1024]{4,3,1,0,2:T(8,128)S(1)}) fusion(pred[2,1024]{1,0:T(4,128)(4,1)S(1)} %compare_and_fusion, bf16[2,2,4,8,128]{4,3,2,1,0:T(8,128)(2,1)S(1)} %reshape.184, bf16[1024,4,128,1,1]{2,1,0,4,3:T(4,128)(2,1)S(1)} %bitcast.93), kind=kOutput, calls=%fused_computation.23 | convolution fusion | flops 33947520 | bytes 1608192 | tf_op jit(solution)/shard_map/rskgd,tkd->rskgt/dot_general | solution.py:72
  16.8 0.3 convert_reduce_fusion
  17.0 1.8 %all-to-all-done = bf16[8,2,8320]{2,1,0:T(2,128)(2,1)S(1)} async-done(((bf16[8,2,8320]{2,1,0:T(2,128)(2,1)}), bf16[8,2,8320]{2,1,0:T(2,128)(2,1)S(1)}, u32[]{:S(2)}, u32[]{:S(2)}) %all-to-all-start) | async-done | bytes 266272 | tf_op jit(solution)/shard_map/all_to_all | solution.py:91
  18.8 0.1 reshape.180
  18.9 0.1 convert_reduce_fusion.3
  19.1 0.6 %gather_fusion.1 = bf16[16,32,512]{2,1,0:T(8,128)(2,1)S(1)} fusion(bf16[8,32,512]{2,1,0:T(8,128)(2,1)S(1)} %copy-done, s32[1024]{0:T(1024)S(1)} %pad_clamp_fusion), kind=kCustom, calls=%fused_computation.1.clone | custom fusion | bytes 1048640 | tf_op jit(solution)/shard_map/jit(_take)/gather | solution.py:99
  19.7 0.4 copy-done.5
  20.1 0.6 %gather_fusion = bf16[16,32,512]{2,1,0:T(8,128)(2,1)S(1)} fusion(bf16[8,32,512]{2,1,0:T(8,128)(2,1)S(1)} %copy-done.5, s32[1024]{0:T(1024)S(1)} %pad_clamp_fusion), kind=kCustom, calls=%fused_computation.clone | custom fusion | bytes 1048640 | tf_op jit(solution)/shard_map/jit(_take)/gather | solution.py:98
  20.6 0.2 broadcast_select_fusion
  20.8 0.1 reshape.187
  21.0 0.1 reshape.181
  21.1 0.5 fusion.28
  21.6 0.5 convert_reduce_fusion.1
  22.1 0.3 fusion.8
  22.5 0.1 reshape.191
  22.6 0.1 reshape.185
  22.8 0.9 %copy-done.3 = bf16[1024,4,128]{2,1,0:T(4,128)(2,1)S(1)} copy-done((bf16[1024,4,128]{2,1,0:T(4,128)(2,1)S(1)}, bf16[1024,4,128]{2,1,0:T(4,128)(2,1)}, u32[]{:S(2)}) %copy-start.3) | copy-done | bytes 1048600
  23.7 0.3 fusion.4
  24.0 0.3 copy.216
  24.4 0.1 constant_dynamic-slice_fusion
  24.4 0.1 fusion.20
  24.6 0.1 collective-permute-start
  24.7 1.5 %collective-permute-done = f32[32,17,128]{2,0,1:T(8,128)S(1)} collective-permute-done((f32[32,17,128]{2,0,1:T(8,128)S(1)}, f32[32,17,128]{2,0,1:T(8,128)S(1)}, u32[]{:S(2)}, u32[]{:S(2)}) %collective-permute-start) | collective-permute-done | bytes 278560 | tf_op jit(solution)/shard_map/ppermute | solution.py:148
  26.2 0.1 fusion.19
  26.3 0.1 copy.144
  26.4 0.1 fusion.18
  26.5 0.2 fusion.11
  26.7 0.9 %copy.145 = f32[32,17,128]{2,1,0:T(8,128)} copy(f32[32,17,128]{2,0,1:T(8,128)S(1)} %pad_maximum_fusion.1) | data formatting | bytes 557056 | tf_op jit(solution)/shard_map/concatenate | solution.py:132
  27.6 4.2 %all-to-all-start.1 = ((f32[32,17,128]{2,1,0:T(8,128)}), f32[32,17,128]{2,1,0:T(8,128)S(1)}, u32[]{:S(2)}, u32[]{:S(2)}) async-start(f32[32,17,128]{2,1,0:T(8,128)} %copy.145), calls=%async_computation.1 | async-start | bytes 786432 | tf_op jit(solution)/shard_map/all_to_all | solution.py:151
  31.9 0.3 select_reduce_fusion.1
  32.2 0.1 reshape.199
  32.3 0.1 convert_reduce_fusion.2
  32.4 0.2 convolution_bitcast_fusion
  32.6 0.1 reshape.204
  32.7 12.7 %all-to-all-done.1 = f32[32,17,128]{2,1,0:T(8,128)S(1)} async-done(((f32[32,17,128]{2,1,0:T(8,128)}), f32[32,17,128]{2,1,0:T(8,128)S(1)}, u32[]{:S(2)}, u32[]{:S(2)}) %all-to-all-start.1) | async-done | bytes 278560 | tf_op jit(solution)/shard_map/all_to_all | solution.py:151
  45.4 0.1 fusion.27
  45.5 0.1 reduce_max.41
  45.6 0.1 dynamic-slice_maximum_fusion
  45.7 0.1 sub.66
  45.8 0.1 copy.149
  45.9 0.2 fusion.12
  46.1 0.1 reduce_sum.64
  46.2 0.1 multiply_add_fusion
  46.3 0.1 fusion.22
  46.4 5.2 %all_gather.3 = bf16[128,128]{1,0:T(8,128)(2,1)S(1)} all-gather(bf16[32,128]{1,0:T(8,128)(2,1)S(1)} %fusion.22), channel_id=1, replica_groups=mesh['ctx'=4,'row'=8] {'ctx'}, dimensions={0}, use_global_device_ids=true | all-gather | bytes 40960 | tf_op jit(solution)/shard_map/all_gather | solution.py:173
  51.6 0.6 %reshape.205 = bf16[2,2,4096]{2,1,0:T(2,128)(2,1)} reshape(bf16[128,128]{1,0:T(8,128)(2,1)S(1)} %all_gather.3) | data formatting | bytes 65536 | tf_op jit(solution)/shard_map/reshape | solution.py:174
  (45 shorter events, 0.6 us)
Async XLA Ops:
  0.0 19.1 %copy-start = (bf16[8,32,512]{2,1,0:T(8,128)(2,1)S(1)}, bf16[8,32,512]{2,1,0:T(8,128)(2,1)}, u32[]{:S(2)}) copy-start(bf16[8,32,512]{2,1,0:T(8,128)(2,1)} %param.15) | copy-start | bytes 786436
  0.0 12.7 %copy-start.1 = (bf16[16,64,512]{2,1,0:T(8,128)(2,1)S(1)}, bf16[16,64,512]{2,1,0:T(8,128)(2,1)}, u32[]{:S(2)}) copy-start(bf16[16,64,512]{2,1,0:T(8,128)(2,1)} %param.16) | copy-start | bytes 3145732
  2.6 16.3 %all-to-all-start = ((bf16[8,2,8320]{2,1,0:T(2,128)(2,1)}), bf16[8,2,8320]{2,1,0:T(2,128)(2,1)S(1)}, u32[]{:S(2)}, u32[]{:S(2)}) async-start(bf16[8,2,8320]{2,1,0:T(2,128)(2,1)} %broadcast_in_dim.105), calls=%async_computation | async-start | bytes 532480 | tf_op jit(solution)/shard_map/all_to_all | solution.py:91
  12.7 1.6 %copy-start.2 = (bf16[16,64,512]{2,1,0:T(8,128)(2,1)S(1)}, bf16[16,64,512]{2,1,0:T(8,128)(2,1)}, u32[]{:S(2)}) copy-start(bf16[16,64,512]{2,1,0:T(8,128)(2,1)} %param.17) | copy-start | bytes 3145732
  14.4 1.9 %copy-start.4 = (bf16[1024,4,128]{2,1,0:T(4,128)(2,1)S(1)}, bf16[1024,4,128]{2,1,0:T(4,128)(2,1)}, u32[]{:S(2)}) copy-start(bf16[1024,4,128]{2,1,0:T(4,128)(2,1)} %reshape.183) | copy-start | bytes 3145732
  15.5 0.7 %copy-start.7 = (s32[2]{0:T(128)S(1)}, s32[2]{0:T(128)}, u32[]{:S(2)}) copy-start(s32[2]{0:T(128)} %param.19) | copy-start | bytes 28
  19.1 1.0 %copy-start.5 = (bf16[8,32,512]{2,1,0:T(8,128)(2,1)S(1)}, bf16[8,32,512]{2,1,0:T(8,128)(2,1)}, u32[]{:S(2)}) copy-start(bf16[8,32,512]{2,1,0:T(8,128)(2,1)} %param.14) | copy-start | bytes 786436
  22.4 1.2 %copy-start.3 = (bf16[1024,4,128]{2,1,0:T(4,128)(2,1)S(1)}, bf16[1024,4,128]{2,1,0:T(4,128)(2,1)}, u32[]{:S(2)}) copy-start(bf16[1024,4,128]{2,1,0:T(4,128)(2,1)} %reshape.188) | copy-start | bytes 3145732
  24.6 1.6 %collective-permute-start = (f32[32,17,128]{2,0,1:T(8,128)S(1)}, f32[32,17,128]{2,0,1:T(8,128)S(1)}, u32[]{:S(2)}, u32[]{:S(2)}) collective-permute-start(f32[32,17,128]{2,0,1:T(8,128)S(1)} %pad_maximum_fusion), channel_id=1, source_target_pairs={{0,8},{8,0},{16,24},{24,16},{1,9},{9,1},{17,25},{25,17},{2,10},{10... | collective-permute-start | bytes 835592 | tf_op jit(solution)/shard_map/ppermute | solution.py:148
  27.6 4.3 %copy-start.8 = (bf16[2,2,512]{2,1,0:T(2,128)(2,1)S(1)}, bf16[2,2,512]{2,1,0:T(2,128)(2,1)}, u32[]{:S(2)}) copy-start(bf16[2,2,512]{2,1,0:T(2,128)(2,1)} %param.20) | copy-start | bytes 12292
  27.6 4.8 %copy-start.6 = (bf16[2,2,512]{2,1,0:T(2,128)(2,1)S(1)}, bf16[2,2,512]{2,1,0:T(2,128)(2,1)}, u32[]{:S(2)}) copy-start(bf16[2,2,512]{2,1,0:T(2,128)(2,1)} %param.21) | copy-start | bytes 12292
  27.6 17.8 %all-to-all-start.1 = ((f32[32,17,128]{2,1,0:T(8,128)}), f32[32,17,128]{2,1,0:T(8,128)S(1)}, u32[]{:S(2)}, u32[]{:S(2)}) async-start(f32[32,17,128]{2,1,0:T(8,128)} %copy.145), calls=%async_computation.1 | async-start | bytes 786432 | tf_op jit(solution)/shard_map/all_to_all | solution.py:151

commit v4 on v3

--- a/solution.py
+++ b/solution.py
@@ -87,8 +87,12 @@
     query_cols = step_count * feature_width
     id_cols = jnp.broadcast_to(prefix_id.astype(jnp.bfloat16)[:, None], (rows_dev, LANES))
     packed = jnp.concatenate([queries.reshape(rows_dev, query_cols), id_cols], axis=1)
-    fanned = jnp.broadcast_to(packed[None], (row_count,) + packed.shape)
-    gathered = lax.all_to_all(fanned, "row", split_axis=0, concat_axis=0, tiled=True)
+    parts = [packed] + [
+        lax.ppermute(packed, "row", [(j, (j + k) % row_count) for j in range(row_count)])
+        for k in range(1, row_count)
+    ]
+    order = (row_index - jnp.arange(row_count, dtype=jnp.int32)) % row_count
+    gathered = jnp.take(jnp.stack(parts), order, axis=0)
     gathered = gathered.reshape(row_count * rows_dev, packed.shape[1])
     total_rows = gathered.shape[0]
     every_query = gathered[:, :query_cols].reshape(total_rows, step_count, KVH, groups, HD)
@@ -170,6 +174,8 @@
     denom = jnp.sum(factor * got_total, axis=0) + fresh_factor * fresh_total
     numer = jnp.sum(factor[..., None] * got_sum, axis=0) + fresh_factor[..., None] * fresh_sum
     result = (numer / denom[..., None]).astype(jnp.bfloat16)
+    if share % H == 0:
+        result = result.reshape(share // H, H * HD)
     whole = lax.all_gather(result, "ctx", axis=0, tiled=True)
     return whole.reshape(rows_dev, step_count, H * HD)
 

time: 52.8 us -> 64.9 us (1.23)
  starting transfers between devices: 11.6 us -> 19.4 us
  local copies, waits for them, and re-layouts: 12.2 us -> 15.2 us
  other arithmetic: 4.7 us -> 6.04 us
    ppermute x0 -> x7, starting transfers between devices: none -> 13.9 us  [per_device(): lax.ppermute(packed, 'row', [(j, (j + k) % row_count) for j in range(row_...]
    all_to_all x1 -> x0, starting transfers between devices: 7.25 us -> none  [per_device(): lax.all_to_all(fanned, 'row', split_axis=0, concat_axis=0, tiled=True)]
    unnamed x22 -> x45, local copies, waits for them, and re-layouts: 3.23 us -> 6.31 us
    all_to_all x1 -> x0, waiting for transfers between devices: 1.81 us -> none  [per_device(): lax.all_to_all(fanned, 'row', split_axis=0, concat_axis=0, tiled=True)]
    ppermute x0 -> x7, waiting for transfers between devices: none -> 1.52 us  [per_device(): lax.ppermute(packed, 'row', [(j, (j + k) % row_count) for j in range(row_...]
    gather x0 -> x2, local copies, waits for them, and re-layouts: none -> 1.31 us  [per_device(): gathered = jnp.take(jnp.stack(parts), order, axis=0)]
    all_to_all x1, starting transfers between devices: 4.24 us -> 5.45 us  [per_device(): lax.all_to_all(outgoing, ('ctx', 'row'), split_axis=0, concat_axis=0, til...]
    reduce_sum x3, other arithmetic: 0.81 us -> 2.02 us  [block_stats(): block_total = jnp.sum(weights.astype(jnp.float32), axis=-1)]
  transfers between devices with their start and end apart: 3 -> 9, of which waited for: 3 -> 3; matrix products, arithmetic and copies ran while one was open for 13% -> 13% of each run, Pallas kernels for 0% -> 0%
where the time goes in v4:
time: 64.9 us; the launch traced here: 64.3 us
  starting transfers between devices  19.4 us (30%)
  waiting for transfers between devices  15.8 us (24%)
  local copies, waits for them, and re-layouts  15.2 us (23%)
  other arithmetic  6.04 us (9%)
  blocking collectives  5.25 us (8%)
  matrix products  2.14 us (3%)
    ppermute x7, starting transfers between devices, per_device(): lax.ppermute(packed, 'row', [(j, (j + k) % row_count) for j in range(row_...  13.9 us
    all_to_all x1, waiting for transfers between devices, per_device(): lax.all_to_all(outgoing, ('ctx', 'row'), split_axis=0, concat_axis=0, til...  12.7 us
    unnamed x45, local copies, waits for them, and re-layouts  6.31 us
    all_to_all x1, starting transfers between devices, per_device(): lax.all_to_all(outgoing, ('ctx', 'row'), split_axis=0, concat_axis=0, til...  5.45 us
    all_gather x1, blocking collectives, per_device(): whole = lax.all_gather(result, 'ctx', axis=0, tiled=True)  5.25 us
    reduce_sum x3, other arithmetic, block_stats(): block_total = jnp.sum(weights.astype(jnp.float32), axis=-1)  2.02 us
    ppermute x1, waiting for transfers between devices, per_device(): partner = lax.ppermute(given, 'ctx', [(c, c ^ 1) for c in range(ctx_count)])  1.52 us
    ppermute x7, waiting for transfers between devices, per_device(): lax.ppermute(packed, 'row', [(j, (j + k) % row_count) for j in range(row_...  1.52 us
  transfers between devices with their start and end apart: 9, of which 3 were waited for; matrix products, arithmetic and copies ran while one was open for 13% of the time, Pallas kernels for 0%

profile of v4, /device:TPU:0, one launch (start us, length us, event | category | flops | bytes accessed | tf_op | source)
XLA Modules:
  0.0 64.3 jit_solution(3680615447198075302)
XLA Ops:
  0.0 0.7 %convert_element_type.33 = bf16[2]{0:T(256)(128)(2,1)S(1)} convert(s32[2]{0:T(128)} %param.13) | non-fusion elementwise | flops 2 | bytes 12 | tf_op jit(solution)/shard_map/convert_element_type | solution.py:88
  0.7 0.8 %copy.171 = bf16[1,2,2,4096]{3,1,2,0:T(2,128)(2,1)S(1)} copy(bf16[1,2,2,4096]{3,2,1,0:T(2,128)(2,1)} %bitcast.124) | data formatting | bytes 65536
  1.6 3.0 %collective-permute-start = (bf16[2,8320]{1,0:T(2,128)(2,1)S(1)}, bf16[2,8320]{1,0:T(2,128)(2,1)}, u32[]{:S(2)}, u32[]{:S(2)}) collective-permute-start(bf16[2,8320]{1,0:T(2,128)(2,1)S(1)} %pad_maximum_fusion.2), channel_id=1, source_target_pairs={{0,1},{1,2},{2,3},{3,4},{4,5},{5,6},{6,7},{7,0},{8,9},{9,10},{10,1... | collective-permute-start | bytes 99848 | tf_op jit(solution)/shard_map/ppermute | solution.py:91
  4.6 1.6 %collective-permute-start.1 = (bf16[2,8320]{1,0:T(2,128)(2,1)S(1)}, bf16[2,8320]{1,0:T(2,128)(2,1)}, u32[]{:S(2)}, u32[]{:S(2)}) collective-permute-start(bf16[2,8320]{1,0:T(2,128)(2,1)S(1)} %pad_maximum_fusion.2), channel_id=1, source_target_pairs={{0,2},{1,3},{2,4},{3,5},{4,6},{5,7},{6,0},{7,1},{8,10},{9,11},{10,... | collective-permute-start | bytes 99848 | tf_op jit(solution)/shard_map/ppermute | solution.py:91
  6.2 2.6 %collective-permute-start.2 = (bf16[2,8320]{1,0:T(2,128)(2,1)S(1)}, bf16[2,8320]{1,0:T(2,128)(2,1)S(1)}, u32[]{:S(2)}, u32[]{:S(2)}) collective-permute-start(bf16[2,8320]{1,0:T(2,128)(2,1)S(1)} %pad_maximum_fusion.2), channel_id=1, source_target_pairs={{0,3},{1,4},{2,5},{3,6},{4,7},{5,0},{6,1},{7,2},{8,11},{9,12},{10,... | collective-permute-start | bytes 99848 | tf_op jit(solution)/shard_map/ppermute | solution.py:91
  8.8 1.2 %collective-permute-start.3 = (bf16[2,8320]{1,0:T(2,128)(2,1)S(1)}, bf16[2,8320]{1,0:T(2,128)(2,1)S(1)}, u32[]{:S(2)}, u32[]{:S(2)}) collective-permute-start(bf16[2,8320]{1,0:T(2,128)(2,1)S(1)} %pad_maximum_fusion.2), channel_id=1, source_target_pairs={{0,4},{1,5},{2,6},{3,7},{4,0},{5,1},{6,2},{7,3},{8,12},{9,13},{10,... | collective-permute-start | bytes 99848 | tf_op jit(solution)/shard_map/ppermute | solution.py:91
  10.0 2.6 %collective-permute-start.4 = (bf16[2,8320]{1,0:T(2,128)(2,1)S(1)}, bf16[2,8320]{1,0:T(2,128)(2,1)S(1)}, u32[]{:S(2)}, u32[]{:S(2)}) collective-permute-start(bf16[2,8320]{1,0:T(2,128)(2,1)S(1)} %pad_maximum_fusion.2), channel_id=1, source_target_pairs={{0,5},{1,6},{2,7},{3,0},{4,1},{5,2},{6,3},{7,4},{8,13},{9,14},{10,... | collective-permute-start | bytes 99848 | tf_op jit(solution)/shard_map/ppermute | solution.py:91
  12.6 0.6 bitcast_dynamic-update-slice_fusion.7
  13.3 0.7 %copy-done.14 = s32[2,32]{1,0:T(2,128)S(1)} copy-done((s32[2,32]{1,0:T(2,128)S(1)}, s32[2,32]{1,0:T(2,128)}, u32[]{:S(2)}) %copy-start.14) | copy-done | bytes 280
  13.9 0.2 compare_reduce_fusion
  14.1 0.2 fusion.17
  14.4 0.6 pad_clamp_fusion.1
  15.0 0.1 and.59
  15.2 0.1 add.129
  15.4 1.4 %reshape.238 = bf16[1024,4,128]{2,1,0:T(4,128)(2,1)S(1)} reshape(bf16[16,64,512]{2,1,0:T(8,128)(2,1)} %param.16) | data formatting | bytes 2097152 | tf_op jit(solution)/shard_map/reshape | solution.py:69
  16.8 0.5 select_reduce_fusion
  17.4 1.5 %convert_reduce_fusion = (f32[2,2,4,8]{3,1,0,2:T(2,128)}, bf16[2,2,4,8,1024]{4,3,1,0,2:T(8,128)(2,1)}) fusion(f32[2,2,4,8,1024]{4,3,1,0,2:T(8,128)S(1)} %get-tuple-element.27, f32[2,2,4,8]{3,1,0,2:T(2,128)S(1)} %get-tuple-element.26, pred[2,1024]{1,0:T(4,128)(4,1)S(1)} %compare_and_fusion), kind=kLoop, calls=%fused_computation.20 | loop fusion | flops 655232 | bytes 789504 | tf_op jit(solution)/shard_map/reduce_sum | solution.py:22
  18.9 0.1 broadcast_in_dim.113
  19.1 0.3 reshape.243
  19.4 1.4 %collective-permute-start.5 = (bf16[2,8320]{1,0:T(2,128)(2,1)S(1)}, bf16[2,8320]{1,0:T(2,128)(2,1)S(1)}, u32[]{:S(2)}, u32[]{:S(2)}) collective-permute-start(bf16[2,8320]{1,0:T(2,128)(2,1)S(1)} %pad_maximum_fusion.2), channel_id=1, source_target_pairs={{0,6},{1,7},{2,0},{3,1},{4,2},{5,3},{6,4},{7,5},{8,14},{9,15},{10,... | collective-permute-start | bytes 99848 | tf_op jit(solution)/shard_map/ppermute | solution.py:91
  20.8 0.8 %bitcast_dynamic-update-slice_fusion.6 = bf16[8,2,8320]{2,1,0:T(2,128)(2,1)S(1)} fusion(bf16[8,2,8320]{2,1,0:T(2,128)(2,1)S(1)} %copy-done.5, bf16[2,8320]{1,0:T(2,128)(2,1)} %collective-permute-done), kind=kLoop, calls=%fused_computation.45 | loop fusion | bytes 66560
  21.6 1.5 %collective-permute-start.6 = (bf16[2,8320]{1,0:T(2,128)(2,1)S(1)}, bf16[2,8320]{1,0:T(2,128)(2,1)S(1)}, u32[]{:S(2)}, u32[]{:S(2)}) collective-permute-start(bf16[2,8320]{1,0:T(2,128)(2,1)S(1)} %pad_maximum_fusion.2), channel_id=1, source_target_pairs={{0,7},{1,0},{2,1},{3,2},{4,3},{5,4},{6,5},{7,6},{8,15},{9,8},{10,9... | collective-permute-start | bytes 99848 | tf_op jit(solution)/shard_map/ppermute | solution.py:91
  23.1 0.8 %bitcast_dynamic-update-slice_fusion.5 = bf16[8,2,8320]{2,1,0:T(2,128)(2,1)S(1)} fusion(bf16[8,2,8320]{2,1,0:T(2,128)(2,1)S(1)} %bitcast_dynamic-update-slice_fusion.6, bf16[2,8320]{1,0:T(2,128)(2,1)} %collective-permute-done.1), kind=kLoop, calls=%fused_computation.44 | loop fusion | bytes 66560
  24.0 1.5 %collective-permute-done.6 = bf16[2,8320]{1,0:T(2,128)(2,1)S(1)} collective-permute-done((bf16[2,8320]{1,0:T(2,128)(2,1)S(1)}, bf16[2,8320]{1,0:T(2,128)(2,1)S(1)}, u32[]{:S(2)}, u32[]{:S(2)}) %collective-permute-start.6) | collective-permute-done | bytes 33312 | tf_op jit(solution)/shard_map/ppermute | solution.py:91
  25.6 1.2 %gather_fusion = bf16[8,2,8320]{2,1,0:T(2,128)(2,1)S(1)} fusion(bf16[8,2,8320]{2,1,0:T(2,128)(2,1)S(1)} %bitcast_dynamic-update-slice_fusion, s32[1024]{0:T(1024)} %pad_clamp_fusion.1), kind=kCustom, calls=%fused_computation.2 | custom fusion | bytes 532512 | tf_op jit(solution)/shard_map/jit(_take)/gather | solution.py:95
  26.8 0.1 gather.10
  26.9 0.1 broadcast_select_fusion.2
  27.0 0.1 convert_reduce_fusion.3
  27.1 0.7 %slice_bitcast_fusion = bf16[2,8,64,128]{3,1,2,0:T(8,128)(2,1)} fusion(bf16[16,8320]{1,0:T(8,128)(2,1)S(1)} %broadcast_select_fusion.2), kind=kLoop, calls=%fused_computation.32 | loop fusion | bytes 524288
  27.9 0.6 gather_fusion.2
  28.5 0.4 copy-done.3
  28.8 0.6 gather_fusion.1
  29.4 0.2 broadcast_select_fusion
  29.6 0.9 %reshape.242 = bf16[16,32,4,128]{3,2,1,0:T(4,128)(2,1)} reshape(bf16[16,32,512]{2,1,0:T(8,128)(2,1)S(1)} %get-tuple-element.22) | data formatting | bytes 1048576 | tf_op jit(solution)/shard_map/reshape | solution.py:103
  30.6 0.1 reshape.236
  30.7 0.5 fusion.31
  31.3 0.5 convert_reduce_fusion.1
  31.7 0.6 copy-done.4
  32.3 0.3 fusion.8
  32.6 0.4 copy-done.9
  33.1 0.1 reshape.246
  33.2 0.1 reshape.240
  33.4 0.9 %copy-done.6 = bf16[2,2,4,8,1024]{4,3,1,0,2:T(8,128)(2,1)S(1)} copy-done((bf16[2,2,4,8,1024]{4,3,1,0,2:T(8,128)(2,1)S(1)}, bf16[2,2,4,8,1024]{4,3,1,0,2:T(8,128)(2,1)}, u32[]{:S(2)}) %copy-start.6) | copy-done | bytes 262168
  34.3 0.3 fusion.4
  34.6 0.3 copy.218
  35.2 1.5 %collective-permute-done.7 = f32[32,17,128]{2,0,1:T(8,128)S(1)} collective-permute-done((f32[32,17,128]{2,0,1:T(8,128)S(1)}, f32[32,17,128]{2,0,1:T(8,128)S(1)}, u32[]{:S(2)}, u32[]{:S(2)}) %collective-permute-start.7) | collective-permute-done | bytes 278560 | tf_op jit(solution)/shard_map/ppermute | solution.py:152
  36.8 0.1 fusion.19
  37.1 0.2 fusion.11
  37.3 0.9 %copy.146 = f32[32,17,128]{2,1,0:T(8,128)} copy(f32[32,17,128]{2,0,1:T(8,128)S(1)} %pad_maximum_fusion.1) | data formatting | bytes 557056 | tf_op jit(solution)/shard_map/concatenate | solution.py:136
  38.2 5.5 %all-to-all-start = ((f32[32,17,128]{2,1,0:T(8,128)}), f32[32,17,128]{2,1,0:T(8,128)S(1)}, u32[]{:S(2)}, u32[]{:S(2)}) async-start(f32[32,17,128]{2,1,0:T(8,128)} %copy.146), calls=%async_computation | async-start | bytes 786432 | tf_op jit(solution)/shard_map/all_to_all | solution.py:155
  43.7 0.3 select_reduce_fusion.1
  44.0 0.1 reshape.254
  44.1 0.1 convert_reduce_fusion.2
  44.2 0.2 convolution_bitcast_fusion
  44.4 0.1 reshape.259
  44.5 12.7 %all-to-all-done = f32[32,17,128]{2,1,0:T(8,128)S(1)} async-done(((f32[32,17,128]{2,1,0:T(8,128)}), f32[32,17,128]{2,1,0:T(8,128)S(1)}, u32[]{:S(2)}, u32[]{:S(2)}) %all-to-all-start) | async-done | bytes 278560 | tf_op jit(solution)/shard_map/all_to_all | solution.py:155
  57.3 0.1 reduce_max.41
  57.5 0.1 sub.89
  57.6 0.1 copy.150
  57.7 0.2 fusion.12
  57.9 0.1 reduce_sum.64
  58.2 5.2 %all-gather = bf16[4,1,4096]{2,1,0:T(2,128)(2,1)S(1)} all-gather(bf16[1,1,4096]{2,1,0:T(2,128)(2,1)S(1)} %reshape.289), channel_id=1, replica_groups=mesh['ctx'=4,'row'=8] {'ctx'}, dimensions={0}, use_global_device_ids=true | all-gather | bytes 40960 | tf_op jit(solution)/shard_map/all_gather | solution.py:179
  63.4 0.2 reduce.4
  63.6 0.6 reshape.261
  (89 shorter events, 2.0 us)
Async XLA Ops:
  0.0 27.9 %copy-start = (bf16[8,32,512]{2,1,0:T(8,128)(2,1)S(1)}, bf16[8,32,512]{2,1,0:T(8,128)(2,1)}, u32[]{:S(2)}) copy-start(bf16[8,32,512]{2,1,0:T(8,128)(2,1)} %param.15) | copy-start | bytes 786436
  1.6 12.7 %copy-start.7 = (bf16[2,2,4096]{2,1,0:T(2,128)(2,1)S(1)}, bf16[2,2,4096]{2,1,0:T(2,128)(2,1)}, u32[]{:S(2)}) copy-start(bf16[2,2,4096]{2,1,0:T(2,128)(2,1)} %param.12) | copy-start | bytes 98308
  1.6 17.7 %collective-permute-start = (bf16[2,8320]{1,0:T(2,128)(2,1)S(1)}, bf16[2,8320]{1,0:T(2,128)(2,1)}, u32[]{:S(2)}, u32[]{:S(2)}) collective-permute-start(bf16[2,8320]{1,0:T(2,128)(2,1)S(1)} %pad_maximum_fusion.2), channel_id=1, source_target_pairs={{0,1},{1,2},{2,3},{3,4},{4,5},{5,6},{6,7},{7,0},{8,9},{9,10},{10,1... | collective-permute-start | bytes 99848 | tf_op jit(solution)/shard_map/ppermute | solution.py:91
  4.6 16.9 %collective-permute-start.1 = (bf16[2,8320]{1,0:T(2,128)(2,1)S(1)}, bf16[2,8320]{1,0:T(2,128)(2,1)}, u32[]{:S(2)}, u32[]{:S(2)}) collective-permute-start(bf16[2,8320]{1,0:T(2,128)(2,1)S(1)} %pad_maximum_fusion.2), channel_id=1, source_target_pairs={{0,2},{1,3},{2,4},{3,5},{4,6},{5,7},{6,0},{7,1},{8,10},{9,11},{10,... | collective-permute-start | bytes 99848 | tf_op jit(solution)/shard_map/ppermute | solution.py:91
  6.2 17.7 %collective-permute-start.2 = (bf16[2,8320]{1,0:T(2,128)(2,1)S(1)}, bf16[2,8320]{1,0:T(2,128)(2,1)S(1)}, u32[]{:S(2)}, u32[]{:S(2)}) collective-permute-start(bf16[2,8320]{1,0:T(2,128)(2,1)S(1)} %pad_maximum_fusion.2), channel_id=1, source_target_pairs={{0,3},{1,4},{2,5},{3,6},{4,7},{5,0},{6,1},{7,2},{8,11},{9,12},{10,... | collective-permute-start | bytes 99848 | tf_op jit(solution)/shard_map/ppermute | solution.py:91
  8.8 15.1 %collective-permute-start.3 = (bf16[2,8320]{1,0:T(2,128)(2,1)S(1)}, bf16[2,8320]{1,0:T(2,128)(2,1)S(1)}, u32[]{:S(2)}, u32[]{:S(2)}) collective-permute-start(bf16[2,8320]{1,0:T(2,128)(2,1)S(1)} %pad_maximum_fusion.2), channel_id=1, source_target_pairs={{0,4},{1,5},{2,6},{3,7},{4,0},{5,1},{6,2},{7,3},{8,12},{9,13},{10,... | collective-permute-start | bytes 99848 | tf_op jit(solution)/shard_map/ppermute | solution.py:91
  10.0 14.0 %collective-permute-start.4 = (bf16[2,8320]{1,0:T(2,128)(2,1)S(1)}, bf16[2,8320]{1,0:T(2,128)(2,1)S(1)}, u32[]{:S(2)}, u32[]{:S(2)}) collective-permute-start(bf16[2,8320]{1,0:T(2,128)(2,1)S(1)} %pad_maximum_fusion.2), channel_id=1, source_target_pairs={{0,5},{1,6},{2,7},{3,0},{4,1},{5,2},{6,3},{7,4},{8,13},{9,14},{10,... | collective-permute-start | bytes 99848 | tf_op jit(solution)/shard_map/ppermute | solution.py:91
  13.3 0.7 %copy-start.14 = (s32[2,32]{1,0:T(2,128)S(1)}, s32[2,32]{1,0:T(2,128)}, u32[]{:S(2)}) copy-start(s32[2,32]{1,0:T(2,128)} %param.18) | copy-start | bytes 772
  14.3 2.5 %copy-start.11 = (bf16[2,2,4,8,128]{4,3,2,1,0:T(8,128)(2,1)}, bf16[2,2,4,8,128]{4,3,2,1,0:T(8,128)(2,1)S(1)}, u32[]{:S(2)}) copy-start(bf16[2,2,4,8,128]{4,3,2,1,0:T(8,128)(2,1)S(1)} %reshape.239) | copy-start | bytes 98308
  15.4 1.4 %copy-start.15 = (s32[2]{0:T(128)S(1)}, s32[2]{0:T(128)}, u32[]{:S(2)}) copy-start(s32[2]{0:T(128)} %param.19) | copy-start | bytes 28
  16.8 2.2 %copy-start.1 = (bf16[16,64,512]{2,1,0:T(8,128)(2,1)S(1)}, bf16[16,64,512]{2,1,0:T(8,128)(2,1)}, u32[]{:S(2)}) copy-start(bf16[16,64,512]{2,1,0:T(8,128)(2,1)} %param.17) | copy-start | bytes 3145732
  17.4 1.5 %copy-start.8 = (f32[2,2,4,8]{3,1,0,2:T(2,128)}, f32[2,2,4,8]{3,1,0,2:T(2,128)S(1)}, u32[]{:S(2)}) copy-start(f32[2,2,4,8]{3,1,0,2:T(2,128)S(1)} %get-tuple-element.26) | copy-start | bytes 1540
  19.0 1.7 %copy-start.5 = (bf16[8,2,8320]{2,1,0:T(2,128)(2,1)S(1)}, bf16[8,2,8320]{2,1,0:T(2,128)(2,1)}, u32[]{:S(2)}) copy-start(bf16[8,2,8320]{2,1,0:T(2,128)(2,1)} %bitcast_dynamic-update-slice_fusion.7) | copy-start | bytes 798724
  19.4 4.6 %collective-permute-start.5 = (bf16[2,8320]{1,0:T(2,128)(2,1)S(1)}, bf16[2,8320]{1,0:T(2,128)(2,1)S(1)}, u32[]{:S(2)}, u32[]{:S(2)}) collective-permute-start(bf16[2,8320]{1,0:T(2,128)(2,1)S(1)} %pad_maximum_fusion.2), channel_id=1, source_target_pairs={{0,6},{1,7},{2,0},{3,1},{4,2},{5,3},{6,4},{7,5},{8,14},{9,15},{10,... | collective-permute-start | bytes 99848 | tf_op jit(solution)/shard_map/ppermute | solution.py:91
  21.6 4.0 %collective-permute-start.6 = (bf16[2,8320]{1,0:T(2,128)(2,1)S(1)}, bf16[2,8320]{1,0:T(2,128)(2,1)S(1)}, u32[]{:S(2)}, u32[]{:S(2)}) collective-permute-start(bf16[2,8320]{1,0:T(2,128)(2,1)S(1)} %pad_maximum_fusion.2), channel_id=1, source_target_pairs={{0,7},{1,0},{2,1},{3,2},{4,3},{5,4},{6,5},{7,6},{8,15},{9,8},{10,9... | collective-permute-start | bytes 99848 | tf_op jit(solution)/shard_map/ppermute | solution.py:91
  27.9 1.0 %copy-start.3 = (bf16[8,32,512]{2,1,0:T(8,128)(2,1)S(1)}, bf16[8,32,512]{2,1,0:T(8,128)(2,1)}, u32[]{:S(2)}) copy-start(bf16[8,32,512]{2,1,0:T(8,128)(2,1)} %param.14) | copy-start | bytes 786436
  29.6 1.0 %copy-start.2 = (bf16[2,8,64,128]{3,1,2,0:T(8,128)(2,1)S(1)}, bf16[2,8,64,128]{3,1,2,0:T(8,128)(2,1)}, u32[]{:S(2)}) copy-start(bf16[2,8,64,128]{3,1,2,0:T(8,128)(2,1)} %slice_bitcast_fusion) | copy-start | bytes 786436
  31.2 1.0 %copy-start.4 = (bf16[16,32,4,128]{3,2,1,0:T(4,128)(2,1)S(1)}, bf16[16,32,4,128]{3,2,1,0:T(4,128)(2,1)}, u32[]{:S(2)}) copy-start(bf16[16,32,4,128]{3,2,1,0:T(4,128)(2,1)} %reshape.242) | copy-start | bytes 1572868
  32.3 0.7 %copy-start.9 = (f32[2,2,4,8]{3,1,0,2:T(2,128)S(1)}, f32[2,2,4,8]{3,1,0,2:T(2,128)}, u32[]{:S(2)}) copy-start(f32[2,2,4,8]{3,1,0,2:T(2,128)} %copy-done.8) | copy-start | bytes 1540
  32.3 0.7 %copy-start.10 = (f32[2,2,4,8]{3,1,0,2:T(2,128)S(1)}, f32[2,2,4,8]{3,1,0,2:T(2,128)}, u32[]{:S(2)}) copy-start(f32[2,2,4,8]{3,1,0,2:T(2,128)} %get-tuple-element.17) | copy-start | bytes 1540
  33.3 1.0 %copy-start.6 = (bf16[2,2,4,8,1024]{4,3,1,0,2:T(8,128)(2,1)S(1)}, bf16[2,2,4,8,1024]{4,3,1,0,2:T(8,128)(2,1)}, u32[]{:S(2)}) copy-start(bf16[2,2,4,8,1024]{4,3,1,0,2:T(8,128)(2,1)} %get-tuple-element.18) | copy-start | bytes 786436
  35.1 1.6 %collective-permute-start.7 = (f32[32,17,128]{2,0,1:T(8,128)S(1)}, f32[32,17,128]{2,0,1:T(8,128)S(1)}, u32[]{:S(2)}, u32[]{:S(2)}) collective-permute-start(f32[32,17,128]{2,0,1:T(8,128)S(1)} %pad_maximum_fusion), channel_id=1, source_target_pairs={{0,8},{8,0},{16,24},{24,16},{1,9},{9,1},{17,25},{25,17},{2,10},{10... | collective-permute-start | bytes 835592 | tf_op jit(solution)/shard_map/ppermute | solution.py:152
  38.2 5.5 %copy-start.12 = (bf16[2,2,4,8,128]{4,3,2,1,0:T(8,128)(2,1)S(1)}, bf16[2,2,4,8,128]{4,3,2,1,0:T(8,128)(2,1)}, u32[]{:S(2)}) copy-start(bf16[2,2,4,8,128]{4,3,2,1,0:T(8,128)(2,1)} %copy-done.11) | copy-start | bytes 98308
  38.2 5.5 %copy-start.16 = (bf16[2,2,512]{2,1,0:T(2,128)(2,1)S(1)}, bf16[2,2,512]{2,1,0:T(2,128)(2,1)}, u32[]{:S(2)}) copy-start(bf16[2,2,512]{2,1,0:T(2,128)(2,1)} %param.20) | copy-start | bytes 12292
  38.2 6.0 %copy-start.13 = (bf16[2,2,512]{2,1,0:T(2,128)(2,1)S(1)}, bf16[2,2,512]{2,1,0:T(2,128)(2,1)}, u32[]{:S(2)}) copy-start(bf16[2,2,512]{2,1,0:T(2,128)(2,1)} %param.21) | copy-start | bytes 12292
  38.2 19.0 %all-to-all-start = ((f32[32,17,128]{2,1,0:T(8,128)}), f32[32,17,128]{2,1,0:T(8,128)S(1)}, u32[]{:S(2)}, u32[]{:S(2)}) async-start(f32[32,17,128]{2,1,0:T(8,128)} %copy.146), calls=%async_computation | async-start | bytes 786432 | tf_op jit(solution)/shard_map/all_to_all | solution.py:155

commit v5 on v3

--- a/solution.py
+++ b/solution.py
@@ -84,15 +84,19 @@
     causal = causal.reshape(1, step_count, 1, 1, step_count)
     fresh_stats = block_stats(fresh_scores, causal, fresh_values, "rskgt,rtkd->rskgd")
 
-    query_cols = step_count * feature_width
-    id_cols = jnp.broadcast_to(prefix_id.astype(jnp.bfloat16)[:, None], (rows_dev, LANES))
-    packed = jnp.concatenate([queries.reshape(rows_dev, query_cols), id_cols], axis=1)
+    query_rows = rows_dev * step_count * feature_width // LANES
+    id_rows = -(-rows_dev // 16) * 16
+    id_block = jnp.zeros((id_rows, LANES), jnp.bfloat16)
+    id_block = id_block.at[:rows_dev, :].set(
+        jnp.broadcast_to(prefix_id.astype(jnp.bfloat16)[:, None], (rows_dev, LANES))
+    )
+    packed = jnp.concatenate([queries.reshape(query_rows, LANES), id_block], axis=0)
     fanned = jnp.broadcast_to(packed[None], (row_count,) + packed.shape)
     gathered = lax.all_to_all(fanned, "row", split_axis=0, concat_axis=0, tiled=True)
-    gathered = gathered.reshape(row_count * rows_dev, packed.shape[1])
-    total_rows = gathered.shape[0]
-    every_query = gathered[:, :query_cols].reshape(total_rows, step_count, KVH, groups, HD)
-    every_prefix = gathered[:, query_cols].astype(jnp.int32)
+    total_rows = row_count * rows_dev
+    every_query = gathered[:, :query_rows, :].reshape(total_rows, step_count, KVH, groups, HD)
+    every_prefix = gathered[:, query_rows : query_rows + rows_dev, 0].reshape(total_rows)
+    every_prefix = every_prefix.astype(jnp.int32)
 
     span_len = prefix_keys.shape[1]
     row_keys = jnp.take(prefix_keys, every_prefix, axis=0).reshape(total_rows, span_len, KVH, HD)

time: 52.8 us -> 52 us (0.985)
  other arithmetic: 4.7 us -> 2.74 us
  waiting for transfers between devices: 16.1 us -> 17.7 us
  starting transfers between devices: 11.6 us -> 11 us
    all_to_all x1, waiting for transfers between devices: 1.81 us -> 3.46 us  [per_device(): lax.all_to_all(fanned, 'row', split_axis=0, concat_axis=0, tiled=True)]
    reshape x1, local copies, waits for them, and re-layouts: 0.1 us -> 0.89 us  [per_device(): queries.reshape(query_rows, LANES)]
    reshape x1, local copies, waits for them, and re-layouts: 0.79 us -> 0.03 us  [per_device(): own_query = queries.reshape(rows_dev, step_count, KVH, groups, HD)]
    convert_element_type x1, other arithmetic: 0.76 us -> 0.01 us  [per_device(): prefix_id.astype(jnp.bfloat16)[:, None]]
    reduce_or x1, other arithmetic: 0.86 us -> 0.18 us  [per_device(): owned = jnp.any(slot_match, axis=1)]
    reduce_sum x1, other arithmetic: 0.86 us -> 0.18 us  [per_device(): jnp.sum(jnp.where(slot_match, entry_pos[None, :, None], 0), axis=1)]
    all_to_all x1, starting transfers between devices: 4.24 us -> 3.63 us  [per_device(): lax.all_to_all(outgoing, ('ctx', 'row'), split_axis=0, concat_axis=0, til...]
    unnamed x22 -> x25, local copies, waits for them, and re-layouts: 3.23 us -> 3.41 us
  transfers between devices with their start and end apart: 3 -> 3, of which waited for: 3 -> 3; matrix products, arithmetic and copies ran while one was open for 13% -> 9% of each run, Pallas kernels for 0% -> 0%
where the time goes in v5:
time: 52 us; the launch traced here: 51.5 us
  waiting for transfers between devices  17.7 us (34%)
  local copies, waits for them, and re-layouts  12.3 us (24%)
  starting transfers between devices  11 us (21%)
  blocking collectives  5.19 us (10%)
  other arithmetic  2.74 us (5%)
  matrix products  2.14 us (4%)
    all_to_all x1, waiting for transfers between devices, per_device(): lax.all_to_all(outgoing, ('ctx', 'row'), split_axis=0, concat_axis=0, til...  12.7 us
    all_to_all x1, starting transfers between devices, per_device(): lax.all_to_all(fanned, 'row', split_axis=0, concat_axis=0, tiled=True)  7.26 us
    all_gather x1, blocking collectives, per_device(): whole = lax.all_gather(result, 'ctx', axis=0, tiled=True)  5.19 us
    all_to_all x1, starting transfers between devices, per_device(): lax.all_to_all(outgoing, ('ctx', 'row'), split_axis=0, concat_axis=0, til...  3.63 us
    all_to_all x1, waiting for transfers between devices, per_device(): lax.all_to_all(fanned, 'row', split_axis=0, concat_axis=0, tiled=True)  3.46 us
    unnamed x25, local copies, waits for them, and re-layouts  3.41 us
    ppermute x1, waiting for transfers between devices, per_device(): partner = lax.ppermute(given, 'ctx', [(c, c ^ 1) for c in range(ctx_count)])  1.52 us
    reshape x1, local copies, waits for them, and re-layouts, per_device(): flat_keys = pool_keys.reshape(slot_count * page_len, KVH, HD)  1.18 us
  transfers between devices with their start and end apart: 3, of which 3 were waited for; matrix products, arithmetic and copies ran while one was open for 9% of the time, Pallas kernels for 0%

profile of v5, /device:TPU:0, one launch (start us, length us, event | category | flops | bytes accessed | tf_op | source)
XLA Modules:
  0.0 51.5 jit_solution(17397109037412986040)
XLA Ops:
  0.0 0.9 %reshape.200 = bf16[128,128]{1,0:T(8,128)(2,1)S(1)} reshape(bf16[2,2,4096]{2,1,0:T(2,128)(2,1)} %param.14) | data formatting | bytes 65536 | tf_op jit(solution)/shard_map/reshape | solution.py:93
  0.9 0.1 pad_maximum_fusion.2
  1.0 0.8 %broadcast_in_dim.103 = bf16[8,144,128]{2,1,0:T(8,128)(2,1)} broadcast(bf16[144,128]{1,0:T(8,128)(2,1)S(1)} %pad_maximum_fusion.2), dimensions={1,2} | broadcast | bytes 331776 | tf_op jit(solution)/shard_map/broadcast_in_dim | solution.py:94
  1.8 7.3 %all-to-all-start = ((bf16[8,144,128]{2,1,0:T(8,128)(2,1)}), bf16[8,144,128]{2,1,0:T(8,128)(2,1)S(1)}, u32[]{:S(2)}, u32[]{:S(2)}) async-start(bf16[8,144,128]{2,1,0:T(8,128)(2,1)} %broadcast_in_dim.103), calls=%async_computation | async-start | bytes 589824 | tf_op jit(solution)/shard_map/all_to_all | solution.py:95
  9.1 0.7 %copy-done.8 = s32[2,32]{1,0:T(2,128)S(1)} copy-done((s32[2,32]{1,0:T(2,128)S(1)}, s32[2,32]{1,0:T(2,128)}, u32[]{:S(2)}) %copy-start.8) | copy-done | bytes 280
  9.7 0.2 compare_reduce_fusion
  9.9 0.2 fusion.17
  10.1 0.1 and.28
  10.2 0.1 and.29
  10.3 0.1 add.96
  10.4 0.1 add.97
  10.5 0.1 add.99
  10.5 0.6 %copy-done.9 = s32[2]{0:T(128)S(1)} copy-done((s32[2]{0:T(128)S(1)}, s32[2]{0:T(128)}, u32[]{:S(2)}) %copy-start.9) | copy-done | bytes 32
  11.1 0.1 compare_and_fusion
  11.3 1.2 %reshape.203 = bf16[1024,4,128]{2,1,0:T(4,128)(2,1)} reshape(bf16[16,64,512]{2,1,0:T(8,128)(2,1)S(1)} %copy-done.1) | data formatting | bytes 2097152 | tf_op jit(solution)/shard_map/reshape | solution.py:69
  12.4 0.4 copy-done.2
  12.8 1.1 %reshape.208 = bf16[1024,4,128]{2,1,0:T(4,128)(2,1)} reshape(bf16[16,64,512]{2,1,0:T(8,128)(2,1)S(1)} %copy-done.2) | data formatting | bytes 2097152 | tf_op jit(solution)/shard_map/reshape | solution.py:70
  13.9 0.5 copy-done.4
  14.4 0.5 %select_reduce_fusion = (f32[2,2,4,8]{3,1,0,2:T(2,128)S(1)}, f32[2,2,4,8,1024]{4,3,1,0,2:T(8,128)S(1)}) fusion(pred[2,1024]{1,0:T(4,128)(4,1)S(1)} %compare_and_fusion, bf16[2,2,4,8,128]{4,3,2,1,0:T(8,128)(2,1)S(1)} %reshape.204, bf16[1024,4,128,1,1]{2,1,0,4,3:T(4,128)(2,1)S(1)} %bitcast.88), kind=kOutput, calls=%fused_computation.23 | convolution fusion | flops 33947520 | bytes 1608192 | tf_op jit(solution)/shard_map/rskgd,tkd->rskgt/dot_general | solution.py:72
  15.0 0.3 convert_reduce_fusion
  15.2 3.5 %all-to-all-done = bf16[8,144,128]{2,1,0:T(8,128)(2,1)S(1)} async-done(((bf16[8,144,128]{2,1,0:T(8,128)(2,1)}), bf16[8,144,128]{2,1,0:T(8,128)(2,1)S(1)}, u32[]{:S(2)}, u32[]{:S(2)}) %all-to-all-start) | async-done | bytes 294944 | tf_op jit(solution)/shard_map/all_to_all | solution.py:95
  18.7 0.2 convert_reduce_fusion.3
  18.9 0.1 reshape.226
  19.0 0.6 %gather_fusion.1 = bf16[16,32,512]{2,1,0:T(8,128)(2,1)S(1)} fusion(bf16[8,32,512]{2,1,0:T(8,128)(2,1)S(1)} %copy-done, s32[1024]{0:T(1024)S(1)} %pad_clamp_fusion), kind=kCustom, calls=%fused_computation.1.clone | custom fusion | bytes 1048640 | tf_op jit(solution)/shard_map/jit(_take)/gather | solution.py:103
  19.6 0.4 copy-done.5
  20.0 0.6 %gather_fusion = bf16[16,32,512]{2,1,0:T(8,128)(2,1)S(1)} fusion(bf16[8,32,512]{2,1,0:T(8,128)(2,1)S(1)} %copy-done.5, s32[1024]{0:T(1024)S(1)} %pad_clamp_fusion), kind=kCustom, calls=%fused_computation.clone | custom fusion | bytes 1048640 | tf_op jit(solution)/shard_map/jit(_take)/gather | solution.py:102
  20.6 0.2 broadcast_select_fusion
  20.7 0.1 reshape.207
  20.9 0.1 reshape.201
  21.0 0.5 %fusion.28 = (f32[16,2,4,8]{3,1,2,0:T(2,128)S(1)}, f32[16,2,4,8,32]{4,3,1,2,0:T(8,128)S(1)}) fusion(bf16[16,2,4,8,128]{4,3,2,1,0:T(8,128)(2,1)S(1)} %bitcast.90, bf16[16,32,4,128,1]{3,2,1,0,4:T(4,128)(2,1)S(1)} %bitcast.85), kind=kOutput, calls=%fused_computation.87 | convolution fusion | flops 8453120 | bytes 921600 | tf_op jit(solution)/shard_map/rskgd,rtkd->rskgt/dot_general | solution.py:107
  21.5 0.5 convert_reduce_fusion.1
  22.0 0.3 fusion.8
  22.4 0.1 reshape.211
  22.5 0.1 reshape.205
  22.7 0.9 %copy-done.3 = bf16[1024,4,128]{2,1,0:T(4,128)(2,1)S(1)} copy-done((bf16[1024,4,128]{2,1,0:T(4,128)(2,1)S(1)}, bf16[1024,4,128]{2,1,0:T(4,128)(2,1)}, u32[]{:S(2)}) %copy-start.3) | copy-done | bytes 1048600
  23.6 0.3 fusion.4
  23.9 0.3 copy.191
  24.3 0.1 constant_dynamic-slice_fusion
  24.3 0.1 fusion.20
  24.4 0.1 collective-permute-start
  24.5 1.5 %collective-permute-done = f32[32,17,128]{2,0,1:T(8,128)S(1)} collective-permute-done((f32[32,17,128]{2,0,1:T(8,128)S(1)}, f32[32,17,128]{2,0,1:T(8,128)S(1)}, u32[]{:S(2)}, u32[]{:S(2)}) %collective-permute-start) | collective-permute-done | bytes 278560 | tf_op jit(solution)/shard_map/ppermute | solution.py:152
  26.1 0.1 fusion.19
  26.2 0.1 copy.121
  26.3 0.1 fusion.18
  26.4 0.2 fusion.11
  26.6 0.9 %copy.122 = f32[32,17,128]{2,1,0:T(8,128)} copy(f32[32,17,128]{2,0,1:T(8,128)S(1)} %pad_maximum_fusion.1) | data formatting | bytes 557056 | tf_op jit(solution)/shard_map/concatenate | solution.py:136
  27.5 3.6 %all-to-all-start.1 = ((f32[32,17,128]{2,1,0:T(8,128)}), f32[32,17,128]{2,1,0:T(8,128)S(1)}, u32[]{:S(2)}, u32[]{:S(2)}) async-start(f32[32,17,128]{2,1,0:T(8,128)} %copy.122), calls=%async_computation.1 | async-start | bytes 786432 | tf_op jit(solution)/shard_map/all_to_all | solution.py:155
  31.2 0.3 select_reduce_fusion.1
  31.5 0.1 reshape.219
  31.6 0.1 convert_reduce_fusion.2
  31.7 0.2 convolution_bitcast_fusion
  31.9 0.1 reshape.224
  32.0 12.7 %all-to-all-done.1 = f32[32,17,128]{2,1,0:T(8,128)S(1)} async-done(((f32[32,17,128]{2,1,0:T(8,128)}), f32[32,17,128]{2,1,0:T(8,128)S(1)}, u32[]{:S(2)}, u32[]{:S(2)}) %all-to-all-start.1) | async-done | bytes 278560 | tf_op jit(solution)/shard_map/all_to_all | solution.py:155
  44.7 0.1 fusion.27
  44.8 0.1 reduce_max.41
  44.9 0.1 dynamic-slice_maximum_fusion
  45.0 0.1 sub.66
  45.1 0.1 copy.126
  45.2 0.2 fusion.12
  45.4 0.1 reduce_sum.64
  45.5 0.1 multiply_add_fusion
  45.6 0.1 fusion.22
  45.7 5.2 %all_gather.3 = bf16[128,128]{1,0:T(8,128)(2,1)S(1)} all-gather(bf16[32,128]{1,0:T(8,128)(2,1)S(1)} %fusion.22), channel_id=1, replica_groups=mesh['ctx'=4,'row'=8] {'ctx'}, dimensions={0}, use_global_device_ids=true | all-gather | bytes 40960 | tf_op jit(solution)/shard_map/all_gather | solution.py:177
  50.8 0.6 %reshape.225 = bf16[2,2,4096]{2,1,0:T(2,128)(2,1)} reshape(bf16[128,128]{1,0:T(8,128)(2,1)S(1)} %all_gather.3) | data formatting | bytes 65536 | tf_op jit(solution)/shard_map/reshape | solution.py:178
  (50 shorter events, 0.6 us)
Async XLA Ops:
  0.0 19.0 %copy-start = (bf16[8,32,512]{2,1,0:T(8,128)(2,1)S(1)}, bf16[8,32,512]{2,1,0:T(8,128)(2,1)}, u32[]{:S(2)}) copy-start(bf16[8,32,512]{2,1,0:T(8,128)(2,1)} %param.17) | copy-start | bytes 786436
  0.0 0.9 %copy-start.11 = (s32[2]{0:T(128)S(1)}, s32[2]{0:T(128)}, u32[]{:S(2)}) copy-start(s32[2]{0:T(128)} %param.15) | copy-start | bytes 28
  0.0 11.2 %copy-start.1 = (bf16[16,64,512]{2,1,0:T(8,128)(2,1)S(1)}, bf16[16,64,512]{2,1,0:T(8,128)(2,1)}, u32[]{:S(2)}) copy-start(bf16[16,64,512]{2,1,0:T(8,128)(2,1)} %param.18) | copy-start | bytes 3145732
  1.8 16.9 %all-to-all-start = ((bf16[8,144,128]{2,1,0:T(8,128)(2,1)}), bf16[8,144,128]{2,1,0:T(8,128)(2,1)S(1)}, u32[]{:S(2)}, u32[]{:S(2)}) async-start(bf16[8,144,128]{2,1,0:T(8,128)(2,1)} %broadcast_in_dim.103), calls=%async_computation | async-start | bytes 589824 | tf_op jit(solution)/shard_map/all_to_all | solution.py:95
  9.1 0.7 %copy-start.8 = (s32[2,32]{1,0:T(2,128)S(1)}, s32[2,32]{1,0:T(2,128)}, u32[]{:S(2)}) copy-start(s32[2,32]{1,0:T(2,128)} %param.20) | copy-start | bytes 772
  10.4 0.8 %copy-start.6 = (bf16[2,2,4096]{2,1,0:T(2,128)(2,1)S(1)}, bf16[2,2,4096]{2,1,0:T(2,128)(2,1)}, u32[]{:S(2)}) copy-start(bf16[2,2,4096]{2,1,0:T(2,128)(2,1)} %param.14) | copy-start | bytes 98308
  10.4 0.7 %copy-start.9 = (s32[2]{0:T(128)S(1)}, s32[2]{0:T(128)}, u32[]{:S(2)}) copy-start(s32[2]{0:T(128)} %param.21) | copy-start | bytes 28
  11.2 1.6 %copy-start.2 = (bf16[16,64,512]{2,1,0:T(8,128)(2,1)S(1)}, bf16[16,64,512]{2,1,0:T(8,128)(2,1)}, u32[]{:S(2)}) copy-start(bf16[16,64,512]{2,1,0:T(8,128)(2,1)} %param.19) | copy-start | bytes 3145732
  12.8 1.6 %copy-start.4 = (bf16[1024,4,128]{2,1,0:T(4,128)(2,1)S(1)}, bf16[1024,4,128]{2,1,0:T(4,128)(2,1)}, u32[]{:S(2)}) copy-start(bf16[1024,4,128]{2,1,0:T(4,128)(2,1)} %reshape.203) | copy-start | bytes 3145732
  19.0 1.0 %copy-start.5 = (bf16[8,32,512]{2,1,0:T(8,128)(2,1)S(1)}, bf16[8,32,512]{2,1,0:T(8,128)(2,1)}, u32[]{:S(2)}) copy-start(bf16[8,32,512]{2,1,0:T(8,128)(2,1)} %param.16) | copy-start | bytes 786436
  22.3 1.2 %copy-start.3 = (bf16[1024,4,128]{2,1,0:T(4,128)(2,1)S(1)}, bf16[1024,4,128]{2,1,0:T(4,128)(2,1)}, u32[]{:S(2)}) copy-start(bf16[1024,4,128]{2,1,0:T(4,128)(2,1)} %reshape.208) | copy-start | bytes 3145732
  24.4 1.6 %collective-permute-start = (f32[32,17,128]{2,0,1:T(8,128)S(1)}, f32[32,17,128]{2,0,1:T(8,128)S(1)}, u32[]{:S(2)}, u32[]{:S(2)}) collective-permute-start(f32[32,17,128]{2,0,1:T(8,128)S(1)} %pad_maximum_fusion), channel_id=1, source_target_pairs={{0,8},{8,0},{16,24},{24,16},{1,9},{9,1},{17,25},{25,17},{2,10},{10... | collective-permute-start | bytes 835592 | tf_op jit(solution)/shard_map/ppermute | solution.py:152
  27.5 3.6 %copy-start.10 = (bf16[2,2,512]{2,1,0:T(2,128)(2,1)S(1)}, bf16[2,2,512]{2,1,0:T(2,128)(2,1)}, u32[]{:S(2)}) copy-start(bf16[2,2,512]{2,1,0:T(2,128)(2,1)} %param.22) | copy-start | bytes 12292
  27.5 4.1 %copy-start.7 = (bf16[2,2,512]{2,1,0:T(2,128)(2,1)S(1)}, bf16[2,2,512]{2,1,0:T(2,128)(2,1)}, u32[]{:S(2)}) copy-start(bf16[2,2,512]{2,1,0:T(2,128)(2,1)} %param.23) | copy-start | bytes 12292
  27.5 17.2 %all-to-all-start.1 = ((f32[32,17,128]{2,1,0:T(8,128)}), f32[32,17,128]{2,1,0:T(8,128)S(1)}, u32[]{:S(2)}, u32[]{:S(2)}) async-start(f32[32,17,128]{2,1,0:T(8,128)} %copy.122), calls=%async_computation.1 | async-start | bytes 786432 | tf_op jit(solution)/shard_map/all_to_all | solution.py:155

commit v6 on v5

--- a/solution.py
+++ b/solution.py
@@ -98,83 +98,105 @@
     every_prefix = gathered[:, query_rows : query_rows + rows_dev, 0].reshape(total_rows)
     every_prefix = every_prefix.astype(jnp.int32)
 
+    core_bit = ctx_index % 2
+    half_kv = KVH // 2
+    half_heads = H // 2
+    swap = [(c, c ^ 1) for c in range(ctx_count)]
     span_len = prefix_keys.shape[1]
-    row_keys = jnp.take(prefix_keys, every_prefix, axis=0).reshape(total_rows, span_len, KVH, HD)
-    row_values = jnp.take(prefix_values, every_prefix, axis=0).reshape(
-        total_rows, span_len, KVH, HD
-    )
-    prefix_scores = (
-        jnp.einsum("rskgd,rtkd->rskgt", every_query, row_keys, preferred_element_type=jnp.float32)
-        * score_scale
-    )
-    always = jnp.ones((1, 1, 1, 1, span_len), dtype=bool)
-    prefix_stats = block_stats(prefix_scores, always, row_values, "rskgt,rtkd->rskgd")
+    prefix_count = prefix_keys.shape[0]
+    kv_both = jnp.stack(
+        [
+            prefix_keys.reshape(prefix_count, span_len, KVH, HD),
+            prefix_values.reshape(prefix_count, span_len, KVH, HD),
+        ]
+    )
+    own_kv = lax.dynamic_slice_in_dim(kv_both, core_bit * half_kv, half_kv, 3)
+    given_kv = lax.dynamic_slice_in_dim(kv_both, (1 - core_bit) * half_kv, half_kv, 3)
+    partner_kv = lax.ppermute(given_kv, "ctx", swap)
+
+    half_query = lax.dynamic_slice_in_dim(every_query, core_bit * half_kv, half_kv, 2)
+
+    def prefix_block(kv):
+        row_keys = jnp.take(kv[0], every_prefix, axis=0)
+        row_values = jnp.take(kv[1], every_prefix, axis=0)
+        scores = (
+            jnp.einsum(
+                "rskgd,rtkd->rskgt", half_query, row_keys, preferred_element_type=jnp.float32
+            )
+            * score_scale
+        )
+        always = jnp.ones((1, 1, 1, 1, span_len), dtype=bool)
+        return block_stats(scores, always, row_values, "rskgt,rtkd->rskgd")
+
+    prefix_stats = combine_pair(prefix_block(own_kv), prefix_block(partner_kv))
+
+    def head_half(member, at):
+        return lax.dynamic_slice_in_dim(member, at * half_kv, half_kv, 2)
+
+    suffix_packed = jnp.concatenate(
+        [suffix_stats[2], suffix_stats[0][..., None], suffix_stats[1][..., None]], axis=-1
+    )
+    suffix_moved = lax.ppermute(head_half(suffix_packed, 1 - core_bit), "ctx", swap)
+    suffix_partner = (suffix_moved[..., HD], suffix_moved[..., HD + 1], suffix_moved[..., :HD])
+    suffix_kept = tuple(head_half(member, core_bit) for member in suffix_stats)
+    suffix_half = combine_pair(suffix_kept, suffix_partner)
 
     row_start = row_index * rows_dev
     own_prefix = tuple(
         lax.dynamic_slice_in_dim(member, row_start, rows_dev, 0) for member in prefix_stats
     )
-    own_merged = combine_pair(own_prefix, suffix_stats)
+    own_merged = combine_pair(own_prefix, suffix_half)
     peak_all, total_all, sum_all = tuple(
         lax.dynamic_update_slice_in_dim(whole_arr, piece_arr, row_start, 0)
         for whole_arr, piece_arr in zip(prefix_stats, own_merged)
     )
 
-    units = rows_dev * step_count * H
-    share = units // ctx_count
-    half = share // 2
-    pt_rows = -(-2 * half // LANES)
+    half_units = rows_dev * step_count * half_heads
+    chunk = half_units // ctx_count
+    pt_rows = -(-2 * chunk // LANES)
     dests = ctx_count * row_count
 
     def by_dest(member, tail=()):
-        shaped = member.reshape((row_count, ctx_count, share) + tail)
-        return jnp.swapaxes(shaped, 0, 1).reshape((dests, share) + tail)
-
-    def pack(peak, total, sums):
-        pt = jnp.concatenate([peak, total], axis=-1)
-        pt = jnp.pad(pt, ((0, 0), (0, pt_rows * LANES - 2 * half)))
-        return jnp.concatenate([sums, pt.reshape(dests, pt_rows, LANES)], axis=1)
-
-    def unpack(packed):
-        pt = packed[:, half:, :].reshape(packed.shape[0], pt_rows * LANES)
-        return (pt[:, :half], pt[:, half : 2 * half], packed[:, :half, :])
-
-    core_bit = ctx_index % 2
-    peak_d, total_d, sum_d = by_dest(peak_all), by_dest(total_all), by_dest(sum_all, (HD,))
-    keep_at = core_bit * half
-    give_at = (1 - core_bit) * half
-    kept = tuple(
-        lax.dynamic_slice_in_dim(member, keep_at, half, 1) for member in (peak_d, total_d, sum_d)
-    )
-    given = pack(
-        *(lax.dynamic_slice_in_dim(member, give_at, half, 1) for member in (peak_d, total_d, sum_d))
-    )
-    partner = lax.ppermute(given, "ctx", [(c, c ^ 1) for c in range(ctx_count)])
-    chip_stats = combine_pair(kept, unpack(partner))
-    outgoing = pack(*chip_stats)
+        shaped = member.reshape((row_count, ctx_count, chunk) + tail)
+        return jnp.swapaxes(shaped, 0, 1).reshape((dests, chunk) + tail)
+
+    pt = jnp.concatenate([by_dest(peak_all), by_dest(total_all)], axis=-1)
+    pt = jnp.pad(pt, ((0, 0), (0, pt_rows * LANES - 2 * chunk)))
+    outgoing = jnp.concatenate(
+        [by_dest(sum_all, (HD,)), pt.reshape(dests, pt_rows, LANES)], axis=1
+    )
     incoming = lax.all_to_all(
         outgoing, ("ctx", "row"), split_axis=0, concat_axis=0, tiled=True
     )
-    got_peak, got_total, got_sum = unpack(incoming)
-    got_peak = got_peak.reshape(ctx_count // 2, 2, row_count, half)
-    got_total = got_total.reshape(ctx_count // 2, 2, row_count, half)
-    got_sum = got_sum.reshape(ctx_count // 2, 2, row_count, half, HD)
-    got_peak = jnp.swapaxes(got_peak, 1, 2).reshape(dests // 2, share)
-    got_total = jnp.swapaxes(got_total, 1, 2).reshape(dests // 2, share)
-    got_sum = jnp.swapaxes(got_sum, 1, 2).reshape(dests // 2, share, HD)
-
-    unit_start = ctx_index * share
-    fresh_peak = lax.dynamic_slice_in_dim(fresh_stats[0].reshape(units), unit_start, share)
-    fresh_total = lax.dynamic_slice_in_dim(fresh_stats[1].reshape(units), unit_start, share)
-    fresh_sum = lax.dynamic_slice_in_dim(fresh_stats[2].reshape(units, HD), unit_start, share)
-
-    top = jnp.maximum(jnp.max(got_peak, axis=0), fresh_peak)
-    factor = jnp.exp(got_peak - top[None])
+    got_pt = incoming[:, chunk:, :].reshape(dests, pt_rows * LANES)
+    pairs = ctx_count // 2
+
+    def by_half(member, tail=()):
+        shaped = member.reshape((pairs, 2, row_count, chunk) + tail)
+        return jnp.swapaxes(shaped, 0, 1).reshape((2, pairs * row_count, chunk) + tail)
+
+    got_peak = by_half(got_pt[:, :chunk])
+    got_total = by_half(got_pt[:, chunk : 2 * chunk])
+    got_sum = by_half(incoming[:, :chunk, :], (HD,))
+
+    def fresh_chunk(member, tail=()):
+        shaped = member.reshape((rows_dev, step_count, 2, half_heads) + tail)
+        shaped = jnp.moveaxis(shaped, 2, 0).reshape((2, half_units) + tail)
+        return lax.dynamic_slice_in_dim(shaped, ctx_index * chunk, chunk, 1)
+
+    fresh_peak = fresh_chunk(fresh_stats[0])
+    fresh_total = fresh_chunk(fresh_stats[1])
+    fresh_sum = fresh_chunk(fresh_stats[2], (HD,))
+
+    top = jnp.maximum(jnp.max(got_peak, axis=1), fresh_peak)
+    factor = jnp.exp(got_peak - top[:, None])
     fresh_factor = jnp.exp(fresh_peak - top)
-    denom = jnp.sum(factor * got_total, axis=0) + fresh_factor * fresh_total
-    numer = jnp.sum(factor[..., None] * got_sum, axis=0) + fresh_factor[..., None] * fresh_sum
+    denom = jnp.sum(factor * got_total, axis=1) + fresh_factor * fresh_total
+    numer = jnp.sum(factor[..., None] * got_sum, axis=1) + fresh_factor[..., None] * fresh_sum
     result = (numer / denom[..., None]).astype(jnp.bfloat16)
-    whole = lax.all_gather(result, "ctx", axis=0, tiled=True)
+    whole = lax.all_gather(result, "ctx", axis=0, tiled=False)
+    whole = jnp.swapaxes(whole, 0, 1).reshape(2, rows_dev, step_count, half_heads, HD)
+    whole = jnp.moveaxis(whole, 0, 2)
     return whole.reshape(rows_dev, step_count, H * HD)
 
 

time: 52 us -> 51.2 us (0.985)
  waiting for transfers between devices: 17.7 us -> 13.4 us
  starting transfers between devices: 11 us -> 14 us
  matrix products: 2.14 us -> 3.91 us
  local copies, waits for them, and re-layouts: 12.3 us -> 10.6 us
    all_to_all x1, waiting for transfers between devices: 3.46 us -> 0.04 us  [per_device(): lax.all_to_all(fanned, 'row', split_axis=0, concat_axis=0, tiled=True)]
    all_to_all x1, starting transfers between devices: 3.63 us -> 6.01 us  [per_device(): lax.all_to_all(outgoing, ('ctx', 'row'), split_axis=0, concat_axis=0, til...]
    gather x2 -> x4, local copies, waits for them, and re-layouts: 1.16 us -> 2.39 us  [the longest x2 1.2 us: prefix_block(): row_values = jnp.take(kv[1], every_prefix, axis=0)]
    dot_general x1, matrix products: 0.54 us -> 1.76 us  [per_device(): jnp.einsum('rskgd,tkd->rskgt', own_query, flat_keys, preferred_element_ty...]
    unnamed x25 -> x21, local copies, waits for them, and re-layouts: 3.41 us -> 2.41 us
    concatenate x1 -> x0, local copies, waits for them, and re-layouts: 0.9 us -> none  [pack(): return jnp.concatenate([sums, pt.reshape(dests, pt_rows, LANES)], axis=1)]
    concatenate x2 -> x3, other arithmetic: 0.05 us -> 0.93 us  [the longest x1 0.77 us: per_device(): jnp.concatenate([by_dest(sum_all, (HD,)), pt.reshape(dests, pt_rows, LANE...]
    reshape x1, local copies, waits for them, and re-layouts: 1.12 us -> 0.27 us  [per_device(): flat_values = pool_values.reshape(slot_count * page_len, KVH, HD)]
  transfers between devices with their start and end apart: 3 -> 4, of which waited for: 3 -> 2; matrix products, arithmetic and copies ran while one was open for 9% -> 13% of each run, Pallas kernels for 0% -> 0%
where the time goes in v6:
time: 51.2 us; the launch traced here: 50.7 us
  starting transfers between devices  14 us (27%)
  waiting for transfers between devices  13.4 us (26%)
  local copies, waits for them, and re-layouts  10.6 us (21%)
  blocking collectives  5.19 us (10%)
  matrix products  3.91 us (8%)
  other arithmetic  3.15 us (6%)
    all_to_all x1, waiting for transfers between devices, per_device(): lax.all_to_all(outgoing, ('ctx', 'row'), split_axis=0, concat_axis=0, til...  12.5 us
    all_to_all x1, starting transfers between devices, per_device(): lax.all_to_all(fanned, 'row', split_axis=0, concat_axis=0, tiled=True)  7.38 us
    all_to_all x1, starting transfers between devices, per_device(): lax.all_to_all(outgoing, ('ctx', 'row'), split_axis=0, concat_axis=0, til...  6.01 us
    all_gather x1, blocking collectives, per_device(): whole = lax.all_gather(result, 'ctx', axis=0, tiled=False)  5.19 us
    unnamed x21, local copies, waits for them, and re-layouts  2.41 us
    dot_general x1, matrix products, per_device(): jnp.einsum('rskgd,tkd->rskgt', own_query, flat_keys, preferred_element_ty...  1.76 us
    gather x2, local copies, waits for them, and re-layouts, prefix_block(): row_values = jnp.take(kv[1], every_prefix, axis=0)  1.2 us
    gather x2, local copies, waits for them, and re-layouts, prefix_block(): row_keys = jnp.take(kv[0], every_prefix, axis=0)  1.2 us
  transfers between devices with their start and end apart: 4, of which 2 were waited for; matrix products, arithmetic and copies ran while one was open for 13% of the time, Pallas kernels for 0%

profile of v6, /device:TPU:0, one launch (start us, length us, event | category | flops | bytes accessed | tf_op | source)
XLA Modules:
  0.0 50.7 jit_solution(10639325995216304882)
XLA Ops:
  0.0 0.8 %reshape.197 = bf16[128,128]{1,0:T(8,128)(2,1)S(1)} reshape(bf16[2,2,4096]{2,1,0:T(2,128)(2,1)} %param.14) | data formatting | bytes 65536 | tf_op jit(solution)/shard_map/reshape | solution.py:93
  0.9 0.1 pad_maximum_fusion.1
  0.9 0.8 %broadcast_in_dim.119 = bf16[8,144,128]{2,1,0:T(8,128)(2,1)} broadcast(bf16[144,128]{1,0:T(8,128)(2,1)S(1)} %pad_maximum_fusion.1), dimensions={1,2} | broadcast | bytes 331776 | tf_op jit(solution)/shard_map/broadcast_in_dim | solution.py:94
  1.7 7.4 %all-to-all-start = ((bf16[8,144,128]{2,1,0:T(8,128)(2,1)}), bf16[8,144,128]{2,1,0:T(8,128)(2,1)S(1)}, u32[]{:S(2)}, u32[]{:S(2)}) async-start(bf16[8,144,128]{2,1,0:T(8,128)(2,1)} %broadcast_in_dim.119), calls=%async_computation | async-start | bytes 589824 | tf_op jit(solution)/shard_map/all_to_all | solution.py:95
  9.1 0.1 stack_reshape.6
  9.3 0.8 %copy-done.4 = bf16[8,32,512]{2,1,0:T(8,128)(2,1)S(1)} copy-done((bf16[8,32,512]{2,1,0:T(8,128)(2,1)S(1)}, bf16[8,32,512]{2,1,0:T(8,128)(2,1)}, u32[]{:S(2)}) %copy-start.4) | copy-done | bytes 262168
  10.2 0.1 copy_dynamic-update-slice_fusion
  10.3 0.1 collective-permute-start
  10.4 0.7 %copy-done.6 = s32[2,32]{1,0:T(2,128)S(1)} copy-done((s32[2,32]{1,0:T(2,128)S(1)}, s32[2,32]{1,0:T(2,128)}, u32[]{:S(2)}) %copy-start.6) | copy-done | bytes 280
  11.1 0.2 fusion.37
  11.2 0.2 compare_reduce_fusion
  11.5 0.1 add.105
  11.5 0.1 add.106
  11.6 0.1 and.29
  11.7 0.1 and.30
  11.8 0.1 add.108
  11.9 1.1 %reshape.199 = bf16[1024,4,128]{2,1,0:T(4,128)(2,1)} reshape(bf16[16,64,512]{2,1,0:T(8,128)(2,1)S(1)} %copy-done.1) | data formatting | bytes 2097152 | tf_op jit(solution)/shard_map/reshape | solution.py:69
  13.0 0.5 copy-done.2
  13.5 0.3 reshape.201
  13.8 0.4 copy-done.7
  14.1 0.1 compare_and_fusion
  14.2 1.8 %select_reduce_fusion = (f32[2,2,4,8]{3,1,0,2:T(2,128)S(1)}, f32[2,2,4,8,1024]{4,3,1,0,2:T(8,128)S(1)}) fusion(pred[2,1024]{1,0:T(4,128)(4,1)S(1)} %compare_and_fusion, bf16[2,2,4,8,128]{4,3,2,1,0:T(8,128)(2,1)S(1)} %reshape.200, bf16[1024,4,128,1,1]{2,1,0,4,3:T(4,128)(2,1)} %bitcast.145), kind=kOutput, calls=%fused_computation.23 | convolution fusion | flops 33947520 | bytes 1608192 | tf_op jit(solution)/shard_map/rskgd,tkd->rskgt/dot_general | solution.py:72
  16.0 0.3 convert_reduce_fusion
  16.2 0.2 copy.144
  16.4 0.2 copy.143
  16.6 0.3 fusion.7
  16.9 0.1 fusion.30
  16.9 0.5 collective-permute-start.1
  17.5 0.9 %collective-permute-done.1 = f32[2,2,2,8,130]{4,3,1,2,0:T(8,128)S(1)} collective-permute-done((f32[2,2,2,8,130]{4,3,1,2,0:T(8,128)S(1)}, f32[2,2,2,8,130]{4,3,1,2,0:T(8,128)S(1)}, u32[]{:S(2)}, u32[]{:S(2)}) %collective-permute-start.1) | collective-permute-done | bytes 33312 | tf_op jit(solution)/shard_map/ppermute | solution.py:139
  18.3 0.1 fusion.54
  18.4 0.1 copy.185
  18.5 0.1 copy.187
  18.7 0.2 convert_reduce_fusion.4
  18.9 0.1 reshape.223
  19.1 0.6 %gather_fusion = bf16[16,32,2,128]{3,1,2,0:T(8,128)(2,1)S(1)} fusion(bf16[8,32,2,128]{3,1,2,0:T(8,128)(2,1)S(1)} %get-tuple-element.34, s32[1024]{0:T(1024)S(1)} %pad_clamp_fusion), kind=kCustom, calls=%fused_computation.clone | custom fusion | bytes 524352 | tf_op jit(solution)/shard_map/jit(_take)/gather | solution.py:120
  19.7 0.6 %gather_fusion.1 = bf16[16,32,2,128]{3,1,2,0:T(8,128)(2,1)S(1)} fusion(bf16[8,32,2,128]{3,1,2,0:T(8,128)(2,1)S(1)} %get-tuple-element.36, s32[1024]{0:T(1024)S(1)} %pad_clamp_fusion), kind=kCustom, calls=%fused_computation.1.clone | custom fusion | bytes 524352 | tf_op jit(solution)/shard_map/jit(_take)/gather | solution.py:120
  20.3 0.4 fusion.57
  20.7 0.4 fusion.56
  21.2 0.6 %gather_fusion.2 = bf16[16,32,2,128]{3,1,2,0:T(8,128)(2,1)S(1)} fusion(bf16[8,32,2,128]{3,1,2,0:T(8,128)(2,1)S(1)} %get-tuple-element.33, s32[1024]{0:T(1024)S(1)} %pad_clamp_fusion), kind=kCustom, calls=%fused_computation.2.clone | custom fusion | bytes 524352 | tf_op jit(solution)/shard_map/jit(_take)/gather | solution.py:121
  21.8 0.6 %gather_fusion.3 = bf16[16,32,2,128]{3,1,2,0:T(8,128)(2,1)S(1)} fusion(bf16[8,32,2,128]{3,1,2,0:T(8,128)(2,1)S(1)} %get-tuple-element.35, s32[1024]{0:T(1024)S(1)} %pad_clamp_fusion), kind=kCustom, calls=%fused_computation.3.clone | custom fusion | bytes 524352 | tf_op jit(solution)/shard_map/jit(_take)/gather | solution.py:121
  22.4 0.5 convert_reduce_fusion.1
  22.9 0.3 fusion.3
  23.2 0.3 fusion.2
  23.5 0.1 fusion.34
  23.7 0.1 reshape.206
  23.8 0.1 reshape.204
  23.9 0.1 select_maximum_fusion
  24.0 0.8 %pad_maximum_fusion = f32[32,17,128]{2,1,0:T(8,128)} fusion(f32[32,1,128]{2,1,0:T(1,128)S(1)} %bitcast.163, f32[32,16,128]{2,1,0:T(8,128)S(1)} %bitcast.148), kind=kLoop, calls=%fused_computation.24 | loop fusion | flops 69632 | bytes 557056 | tf_op jit(solution)/shard_map/concatenate | solution.py:165
  24.8 6.0 %all-to-all-start.1 = ((f32[32,17,128]{2,1,0:T(8,128)}), f32[32,17,128]{2,1,0:T(8,128)S(1)}, u32[]{:S(2)}, u32[]{:S(2)}) async-start(f32[32,17,128]{2,1,0:T(8,128)} %pad_maximum_fusion), calls=%async_computation.1 | async-start | bytes 786432 | tf_op jit(solution)/shard_map/all_to_all | solution.py:168
  30.8 0.3 select_reduce_fusion.1
  31.1 0.1 reshape.212
  31.2 0.1 reshape.213
  31.3 0.1 convert_reduce_fusion.3
  31.4 0.1 reshape.219
  31.5 0.1 reshape.220
  31.5 0.2 convolution_bitcast_fusion.2
  31.8 12.5 %all-to-all-done.1 = f32[32,17,128]{2,1,0:T(8,128)S(1)} async-done(((f32[32,17,128]{2,1,0:T(8,128)}), f32[32,17,128]{2,1,0:T(8,128)S(1)}, u32[]{:S(2)}, u32[]{:S(2)}) %all-to-all-start.1) | async-done | bytes 278560 | tf_op jit(solution)/shard_map/all_to_all | solution.py:168
  44.3 0.1 fusion.55
  44.4 0.1 fusion.48
  44.6 0.1 multiply_reduce_fusion
  44.7 0.1 fusion.47
  44.8 0.1 divide_convert_fusion
  44.9 5.2 %all-gather = bf16[8,16,128]{2,1,0:T(8,128)(2,1)S(1)} all-gather(bf16[2,16,128]{2,1,0:T(8,128)(2,1)S(1)} %divide_convert_fusion), channel_id=2, replica_groups=mesh['ctx'=4,'row'=8] {'ctx'}, dimensions={0}, use_global_device_ids=true | all-gather | bytes 40960 | tf_op jit(solution)/shard_map/all_gather | solution.py:197
  50.1 0.6 %reshape.222 = bf16[2,2,4096]{2,1,0:T(2,128)(2,1)} reshape(bf16[2,2,2,16,128]{4,3,2,1,0:T(8,128)(2,1)S(1)} %bitcast.155) | data formatting | bytes 65536 | tf_op jit(solution)/shard_map/reshape | solution.py:200
  (54 shorter events, 0.7 us)
Async XLA Ops:
  0.0 31.5 %copy-start = (bf16[2,2,512]{2,1,0:T(2,128)(2,1)S(1)}, bf16[2,2,512]{2,1,0:T(2,128)(2,1)}, u32[]{:S(2)}) copy-start(bf16[2,2,512]{2,1,0:T(2,128)(2,1)} %param.23) | copy-start | bytes 12292
  0.0 0.8 %copy-start.9 = (s32[2]{0:T(128)S(1)}, s32[2]{0:T(128)}, u32[]{:S(2)}) copy-start(s32[2]{0:T(128)} %param.15) | copy-start | bytes 28
  1.7 7.4 %copy-start.3 = (bf16[8,32,512]{2,1,0:T(8,128)(2,1)S(1)}, bf16[8,32,512]{2,1,0:T(8,128)(2,1)}, u32[]{:S(2)}) copy-start(bf16[8,32,512]{2,1,0:T(8,128)(2,1)} %param.16) | copy-start | bytes 786436
  1.7 17.0 %all-to-all-start = ((bf16[8,144,128]{2,1,0:T(8,128)(2,1)}), bf16[8,144,128]{2,1,0:T(8,128)(2,1)S(1)}, u32[]{:S(2)}, u32[]{:S(2)}) async-start(bf16[8,144,128]{2,1,0:T(8,128)(2,1)} %broadcast_in_dim.119), calls=%async_computation | async-start | bytes 589824 | tf_op jit(solution)/shard_map/all_to_all | solution.py:95
  9.1 1.0 %copy-start.4 = (bf16[8,32,512]{2,1,0:T(8,128)(2,1)S(1)}, bf16[8,32,512]{2,1,0:T(8,128)(2,1)}, u32[]{:S(2)}) copy-start(bf16[8,32,512]{2,1,0:T(8,128)(2,1)} %param.17) | copy-start | bytes 786436
  9.2 2.7 %copy-start.1 = (bf16[16,64,512]{2,1,0:T(8,128)(2,1)S(1)}, bf16[16,64,512]{2,1,0:T(8,128)(2,1)}, u32[]{:S(2)}) copy-start(bf16[16,64,512]{2,1,0:T(8,128)(2,1)} %param.18) | copy-start | bytes 3145732
  10.2 1.2 %copy-start.5 = (bf16[2,2,4096]{2,1,0:T(2,128)(2,1)S(1)}, bf16[2,2,4096]{2,1,0:T(2,128)(2,1)}, u32[]{:S(2)}) copy-start(bf16[2,2,4096]{2,1,0:T(2,128)(2,1)} %param.14) | copy-start | bytes 98308
  10.3 8.4 %collective-permute-start = (bf16[2,8,32,2,128]{4,2,3,1,0:T(8,128)(2,1)S(1)}, bf16[2,8,32,2,128]{4,2,3,1,0:T(8,128)(2,1)S(1)}, u32[]{:S(2)}, u32[]{:S(2)}) collective-permute-start(bf16[2,8,32,2,128]{4,2,3,1,0:T(8,128)(2,1)S(1)} %constant_dynamic-slice_fusion.6), channel_id=1, source_target_pairs={{0,8},{8,0},{16,24},{24,16},{1,9},{9,1},{17,25},{25,17},{2,10},{10... | collective-permute-start | bytes 786440 | tf_op jit(solution)/shard_map/ppermute | solution.py:115
  10.4 0.7 %copy-start.6 = (s32[2,32]{1,0:T(2,128)S(1)}, s32[2,32]{1,0:T(2,128)}, u32[]{:S(2)}) copy-start(s32[2,32]{1,0:T(2,128)} %param.20) | copy-start | bytes 772
  11.9 1.6 %copy-start.2 = (bf16[16,64,512]{2,1,0:T(8,128)(2,1)S(1)}, bf16[16,64,512]{2,1,0:T(8,128)(2,1)}, u32[]{:S(2)}) copy-start(bf16[16,64,512]{2,1,0:T(8,128)(2,1)} %param.19) | copy-start | bytes 3145732
  13.5 0.7 %copy-start.7 = (s32[2]{0:T(128)S(1)}, s32[2]{0:T(128)}, u32[]{:S(2)}) copy-start(s32[2]{0:T(128)} %param.21) | copy-start | bytes 28
  16.9 1.4 %collective-permute-start.1 = (f32[2,2,2,8,130]{4,3,1,2,0:T(8,128)S(1)}, f32[2,2,2,8,130]{4,3,1,2,0:T(8,128)S(1)}, u32[]{:S(2)}, u32[]{:S(2)}) collective-permute-start(f32[2,2,2,8,130]{4,3,1,2,0:T(8,128)S(1)} %fusion.30), channel_id=1, source_target_pairs={{0,8},{8,0},{16,24},{24,16},{1,9},{9,1},{17,25},{25,17},{2,10},{10... | collective-permute-start | bytes 99848 | tf_op jit(solution)/shard_map/ppermute | solution.py:139
  24.8 6.0 %copy-start.8 = (bf16[2,2,512]{2,1,0:T(2,128)(2,1)S(1)}, bf16[2,2,512]{2,1,0:T(2,128)(2,1)}, u32[]{:S(2)}) copy-start(bf16[2,2,512]{2,1,0:T(2,128)(2,1)} %param.22) | copy-start | bytes 12292
  24.8 19.6 %all-to-all-start.1 = ((f32[32,17,128]{2,1,0:T(8,128)}), f32[32,17,128]{2,1,0:T(8,128)S(1)}, u32[]{:S(2)}, u32[]{:S(2)}) async-start(f32[32,17,128]{2,1,0:T(8,128)} %pad_maximum_fusion), calls=%async_computation.1 | async-start | bytes 786432 | tf_op jit(solution)/shard_map/all_to_all | solution.py:168

commit v7 on v6

--- a/solution.py
+++ b/solution.py
@@ -166,8 +166,13 @@
         [by_dest(sum_all, (HD,)), pt.reshape(dests, pt_rows, LANES)], axis=1
     )
     incoming = lax.all_to_all(
-        outgoing, ("ctx", "row"), split_axis=0, concat_axis=0, tiled=True
-    )
+        outgoing.reshape(dests, 1, (chunk + pt_rows) * LANES),
+        ("ctx", "row"),
+        split_axis=0,
+        concat_axis=0,
+        tiled=True,
+    )
+    incoming = incoming.reshape(dests, chunk + pt_rows, LANES)
     got_pt = incoming[:, chunk:, :].reshape(dests, pt_rows * LANES)
     pairs = ctx_count // 2
 

time: 51.2 us -> 49.7 us (0.971)
  waiting for transfers between devices: 13.4 us -> 11 us
  local copies, waits for them, and re-layouts: 10.6 us -> 11.6 us
    all_to_all x1, waiting for transfers between devices: 12.5 us -> 10.1 us  [per_device(): lax.all_to_all(outgoing.reshape(dests, 1, (chunk + pt_rows) * LANES), ('c...]
    reshape x0 -> x2, local copies, waits for them, and re-layouts: none -> 1.03 us  [the longest x1 0.98 us: per_device(): outgoing.reshape(dests, 1, (chunk + pt_rows) * LANES)]
    concatenate x1, other arithmetic: 0.77 us -> 0.04 us  [per_device(): jnp.concatenate([by_dest(sum_all, (HD,)), pt.reshape(dests, pt_rows, LANE...]
    all_to_all x0 -> x1, other arithmetic: none -> 0.65 us  [per_device(): lax.all_to_all(outgoing.reshape(dests, 1, (chunk + pt_rows) * LANES), ('c...]
where the time goes in v7:
time: 49.7 us; the launch traced here: 49.2 us
  starting transfers between devices  14 us (28%)
  local copies, waits for them, and re-layouts  11.6 us (23%)
  waiting for transfers between devices  11 us (22%)
  blocking collectives  5.19 us (10%)
  matrix products  3.91 us (8%)
  other arithmetic  3.07 us (6%)
    all_to_all x1, waiting for transfers between devices, per_device(): lax.all_to_all(outgoing.reshape(dests, 1, (chunk + pt_rows) * LANES), ('c...  10.1 us
    all_to_all x1, starting transfers between devices, per_device(): lax.all_to_all(fanned, 'row', split_axis=0, concat_axis=0, tiled=True)  7.38 us
    all_to_all x1, starting transfers between devices, per_device(): lax.all_to_all(outgoing.reshape(dests, 1, (chunk + pt_rows) * LANES), ('c...  6.01 us
    all_gather x1, blocking collectives, per_device(): whole = lax.all_gather(result, 'ctx', axis=0, tiled=False)  5.19 us
    unnamed x21, local copies, waits for them, and re-layouts  2.41 us
    dot_general x1, matrix products, per_device(): jnp.einsum('rskgd,tkd->rskgt', own_query, flat_keys, preferred_element_ty...  1.76 us
    gather x2, local copies, waits for them, and re-layouts, prefix_block(): row_values = jnp.take(kv[1], every_prefix, axis=0)  1.2 us
    gather x2, local copies, waits for them, and re-layouts, prefix_block(): row_keys = jnp.take(kv[0], every_prefix, axis=0)  1.2 us
  transfers between devices with their start and end apart: 4, of which 2 were waited for; matrix products, arithmetic and copies ran while one was open for 13% of the time, Pallas kernels for 0%

profile of v7, /device:TPU:0, one launch (start us, length us, event | category | flops | bytes accessed | tf_op | source)
XLA Modules:
  0.0 49.2 jit_solution(12697239341367830775)
XLA Ops:
  0.0 0.8 %reshape.203 = bf16[128,128]{1,0:T(8,128)(2,1)S(1)} reshape(bf16[2,2,4096]{2,1,0:T(2,128)(2,1)} %param.14) | data formatting | bytes 65536 | tf_op jit(solution)/shard_map/reshape | solution.py:93
  0.9 0.1 pad_maximum_fusion.1
  0.9 0.8 %broadcast_in_dim.119 = bf16[8,144,128]{2,1,0:T(8,128)(2,1)} broadcast(bf16[144,128]{1,0:T(8,128)(2,1)S(1)} %pad_maximum_fusion.1), dimensions={1,2} | broadcast | bytes 331776 | tf_op jit(solution)/shard_map/broadcast_in_dim | solution.py:94
  1.7 7.4 %all-to-all-start = ((bf16[8,144,128]{2,1,0:T(8,128)(2,1)}), bf16[8,144,128]{2,1,0:T(8,128)(2,1)S(1)}, u32[]{:S(2)}, u32[]{:S(2)}) async-start(bf16[8,144,128]{2,1,0:T(8,128)(2,1)} %broadcast_in_dim.119), calls=%async_computation | async-start | bytes 589824 | tf_op jit(solution)/shard_map/all_to_all | solution.py:95
  9.3 0.8 %copy-done.4 = bf16[8,32,512]{2,1,0:T(8,128)(2,1)S(1)} copy-done((bf16[8,32,512]{2,1,0:T(8,128)(2,1)S(1)}, bf16[8,32,512]{2,1,0:T(8,128)(2,1)}, u32[]{:S(2)}) %copy-start.4) | copy-done | bytes 262168
  10.2 0.1 copy_dynamic-update-slice_fusion
  10.3 0.1 collective-permute-start
  10.4 0.7 %copy-done.6 = s32[2,32]{1,0:T(2,128)S(1)} copy-done((s32[2,32]{1,0:T(2,128)S(1)}, s32[2,32]{1,0:T(2,128)}, u32[]{:S(2)}) %copy-start.6) | copy-done | bytes 280
  11.1 0.2 fusion.37
  11.2 0.2 compare_reduce_fusion
  11.5 0.1 add.105
  11.5 0.1 add.106
  11.6 0.1 and.29
  11.7 0.1 and.30
  11.8 0.1 add.108
  11.9 1.1 %reshape.205 = bf16[1024,4,128]{2,1,0:T(4,128)(2,1)} reshape(bf16[16,64,512]{2,1,0:T(8,128)(2,1)S(1)} %copy-done.1) | data formatting | bytes 2097152 | tf_op jit(solution)/shard_map/reshape | solution.py:69
  13.0 0.5 copy-done.2
  13.5 0.3 reshape.207
  13.8 0.4 copy-done.7
  14.1 0.1 compare_and_fusion
  14.2 1.8 %select_reduce_fusion = (f32[2,2,4,8]{3,1,0,2:T(2,128)S(1)}, f32[2,2,4,8,1024]{4,3,1,0,2:T(8,128)S(1)}) fusion(pred[2,1024]{1,0:T(4,128)(4,1)S(1)} %compare_and_fusion, bf16[2,2,4,8,128]{4,3,2,1,0:T(8,128)(2,1)S(1)} %reshape.206, bf16[1024,4,128,1,1]{2,1,0,4,3:T(4,128)(2,1)} %bitcast.145), kind=kOutput, calls=%fused_computation.23 | convolution fusion | flops 33947520 | bytes 1608192 | tf_op jit(solution)/shard_map/rskgd,tkd->rskgt/dot_general | solution.py:72
  16.0 0.3 convert_reduce_fusion
  16.2 0.2 copy.145
  16.4 0.2 copy.144
  16.6 0.3 fusion.7
  16.9 0.1 fusion.30
  16.9 0.5 collective-permute-start.1
  17.5 0.9 %collective-permute-done.1 = f32[2,2,2,8,130]{4,3,1,2,0:T(8,128)S(1)} collective-permute-done((f32[2,2,2,8,130]{4,3,1,2,0:T(8,128)S(1)}, f32[2,2,2,8,130]{4,3,1,2,0:T(8,128)S(1)}, u32[]{:S(2)}, u32[]{:S(2)}) %collective-permute-start.1) | collective-permute-done | bytes 33312 | tf_op jit(solution)/shard_map/ppermute | solution.py:139
  18.3 0.1 fusion.54
  18.4 0.1 copy.187
  18.5 0.1 copy.189
  18.7 0.2 convert_reduce_fusion.4
  18.9 0.1 reshape.231
  19.1 0.6 %gather_fusion = bf16[16,32,2,128]{3,1,2,0:T(8,128)(2,1)S(1)} fusion(bf16[8,32,2,128]{3,1,2,0:T(8,128)(2,1)S(1)} %get-tuple-element.34, s32[1024]{0:T(1024)S(1)} %pad_clamp_fusion), kind=kCustom, calls=%fused_computation.clone | custom fusion | bytes 524352 | tf_op jit(solution)/shard_map/jit(_take)/gather | solution.py:120
  19.7 0.6 %gather_fusion.1 = bf16[16,32,2,128]{3,1,2,0:T(8,128)(2,1)S(1)} fusion(bf16[8,32,2,128]{3,1,2,0:T(8,128)(2,1)S(1)} %get-tuple-element.36, s32[1024]{0:T(1024)S(1)} %pad_clamp_fusion), kind=kCustom, calls=%fused_computation.1.clone | custom fusion | bytes 524352 | tf_op jit(solution)/shard_map/jit(_take)/gather | solution.py:120
  20.3 0.4 fusion.57
  20.7 0.4 fusion.56
  21.2 0.6 %gather_fusion.2 = bf16[16,32,2,128]{3,1,2,0:T(8,128)(2,1)S(1)} fusion(bf16[8,32,2,128]{3,1,2,0:T(8,128)(2,1)S(1)} %get-tuple-element.33, s32[1024]{0:T(1024)S(1)} %pad_clamp_fusion), kind=kCustom, calls=%fused_computation.2.clone | custom fusion | bytes 524352 | tf_op jit(solution)/shard_map/jit(_take)/gather | solution.py:121
  21.8 0.6 %gather_fusion.3 = bf16[16,32,2,128]{3,1,2,0:T(8,128)(2,1)S(1)} fusion(bf16[8,32,2,128]{3,1,2,0:T(8,128)(2,1)S(1)} %get-tuple-element.35, s32[1024]{0:T(1024)S(1)} %pad_clamp_fusion), kind=kCustom, calls=%fused_computation.3.clone | custom fusion | bytes 524352 | tf_op jit(solution)/shard_map/jit(_take)/gather | solution.py:121
  22.4 0.5 convert_reduce_fusion.1
  22.9 0.3 fusion.3
  23.2 0.3 fusion.2
  23.5 0.1 fusion.34
  23.7 0.1 reshape.212
  23.8 0.1 reshape.210
  23.9 0.1 select_maximum_fusion
  24.0 1.0 %reshape.285 = f32[32,1,2176]{2,1,0:T(1,128)} reshape(f32[32,17,128]{2,1,0:T(8,128)S(1)} %pad_maximum_fusion) | data formatting | bytes 557056 | tf_op jit(solution)/shard_map/reshape | solution.py:169
  25.0 6.0 %all-to-all-start.1 = ((f32[32,1,2176]{2,1,0:T(1,128)}), f32[32,1,2176]{2,1,0:T(1,128)S(1)}, u32[]{:S(2)}, u32[]{:S(2)}) async-start(f32[32,1,2176]{2,1,0:T(1,128)} %reshape.285), calls=%async_computation.1 | async-start | bytes 557056 | tf_op jit(solution)/shard_map/all_to_all | solution.py:168
  31.0 0.3 select_reduce_fusion.1
  31.3 0.1 reshape.220
  31.4 0.1 reshape.221
  31.5 0.1 convert_reduce_fusion.3
  31.6 0.1 reshape.227
  31.7 0.1 reshape.228
  31.8 0.2 convolution_bitcast_fusion.2
  32.0 10.1 %all-to-all-done.1 = f32[32,1,2176]{2,1,0:T(1,128)S(1)} async-done(((f32[32,1,2176]{2,1,0:T(1,128)}), f32[32,1,2176]{2,1,0:T(1,128)S(1)}, u32[]{:S(2)}, u32[]{:S(2)}) %all-to-all-start.1) | async-done | bytes 278560 | tf_op jit(solution)/shard_map/all_to_all | solution.py:168
  42.1 0.7 %reduce.6 = f32[32,2176]{1,0:T(8,128)S(1)} reduce(f32[32,1,2176]{2,1,0:T(1,128)S(1)} %all-to-all-done.1, f32[]{:T(128)} %constant.97), dimensions={1}, to_apply=%all_to_all.7.reduce_sub_computation | reduce | bytes 557060 | tf_op jit(solution)/shard_map/all_to_all | solution.py:168
  42.9 0.1 fusion.55
  43.0 0.1 fusion.48
  43.1 0.1 multiply_reduce_fusion
  43.2 0.1 fusion.47
  43.3 0.1 divide_convert_fusion
  43.4 5.2 %all-gather = bf16[8,16,128]{2,1,0:T(8,128)(2,1)S(1)} all-gather(bf16[2,16,128]{2,1,0:T(8,128)(2,1)S(1)} %divide_convert_fusion), channel_id=2, replica_groups=mesh['ctx'=4,'row'=8] {'ctx'}, dimensions={0}, use_global_device_ids=true | all-gather | bytes 40960 | tf_op jit(solution)/shard_map/all_gather | solution.py:202
  48.6 0.6 %reshape.230 = bf16[2,2,4096]{2,1,0:T(2,128)(2,1)} reshape(bf16[2,2,2,16,128]{4,3,2,1,0:T(8,128)(2,1)S(1)} %bitcast.155) | data formatting | bytes 65536 | tf_op jit(solution)/shard_map/reshape | solution.py:205
  (57 shorter events, 0.8 us)
Async XLA Ops:
  0.0 31.8 %copy-start = (bf16[2,2,512]{2,1,0:T(2,128)(2,1)S(1)}, bf16[2,2,512]{2,1,0:T(2,128)(2,1)}, u32[]{:S(2)}) copy-start(bf16[2,2,512]{2,1,0:T(2,128)(2,1)} %param.23) | copy-start | bytes 12292
  0.0 0.8 %copy-start.9 = (s32[2]{0:T(128)S(1)}, s32[2]{0:T(128)}, u32[]{:S(2)}) copy-start(s32[2]{0:T(128)} %param.15) | copy-start | bytes 28
  1.7 7.4 %copy-start.3 = (bf16[8,32,512]{2,1,0:T(8,128)(2,1)S(1)}, bf16[8,32,512]{2,1,0:T(8,128)(2,1)}, u32[]{:S(2)}) copy-start(bf16[8,32,512]{2,1,0:T(8,128)(2,1)} %param.16) | copy-start | bytes 786436
  1.7 17.0 %all-to-all-start = ((bf16[8,144,128]{2,1,0:T(8,128)(2,1)}), bf16[8,144,128]{2,1,0:T(8,128)(2,1)S(1)}, u32[]{:S(2)}, u32[]{:S(2)}) async-start(bf16[8,144,128]{2,1,0:T(8,128)(2,1)} %broadcast_in_dim.119), calls=%async_computation | async-start | bytes 589824 | tf_op jit(solution)/shard_map/all_to_all | solution.py:95
  9.1 1.0 %copy-start.4 = (bf16[8,32,512]{2,1,0:T(8,128)(2,1)S(1)}, bf16[8,32,512]{2,1,0:T(8,128)(2,1)}, u32[]{:S(2)}) copy-start(bf16[8,32,512]{2,1,0:T(8,128)(2,1)} %param.17) | copy-start | bytes 786436
  9.2 2.7 %copy-start.1 = (bf16[16,64,512]{2,1,0:T(8,128)(2,1)S(1)}, bf16[16,64,512]{2,1,0:T(8,128)(2,1)}, u32[]{:S(2)}) copy-start(bf16[16,64,512]{2,1,0:T(8,128)(2,1)} %param.18) | copy-start | bytes 3145732
  10.2 1.2 %copy-start.5 = (bf16[2,2,4096]{2,1,0:T(2,128)(2,1)S(1)}, bf16[2,2,4096]{2,1,0:T(2,128)(2,1)}, u32[]{:S(2)}) copy-start(bf16[2,2,4096]{2,1,0:T(2,128)(2,1)} %param.14) | copy-start | bytes 98308
  10.3 8.4 %collective-permute-start = (bf16[2,8,32,2,128]{4,2,3,1,0:T(8,128)(2,1)S(1)}, bf16[2,8,32,2,128]{4,2,3,1,0:T(8,128)(2,1)S(1)}, u32[]{:S(2)}, u32[]{:S(2)}) collective-permute-start(bf16[2,8,32,2,128]{4,2,3,1,0:T(8,128)(2,1)S(1)} %constant_dynamic-slice_fusion.6), channel_id=1, source_target_pairs={{0,8},{8,0},{16,24},{24,16},{1,9},{9,1},{17,25},{25,17},{2,10},{10... | collective-permute-start | bytes 786440 | tf_op jit(solution)/shard_map/ppermute | solution.py:115
  10.4 0.7 %copy-start.6 = (s32[2,32]{1,0:T(2,128)S(1)}, s32[2,32]{1,0:T(2,128)}, u32[]{:S(2)}) copy-start(s32[2,32]{1,0:T(2,128)} %param.20) | copy-start | bytes 772
  11.9 1.6 %copy-start.2 = (bf16[16,64,512]{2,1,0:T(8,128)(2,1)S(1)}, bf16[16,64,512]{2,1,0:T(8,128)(2,1)}, u32[]{:S(2)}) copy-start(bf16[16,64,512]{2,1,0:T(8,128)(2,1)} %param.19) | copy-start | bytes 3145732
  13.5 0.7 %copy-start.7 = (s32[2]{0:T(128)S(1)}, s32[2]{0:T(128)}, u32[]{:S(2)}) copy-start(s32[2]{0:T(128)} %param.21) | copy-start | bytes 28
  16.9 1.4 %collective-permute-start.1 = (f32[2,2,2,8,130]{4,3,1,2,0:T(8,128)S(1)}, f32[2,2,2,8,130]{4,3,1,2,0:T(8,128)S(1)}, u32[]{:S(2)}, u32[]{:S(2)}) collective-permute-start(f32[2,2,2,8,130]{4,3,1,2,0:T(8,128)S(1)} %fusion.30), channel_id=1, source_target_pairs={{0,8},{8,0},{16,24},{24,16},{1,9},{9,1},{17,25},{25,17},{2,10},{10... | collective-permute-start | bytes 99848 | tf_op jit(solution)/shard_map/ppermute | solution.py:139
  25.0 6.0 %copy-start.8 = (bf16[2,2,512]{2,1,0:T(2,128)(2,1)S(1)}, bf16[2,2,512]{2,1,0:T(2,128)(2,1)}, u32[]{:S(2)}) copy-start(bf16[2,2,512]{2,1,0:T(2,128)(2,1)} %param.22) | copy-start | bytes 12292
  25.0 17.1 %all-to-all-start.1 = ((f32[32,1,2176]{2,1,0:T(1,128)}), f32[32,1,2176]{2,1,0:T(1,128)S(1)}, u32[]{:S(2)}, u32[]{:S(2)}) async-start(f32[32,1,2176]{2,1,0:T(1,128)} %reshape.285), calls=%async_computation.1 | async-start | bytes 557056 | tf_op jit(solution)/shard_map/all_to_all | solution.py:168

commit v8 on v7

--- a/solution.py
+++ b/solution.py
@@ -162,11 +162,10 @@
 
     pt = jnp.concatenate([by_dest(peak_all), by_dest(total_all)], axis=-1)
     pt = jnp.pad(pt, ((0, 0), (0, pt_rows * LANES - 2 * chunk)))
-    outgoing = jnp.concatenate(
-        [by_dest(sum_all, (HD,)), pt.reshape(dests, pt_rows, LANES)], axis=1
-    )
+    flat_len = (chunk + pt_rows) * LANES
+    outgoing = jnp.concatenate([by_dest(sum_all, (HD,)).reshape(dests, chunk * HD), pt], axis=1)
     incoming = lax.all_to_all(
-        outgoing.reshape(dests, 1, (chunk + pt_rows) * LANES),
+        outgoing.reshape(dests, 1, flat_len),
         ("ctx", "row"),
         split_axis=0,
         concat_axis=0,

time: 49.7 us -> 49.8 us (level)
    unnamed x21 -> x22, local copies, waits for them, and re-layouts: 2.41 us -> 2.5 us
where the time goes in v8:
time: 49.8 us; the launch traced here: 49.3 us
  starting transfers between devices  14 us (28%)
  local copies, waits for them, and re-layouts  11.7 us (23%)
  waiting for transfers between devices  11 us (22%)
  blocking collectives  5.19 us (10%)
  matrix products  3.91 us (8%)
  other arithmetic  3.06 us (6%)
    all_to_all x1, waiting for transfers between devices, per_device(): lax.all_to_all(outgoing.reshape(dests, 1, flat_len), ('ctx', 'row'), spli...  10.1 us
    all_to_all x1, starting transfers between devices, per_device(): lax.all_to_all(fanned, 'row', split_axis=0, concat_axis=0, tiled=True)  7.38 us
    all_to_all x1, starting transfers between devices, per_device(): lax.all_to_all(outgoing.reshape(dests, 1, flat_len), ('ctx', 'row'), spli...  6.01 us
    all_gather x1, blocking collectives, per_device(): whole = lax.all_gather(result, 'ctx', axis=0, tiled=False)  5.19 us
    unnamed x22, local copies, waits for them, and re-layouts  2.5 us
    dot_general x1, matrix products, per_device(): jnp.einsum('rskgd,tkd->rskgt', own_query, flat_keys, preferred_element_ty...  1.76 us
    gather x2, local copies, waits for them, and re-layouts, prefix_block(): row_values = jnp.take(kv[1], every_prefix, axis=0)  1.2 us
    gather x2, local copies, waits for them, and re-layouts, prefix_block(): row_keys = jnp.take(kv[0], every_prefix, axis=0)  1.2 us
  transfers between devices with their start and end apart: 4, of which 2 were waited for; matrix products, arithmetic and copies ran while one was open for 13% of the time, Pallas kernels for 0%

profile of v8, /device:TPU:0, one launch (start us, length us, event | category | flops | bytes accessed | tf_op | source)
XLA Modules:
  0.0 49.3 jit_solution(5092667109875482859)
XLA Ops:
  0.0 0.8 %reshape.197 = bf16[128,128]{1,0:T(8,128)(2,1)S(1)} reshape(bf16[2,2,4096]{2,1,0:T(2,128)(2,1)} %param.14) | data formatting | bytes 65536 | tf_op jit(solution)/shard_map/reshape | solution.py:93
  0.9 0.1 pad_maximum_fusion
  0.9 0.8 %broadcast_in_dim.119 = bf16[8,144,128]{2,1,0:T(8,128)(2,1)} broadcast(bf16[144,128]{1,0:T(8,128)(2,1)S(1)} %pad_maximum_fusion), dimensions={1,2} | broadcast | bytes 331776 | tf_op jit(solution)/shard_map/broadcast_in_dim | solution.py:94
  1.7 7.4 %all-to-all-start = ((bf16[8,144,128]{2,1,0:T(8,128)(2,1)}), bf16[8,144,128]{2,1,0:T(8,128)(2,1)S(1)}, u32[]{:S(2)}, u32[]{:S(2)}) async-start(bf16[8,144,128]{2,1,0:T(8,128)(2,1)} %broadcast_in_dim.119), calls=%async_computation | async-start | bytes 589824 | tf_op jit(solution)/shard_map/all_to_all | solution.py:95
  9.3 0.8 %copy-done.4 = bf16[8,32,512]{2,1,0:T(8,128)(2,1)S(1)} copy-done((bf16[8,32,512]{2,1,0:T(8,128)(2,1)S(1)}, bf16[8,32,512]{2,1,0:T(8,128)(2,1)}, u32[]{:S(2)}) %copy-start.4) | copy-done | bytes 262168
  10.3 0.1 collective-permute-start
  10.4 0.7 %copy-done.6 = s32[2,32]{1,0:T(2,128)S(1)} copy-done((s32[2,32]{1,0:T(2,128)S(1)}, s32[2,32]{1,0:T(2,128)}, u32[]{:S(2)}) %copy-start.6) | copy-done | bytes 280
  11.1 0.2 fusion.37
  11.2 0.2 compare_reduce_fusion
  11.5 0.1 add.105
  11.5 0.1 add.106
  11.6 0.1 and.29
  11.7 0.1 and.30
  11.8 0.1 add.108
  11.9 1.1 %reshape.199 = bf16[1024,4,128]{2,1,0:T(4,128)(2,1)} reshape(bf16[16,64,512]{2,1,0:T(8,128)(2,1)S(1)} %copy-done.1) | data formatting | bytes 2097152 | tf_op jit(solution)/shard_map/reshape | solution.py:69
  13.0 0.5 copy-done.2
  13.5 0.3 reshape.201
  13.8 0.4 copy-done.7
  14.1 0.1 compare_and_fusion
  14.2 1.8 %select_reduce_fusion = (f32[2,2,4,8]{3,1,0,2:T(2,128)S(1)}, f32[2,2,4,8,1024]{4,3,1,0,2:T(8,128)S(1)}) fusion(pred[2,1024]{1,0:T(4,128)(4,1)S(1)} %compare_and_fusion, bf16[2,2,4,8,128]{4,3,2,1,0:T(8,128)(2,1)S(1)} %reshape.200, bf16[1024,4,128,1,1]{2,1,0,4,3:T(4,128)(2,1)} %bitcast.152), kind=kOutput, calls=%fused_computation.23 | convolution fusion | flops 33947520 | bytes 1608192 | tf_op jit(solution)/shard_map/rskgd,tkd->rskgt/dot_general | solution.py:72
  16.0 0.3 convert_reduce_fusion
  16.2 0.2 copy.145
  16.4 0.2 copy.144
  16.6 0.3 fusion.7
  16.9 0.1 fusion.30
  16.9 0.5 collective-permute-start.1
  17.5 0.9 %collective-permute-done.1 = f32[2,2,2,8,130]{4,3,1,2,0:T(8,128)S(1)} collective-permute-done((f32[2,2,2,8,130]{4,3,1,2,0:T(8,128)S(1)}, f32[2,2,2,8,130]{4,3,1,2,0:T(8,128)S(1)}, u32[]{:S(2)}, u32[]{:S(2)}) %collective-permute-start.1) | collective-permute-done | bytes 33312 | tf_op jit(solution)/shard_map/ppermute | solution.py:139
  18.3 0.1 fusion.54
  18.4 0.1 copy.187
  18.5 0.1 copy.189
  18.7 0.2 convert_reduce_fusion.4
  18.9 0.1 reshape.223
  19.1 0.6 %gather_fusion = bf16[16,32,2,128]{3,1,2,0:T(8,128)(2,1)S(1)} fusion(bf16[8,32,2,128]{3,1,2,0:T(8,128)(2,1)S(1)} %get-tuple-element.34, s32[1024]{0:T(1024)S(1)} %pad_clamp_fusion), kind=kCustom, calls=%fused_computation.clone | custom fusion | bytes 524352 | tf_op jit(solution)/shard_map/jit(_take)/gather | solution.py:120
  19.7 0.6 %gather_fusion.1 = bf16[16,32,2,128]{3,1,2,0:T(8,128)(2,1)S(1)} fusion(bf16[8,32,2,128]{3,1,2,0:T(8,128)(2,1)S(1)} %get-tuple-element.36, s32[1024]{0:T(1024)S(1)} %pad_clamp_fusion), kind=kCustom, calls=%fused_computation.1.clone | custom fusion | bytes 524352 | tf_op jit(solution)/shard_map/jit(_take)/gather | solution.py:120
  20.3 0.4 fusion.57
  20.7 0.4 fusion.56
  21.2 0.6 %gather_fusion.2 = bf16[16,32,2,128]{3,1,2,0:T(8,128)(2,1)S(1)} fusion(bf16[8,32,2,128]{3,1,2,0:T(8,128)(2,1)S(1)} %get-tuple-element.33, s32[1024]{0:T(1024)S(1)} %pad_clamp_fusion), kind=kCustom, calls=%fused_computation.2.clone | custom fusion | bytes 524352 | tf_op jit(solution)/shard_map/jit(_take)/gather | solution.py:121
  21.8 0.6 %gather_fusion.3 = bf16[16,32,2,128]{3,1,2,0:T(8,128)(2,1)S(1)} fusion(bf16[8,32,2,128]{3,1,2,0:T(8,128)(2,1)S(1)} %get-tuple-element.35, s32[1024]{0:T(1024)S(1)} %pad_clamp_fusion), kind=kCustom, calls=%fused_computation.3.clone | custom fusion | bytes 524352 | tf_op jit(solution)/shard_map/jit(_take)/gather | solution.py:121
  22.4 0.5 convert_reduce_fusion.1
  22.9 0.3 fusion.3
  23.2 0.3 fusion.2
  23.5 0.1 fusion.34
  23.7 0.1 copy.247
  23.8 0.1 reshape.205
  23.9 0.1 reshape.203
  24.0 0.1 select_maximum_fusion
  24.1 1.0 %copy.159 = f32[32,1,2176]{2,1,0:T(1,128)} copy(f32[32,1,2176]{2,0,1:T(8,128)S(1)} %maximum_bitcast_fusion) | data formatting | bytes 557056 | tf_op jit(solution)/shard_map/reshape | solution.py:168
  25.1 6.0 %all-to-all-start.1 = ((f32[32,1,2176]{2,1,0:T(1,128)}), f32[32,1,2176]{2,1,0:T(1,128)S(1)}, u32[]{:S(2)}, u32[]{:S(2)}) async-start(f32[32,1,2176]{2,1,0:T(1,128)} %copy.159), calls=%async_computation.1 | async-start | bytes 557056 | tf_op jit(solution)/shard_map/all_to_all | solution.py:167
  31.1 0.3 select_reduce_fusion.1
  31.4 0.1 reshape.212
  31.5 0.1 reshape.213
  31.6 0.1 convert_reduce_fusion.3
  31.7 0.1 reshape.219
  31.8 0.1 reshape.220
  31.9 0.2 convolution_bitcast_fusion.2
  32.1 10.1 %all-to-all-done.1 = f32[32,1,2176]{2,1,0:T(1,128)S(1)} async-done(((f32[32,1,2176]{2,1,0:T(1,128)}), f32[32,1,2176]{2,1,0:T(1,128)S(1)}, u32[]{:S(2)}, u32[]{:S(2)}) %all-to-all-start.1) | async-done | bytes 278560 | tf_op jit(solution)/shard_map/all_to_all | solution.py:167
  42.2 0.7 %reduce.6 = f32[32,2176]{1,0:T(8,128)S(1)} reduce(f32[32,1,2176]{2,1,0:T(1,128)S(1)} %all-to-all-done.1, f32[]{:T(128)} %constant.97), dimensions={1}, to_apply=%all_to_all.7.reduce_sub_computation | reduce | bytes 557060 | tf_op jit(solution)/shard_map/all_to_all | solution.py:167
  43.0 0.1 fusion.55
  43.1 0.1 fusion.48
  43.2 0.1 multiply_reduce_fusion
  43.3 0.1 fusion.47
  43.4 0.1 divide_convert_fusion
  43.5 5.2 %all-gather = bf16[8,16,128]{2,1,0:T(8,128)(2,1)S(1)} all-gather(bf16[2,16,128]{2,1,0:T(8,128)(2,1)S(1)} %divide_convert_fusion), channel_id=2, replica_groups=mesh['ctx'=4,'row'=8] {'ctx'}, dimensions={0}, use_global_device_ids=true | all-gather | bytes 40960 | tf_op jit(solution)/shard_map/all_gather | solution.py:201
  48.7 0.6 %reshape.222 = bf16[2,2,4096]{2,1,0:T(2,128)(2,1)} reshape(bf16[2,2,2,16,128]{4,3,2,1,0:T(8,128)(2,1)S(1)} %bitcast.162) | data formatting | bytes 65536 | tf_op jit(solution)/shard_map/reshape | solution.py:204
  (58 shorter events, 0.9 us)
Async XLA Ops:
  0.0 31.9 %copy-start = (bf16[2,2,512]{2,1,0:T(2,128)(2,1)S(1)}, bf16[2,2,512]{2,1,0:T(2,128)(2,1)}, u32[]{:S(2)}) copy-start(bf16[2,2,512]{2,1,0:T(2,128)(2,1)} %param.23) | copy-start | bytes 12292
  0.0 0.8 %copy-start.9 = (s32[2]{0:T(128)S(1)}, s32[2]{0:T(128)}, u32[]{:S(2)}) copy-start(s32[2]{0:T(128)} %param.15) | copy-start | bytes 28
  1.7 7.4 %copy-start.3 = (bf16[8,32,512]{2,1,0:T(8,128)(2,1)S(1)}, bf16[8,32,512]{2,1,0:T(8,128)(2,1)}, u32[]{:S(2)}) copy-start(bf16[8,32,512]{2,1,0:T(8,128)(2,1)} %param.16) | copy-start | bytes 786436
  1.7 17.0 %all-to-all-start = ((bf16[8,144,128]{2,1,0:T(8,128)(2,1)}), bf16[8,144,128]{2,1,0:T(8,128)(2,1)S(1)}, u32[]{:S(2)}, u32[]{:S(2)}) async-start(bf16[8,144,128]{2,1,0:T(8,128)(2,1)} %broadcast_in_dim.119), calls=%async_computation | async-start | bytes 589824 | tf_op jit(solution)/shard_map/all_to_all | solution.py:95
  9.1 1.0 %copy-start.4 = (bf16[8,32,512]{2,1,0:T(8,128)(2,1)S(1)}, bf16[8,32,512]{2,1,0:T(8,128)(2,1)}, u32[]{:S(2)}) copy-start(bf16[8,32,512]{2,1,0:T(8,128)(2,1)} %param.17) | copy-start | bytes 786436
  9.2 2.7 %copy-start.1 = (bf16[16,64,512]{2,1,0:T(8,128)(2,1)S(1)}, bf16[16,64,512]{2,1,0:T(8,128)(2,1)}, u32[]{:S(2)}) copy-start(bf16[16,64,512]{2,1,0:T(8,128)(2,1)} %param.18) | copy-start | bytes 3145732
  10.2 1.2 %copy-start.5 = (bf16[2,2,4096]{2,1,0:T(2,128)(2,1)S(1)}, bf16[2,2,4096]{2,1,0:T(2,128)(2,1)}, u32[]{:S(2)}) copy-start(bf16[2,2,4096]{2,1,0:T(2,128)(2,1)} %param.14) | copy-start | bytes 98308
  10.3 8.4 %collective-permute-start = (bf16[2,8,32,2,128]{4,2,3,1,0:T(8,128)(2,1)S(1)}, bf16[2,8,32,2,128]{4,2,3,1,0:T(8,128)(2,1)S(1)}, u32[]{:S(2)}, u32[]{:S(2)}) collective-permute-start(bf16[2,8,32,2,128]{4,2,3,1,0:T(8,128)(2,1)S(1)} %constant_dynamic-slice_fusion.6), channel_id=1, source_target_pairs={{0,8},{8,0},{16,24},{24,16},{1,9},{9,1},{17,25},{25,17},{2,10},{10... | collective-permute-start | bytes 786440 | tf_op jit(solution)/shard_map/ppermute | solution.py:115
  10.4 0.7 %copy-start.6 = (s32[2,32]{1,0:T(2,128)S(1)}, s32[2,32]{1,0:T(2,128)}, u32[]{:S(2)}) copy-start(s32[2,32]{1,0:T(2,128)} %param.20) | copy-start | bytes 772
  11.9 1.6 %copy-start.2 = (bf16[16,64,512]{2,1,0:T(8,128)(2,1)S(1)}, bf16[16,64,512]{2,1,0:T(8,128)(2,1)}, u32[]{:S(2)}) copy-start(bf16[16,64,512]{2,1,0:T(8,128)(2,1)} %param.19) | copy-start | bytes 3145732
  13.5 0.7 %copy-start.7 = (s32[2]{0:T(128)S(1)}, s32[2]{0:T(128)}, u32[]{:S(2)}) copy-start(s32[2]{0:T(128)} %param.21) | copy-start | bytes 28
  16.9 1.4 %collective-permute-start.1 = (f32[2,2,2,8,130]{4,3,1,2,0:T(8,128)S(1)}, f32[2,2,2,8,130]{4,3,1,2,0:T(8,128)S(1)}, u32[]{:S(2)}, u32[]{:S(2)}) collective-permute-start(f32[2,2,2,8,130]{4,3,1,2,0:T(8,128)S(1)} %fusion.30), channel_id=1, source_target_pairs={{0,8},{8,0},{16,24},{24,16},{1,9},{9,1},{17,25},{25,17},{2,10},{10... | collective-permute-start | bytes 99848 | tf_op jit(solution)/shard_map/ppermute | solution.py:139
  25.1 6.0 %copy-start.8 = (bf16[2,2,512]{2,1,0:T(2,128)(2,1)S(1)}, bf16[2,2,512]{2,1,0:T(2,128)(2,1)}, u32[]{:S(2)}) copy-start(bf16[2,2,512]{2,1,0:T(2,128)(2,1)} %param.22) | copy-start | bytes 12292
  25.1 17.1 %all-to-all-start.1 = ((f32[32,1,2176]{2,1,0:T(1,128)}), f32[32,1,2176]{2,1,0:T(1,128)S(1)}, u32[]{:S(2)}, u32[]{:S(2)}) async-start(f32[32,1,2176]{2,1,0:T(1,128)} %copy.159), calls=%async_computation.1 | async-start | bytes 557056 | tf_op jit(solution)/shard_map/all_to_all | solution.py:167

commit v9 on v8

--- a/solution.py
+++ b/solution.py
@@ -116,17 +116,27 @@
 
     half_query = lax.dynamic_slice_in_dim(every_query, core_bit * half_kv, half_kv, 2)
 
+    prefix_count_iota = jnp.arange(prefix_count, dtype=jnp.int32)
+    chosen = (every_prefix[:, None] == prefix_count_iota[None, :]).reshape(
+        total_rows, 1, 1, 1, prefix_count, 1
+    )
+
     def prefix_block(kv):
-        row_keys = jnp.take(kv[0], every_prefix, axis=0)
-        row_values = jnp.take(kv[1], every_prefix, axis=0)
         scores = (
             jnp.einsum(
-                "rskgd,rtkd->rskgt", half_query, row_keys, preferred_element_type=jnp.float32
+                "rskgd,ptkd->rskgpt", half_query, kv[0], preferred_element_type=jnp.float32
             )
             * score_scale
         )
-        always = jnp.ones((1, 1, 1, 1, span_len), dtype=bool)
-        return block_stats(scores, always, row_values, "rskgt,rtkd->rskgd")
+        block_peak = jnp.max(jnp.where(chosen, scores, MASKED_SCORE), axis=(4, 5))
+        weights = jnp.where(
+            chosen, jnp.exp(scores - block_peak[..., None, None]), 0.0
+        ).astype(jnp.bfloat16)
+        block_total = jnp.sum(weights.astype(jnp.float32), axis=(4, 5))
+        block_sum = jnp.einsum(
+            "rskgpt,ptkd->rskgd", weights, kv[1], preferred_element_type=jnp.float32
+        )
+        return (block_peak, block_total, block_sum)
 
     prefix_stats = combine_pair(prefix_block(own_kv), prefix_block(partner_kv))
 

time: 49.8 us -> 54.6 us (1.096)
  waiting for transfers between devices: 11 us -> 16 us
  matrix products: 3.91 us -> 7.12 us
  local copies, waits for them, and re-layouts: 11.7 us -> 9.24 us
  starting transfers between devices: 14 us -> 12.2 us
  other arithmetic: 3.06 us -> 4.02 us
    all_to_all x1, waiting for transfers between devices: 0.04 us -> 5.13 us  [per_device(): lax.all_to_all(fanned, 'row', split_axis=0, concat_axis=0, tiled=True)]
    dot_general x2 -> x4, matrix products: 0.85 us -> 5.77 us  [the longest x2 3.48 us: prefix_block(): jnp.einsum('rskgpt,ptkd->rskgd', weights, kv[1], preferred_element_type=j...]
    gather x4 -> x0, local copies, waits for them, and re-layouts: 2.39 us -> none  [the longest x2 1.2 us: prefix_block(): row_values = jnp.take(kv[1], every_prefix, axis=0)]
    unnamed x22 -> x24, local copies, waits for them, and re-layouts: 2.5 us -> 0.43 us
    another operation x3, local copies, waits for them, and re-layouts: 0.2 us -> 2.19 us  [per_device(): jnp.stack([prefix_keys.reshape(prefix_count, span_len, KVH, HD), prefix_v...]
    all_to_all x1, starting transfers between devices: 6.01 us -> 4.64 us  [per_device(): lax.all_to_all(outgoing.reshape(dests, 1, flat_len), ('ctx', 'row'), spli...]
    reduce_sum x0 -> x1, other arithmetic: none -> 1.23 us  [prefix_block(): block_total = jnp.sum(weights.astype(jnp.float32), axis=(4, 5))]
    dot_general x1, matrix products: 1.76 us -> 0.54 us  [per_device(): jnp.einsum('rskgd,tkd->rskgt', own_query, flat_keys, preferred_element_ty...]
  transfers between devices with their start and end apart: 4 -> 4, of which waited for: 2 -> 3; matrix products, arithmetic and copies ran while one was open for 13% -> 11% of each run, Pallas kernels for 0% -> 0%
where the time goes in v9:
time: 54.6 us; the launch traced here: 54.2 us
  waiting for transfers between devices  16 us (29%)
  starting transfers between devices  12.2 us (22%)
  local copies, waits for them, and re-layouts  9.24 us (17%)
  matrix products  7.12 us (13%)
  blocking collectives  5.19 us (10%)
  other arithmetic  4.02 us (7%)
    all_to_all x1, waiting for transfers between devices, per_device(): lax.all_to_all(outgoing.reshape(dests, 1, flat_len), ('ctx', 'row'), spli...  10.1 us
    all_to_all x1, starting transfers between devices, per_device(): lax.all_to_all(fanned, 'row', split_axis=0, concat_axis=0, tiled=True)  6.8 us
    all_gather x1, blocking collectives, per_device(): whole = lax.all_gather(result, 'ctx', axis=0, tiled=False)  5.19 us
    all_to_all x1, waiting for transfers between devices, per_device(): lax.all_to_all(fanned, 'row', split_axis=0, concat_axis=0, tiled=True)  5.13 us
    all_to_all x1, starting transfers between devices, per_device(): lax.all_to_all(outgoing.reshape(dests, 1, flat_len), ('ctx', 'row'), spli...  4.64 us
    dot_general x2, matrix products, prefix_block(): jnp.einsum('rskgpt,ptkd->rskgd', weights, kv[1], preferred_element_type=j...  3.48 us
    dot_general x2, matrix products, prefix_block(): jnp.einsum('rskgd,ptkd->rskgpt', half_query, kv[0], preferred_element_typ...  2.29 us
    another operation x3, local copies, waits for them, and re-layouts, per_device(): jnp.stack([prefix_keys.reshape(prefix_count, span_len, KVH, HD), prefix_v...  2.19 us
  transfers between devices with their start and end apart: 4, of which 3 were waited for; matrix products, arithmetic and copies ran while one was open for 11% of the time, Pallas kernels for 0%

profile of v9, /device:TPU:0, one launch (start us, length us, event | category | flops | bytes accessed | tf_op | source)
XLA Modules:
  0.0 54.2 jit_solution(3102229377091487818)
XLA Ops:
  0.0 1.1 %stack_reshape.6 = bf16[1,8,32,4,128]{4,3,2,1,0:T(4,128)(2,1)S(1)} reshape(bf16[8,32,512]{2,1,0:T(8,128)(2,1)} %param.14) | data formatting | bytes 524288 | tf_op jit(solution)/shard_map/stack;reshape | solution.py:107
  1.2 1.0 %stack_reshape.7 = bf16[1,8,32,4,128]{4,3,2,1,0:T(4,128)(2,1)S(1)} reshape(bf16[8,32,512]{2,1,0:T(8,128)(2,1)} %param.15) | data formatting | bytes 524288 | tf_op jit(solution)/shard_map/stack;reshape | solution.py:107
  2.3 0.7 %constant_dynamic-slice_fusion.4 = bf16[2,8,32,2,128]{4,2,1,3,0:T(8,128)(2,1)} fusion(bf16[2,8,32,4,128]{4,2,1,3,0:T(8,128)(2,1)S(1)} %copy_dynamic-update-slice_fusion, s32[]{:T(128)S(6)} %select_n.65), kind=kLoop, calls=%fused_computation.86 | loop fusion | bytes 524292 | tf_op jit(solution)/shard_map/dynamic_slice | solution.py:114
  3.1 0.5 collective-permute-start
  3.6 0.1 pad_maximum_fusion
  3.7 0.7 %broadcast_in_dim.118 = bf16[8,144,128]{2,1,0:T(8,128)(2,1)} broadcast(bf16[144,128]{1,0:T(8,128)(2,1)S(1)} %pad_maximum_fusion), dimensions={1,2} | broadcast | bytes 331776 | tf_op jit(solution)/shard_map/broadcast_in_dim | solution.py:94
  4.4 6.8 %all-to-all-start = ((bf16[8,144,128]{2,1,0:T(8,128)(2,1)}), bf16[8,144,128]{2,1,0:T(8,128)(2,1)S(1)}, u32[]{:S(2)}, u32[]{:S(2)}) async-start(bf16[8,144,128]{2,1,0:T(8,128)(2,1)} %broadcast_in_dim.118), calls=%async_computation | async-start | bytes 589824 | tf_op jit(solution)/shard_map/all_to_all | solution.py:95
  11.3 0.2 fusion.28
  11.4 0.2 compare_reduce_fusion
  11.7 0.1 add.103
  11.9 0.1 and.26
  12.1 0.3 reshape.220
  12.4 0.3 reshape.222
  12.7 0.1 compare_and_fusion
  12.8 0.5 select_reduce_fusion
  13.3 0.3 convert_reduce_fusion.2
  13.6 0.3 fusion.13
  14.0 0.2 copy.157
  14.2 0.2 copy.156
  14.4 0.1 fusion.19
  14.5 0.3 collective-permute-start.1
  14.8 0.1 copy.201
  14.9 0.1 copy.202
  15.0 0.8 %collective-permute-done.1 = f32[2,2,2,8,130]{4,0,3,1,2:T(2,128)S(1)} collective-permute-done((f32[2,2,2,8,130]{4,0,3,1,2:T(2,128)S(1)}, f32[2,2,2,8,130]{4,0,3,1,2:T(2,128)S(1)}, u32[]{:S(2)}, u32[]{:S(2)}) %collective-permute-start.1) | collective-permute-done | bytes 33312 | tf_op jit(solution)/shard_map/ppermute | solution.py:149
  15.8 0.1 fusion.42
  15.9 0.1 copy.158
  16.0 0.1 copy.159
  16.1 0.1 copy.167
  16.2 0.1 copy.168
  16.3 5.1 %all-to-all-done = bf16[8,144,128]{2,1,0:T(8,128)(2,1)S(1)} async-done(((bf16[8,144,128]{2,1,0:T(8,128)(2,1)}), bf16[8,144,128]{2,1,0:T(8,128)(2,1)S(1)}, u32[]{:S(2)}, u32[]{:S(2)}) %all-to-all-start) | async-done | bytes 294944 | tf_op jit(solution)/shard_map/all_to_all | solution.py:95
  21.5 0.2 convert_reduce_fusion.4
  21.7 0.1 reshape.244
  21.8 1.3 %fusion.16 = f32[2,8,32,16,2,8]{2,3,5,4,1,0:T(8,128)S(1)} fusion(bf16[2,8,32,2,128]{4,2,1,3,0:T(8,128)(2,1)} %collective-permute-done, bf16[16,2,2,8,128]{4,3,2,1,0:T(8,128)(2,1)S(1)} %constant_dynamic-slice_fusion.5), kind=kOutput, calls=%fused_computation.39 | convolution fusion | flops 33554432 | bytes 786432 | tf_op jit(solution)/shard_map/rskgd,ptkd->rskgpt/dot_general | solution.py:126
  23.2 0.9 %fusion.4 = (f32[16,2,2,8]{0,3,1,2:T(8,128)S(1)}, f32[16,2,2,8]{0,3,1,2:T(8,128)S(1)}, f32[2,8,32,16,2,8]{2,3,5,4,1,0:T(8,128)S(1)}) fusion(pred[16,8]{0,1:T(8,128)(4,1)S(1)} %iota_compare_fusion.1, f32[2,8,32,16,2,8]{2,3,5,4,1,0:T(8,128)S(1)} %fusion.16, bf16[16,2,2,8,128]{4,3,2,1,0:T(8,128)(2,1)S(1)} %constant_dynamic-slice_fusion.5, ...), kind=kOutput, calls=%fused_computation.8 | convolution fusion | flops 34339840 | bytes 2888708 | tf_op jit(solution)/shard_map/rskgd,ptkd->rskgpt/dot_general | solution.py:126
  24.1 1.2 %convert_reduce_fusion.1 = (f32[16,2,2,8]{0,3,1,2:T(8,128)S(1)}, f32[16,2,2,8]{0,3,1,2:T(8,128)S(1)}) fusion(f32[16,2,2,8]{0,3,1,2:T(8,128)S(1)} %get-tuple-element.19, f32[2,8,32,16,2,8]{2,3,5,4,1,0:T(8,128)S(1)} %get-tuple-element.41, pred[16,8]{0,1:T(8,128)(4,1)S(1)} %iota_compare_fusion.1, f32[16,2,2,8]{0,3,1,2:T(8,128)S(1)} %get-tuple-element.20, ...), kind=kLoop, calls=%fused_computation.13 | loop fusion | flops 1571840 | bytes 1056896 | tf_op jit(solution)/shard_map/reduce_sum | solution.py:135
  25.4 1.3 %fusion.11 = f32[16,2,2,8,128]{4,0,3,1,2:T(8,128)S(1)} fusion(bf16[2,8,32,4,128]{4,2,1,3,0:T(8,128)(2,1)S(1)} %copy-done.4, s32[]{:T(128)S(6)} %add.118, s32[]{:T(128)S(6)} %select_n.63, f32[16,2,2,8]{0,3,1,2:T(8,128)S(1)} %get-tuple-element.32, f32[2,8,32,16,2,8]{2,3,5,4,1,0:T(8,128)S(1)} %get-tuple-element.41, f32[16,2,2,8]{0,3,1,2:T(8,128)S(1)} %get-tuple-element.19, ...), kind=kOutput, calls=%fused_computation.20 | convolution fusion | flops 34144256 | bytes 2524168 | tf_op jit(solution)/shard_map/rskgpt,ptkd->rskgd/dot_general | solution.py:136
  26.7 0.1 multiply_add_fusion
  26.8 2.2 %fusion.10 = f32[16,2,2,8,128]{4,0,3,1,2:T(8,128)S(1)} fusion(f32[16,2,2,8,128]{4,0,3,1,2:T(8,128)S(1)} %fusion.11, bf16[2,8,32,2,128]{4,2,1,3,0:T(8,128)(2,1)} %collective-permute-done, f32[16,2,2,8]{0,3,1,2:T(8,128)S(1)} %get-tuple-element.33, f32[2,8,32,16,2,8]{2,3,5,4,1,0:T(8,128)S(1)} %fusion.16, f32[16,2,2,8]{0,3,1,2:T(8,128)S(1)} %get-tuple-element.20, ...), kind=kOutput, calls=%fused_computation.18 | convolution fusion | flops 34209792 | bytes 1183872 | tf_op jit(solution)/shard_map/rskgpt,ptkd->rskgd/dot_general | solution.py:136
  29.0 0.3 fusion.23
  29.2 0.1 copy.162
  29.4 0.1 copy.231
  29.5 0.2 dynamic_update_slice.10
  29.7 0.1 copy.164
  29.8 0.1 reshape.224
  29.9 0.2 dynamic_update_slice.11
  30.1 0.1 copy.169
  30.2 0.1 reshape.226
  30.3 0.1 select_maximum_fusion
  30.4 1.0 %copy.171 = f32[32,1,2176]{2,1,0:T(1,128)} copy(f32[32,1,2176]{2,0,1:T(8,128)S(1)} %maximum_bitcast_fusion) | data formatting | bytes 557056 | tf_op jit(solution)/shard_map/reshape | solution.py:178
  31.4 4.6 %all-to-all-start.1 = ((f32[32,1,2176]{2,1,0:T(1,128)}), f32[32,1,2176]{2,1,0:T(1,128)S(1)}, u32[]{:S(2)}, u32[]{:S(2)}) async-start(f32[32,1,2176]{2,1,0:T(1,128)} %copy.171), calls=%async_computation.1 | async-start | bytes 557056 | tf_op jit(solution)/shard_map/all_to_all | solution.py:177
  36.1 0.3 select_reduce_fusion.1
  36.4 0.1 reshape.233
  36.4 0.1 reshape.234
  36.5 0.1 convert_reduce_fusion.3
  36.7 0.1 reshape.240
  36.7 0.1 reshape.241
  36.8 0.2 convolution_bitcast_fusion.2
  37.0 10.1 %all-to-all-done.1 = f32[32,1,2176]{2,1,0:T(1,128)S(1)} async-done(((f32[32,1,2176]{2,1,0:T(1,128)}), f32[32,1,2176]{2,1,0:T(1,128)S(1)}, u32[]{:S(2)}, u32[]{:S(2)}) %all-to-all-start.1) | async-done | bytes 278560 | tf_op jit(solution)/shard_map/all_to_all | solution.py:177
  47.1 0.7 %reduce.6 = f32[32,2176]{1,0:T(8,128)S(1)} reduce(f32[32,1,2176]{2,1,0:T(1,128)S(1)} %all-to-all-done.1, f32[]{:T(128)} %constant.86), dimensions={1}, to_apply=%all_to_all.7.reduce_sub_computation | reduce | bytes 557060 | tf_op jit(solution)/shard_map/all_to_all | solution.py:177
  48.1 0.1 multiply_reduce_fusion
  48.2 0.1 fusion.34
  48.3 0.1 divide_convert_fusion
  48.4 5.2 %all-gather = bf16[8,16,128]{2,1,0:T(8,128)(2,1)S(1)} all-gather(bf16[2,16,128]{2,1,0:T(8,128)(2,1)S(1)} %divide_convert_fusion), channel_id=2, replica_groups=mesh['ctx'=4,'row'=8] {'ctx'}, dimensions={0}, use_global_device_ids=true | all-gather | bytes 40960 | tf_op jit(solution)/shard_map/all_gather | solution.py:211
  53.6 0.6 %reshape.243 = bf16[2,2,4096]{2,1,0:T(2,128)(2,1)} reshape(bf16[2,2,2,16,128]{4,3,2,1,0:T(8,128)(2,1)S(1)} %bitcast.182) | data formatting | bytes 65536 | tf_op jit(solution)/shard_map/reshape | solution.py:214
  (58 shorter events, 1.0 us)
Async XLA Ops:
  0.0 36.8 %copy-start = (bf16[2,2,512]{2,1,0:T(2,128)(2,1)S(1)}, bf16[2,2,512]{2,1,0:T(2,128)(2,1)}, u32[]{:S(2)}) copy-start(bf16[2,2,512]{2,1,0:T(2,128)(2,1)} %param.21) | copy-start | bytes 12292
  0.0 3.5 %copy-start.5 = (bf16[2,2,4096]{2,1,0:T(2,128)(2,1)S(1)}, bf16[2,2,4096]{2,1,0:T(2,128)(2,1)}, u32[]{:S(2)}) copy-start(bf16[2,2,4096]{2,1,0:T(2,128)(2,1)} %param.12) | copy-start | bytes 98308
  0.0 3.6 %copy-start.9 = (s32[2]{0:T(128)S(1)}, s32[2]{0:T(128)}, u32[]{:S(2)}) copy-start(s32[2]{0:T(128)} %param.13) | copy-start | bytes 28
  0.0 11.2 %copy-start.6 = (s32[2,32]{1,0:T(2,128)S(1)}, s32[2,32]{1,0:T(2,128)}, u32[]{:S(2)}) copy-start(s32[2,32]{1,0:T(2,128)} %param.18) | copy-start | bytes 772
  0.0 12.1 %copy-start.1 = (bf16[16,64,512]{2,1,0:T(8,128)(2,1)S(1)}, bf16[16,64,512]{2,1,0:T(8,128)(2,1)}, u32[]{:S(2)}) copy-start(bf16[16,64,512]{2,1,0:T(8,128)(2,1)} %param.16) | copy-start | bytes 3145732
  2.2 10.1 %copy-start.2 = (bf16[16,64,512]{2,1,0:T(8,128)(2,1)S(1)}, bf16[16,64,512]{2,1,0:T(8,128)(2,1)}, u32[]{:S(2)}) copy-start(bf16[16,64,512]{2,1,0:T(8,128)(2,1)} %param.17) | copy-start | bytes 3145732
  2.3 9.7 %copy-start.3 = (bf16[2,8,32,4,128]{4,2,1,3,0:T(8,128)(2,1)}, bf16[2,8,32,4,128]{4,2,1,3,0:T(8,128)(2,1)S(1)}, u32[]{:S(2)}) copy-start(bf16[2,8,32,4,128]{4,2,1,3,0:T(8,128)(2,1)S(1)} %copy_dynamic-update-slice_fusion) | copy-start | bytes 1572868
  3.1 18.8 %collective-permute-start = (bf16[2,8,32,2,128]{4,2,1,3,0:T(8,128)(2,1)}, bf16[2,8,32,2,128]{4,2,1,3,0:T(8,128)(2,1)}, u32[]{:S(2)}, u32[]{:S(2)}) collective-permute-start(bf16[2,8,32,2,128]{4,2,1,3,0:T(8,128)(2,1)} %constant_dynamic-slice_fusion.4), channel_id=1, source_target_pairs={{0,8},{8,0},{16,24},{24,16},{1,9},{9,1},{17,25},{25,17},{2,10},{10... | collective-permute-start | bytes 786440 | tf_op jit(solution)/shard_map/ppermute | solution.py:115
  4.4 17.0 %all-to-all-start = ((bf16[8,144,128]{2,1,0:T(8,128)(2,1)}), bf16[8,144,128]{2,1,0:T(8,128)(2,1)S(1)}, u32[]{:S(2)}, u32[]{:S(2)}) async-start(bf16[8,144,128]{2,1,0:T(8,128)(2,1)} %broadcast_in_dim.118), calls=%async_computation | async-start | bytes 589824 | tf_op jit(solution)/shard_map/all_to_all | solution.py:95
  12.1 0.7 %copy-start.7 = (s32[2]{0:T(128)S(1)}, s32[2]{0:T(128)}, u32[]{:S(2)}) copy-start(s32[2]{0:T(128)} %param.19) | copy-start | bytes 28
  14.0 9.2 %copy-start.4 = (bf16[2,8,32,4,128]{4,2,1,3,0:T(8,128)(2,1)S(1)}, bf16[2,8,32,4,128]{4,2,1,3,0:T(8,128)(2,1)}, u32[]{:S(2)}) copy-start(bf16[2,8,32,4,128]{4,2,1,3,0:T(8,128)(2,1)} %copy-done.3) | copy-start | bytes 1572868
  14.5 1.3 %collective-permute-start.1 = (f32[2,2,2,8,130]{4,0,3,1,2:T(2,128)S(1)}, f32[2,2,2,8,130]{4,0,3,1,2:T(2,128)S(1)}, u32[]{:S(2)}, u32[]{:S(2)}) collective-permute-start(f32[2,2,2,8,130]{4,0,3,1,2:T(2,128)S(1)} %fusion.19), channel_id=1, source_target_pairs={{0,8},{8,0},{16,24},{24,16},{1,9},{9,1},{17,25},{25,17},{2,10},{10... | collective-permute-start | bytes 99848 | tf_op jit(solution)/shard_map/ppermute | solution.py:149
  29.0 7.1 %copy-start.8 = (bf16[2,2,512]{2,1,0:T(2,128)(2,1)S(1)}, bf16[2,2,512]{2,1,0:T(2,128)(2,1)}, u32[]{:S(2)}) copy-start(bf16[2,2,512]{2,1,0:T(2,128)(2,1)} %param.20) | copy-start | bytes 12292
  31.4 15.7 %all-to-all-start.1 = ((f32[32,1,2176]{2,1,0:T(1,128)}), f32[32,1,2176]{2,1,0:T(1,128)S(1)}, u32[]{:S(2)}, u32[]{:S(2)}) async-start(f32[32,1,2176]{2,1,0:T(1,128)} %copy.171), calls=%async_computation.1 | async-start | bytes 557056 | tf_op jit(solution)/shard_map/all_to_all | solution.py:177

commit v10 on v7

--- a/solution.py
+++ b/solution.py
@@ -116,19 +116,26 @@
 
     half_query = lax.dynamic_slice_in_dim(every_query, core_bit * half_kv, half_kv, 2)
 
-    def prefix_block(kv):
-        row_keys = jnp.take(kv[0], every_prefix, axis=0)
-        row_values = jnp.take(kv[1], every_prefix, axis=0)
-        scores = (
-            jnp.einsum(
-                "rskgd,rtkd->rskgt", half_query, row_keys, preferred_element_type=jnp.float32
-            )
-            * score_scale
+    kv_pair = jnp.concatenate([own_kv, partner_kv], axis=2)
+    row_kv = jnp.take(kv_pair, every_prefix, axis=1).reshape(
+        2, total_rows, 2, span_len, half_kv, HD
+    )
+    pair_scores = (
+        jnp.einsum(
+            "rskgd,rbtkd->rskgbt", half_query, row_kv[0], preferred_element_type=jnp.float32
         )
-        always = jnp.ones((1, 1, 1, 1, span_len), dtype=bool)
-        return block_stats(scores, always, row_values, "rskgt,rtkd->rskgd")
-
-    prefix_stats = combine_pair(prefix_block(own_kv), prefix_block(partner_kv))
+        * score_scale
+    )
+    pair_peak = jnp.max(pair_scores, axis=-1)
+    pair_weights = jnp.exp(pair_scores - pair_peak[..., None]).astype(jnp.bfloat16)
+    pair_total = jnp.sum(pair_weights.astype(jnp.float32), axis=-1)
+    pair_sum = jnp.einsum(
+        "rskgbt,rbtkd->rskgbd", pair_weights, row_kv[1], preferred_element_type=jnp.float32
+    )
+    prefix_stats = combine_pair(
+        (pair_peak[..., 0], pair_total[..., 0], pair_sum[..., 0, :]),
+        (pair_peak[..., 1], pair_total[..., 1], pair_sum[..., 1, :]),
+    )
 
     def head_half(member, at):
         return lax.dynamic_slice_in_dim(member, at * half_kv, half_kv, 2)

time: 49.7 us -> 51.6 us (1.038)
  other arithmetic: 3.07 us -> 5.77 us
  matrix products: 3.91 us -> 2.54 us
  starting transfers between devices: 14 us -> 14.9 us
    gather x4 -> x1, local copies, waits for them, and re-layouts: 2.39 us -> 0.75 us  [per_device(): jnp.take(kv_pair, every_prefix, axis=1)]
    dot_general x1, matrix products: 1.76 us -> 0.54 us  [per_device(): jnp.einsum('rskgd,tkd->rskgt', own_query, flat_keys, preferred_element_ty...]
    concatenate x0 -> x1, other arithmetic: none -> 1.01 us  [per_device(): kv_pair = jnp.concatenate([own_kv, partner_kv], axis=2)]
    all_to_all x1, starting transfers between devices: 6.01 us -> 6.96 us  [per_device(): lax.all_to_all(outgoing.reshape(dests, 1, (chunk + pt_rows) * LANES), ('c...]
    reshape x1, local copies, waits for them, and re-layouts: 1.12 us -> 0.29 us  [per_device(): flat_keys = pool_keys.reshape(slot_count * page_len, KVH, HD)]
    unnamed x21 -> x31, local copies, waits for them, and re-layouts: 2.41 us -> 3.19 us
    convert_element_type x1, other arithmetic: 0.01 us -> 0.67 us  [per_device(): prefix_id.astype(jnp.bfloat16)[:, None]]
    dynamic_update_slice x3 -> x5, local copies, waits for them, and re-layouts: 0.05 us -> 0.65 us  [per_device(): lax.dynamic_update_slice_in_dim(whole_arr, piece_arr, row_start, 0)]
where the time goes in v10:
time: 51.6 us; the launch traced here: 51.1 us
  starting transfers between devices  14.9 us (29%)
  local copies, waits for them, and re-layouts  11.4 us (22%)
  waiting for transfers between devices  10.8 us (21%)
  other arithmetic  5.77 us (11%)
  blocking collectives  5.19 us (10%)
  matrix products  2.54 us (5%)
    all_to_all x1, waiting for transfers between devices, per_device(): lax.all_to_all(outgoing.reshape(dests, 1, (chunk + pt_rows) * LANES), ('c...  10.1 us
    all_to_all x1, starting transfers between devices, per_device(): lax.all_to_all(fanned, 'row', split_axis=0, concat_axis=0, tiled=True)  7.38 us
    all_to_all x1, starting transfers between devices, per_device(): lax.all_to_all(outgoing.reshape(dests, 1, (chunk + pt_rows) * LANES), ('c...  6.96 us
    all_gather x1, blocking collectives, per_device(): whole = lax.all_gather(result, 'ctx', axis=0, tiled=False)  5.19 us
    unnamed x31, local copies, waits for them, and re-layouts  3.19 us
  transfers between devices with their start and end apart: 4, of which 2 were waited for; matrix products, arithmetic and copies ran while one was open for 13% of the time, Pallas kernels for 0%

profile of v10, /device:TPU:0, one launch (start us, length us, event | category | flops | bytes accessed | tf_op | source)
XLA Modules:
  0.0 51.1 jit_solution(2636916902783191157)
XLA Ops:
  0.0 0.7 %convert_element_type.46 = bf16[2]{0:T(256)(128)(2,1)S(1)} convert(s32[2]{0:T(128)} %param.13) | non-fusion elementwise | flops 2 | bytes 12 | tf_op jit(solution)/shard_map/convert_element_type | solution.py:91
  0.7 0.8 %reshape.216 = bf16[128,128]{1,0:T(8,128)(2,1)S(1)} reshape(bf16[2,2,4096]{2,1,0:T(2,128)(2,1)} %param.12) | data formatting | bytes 65536 | tf_op jit(solution)/shard_map/reshape | solution.py:93
  1.5 0.1 pad_maximum_fusion.2
  1.6 0.7 %broadcast_in_dim.99 = bf16[8,144,128]{2,1,0:T(8,128)(2,1)} broadcast(bf16[144,128]{1,0:T(8,128)(2,1)S(1)} %pad_maximum_fusion.2), dimensions={1,2} | broadcast | bytes 331776 | tf_op jit(solution)/shard_map/broadcast_in_dim | solution.py:94
  2.3 7.4 %all-to-all-start = ((bf16[8,144,128]{2,1,0:T(8,128)(2,1)}), bf16[8,144,128]{2,1,0:T(8,128)(2,1)S(1)}, u32[]{:S(2)}, u32[]{:S(2)}) async-start(bf16[8,144,128]{2,1,0:T(8,128)(2,1)} %broadcast_in_dim.99), calls=%async_computation | async-start | bytes 589824 | tf_op jit(solution)/shard_map/all_to_all | solution.py:95
  9.8 0.9 %copy-done.5 = bf16[8,32,512]{2,1,0:T(8,128)(2,1)S(1)} copy-done((bf16[8,32,512]{2,1,0:T(8,128)(2,1)S(1)}, bf16[8,32,512]{2,1,0:T(8,128)(2,1)}, u32[]{:S(2)}) %copy-start.5) | copy-done | bytes 262168
  11.1 0.7 %copy-done.9 = s32[2,32]{1,0:T(2,128)S(1)} copy-done((s32[2,32]{1,0:T(2,128)S(1)}, s32[2,32]{1,0:T(2,128)}, u32[]{:S(2)}) %copy-start.9) | copy-done | bytes 280
  11.7 0.2 compare_reduce_fusion
  11.9 0.2 fusion.18
  12.2 0.1 and.34
  12.6 0.3 reshape.218
  12.9 0.4 copy-done.10
  13.3 0.5 %select_reduce_fusion = (f32[2,2,4,8]{3,1,0,2:T(2,128)S(1)}, f32[2,2,4,8,1024]{4,3,1,0,2:T(8,128)S(1)}) fusion(pred[2,1024]{1,0:T(4,128)(4,1)S(1)} %compare_and_fusion, bf16[2,2,4,8,128]{4,3,2,1,0:T(8,128)(2,1)S(1)} %reshape.219, bf16[1024,4,128,1,1]{2,1,0,4,3:T(4,128)(2,1)S(1)} %bitcast.162), kind=kOutput, calls=%fused_computation.17 | convolution fusion | flops 33947520 | bytes 1608192 | tf_op jit(solution)/shard_map/rskgd,tkd->rskgt/dot_general | solution.py:72
  13.9 0.9 %convert_reduce_fusion.1 = (f32[2,2,4,8]{3,1,0,2:T(2,128)S(1)}, bf16[2,2,4,8,1024]{4,3,1,0,2:T(8,128)(2,1)}) fusion(f32[2,2,4,8,1024]{4,3,1,0,2:T(8,128)S(1)} %get-tuple-element.46, f32[2,2,4,8]{3,1,0,2:T(2,128)S(1)} %get-tuple-element.45, pred[2,1024]{1,0:T(4,128)(4,1)S(1)} %compare_and_fusion), kind=kLoop, calls=%fused_computation.15 | loop fusion | flops 655232 | bytes 789504 | tf_op jit(solution)/shard_map/reduce_sum | solution.py:22
  14.7 0.2 copy.198
  14.9 0.2 copy.199
  15.1 0.3 reshape.220
  15.4 0.7 %copy-done.3 = bf16[2,2,4,8,1024]{4,3,1,0,2:T(8,128)(2,1)S(1)} copy-done((bf16[2,2,4,8,1024]{4,3,1,0,2:T(8,128)(2,1)S(1)}, bf16[2,2,4,8,1024]{4,3,1,0,2:T(8,128)(2,1)}, u32[]{:S(2)}) %copy-start.3) | copy-done | bytes 262168
  16.0 0.3 fusion.3
  16.3 0.1 fusion.11
  16.4 0.5 collective-permute-start.1
  16.9 0.1 copy.253
  17.0 0.1 copy.250
  17.1 0.7 %collective-permute-done.1 = f32[2,2,2,8,130]{4,3,1,2,0:T(8,128)S(1)} collective-permute-done((f32[2,2,2,8,130]{4,3,1,2,0:T(8,128)S(1)}, f32[2,2,2,8,130]{4,3,1,2,0:T(8,128)S(1)}, u32[]{:S(2)}, u32[]{:S(2)}) %collective-permute-start.1) | collective-permute-done | bytes 33312 | tf_op jit(solution)/shard_map/ppermute | solution.py:146
  17.9 0.1 copy.200
  18.0 0.1 copy.215
  18.1 0.1 copy.216
  18.2 0.1 copy.201
  18.3 1.0 %pad_maximum_fusion = bf16[2,8,64,2,128]{4,2,3,1,0:T(8,128)(2,1)S(1)} fusion(bf16[2,8,32,2,128]{4,2,3,1,0:T(8,128)(2,1)} %collective-permute-done, bf16[2,8,32,2,128]{4,2,3,1,0:T(8,128)(2,1)S(1)} %get-tuple-element.31), kind=kLoop, calls=%fused_computation.13 | loop fusion | flops 1048576 | bytes 1048576 | tf_op jit(solution)/shard_map/concatenate | solution.py:119
  19.3 0.2 convert_reduce_fusion.3
  19.7 0.7 %gather_fusion = bf16[16,2,64,2,128]{4,2,3,1,0:T(8,128)(2,1)S(1)} fusion(bf16[2,8,64,2,128]{4,2,3,1,0:T(8,128)(2,1)S(1)} %pad_maximum_fusion, s32[1024]{0:T(1024)S(1)} %pad_clamp_fusion), kind=kCustom, calls=%fused_computation | custom fusion | bytes 2097216 | tf_op jit(solution)/shard_map/jit(_take)/gather | solution.py:120
  20.5 0.2 select_bitcast_fusion
  20.8 0.9 %fusion.38 = (f32[16,2,2,8,2]{3,1,4,2,0:T(2,128)S(1)}, f32[16,2,2,8,2,32]{5,3,1,4,2,0:T(8,128)S(1)}) fusion(bf16[16,2,32,2,128,1]{4,2,5,1,3,0:T(8,128)(2,1)S(1)} %bitcast.161, bf16[16,2,4,8,128]{4,3,2,1,0:T(8,128)(2,1)S(1)} %bitcast.167, s32[]{:T(128)S(6)} %select_n.71), kind=kOutput, calls=%fused_computation.107 | convolution fusion | flops 8453120 | bytes 790532 | tf_op jit(solution)/shard_map/rskgd,rbtkd->rskgbt/dot_general | solution.py:124
  21.9 0.5 convert_reduce_fusion
  22.4 0.3 convolution_bitcast_fusion
  22.8 0.1 copy.190
  22.9 0.1 copy.188
  23.1 0.1 multiply_add_fusion
  23.2 0.2 dynamic_update_slice.10
  23.4 0.2 dynamic_update_slice.11
  23.7 0.1 copy.202
  23.8 0.1 copy.204
  23.9 0.1 copy.207
  24.0 0.1 copy.203
  24.1 0.2 fusion.7
  24.3 0.1 fusion.15
  24.4 0.1 copy.217
  24.5 0.1 reshape.225
  24.6 0.1 copy.210
  24.7 0.1 reshape.223
  25.0 1.0 %reshape.262 = f32[32,1,2176]{2,1,0:T(1,128)} reshape(f32[32,17,128]{2,1,0:T(8,128)S(1)} %pad_maximum_fusion.1) | data formatting | bytes 557056 | tf_op jit(solution)/shard_map/reshape | solution.py:176
  25.9 7.0 %all-to-all-start.1 = ((f32[32,1,2176]{2,1,0:T(1,128)}), f32[32,1,2176]{2,1,0:T(1,128)S(1)}, u32[]{:S(2)}, u32[]{:S(2)}) async-start(f32[32,1,2176]{2,1,0:T(1,128)} %reshape.262), calls=%async_computation.1 | async-start | bytes 557056 | tf_op jit(solution)/shard_map/all_to_all | solution.py:175
  32.9 0.3 select_reduce_fusion.1
  33.2 0.1 reshape.233
  33.3 0.1 reshape.234
  33.4 0.1 convert_reduce_fusion.2
  33.5 0.1 reshape.240
  33.6 0.1 reshape.241
  33.7 0.2 convolution_bitcast_fusion.1
  33.9 10.1 %all-to-all-done.1 = f32[32,1,2176]{2,1,0:T(1,128)S(1)} async-done(((f32[32,1,2176]{2,1,0:T(1,128)}), f32[32,1,2176]{2,1,0:T(1,128)S(1)}, u32[]{:S(2)}, u32[]{:S(2)}) %all-to-all-start.1) | async-done | bytes 278560 | tf_op jit(solution)/shard_map/all_to_all | solution.py:175
  44.0 0.7 %reduce.7 = f32[32,2176]{1,0:T(8,128)S(1)} reduce(f32[32,1,2176]{2,1,0:T(1,128)S(1)} %all-to-all-done.1, f32[]{:T(128)} %constant.101), dimensions={1}, to_apply=%all_to_all.7.reduce_sub_computation | reduce | bytes 557060 | tf_op jit(solution)/shard_map/all_to_all | solution.py:175
  44.9 0.1 multiply_reduce_fusion
  45.3 5.2 %all-gather = bf16[8,16,128]{2,1,0:T(8,128)(2,1)S(1)} all-gather(bf16[2,16,128]{2,1,0:T(8,128)(2,1)S(1)} %divide_convert_fusion), channel_id=2, replica_groups=mesh['ctx'=4,'row'=8] {'ctx'}, dimensions={0}, use_global_device_ids=true | all-gather | bytes 40960 | tf_op jit(solution)/shard_map/all_gather | solution.py:209
  50.4 0.6 %reshape.243 = bf16[2,2,4096]{2,1,0:T(2,128)(2,1)} reshape(bf16[2,2,2,16,128]{4,3,2,1,0:T(8,128)(2,1)S(1)} %bitcast.173) | data formatting | bytes 65536 | tf_op jit(solution)/shard_map/reshape | solution.py:212
  (79 shorter events, 2.2 us)
Async XLA Ops:
  0.0 33.7 %copy-start = (bf16[2,2,512]{2,1,0:T(2,128)(2,1)S(1)}, bf16[2,2,512]{2,1,0:T(2,128)(2,1)}, u32[]{:S(2)}) copy-start(bf16[2,2,512]{2,1,0:T(2,128)(2,1)} %param.21) | copy-start | bytes 12292
  2.3 7.4 %copy-start.4 = (bf16[8,32,512]{2,1,0:T(8,128)(2,1)S(1)}, bf16[8,32,512]{2,1,0:T(8,128)(2,1)}, u32[]{:S(2)}) copy-start(bf16[8,32,512]{2,1,0:T(8,128)(2,1)} %param.14) | copy-start | bytes 786436
  2.3 17.0 %all-to-all-start = ((bf16[8,144,128]{2,1,0:T(8,128)(2,1)}), bf16[8,144,128]{2,1,0:T(8,128)(2,1)S(1)}, u32[]{:S(2)}, u32[]{:S(2)}) async-start(bf16[8,144,128]{2,1,0:T(8,128)(2,1)} %broadcast_in_dim.99), calls=%async_computation | async-start | bytes 589824 | tf_op jit(solution)/shard_map/all_to_all | solution.py:95
  9.8 1.0 %copy-start.5 = (bf16[8,32,512]{2,1,0:T(8,128)(2,1)S(1)}, bf16[8,32,512]{2,1,0:T(8,128)(2,1)}, u32[]{:S(2)}) copy-start(bf16[8,32,512]{2,1,0:T(8,128)(2,1)} %param.15) | copy-start | bytes 786436
  10.7 1.8 %copy-start.1 = (bf16[16,64,512]{2,1,0:T(8,128)(2,1)S(1)}, bf16[16,64,512]{2,1,0:T(8,128)(2,1)}, u32[]{:S(2)}) copy-start(bf16[16,64,512]{2,1,0:T(8,128)(2,1)} %param.16) | copy-start | bytes 3145732
  10.9 1.2 %copy-start.6 = (bf16[2,2,4096]{2,1,0:T(2,128)(2,1)S(1)}, bf16[2,2,4096]{2,1,0:T(2,128)(2,1)}, u32[]{:S(2)}) copy-start(bf16[2,2,4096]{2,1,0:T(2,128)(2,1)} %param.12) | copy-start | bytes 98308
  11.0 7.3 %collective-permute-start = (bf16[2,8,32,2,128]{4,2,3,1,0:T(8,128)(2,1)S(1)}, bf16[2,8,32,2,128]{4,2,3,1,0:T(8,128)(2,1)}, u32[]{:S(2)}, u32[]{:S(2)}) collective-permute-start(bf16[2,8,32,2,128]{4,2,3,1,0:T(8,128)(2,1)S(1)} %get-tuple-element.32), channel_id=1, source_target_pairs={{0,8},{8,0},{16,24},{24,16},{1,9},{9,1},{17,25},{25,17},{2,10},{10... | collective-permute-start | bytes 786440 | tf_op jit(solution)/shard_map/ppermute | solution.py:115
  11.0 0.7 %copy-start.9 = (s32[2,32]{1,0:T(2,128)S(1)}, s32[2,32]{1,0:T(2,128)}, u32[]{:S(2)}) copy-start(s32[2,32]{1,0:T(2,128)} %param.18) | copy-start | bytes 772
  12.1 1.2 %copy-start.7 = (bf16[2,2,4,8,128]{4,3,2,1,0:T(8,128)(2,1)}, bf16[2,2,4,8,128]{4,3,2,1,0:T(8,128)(2,1)S(1)}, u32[]{:S(2)}) copy-start(bf16[2,2,4,8,128]{4,3,2,1,0:T(8,128)(2,1)S(1)} %reshape.219) | copy-start | bytes 98308
  12.6 0.7 %copy-start.10 = (s32[2]{0:T(128)S(1)}, s32[2]{0:T(128)}, u32[]{:S(2)}) copy-start(s32[2]{0:T(128)} %param.19) | copy-start | bytes 28
  13.3 1.8 %copy-start.2 = (bf16[16,64,512]{2,1,0:T(8,128)(2,1)S(1)}, bf16[16,64,512]{2,1,0:T(8,128)(2,1)}, u32[]{:S(2)}) copy-start(bf16[16,64,512]{2,1,0:T(8,128)(2,1)} %param.17) | copy-start | bytes 3145732
  15.1 1.0 %copy-start.3 = (bf16[2,2,4,8,1024]{4,3,1,0,2:T(8,128)(2,1)S(1)}, bf16[2,2,4,8,1024]{4,3,1,0,2:T(8,128)(2,1)}, u32[]{:S(2)}) copy-start(bf16[2,2,4,8,1024]{4,3,1,0,2:T(8,128)(2,1)} %get-tuple-element.28) | copy-start | bytes 786436
  16.4 1.4 %collective-permute-start.1 = (f32[2,2,2,8,130]{4,3,1,2,0:T(8,128)S(1)}, f32[2,2,2,8,130]{4,3,1,2,0:T(8,128)S(1)}, u32[]{:S(2)}, u32[]{:S(2)}) collective-permute-start(f32[2,2,2,8,130]{4,3,1,2,0:T(8,128)S(1)} %fusion.11), channel_id=1, source_target_pairs={{0,8},{8,0},{16,24},{24,16},{1,9},{9,1},{17,25},{25,17},{2,10},{10... | collective-permute-start | bytes 99848 | tf_op jit(solution)/shard_map/ppermute | solution.py:146
  25.9 7.0 %copy-start.8 = (bf16[2,2,4,8,128]{4,3,2,1,0:T(8,128)(2,1)S(1)}, bf16[2,2,4,8,128]{4,3,2,1,0:T(8,128)(2,1)}, u32[]{:S(2)}) copy-start(bf16[2,2,4,8,128]{4,3,2,1,0:T(8,128)(2,1)} %copy-done.7) | copy-start | bytes 98308
  25.9 7.0 %copy-start.11 = (bf16[2,2,512]{2,1,0:T(2,128)(2,1)S(1)}, bf16[2,2,512]{2,1,0:T(2,128)(2,1)}, u32[]{:S(2)}) copy-start(bf16[2,2,512]{2,1,0:T(2,128)(2,1)} %param.20) | copy-start | bytes 12292
  25.9 18.0 %all-to-all-start.1 = ((f32[32,1,2176]{2,1,0:T(1,128)}), f32[32,1,2176]{2,1,0:T(1,128)S(1)}, u32[]{:S(2)}, u32[]{:S(2)}) async-start(f32[32,1,2176]{2,1,0:T(1,128)} %reshape.262), calls=%async_computation.1 | async-start | bytes 557056 | tf_op jit(solution)/shard_map/all_to_all | solution.py:175

commit v11 on v7

--- a/solution.py
+++ b/solution.py
@@ -84,23 +84,26 @@
     causal = causal.reshape(1, step_count, 1, 1, step_count)
     fresh_stats = block_stats(fresh_scores, causal, fresh_values, "rskgt,rtkd->rskgd")
 
-    query_rows = rows_dev * step_count * feature_width // LANES
+    core_bit = ctx_index % 2
+    half_kv = KVH // 2
+    half_heads = H // 2
+    own_half_query = lax.dynamic_slice_in_dim(own_query, core_bit * half_kv, half_kv, 2)
+    query_rows = rows_dev * step_count * half_heads * HD // LANES
     id_rows = -(-rows_dev // 16) * 16
     id_block = jnp.zeros((id_rows, LANES), jnp.bfloat16)
     id_block = id_block.at[:rows_dev, :].set(
         jnp.broadcast_to(prefix_id.astype(jnp.bfloat16)[:, None], (rows_dev, LANES))
     )
-    packed = jnp.concatenate([queries.reshape(query_rows, LANES), id_block], axis=0)
+    packed = jnp.concatenate([own_half_query.reshape(query_rows, LANES), id_block], axis=0)
     fanned = jnp.broadcast_to(packed[None], (row_count,) + packed.shape)
     gathered = lax.all_to_all(fanned, "row", split_axis=0, concat_axis=0, tiled=True)
     total_rows = row_count * rows_dev
-    every_query = gathered[:, :query_rows, :].reshape(total_rows, step_count, KVH, groups, HD)
+    half_query = gathered[:, :query_rows, :].reshape(
+        total_rows, step_count, half_kv, groups, HD
+    )
     every_prefix = gathered[:, query_rows : query_rows + rows_dev, 0].reshape(total_rows)
     every_prefix = every_prefix.astype(jnp.int32)
 
-    core_bit = ctx_index % 2
-    half_kv = KVH // 2
-    half_heads = H // 2
     swap = [(c, c ^ 1) for c in range(ctx_count)]
     span_len = prefix_keys.shape[1]
     prefix_count = prefix_keys.shape[0]
@@ -114,7 +117,6 @@
     given_kv = lax.dynamic_slice_in_dim(kv_both, (1 - core_bit) * half_kv, half_kv, 3)
     partner_kv = lax.ppermute(given_kv, "ctx", swap)
 
-    half_query = lax.dynamic_slice_in_dim(every_query, core_bit * half_kv, half_kv, 2)
 
     def prefix_block(kv):
         row_keys = jnp.take(kv[0], every_prefix, axis=0)

time: 49.7 us -> 50.1 us (level)
    unnamed x21, local copies, waits for them, and re-layouts: 2.41 us -> 3.79 us
    reshape x1 -> x0, local copies, waits for them, and re-layouts: 0.82 us -> none  [per_device(): queries.reshape(query_rows, LANES)]
where the time goes in v11:
time: 50.1 us; the launch traced here: 49.5 us
  starting transfers between devices  13.9 us (28%)
  local copies, waits for them, and re-layouts  12.1 us (24%)
  waiting for transfers between devices  11 us (22%)
  blocking collectives  5.19 us (10%)
  matrix products  3.91 us (8%)
  other arithmetic  3.13 us (6%)
    all_to_all x1, waiting for transfers between devices, per_device(): lax.all_to_all(outgoing.reshape(dests, 1, (chunk + pt_rows) * LANES), ('c...  10.1 us
    all_to_all x1, starting transfers between devices, per_device(): lax.all_to_all(fanned, 'row', split_axis=0, concat_axis=0, tiled=True)  7.25 us
    all_to_all x1, starting transfers between devices, per_device(): lax.all_to_all(outgoing.reshape(dests, 1, (chunk + pt_rows) * LANES), ('c...  6.04 us
    all_gather x1, blocking collectives, per_device(): whole = lax.all_gather(result, 'ctx', axis=0, tiled=False)  5.19 us
    unnamed x21, local copies, waits for them, and re-layouts  3.79 us
    dot_general x1, matrix products, per_device(): jnp.einsum('rskgd,tkd->rskgt', own_query, flat_keys, preferred_element_ty...  1.76 us
    gather x2, local copies, waits for them, and re-layouts, prefix_block(): row_values = jnp.take(kv[1], every_prefix, axis=0)  1.2 us
    gather x2, local copies, waits for them, and re-layouts, prefix_block(): row_keys = jnp.take(kv[0], every_prefix, axis=0)  1.2 us
  transfers between devices with their start and end apart: 4, of which 2 were waited for; matrix products, arithmetic and copies ran while one was open for 13% of the time, Pallas kernels for 0%

profile of v11, /device:TPU:0, one launch (start us, length us, event | category | flops | bytes accessed | tf_op | source)
XLA Modules:
  0.0 49.5 jit_solution(1611978644379598510)
XLA Ops:
  0.0 0.8 %copy-done.5 = bf16[2,2,4096]{2,1,0:T(2,128)(2,1)S(1)} copy-done((bf16[2,2,4096]{2,1,0:T(2,128)(2,1)S(1)}, bf16[2,2,4096]{2,1,0:T(2,128)(2,1)}, u32[]{:S(2)}) %copy-start.5) | copy-done | bytes 32792
  0.8 0.6 %copy-done.9 = s32[2]{0:T(128)S(1)} copy-done((s32[2]{0:T(128)S(1)}, s32[2]{0:T(128)}, u32[]{:S(2)}) %copy-start.9) | copy-done | bytes 32
  1.4 0.1 compare_select_fusion.2
  1.5 0.1 pad_maximum_fusion.1
  1.6 0.7 %broadcast_in_dim.119 = bf16[8,80,128]{2,1,0:T(8,128)(2,1)} broadcast(bf16[80,128]{1,0:T(8,128)(2,1)S(1)} %pad_maximum_fusion.1), dimensions={1,2} | broadcast | bytes 184320 | tf_op jit(solution)/shard_map/broadcast_in_dim | solution.py:98
  2.3 7.3 %all-to-all-start = ((bf16[8,80,128]{2,1,0:T(8,128)(2,1)}), bf16[8,80,128]{2,1,0:T(8,128)(2,1)S(1)}, u32[]{:S(2)}, u32[]{:S(2)}) async-start(bf16[8,80,128]{2,1,0:T(8,128)(2,1)} %broadcast_in_dim.119), calls=%async_computation | async-start | bytes 327680 | tf_op jit(solution)/shard_map/all_to_all | solution.py:99
  9.7 0.8 %copy-done.4 = bf16[8,32,512]{2,1,0:T(8,128)(2,1)S(1)} copy-done((bf16[8,32,512]{2,1,0:T(8,128)(2,1)S(1)}, bf16[8,32,512]{2,1,0:T(8,128)(2,1)}, u32[]{:S(2)}) %copy-start.4) | copy-done | bytes 262168
  10.7 0.1 collective-permute-start
  10.8 0.7 %copy-done.6 = s32[2,32]{1,0:T(2,128)S(1)} copy-done((s32[2,32]{1,0:T(2,128)S(1)}, s32[2,32]{1,0:T(2,128)}, u32[]{:S(2)}) %copy-start.6) | copy-done | bytes 280
  11.5 0.2 fusion.37
  11.6 0.2 compare_reduce_fusion
  11.8 0.1 add.105
  11.9 0.1 add.106
  12.0 0.1 and.29
  12.1 0.1 and.30
  12.2 1.1 %reshape.206 = bf16[1024,4,128]{2,1,0:T(4,128)(2,1)} reshape(bf16[16,64,512]{2,1,0:T(8,128)(2,1)S(1)} %copy-done.1) | data formatting | bytes 2097152 | tf_op jit(solution)/shard_map/reshape | solution.py:69
  13.4 0.5 copy-done.2
  13.8 0.3 reshape.207
  14.1 0.4 copy-done.7
  14.5 0.1 compare_and_fusion
  14.6 1.8 %select_reduce_fusion = (f32[2,2,4,8]{3,1,0,2:T(2,128)S(1)}, f32[2,2,4,8,1024]{4,3,1,0,2:T(8,128)S(1)}) fusion(pred[2,1024]{1,0:T(4,128)(4,1)S(1)} %compare_and_fusion, bf16[2,2,4,8,128]{4,3,2,1,0:T(8,128)(2,1)S(1)} %reshape.203, bf16[1024,4,128,1,1]{2,1,0,4,3:T(4,128)(2,1)} %bitcast.146), kind=kOutput, calls=%fused_computation.23 | convolution fusion | flops 33947520 | bytes 1608192 | tf_op jit(solution)/shard_map/rskgd,tkd->rskgt/dot_general | solution.py:72
  16.3 0.3 convert_reduce_fusion
  16.6 0.2 copy.148
  16.8 0.2 copy.147
  16.9 0.3 fusion.7
  17.2 0.1 fusion.30
  17.3 0.5 collective-permute-start.1
  17.8 0.9 %collective-permute-done.1 = f32[2,2,2,8,130]{4,3,1,2,0:T(8,128)S(1)} collective-permute-done((f32[2,2,2,8,130]{4,3,1,2,0:T(8,128)S(1)}, f32[2,2,2,8,130]{4,3,1,2,0:T(8,128)S(1)}, u32[]{:S(2)}, u32[]{:S(2)}) %collective-permute-start.1) | collective-permute-done | bytes 33312 | tf_op jit(solution)/shard_map/ppermute | solution.py:141
  18.7 0.1 fusion.54
  18.8 0.1 copy.190
  18.9 0.1 copy.192
  19.1 0.2 convert_reduce_fusion.4
  19.3 0.1 reshape.231
  19.4 0.6 %gather_fusion = bf16[16,32,2,128]{3,1,2,0:T(8,128)(2,1)S(1)} fusion(bf16[8,32,2,128]{3,1,2,0:T(8,128)(2,1)S(1)} %get-tuple-element.34, s32[1024]{0:T(1024)S(1)} %pad_clamp_fusion), kind=kCustom, calls=%fused_computation.clone | custom fusion | bytes 524352 | tf_op jit(solution)/shard_map/jit(_take)/gather | solution.py:122
  20.0 0.6 %gather_fusion.1 = bf16[16,32,2,128]{3,1,2,0:T(8,128)(2,1)S(1)} fusion(bf16[8,32,2,128]{3,1,2,0:T(8,128)(2,1)S(1)} %get-tuple-element.36, s32[1024]{0:T(1024)S(1)} %pad_clamp_fusion), kind=kCustom, calls=%fused_computation.1.clone | custom fusion | bytes 524352 | tf_op jit(solution)/shard_map/jit(_take)/gather | solution.py:122
  20.6 0.4 fusion.57
  21.1 0.4 fusion.56
  21.5 0.6 %gather_fusion.2 = bf16[16,32,2,128]{3,1,2,0:T(8,128)(2,1)S(1)} fusion(bf16[8,32,2,128]{3,1,2,0:T(8,128)(2,1)S(1)} %get-tuple-element.33, s32[1024]{0:T(1024)S(1)} %pad_clamp_fusion), kind=kCustom, calls=%fused_computation.2.clone | custom fusion | bytes 524352 | tf_op jit(solution)/shard_map/jit(_take)/gather | solution.py:123
  22.1 0.6 %gather_fusion.3 = bf16[16,32,2,128]{3,1,2,0:T(8,128)(2,1)S(1)} fusion(bf16[8,32,2,128]{3,1,2,0:T(8,128)(2,1)S(1)} %get-tuple-element.35, s32[1024]{0:T(1024)S(1)} %pad_clamp_fusion), kind=kCustom, calls=%fused_computation.3.clone | custom fusion | bytes 524352 | tf_op jit(solution)/shard_map/jit(_take)/gather | solution.py:123
  22.7 0.5 convert_reduce_fusion.1
  23.2 0.3 fusion.3
  23.5 0.3 fusion.2
  23.8 0.1 fusion.34
  24.0 0.1 reshape.212
  24.1 0.1 reshape.210
  24.2 0.1 select_maximum_fusion
  24.4 1.0 %reshape.285 = f32[32,1,2176]{2,1,0:T(1,128)} reshape(f32[32,17,128]{2,1,0:T(8,128)S(1)} %pad_maximum_fusion) | data formatting | bytes 557056 | tf_op jit(solution)/shard_map/reshape | solution.py:171
  25.3 6.0 %all-to-all-start.1 = ((f32[32,1,2176]{2,1,0:T(1,128)}), f32[32,1,2176]{2,1,0:T(1,128)S(1)}, u32[]{:S(2)}, u32[]{:S(2)}) async-start(f32[32,1,2176]{2,1,0:T(1,128)} %reshape.285), calls=%async_computation.1 | async-start | bytes 557056 | tf_op jit(solution)/shard_map/all_to_all | solution.py:170
  31.4 0.3 select_reduce_fusion.1
  31.7 0.1 reshape.220
  31.8 0.1 reshape.221
  31.9 0.1 convert_reduce_fusion.3
  32.0 0.1 reshape.227
  32.1 0.1 reshape.228
  32.2 0.2 convolution_bitcast_fusion.2
  32.4 10.1 %all-to-all-done.1 = f32[32,1,2176]{2,1,0:T(1,128)S(1)} async-done(((f32[32,1,2176]{2,1,0:T(1,128)}), f32[32,1,2176]{2,1,0:T(1,128)S(1)}, u32[]{:S(2)}, u32[]{:S(2)}) %all-to-all-start.1) | async-done | bytes 278560 | tf_op jit(solution)/shard_map/all_to_all | solution.py:170
  42.5 0.7 %reduce.6 = f32[32,2176]{1,0:T(8,128)S(1)} reduce(f32[32,1,2176]{2,1,0:T(1,128)S(1)} %all-to-all-done.1, f32[]{:T(128)} %constant.97), dimensions={1}, to_apply=%all_to_all.7.reduce_sub_computation | reduce | bytes 557060 | tf_op jit(solution)/shard_map/all_to_all | solution.py:170
  43.2 0.1 fusion.55
  43.3 0.1 fusion.48
  43.4 0.1 multiply_reduce_fusion
  43.6 0.1 fusion.47
  43.6 0.1 divide_convert_fusion
  43.7 5.2 %all-gather = bf16[8,16,128]{2,1,0:T(8,128)(2,1)S(1)} all-gather(bf16[2,16,128]{2,1,0:T(8,128)(2,1)S(1)} %divide_convert_fusion), channel_id=2, replica_groups=mesh['ctx'=4,'row'=8] {'ctx'}, dimensions={0}, use_global_device_ids=true | all-gather | bytes 40960 | tf_op jit(solution)/shard_map/all_gather | solution.py:204
  48.9 0.6 %reshape.230 = bf16[2,2,4096]{2,1,0:T(2,128)(2,1)} reshape(bf16[2,2,2,16,128]{4,3,2,1,0:T(8,128)(2,1)S(1)} %bitcast.154) | data formatting | bytes 65536 | tf_op jit(solution)/shard_map/reshape | solution.py:207
  (57 shorter events, 0.9 us)
Async XLA Ops:
  0.0 32.2 %copy-start = (bf16[2,2,512]{2,1,0:T(2,128)(2,1)S(1)}, bf16[2,2,512]{2,1,0:T(2,128)(2,1)}, u32[]{:S(2)}) copy-start(bf16[2,2,512]{2,1,0:T(2,128)(2,1)} %param.23) | copy-start | bytes 12292
  0.0 0.8 %copy-start.5 = (bf16[2,2,4096]{2,1,0:T(2,128)(2,1)S(1)}, bf16[2,2,4096]{2,1,0:T(2,128)(2,1)}, u32[]{:S(2)}) copy-start(bf16[2,2,4096]{2,1,0:T(2,128)(2,1)} %param.14) | copy-start | bytes 98308
  0.8 0.7 %copy-start.9 = (s32[2]{0:T(128)S(1)}, s32[2]{0:T(128)}, u32[]{:S(2)}) copy-start(s32[2]{0:T(128)} %param.15) | copy-start | bytes 28
  1.6 8.0 %copy-start.3 = (bf16[8,32,512]{2,1,0:T(8,128)(2,1)S(1)}, bf16[8,32,512]{2,1,0:T(8,128)(2,1)}, u32[]{:S(2)}) copy-start(bf16[8,32,512]{2,1,0:T(8,128)(2,1)} %param.16) | copy-start | bytes 786436
  2.3 16.8 %all-to-all-start = ((bf16[8,80,128]{2,1,0:T(8,128)(2,1)}), bf16[8,80,128]{2,1,0:T(8,128)(2,1)S(1)}, u32[]{:S(2)}, u32[]{:S(2)}) async-start(bf16[8,80,128]{2,1,0:T(8,128)(2,1)} %broadcast_in_dim.119), calls=%async_computation | async-start | bytes 327680 | tf_op jit(solution)/shard_map/all_to_all | solution.py:99
  9.5 1.0 %copy-start.4 = (bf16[8,32,512]{2,1,0:T(8,128)(2,1)S(1)}, bf16[8,32,512]{2,1,0:T(8,128)(2,1)}, u32[]{:S(2)}) copy-start(bf16[8,32,512]{2,1,0:T(8,128)(2,1)} %param.17) | copy-start | bytes 786436
  9.6 2.6 %copy-start.1 = (bf16[16,64,512]{2,1,0:T(8,128)(2,1)S(1)}, bf16[16,64,512]{2,1,0:T(8,128)(2,1)}, u32[]{:S(2)}) copy-start(bf16[16,64,512]{2,1,0:T(8,128)(2,1)} %param.18) | copy-start | bytes 3145732
  10.7 8.3 %collective-permute-start = (bf16[2,8,32,2,128]{4,2,3,1,0:T(8,128)(2,1)S(1)}, bf16[2,8,32,2,128]{4,2,3,1,0:T(8,128)(2,1)S(1)}, u32[]{:S(2)}, u32[]{:S(2)}) collective-permute-start(bf16[2,8,32,2,128]{4,2,3,1,0:T(8,128)(2,1)S(1)} %constant_dynamic-slice_fusion.6), channel_id=1, source_target_pairs={{0,8},{8,0},{16,24},{24,16},{1,9},{9,1},{17,25},{25,17},{2,10},{10... | collective-permute-start | bytes 786440 | tf_op jit(solution)/shard_map/ppermute | solution.py:118
  10.8 0.7 %copy-start.6 = (s32[2,32]{1,0:T(2,128)S(1)}, s32[2,32]{1,0:T(2,128)}, u32[]{:S(2)}) copy-start(s32[2,32]{1,0:T(2,128)} %param.20) | copy-start | bytes 772
  12.2 1.6 %copy-start.2 = (bf16[16,64,512]{2,1,0:T(8,128)(2,1)S(1)}, bf16[16,64,512]{2,1,0:T(8,128)(2,1)}, u32[]{:S(2)}) copy-start(bf16[16,64,512]{2,1,0:T(8,128)(2,1)} %param.19) | copy-start | bytes 3145732
  13.8 0.7 %copy-start.7 = (s32[2]{0:T(128)S(1)}, s32[2]{0:T(128)}, u32[]{:S(2)}) copy-start(s32[2]{0:T(128)} %param.21) | copy-start | bytes 28
  17.3 1.4 %collective-permute-start.1 = (f32[2,2,2,8,130]{4,3,1,2,0:T(8,128)S(1)}, f32[2,2,2,8,130]{4,3,1,2,0:T(8,128)S(1)}, u32[]{:S(2)}, u32[]{:S(2)}) collective-permute-start(f32[2,2,2,8,130]{4,3,1,2,0:T(8,128)S(1)} %fusion.30), channel_id=1, source_target_pairs={{0,8},{8,0},{16,24},{24,16},{1,9},{9,1},{17,25},{25,17},{2,10},{10... | collective-permute-start | bytes 99848 | tf_op jit(solution)/shard_map/ppermute | solution.py:141
  25.3 6.0 %copy-start.8 = (bf16[2,2,512]{2,1,0:T(2,128)(2,1)S(1)}, bf16[2,2,512]{2,1,0:T(2,128)(2,1)}, u32[]{:S(2)}) copy-start(bf16[2,2,512]{2,1,0:T(2,128)(2,1)} %param.22) | copy-start | bytes 12292
  25.3 17.1 %all-to-all-start.1 = ((f32[32,1,2176]{2,1,0:T(1,128)}), f32[32,1,2176]{2,1,0:T(1,128)S(1)}, u32[]{:S(2)}, u32[]{:S(2)}) async-start(f32[32,1,2176]{2,1,0:T(1,128)} %reshape.285), calls=%async_computation.1 | async-start | bytes 557056 | tf_op jit(solution)/shard_map/all_to_all | solution.py:170

commit v12 on v11

--- a/solution.py
+++ b/solution.py
@@ -66,13 +66,25 @@
     )
     live_mask = owned[:, :, None] & (token_pos < suffix_len[:, None, None])
     live_mask = live_mask.reshape(rows_dev, 1, 1, 1, slot_count * page_len)
-    flat_keys = pool_keys.reshape(slot_count * page_len, KVH, HD)
-    flat_values = pool_values.reshape(slot_count * page_len, KVH, HD)
+    flat_keys = pool_keys.reshape(slot_count * page_len, kv_width)
+    flat_values = pool_values.reshape(slot_count * page_len, kv_width)
+    head_eye = (jnp.arange(KVH)[:, None] == jnp.arange(KVH)[None, :]).reshape(
+        1, 1, KVH, 1, KVH, 1
+    )
+    wide_query = jnp.where(head_eye, own_query[:, :, :, :, None, :], 0).reshape(
+        rows_dev, step_count, KVH, groups, kv_width
+    )
     suffix_scores = (
-        jnp.einsum("rskgd,tkd->rskgt", own_query, flat_keys, preferred_element_type=jnp.float32)
+        jnp.einsum("rskgw,tw->rskgt", wide_query, flat_keys, preferred_element_type=jnp.float32)
         * score_scale
     )
-    suffix_stats = block_stats(suffix_scores, live_mask, flat_values, "rskgt,tkd->rskgd")
+    wide_stats = block_stats(suffix_scores, live_mask, flat_values, "rskgt,tw->rskgw")
+    wide_sum = wide_stats[2].reshape(rows_dev, step_count, KVH, groups, KVH, HD)
+    suffix_stats = (
+        wide_stats[0],
+        wide_stats[1],
+        jnp.sum(jnp.where(head_eye, wide_sum, 0.0), axis=4),
+    )
 
     fresh_keys = new_keys.reshape(rows_dev, step_count, KVH, HD)
     fresh_values = new_values.reshape(rows_dev, step_count, KVH, HD)

time: 50.1 us -> 48.6 us (0.970)
  matrix products: 3.91 us -> 2.93 us
  waiting for transfers between devices: 11 us -> 10.3 us
    reshape x2 -> x0, local copies, waits for them, and re-layouts: 1.39 us -> none  [the longest x1 1.12 us: per_device(): flat_keys = pool_keys.reshape(slot_count * page_len, KVH, HD)]
    dot_general x0 -> x1, local copies, waits for them, and re-layouts: none -> 1.33 us  [block_stats(): jnp.einsum(einsum_form, weights, values, preferred_element_type=jnp.float32)]
    dot_general x1, matrix products: 1.76 us -> 0.58 us  [per_device(): jnp.einsum('rskgw,tw->rskgt', wide_query, flat_keys, preferred_element_ty...]
    all_to_all x1, waiting for transfers between devices: 10.1 us -> 9.49 us  [per_device(): lax.all_to_all(outgoing.reshape(dests, 1, (chunk + pt_rows) * LANES), ('c...]
    unnamed x21 -> x23, local copies, waits for them, and re-layouts: 3.79 us -> 4 us
  transfers between devices with their start and end apart: 4 -> 4, of which waited for: 2 -> 2; matrix products, arithmetic and copies ran while one was open for 13% -> 11% of each run, Pallas kernels for 0% -> 0%
where the time goes in v12:
time: 48.6 us; the launch traced here: 48.1 us
  starting transfers between devices  13.9 us (29%)
  local copies, waits for them, and re-layouts  12.3 us (25%)
  waiting for transfers between devices  10.3 us (21%)
  blocking collectives  5.19 us (11%)
  other arithmetic  3.13 us (6%)
  matrix products  2.93 us (6%)
    all_to_all x1, waiting for transfers between devices, per_device(): lax.all_to_all(outgoing.reshape(dests, 1, (chunk + pt_rows) * LANES), ('c...  9.49 us
    all_to_all x1, starting transfers between devices, per_device(): lax.all_to_all(fanned, 'row', split_axis=0, concat_axis=0, tiled=True)  7.25 us
    all_to_all x1, starting transfers between devices, per_device(): lax.all_to_all(outgoing.reshape(dests, 1, (chunk + pt_rows) * LANES), ('c...  6.03 us
    all_gather x1, blocking collectives, per_device(): whole = lax.all_gather(result, 'ctx', axis=0, tiled=False)  5.19 us
    unnamed x23, local copies, waits for them, and re-layouts  4 us
    dot_general x1, local copies, waits for them, and re-layouts, block_stats(): jnp.einsum(einsum_form, weights, values, preferred_element_type=jnp.float32)  1.33 us
    dot_general x4, matrix products, block_stats(): jnp.einsum(einsum_form, weights, values, preferred_element_type=jnp.float32)  1.23 us
    gather x2, local copies, waits for them, and re-layouts, prefix_block(): row_values = jnp.take(kv[1], every_prefix, axis=0)  1.2 us
  transfers between devices with their start and end apart: 4, of which 2 were waited for; matrix products, arithmetic and copies ran while one was open for 11% of the time, Pallas kernels for 0%

profile of v12, /device:TPU:0, one launch (start us, length us, event | category | flops | bytes accessed | tf_op | source)
XLA Modules:
  0.0 48.1 jit_solution(12680112048746706072)
XLA Ops:
  0.0 0.8 %copy-done.5 = bf16[2,2,4096]{2,1,0:T(2,128)(2,1)S(1)} copy-done((bf16[2,2,4096]{2,1,0:T(2,128)(2,1)S(1)}, bf16[2,2,4096]{2,1,0:T(2,128)(2,1)}, u32[]{:S(2)}) %copy-start.5) | copy-done | bytes 32792
  0.9 0.6 %copy-done.10 = s32[2]{0:T(128)S(1)} copy-done((s32[2]{0:T(128)S(1)}, s32[2]{0:T(128)}, u32[]{:S(2)}) %copy-start.10) | copy-done | bytes 32
  1.5 0.1 compare_select_fusion.2
  1.6 0.1 pad_maximum_fusion.1
  1.7 0.7 %broadcast_in_dim.153 = bf16[8,80,128]{2,1,0:T(8,128)(2,1)} broadcast(bf16[80,128]{1,0:T(8,128)(2,1)S(1)} %pad_maximum_fusion.1), dimensions={1,2} | broadcast | bytes 184320 | tf_op jit(solution)/shard_map/broadcast_in_dim | solution.py:110
  2.4 7.3 %all-to-all-start = ((bf16[8,80,128]{2,1,0:T(8,128)(2,1)}), bf16[8,80,128]{2,1,0:T(8,128)(2,1)S(1)}, u32[]{:S(2)}, u32[]{:S(2)}) async-start(bf16[8,80,128]{2,1,0:T(8,128)(2,1)} %broadcast_in_dim.153), calls=%async_computation | async-start | bytes 327680 | tf_op jit(solution)/shard_map/all_to_all | solution.py:111
  9.8 0.8 %copy-done.4 = bf16[8,32,512]{2,1,0:T(8,128)(2,1)S(1)} copy-done((bf16[8,32,512]{2,1,0:T(8,128)(2,1)S(1)}, bf16[8,32,512]{2,1,0:T(8,128)(2,1)}, u32[]{:S(2)}) %copy-start.4) | copy-done | bytes 262168
  10.8 0.1 collective-permute-start
  10.9 0.7 %copy-done.7 = s32[2,32]{1,0:T(2,128)S(1)} copy-done((s32[2,32]{1,0:T(2,128)S(1)}, s32[2,32]{1,0:T(2,128)}, u32[]{:S(2)}) %copy-start.7) | copy-done | bytes 280
  11.5 0.2 fusion.38
  11.7 0.2 compare_reduce_fusion
  11.9 0.1 add.105
  12.0 0.1 add.106
  12.1 0.1 and.29
  12.1 0.1 and.30
  12.2 0.1 add.108
  12.3 1.3 %copy.155 = bf16[512,1024]{1,0:T(8,128)(2,1)} copy(bf16[512,1024]{0,1:T(8,128)(2,1)S(1)} %bitcast.162) | data formatting | bytes 2097152 | tf_op jit(solution)/shard_map/rskgt,tw->rskgw/dot_general | solution.py:23
  13.6 0.1 compare_and_fusion
  13.7 0.6 %select_reduce_fusion = (f32[2,2,4,8]{3,2,1,0:T(4,128)S(1)}, f32[2,2,4,8,1024]{4,3,2,1,0:T(8,128)S(1)}) fusion(pred[2,1024]{1,0:T(4,128)(4,1)S(1)} %compare_and_fusion, bf16[1024,512,1,1,1]{1,0,4,3,2:T(8,128)(2,1)S(1)} %bitcast.161, pred[4,4]{1,0:T(4,128)(4,1)S(1)} %iota_compare_fusion.1, bf16[2,2,4,8,128]{4,3,2,1,0:T(8,128)(2,1)S(1)} %reshape.241), kind=kOutput, calls=%fused_computation.21 | convolution fusion | flops 134676352 | bytes 1608208 | tf_op jit(solution)/shard_map/rskgw,tw->rskgt/dot_general | solution.py:78
  14.3 0.2 convert_reduce_fusion
  14.6 0.4 copy-done.2
  15.0 0.5 %fusion.5 = f32[2,2,4,8,128]{4,3,2,1,0:T(8,128)S(1)} fusion(bf16[4,128,1024,1,1,1]{2,1,0,5,4,3:T(8,128)(2,1)S(1)} %bitcast.163, pred[4,4]{1,0:T(4,128)(4,1)S(1)} %iota_compare_fusion.1, f32[2,2,4,8,1024]{4,3,2,1,0:T(8,128)S(1)} %get-tuple-element.45, f32[2,2,4,8]{3,2,1,0:T(4,128)S(1)} %get-tuple-element.44, pred[2,1024]{1,0:T(4,128)(4,1)S(1)} %compare_and_fusion), kind=kOutput, calls=%fused_computation.15 | convolution fusion | flops 134725632 | bytes 1640976 | tf_op jit(solution)/shard_map/rskgt,tw->rskgw/dot_general | solution.py:23
  15.5 0.2 copy.158
  15.6 0.2 copy.157
  15.8 0.1 fusion.30
  15.9 0.5 %collective-permute-start.1 = (f32[2,2,2,8,130]{4,3,1,2,0:T(8,128)S(1)}, f32[2,2,2,8,130]{4,3,1,2,0:T(8,128)S(1)}, u32[]{:S(2)}, u32[]{:S(2)}) collective-permute-start(f32[2,2,2,8,130]{4,3,1,2,0:T(8,128)S(1)} %fusion.30), channel_id=1, source_target_pairs={{0,8},{8,0},{16,24},{24,16},{1,9},{9,1},{17,25},{25,17},{2,10},{10... | collective-permute-start | bytes 99848 | tf_op jit(solution)/shard_map/ppermute | solution.py:153
  16.5 0.8 %collective-permute-done.1 = f32[2,2,2,8,130]{4,3,1,2,0:T(8,128)S(1)} collective-permute-done((f32[2,2,2,8,130]{4,3,1,2,0:T(8,128)S(1)}, f32[2,2,2,8,130]{4,3,1,2,0:T(8,128)S(1)}, u32[]{:S(2)}, u32[]{:S(2)}) %collective-permute-start.1) | collective-permute-done | bytes 33312 | tf_op jit(solution)/shard_map/ppermute | solution.py:153
  17.3 0.1 fusion.57
  17.4 0.1 copy.191
  17.5 0.1 copy.193
  17.7 0.2 convert_reduce_fusion.4
  17.9 0.1 reshape.269
  18.0 0.6 %gather_fusion = bf16[16,32,2,128]{3,1,2,0:T(8,128)(2,1)S(1)} fusion(bf16[8,32,2,128]{3,1,2,0:T(8,128)(2,1)S(1)} %get-tuple-element.32, s32[1024]{0:T(1024)S(1)} %pad_clamp_fusion), kind=kCustom, calls=%fused_computation.clone | custom fusion | bytes 524352 | tf_op jit(solution)/shard_map/jit(_take)/gather | solution.py:134
  18.6 0.6 %gather_fusion.1 = bf16[16,32,2,128]{3,1,2,0:T(8,128)(2,1)S(1)} fusion(bf16[8,32,2,128]{3,1,2,0:T(8,128)(2,1)S(1)} %get-tuple-element.34, s32[1024]{0:T(1024)S(1)} %pad_clamp_fusion), kind=kCustom, calls=%fused_computation.1.clone | custom fusion | bytes 524352 | tf_op jit(solution)/shard_map/jit(_take)/gather | solution.py:134
  19.2 0.4 fusion.60
  19.6 0.4 fusion.59
  20.1 0.6 %gather_fusion.2 = bf16[16,32,2,128]{3,1,2,0:T(8,128)(2,1)S(1)} fusion(bf16[8,32,2,128]{3,1,2,0:T(8,128)(2,1)S(1)} %get-tuple-element.31, s32[1024]{0:T(1024)S(1)} %pad_clamp_fusion), kind=kCustom, calls=%fused_computation.2.clone | custom fusion | bytes 524352 | tf_op jit(solution)/shard_map/jit(_take)/gather | solution.py:135
  20.7 0.6 %gather_fusion.3 = bf16[16,32,2,128]{3,1,2,0:T(8,128)(2,1)S(1)} fusion(bf16[8,32,2,128]{3,1,2,0:T(8,128)(2,1)S(1)} %get-tuple-element.33, s32[1024]{0:T(1024)S(1)} %pad_clamp_fusion), kind=kCustom, calls=%fused_computation.3.clone | custom fusion | bytes 524352 | tf_op jit(solution)/shard_map/jit(_take)/gather | solution.py:135
  21.3 0.5 convert_reduce_fusion.1
  21.8 0.3 fusion.2
  22.1 0.3 fusion.1
  22.4 0.1 fusion.36
  22.6 0.1 reshape.250
  22.7 0.1 reshape.248
  22.8 0.1 select_maximum_fusion
  22.9 1.0 %reshape.324 = f32[32,1,2176]{2,1,0:T(1,128)} reshape(f32[32,17,128]{2,1,0:T(8,128)S(1)} %pad_maximum_fusion) | data formatting | bytes 557056 | tf_op jit(solution)/shard_map/reshape | solution.py:183
  23.9 6.0 %all-to-all-start.1 = ((f32[32,1,2176]{2,1,0:T(1,128)}), f32[32,1,2176]{2,1,0:T(1,128)S(1)}, u32[]{:S(2)}, u32[]{:S(2)}) async-start(f32[32,1,2176]{2,1,0:T(1,128)} %reshape.324), calls=%async_computation.1 | async-start | bytes 557056 | tf_op jit(solution)/shard_map/all_to_all | solution.py:182
  30.0 0.3 select_reduce_fusion.1
  30.3 0.1 reshape.258
  30.4 0.1 reshape.259
  30.4 0.1 convert_reduce_fusion.3
  30.6 0.1 reshape.265
  30.6 0.1 reshape.266
  30.7 0.6 %copy-done.6 = bf16[2,2,512]{2,1,0:T(2,128)(2,1)S(1)} copy-done((bf16[2,2,512]{2,1,0:T(2,128)(2,1)S(1)}, bf16[2,2,512]{2,1,0:T(2,128)(2,1)}, u32[]{:S(2)}) %copy-start.6) | copy-done | bytes 4120
  31.3 0.2 convolution_bitcast_fusion.2
  31.5 9.5 %all-to-all-done.1 = f32[32,1,2176]{2,1,0:T(1,128)S(1)} async-done(((f32[32,1,2176]{2,1,0:T(1,128)}), f32[32,1,2176]{2,1,0:T(1,128)S(1)}, u32[]{:S(2)}, u32[]{:S(2)}) %all-to-all-start.1) | async-done | bytes 278560 | tf_op jit(solution)/shard_map/all_to_all | solution.py:182
  41.0 0.7 %reduce.6 = f32[32,2176]{1,0:T(8,128)S(1)} reduce(f32[32,1,2176]{2,1,0:T(1,128)S(1)} %all-to-all-done.1, f32[]{:T(128)} %constant.98), dimensions={1}, to_apply=%all_to_all.7.reduce_sub_computation | reduce | bytes 557060 | tf_op jit(solution)/shard_map/all_to_all | solution.py:182
  41.8 0.1 fusion.58
  41.9 0.1 fusion.49
  42.0 0.1 multiply_reduce_fusion
  42.1 0.1 fusion.48
  42.2 0.1 divide_convert_fusion
  42.3 5.2 %all-gather = bf16[8,16,128]{2,1,0:T(8,128)(2,1)S(1)} all-gather(bf16[2,16,128]{2,1,0:T(8,128)(2,1)S(1)} %divide_convert_fusion), channel_id=2, replica_groups=mesh['ctx'=4,'row'=8] {'ctx'}, dimensions={0}, use_global_device_ids=true | all-gather | bytes 40960 | tf_op jit(solution)/shard_map/all_gather | solution.py:216
  47.5 0.6 %reshape.268 = bf16[2,2,4096]{2,1,0:T(2,128)(2,1)} reshape(bf16[2,2,2,16,128]{4,3,2,1,0:T(8,128)(2,1)S(1)} %bitcast.170) | data formatting | bytes 65536 | tf_op jit(solution)/shard_map/reshape | solution.py:219
  (60 shorter events, 0.9 us)
Async XLA Ops:
  0.0 13.7 %copy-start = (bf16[16,64,512]{2,1,0:T(8,128)(2,1)S(1)}, bf16[16,64,512]{2,1,0:T(8,128)(2,1)}, u32[]{:S(2)}) copy-start(bf16[16,64,512]{2,1,0:T(8,128)(2,1)} %param.18) | copy-start | bytes 3145732
  0.0 0.8 %copy-start.5 = (bf16[2,2,4096]{2,1,0:T(2,128)(2,1)S(1)}, bf16[2,2,4096]{2,1,0:T(2,128)(2,1)}, u32[]{:S(2)}) copy-start(bf16[2,2,4096]{2,1,0:T(2,128)(2,1)} %param.14) | copy-start | bytes 98308
  0.9 0.7 %copy-start.10 = (s32[2]{0:T(128)S(1)}, s32[2]{0:T(128)}, u32[]{:S(2)}) copy-start(s32[2]{0:T(128)} %param.15) | copy-start | bytes 28
  1.7 8.0 %copy-start.3 = (bf16[8,32,512]{2,1,0:T(8,128)(2,1)S(1)}, bf16[8,32,512]{2,1,0:T(8,128)(2,1)}, u32[]{:S(2)}) copy-start(bf16[8,32,512]{2,1,0:T(8,128)(2,1)} %param.16) | copy-start | bytes 786436
  2.4 15.3 %all-to-all-start = ((bf16[8,80,128]{2,1,0:T(8,128)(2,1)}), bf16[8,80,128]{2,1,0:T(8,128)(2,1)S(1)}, u32[]{:S(2)}, u32[]{:S(2)}) async-start(bf16[8,80,128]{2,1,0:T(8,128)(2,1)} %broadcast_in_dim.153), calls=%async_computation | async-start | bytes 327680 | tf_op jit(solution)/shard_map/all_to_all | solution.py:111
  9.6 1.0 %copy-start.4 = (bf16[8,32,512]{2,1,0:T(8,128)(2,1)S(1)}, bf16[8,32,512]{2,1,0:T(8,128)(2,1)}, u32[]{:S(2)}) copy-start(bf16[8,32,512]{2,1,0:T(8,128)(2,1)} %param.17) | copy-start | bytes 786436
  9.7 2.6 %copy-start.1 = (bf16[16,64,512]{2,1,0:T(8,128)(2,1)S(1)}, bf16[16,64,512]{2,1,0:T(8,128)(2,1)}, u32[]{:S(2)}) copy-start(bf16[16,64,512]{2,1,0:T(8,128)(2,1)} %param.19) | copy-start | bytes 3145732
  10.8 6.8 %collective-permute-start = (bf16[2,8,32,2,128]{4,2,3,1,0:T(8,128)(2,1)S(1)}, bf16[2,8,32,2,128]{4,2,3,1,0:T(8,128)(2,1)S(1)}, u32[]{:S(2)}, u32[]{:S(2)}) collective-permute-start(bf16[2,8,32,2,128]{4,2,3,1,0:T(8,128)(2,1)S(1)} %constant_dynamic-slice_fusion.6), channel_id=1, source_target_pairs={{0,8},{8,0},{16,24},{24,16},{1,9},{9,1},{17,25},{25,17},{2,10},{10... | collective-permute-start | bytes 786440 | tf_op jit(solution)/shard_map/ppermute | solution.py:130
  10.8 0.7 %copy-start.7 = (s32[2,32]{1,0:T(2,128)S(1)}, s32[2,32]{1,0:T(2,128)}, u32[]{:S(2)}) copy-start(s32[2,32]{1,0:T(2,128)} %param.20) | copy-start | bytes 772
  12.3 1.3 %copy-start.8 = (s32[2]{0:T(128)S(1)}, s32[2]{0:T(128)}, u32[]{:S(2)}) copy-start(s32[2]{0:T(128)} %param.21) | copy-start | bytes 28
  13.7 1.2 %copy-start.2 = (bf16[512,1024]{1,0:T(8,128)(2,1)S(1)}, bf16[512,1024]{1,0:T(8,128)(2,1)}, u32[]{:S(2)}) copy-start(bf16[512,1024]{1,0:T(8,128)(2,1)} %copy.155) | copy-start | bytes 3145732
  15.9 1.4 %collective-permute-start.1 = (f32[2,2,2,8,130]{4,3,1,2,0:T(8,128)S(1)}, f32[2,2,2,8,130]{4,3,1,2,0:T(8,128)S(1)}, u32[]{:S(2)}, u32[]{:S(2)}) collective-permute-start(f32[2,2,2,8,130]{4,3,1,2,0:T(8,128)S(1)} %fusion.30), channel_id=1, source_target_pairs={{0,8},{8,0},{16,24},{24,16},{1,9},{9,1},{17,25},{25,17},{2,10},{10... | collective-permute-start | bytes 99848 | tf_op jit(solution)/shard_map/ppermute | solution.py:153
  23.9 6.0 %copy-start.9 = (bf16[2,2,512]{2,1,0:T(2,128)(2,1)S(1)}, bf16[2,2,512]{2,1,0:T(2,128)(2,1)}, u32[]{:S(2)}) copy-start(bf16[2,2,512]{2,1,0:T(2,128)(2,1)} %param.22) | copy-start | bytes 12292
  23.9 17.1 %all-to-all-start.1 = ((f32[32,1,2176]{2,1,0:T(1,128)}), f32[32,1,2176]{2,1,0:T(1,128)S(1)}, u32[]{:S(2)}, u32[]{:S(2)}) async-start(f32[32,1,2176]{2,1,0:T(1,128)} %reshape.324), calls=%async_computation.1 | async-start | bytes 557056 | tf_op jit(solution)/shard_map/all_to_all | solution.py:182
  30.6 0.7 %copy-start.6 = (bf16[2,2,512]{2,1,0:T(2,128)(2,1)S(1)}, bf16[2,2,512]{2,1,0:T(2,128)(2,1)}, u32[]{:S(2)}) copy-start(bf16[2,2,512]{2,1,0:T(2,128)(2,1)} %param.23) | copy-start | bytes 12292

commit v13 on v12

--- a/solution.py
+++ b/solution.py
@@ -67,7 +67,7 @@
     live_mask = owned[:, :, None] & (token_pos < suffix_len[:, None, None])
     live_mask = live_mask.reshape(rows_dev, 1, 1, 1, slot_count * page_len)
     flat_keys = pool_keys.reshape(slot_count * page_len, kv_width)
-    flat_values = pool_values.reshape(slot_count * page_len, kv_width)
+    flat_values = pool_values.reshape(slot_count * page_len, KVH, HD)
     head_eye = (jnp.arange(KVH)[:, None] == jnp.arange(KVH)[None, :]).reshape(
         1, 1, KVH, 1, KVH, 1
     )
@@ -78,13 +78,7 @@
         jnp.einsum("rskgw,tw->rskgt", wide_query, flat_keys, preferred_element_type=jnp.float32)
         * score_scale
     )
-    wide_stats = block_stats(suffix_scores, live_mask, flat_values, "rskgt,tw->rskgw")
-    wide_sum = wide_stats[2].reshape(rows_dev, step_count, KVH, groups, KVH, HD)
-    suffix_stats = (
-        wide_stats[0],
-        wide_stats[1],
-        jnp.sum(jnp.where(head_eye, wide_sum, 0.0), axis=4),
-    )
+    suffix_stats = block_stats(suffix_scores, live_mask, flat_values, "rskgt,tkd->rskgd")
 
     fresh_keys = new_keys.reshape(rows_dev, step_count, KVH, HD)
     fresh_values = new_values.reshape(rows_dev, step_count, KVH, HD)

time: 48.6 us -> 48.8 us (level)
    dot_general x1 -> x0, local copies, waits for them, and re-layouts: 1.33 us -> none  [block_stats(): jnp.einsum(einsum_form, weights, values, preferred_element_type=jnp.float32)]
    reshape x0 -> x1, local copies, waits for them, and re-layouts: none -> 1.12 us  [per_device(): flat_values = pool_values.reshape(slot_count * page_len, KVH, HD)]
    squeeze x2, local copies, waits for them, and re-layouts: 0.05 us -> 1.03 us  [prefix_block(): row_values = jnp.take(kv[1], every_prefix, axis=0)]
  transfers between devices with their start and end apart: 4 -> 4, of which waited for: 2 -> 2; matrix products, arithmetic and copies ran while one was open for 11% -> 13% of each run, Pallas kernels for 0% -> 0%
where the time goes in v13:
time: 48.8 us; the launch traced here: 48.3 us
  starting transfers between devices  13.9 us (28%)
  local copies, waits for them, and re-layouts  12.7 us (26%)
  waiting for transfers between devices  10.3 us (21%)
  blocking collectives  5.19 us (11%)
  other arithmetic  3.14 us (6%)
  matrix products  2.71 us (6%)
    all_to_all x1, waiting for transfers between devices, per_device(): lax.all_to_all(outgoing.reshape(dests, 1, (chunk + pt_rows) * LANES), ('c...  9.49 us
    all_to_all x1, starting transfers between devices, per_device(): lax.all_to_all(fanned, 'row', split_axis=0, concat_axis=0, tiled=True)  7.25 us
    all_to_all x1, starting transfers between devices, per_device(): lax.all_to_all(outgoing.reshape(dests, 1, (chunk + pt_rows) * LANES), ('c...  6.04 us
    all_gather x1, blocking collectives, per_device(): whole = lax.all_gather(result, 'ctx', axis=0, tiled=False)  5.19 us
    unnamed x23, local copies, waits for them, and re-layouts  3.66 us
    gather x2, local copies, waits for them, and re-layouts, prefix_block(): row_values = jnp.take(kv[1], every_prefix, axis=0)  1.2 us
    gather x2, local copies, waits for them, and re-layouts, prefix_block(): row_keys = jnp.take(kv[0], every_prefix, axis=0)  1.19 us
    reshape x1, local copies, waits for them, and re-layouts, per_device(): flat_values = pool_values.reshape(slot_count * page_len, KVH, HD)  1.12 us
  transfers between devices with their start and end apart: 4, of which 2 were waited for; matrix products, arithmetic and copies ran while one was open for 13% of the time, Pallas kernels for 0%

profile of v13, /device:TPU:0, one launch (start us, length us, event | category | flops | bytes accessed | tf_op | source)
XLA Modules:
  0.0 48.3 jit_solution(18281007540338016862)
XLA Ops:
  0.0 0.8 %copy-done.5 = bf16[2,2,4096]{2,1,0:T(2,128)(2,1)S(1)} copy-done((bf16[2,2,4096]{2,1,0:T(2,128)(2,1)S(1)}, bf16[2,2,4096]{2,1,0:T(2,128)(2,1)}, u32[]{:S(2)}) %copy-start.5) | copy-done | bytes 32792
  0.9 0.6 %copy-done.10 = s32[2]{0:T(128)S(1)} copy-done((s32[2]{0:T(128)S(1)}, s32[2]{0:T(128)}, u32[]{:S(2)}) %copy-start.10) | copy-done | bytes 32
  1.5 0.1 compare_select_fusion.2
  1.6 0.1 pad_maximum_fusion.1
  1.7 0.7 %broadcast_in_dim.141 = bf16[8,80,128]{2,1,0:T(8,128)(2,1)} broadcast(bf16[80,128]{1,0:T(8,128)(2,1)S(1)} %pad_maximum_fusion.1), dimensions={1,2} | broadcast | bytes 184320 | tf_op jit(solution)/shard_map/broadcast_in_dim | solution.py:104
  2.4 7.3 %all-to-all-start = ((bf16[8,80,128]{2,1,0:T(8,128)(2,1)}), bf16[8,80,128]{2,1,0:T(8,128)(2,1)S(1)}, u32[]{:S(2)}, u32[]{:S(2)}) async-start(bf16[8,80,128]{2,1,0:T(8,128)(2,1)} %broadcast_in_dim.141), calls=%async_computation | async-start | bytes 327680 | tf_op jit(solution)/shard_map/all_to_all | solution.py:105
  9.8 0.8 %copy-done.4 = bf16[8,32,512]{2,1,0:T(8,128)(2,1)S(1)} copy-done((bf16[8,32,512]{2,1,0:T(8,128)(2,1)S(1)}, bf16[8,32,512]{2,1,0:T(8,128)(2,1)}, u32[]{:S(2)}) %copy-start.4) | copy-done | bytes 262168
  10.8 0.1 collective-permute-start
  10.9 0.7 %copy-done.7 = s32[2,32]{1,0:T(2,128)S(1)} copy-done((s32[2,32]{1,0:T(2,128)S(1)}, s32[2,32]{1,0:T(2,128)}, u32[]{:S(2)}) %copy-start.7) | copy-done | bytes 280
  11.5 0.2 fusion.39
  11.7 0.2 compare_reduce_fusion
  11.9 0.1 add.105
  12.0 0.1 add.106
  12.1 0.1 and.29
  12.1 0.1 and.30
  12.2 0.1 add.108
  12.3 1.1 %reshape.243 = bf16[1024,4,128]{2,1,0:T(4,128)(2,1)} reshape(bf16[16,64,512]{2,1,0:T(8,128)(2,1)S(1)} %copy-done.1) | data formatting | bytes 2097152 | tf_op jit(solution)/shard_map/reshape | solution.py:70
  13.4 0.1 compare_and_fusion
  13.5 0.6 %select_reduce_fusion = (f32[2,2,4,8]{3,2,1,0:T(4,128)S(1)}, f32[2,2,4,8,1024]{4,3,2,1,0:T(8,128)S(1)}) fusion(pred[2,1024]{1,0:T(4,128)(4,1)S(1)} %compare_and_fusion, bf16[1024,512,1,1,1]{1,0,4,3,2:T(8,128)(2,1)S(1)} %bitcast.153, pred[4,4]{1,0:T(4,128)(4,1)S(1)} %iota_compare_fusion.1, bf16[2,2,4,8,128]{4,3,2,1,0:T(8,128)(2,1)S(1)} %reshape.239), kind=kOutput, calls=%fused_computation.21 | convolution fusion | flops 134676352 | bytes 1608208 | tf_op jit(solution)/shard_map/rskgw,tw->rskgt/dot_general | solution.py:78
  14.1 0.3 convert_reduce_fusion
  14.4 0.2 copy.170
  14.5 0.2 copy.169
  14.7 0.3 fusion.6
  15.0 0.1 fusion.31
  15.1 0.5 %collective-permute-start.1 = (f32[2,2,2,8,130]{4,3,1,2,0:T(8,128)S(1)}, f32[2,2,2,8,130]{4,3,1,2,0:T(8,128)S(1)}, u32[]{:S(2)}, u32[]{:S(2)}) collective-permute-start(f32[2,2,2,8,130]{4,3,1,2,0:T(8,128)S(1)} %fusion.31), channel_id=1, source_target_pairs={{0,8},{8,0},{16,24},{24,16},{1,9},{9,1},{17,25},{25,17},{2,10},{10... | collective-permute-start | bytes 99848 | tf_op jit(solution)/shard_map/ppermute | solution.py:147
  15.7 0.8 %collective-permute-done.1 = f32[2,2,2,8,130]{4,3,1,2,0:T(8,128)S(1)} collective-permute-done((f32[2,2,2,8,130]{4,3,1,2,0:T(8,128)S(1)}, f32[2,2,2,8,130]{4,3,1,2,0:T(8,128)S(1)}, u32[]{:S(2)}, u32[]{:S(2)}) %collective-permute-start.1) | collective-permute-done | bytes 33312 | tf_op jit(solution)/shard_map/ppermute | solution.py:147
  16.5 0.1 fusion.57
  16.6 0.1 copy.207
  16.7 0.1 copy.209
  16.8 1.0 %slice_bitcast_fusion = (bf16[8,32,2,128]{3,1,2,0:T(8,128)(2,1)S(1)}, bf16[8,32,2,128]{3,1,2,0:T(8,128)(2,1)S(1)}) fusion(bf16[2,8,32,2,128]{4,2,3,1,0:T(8,128)(2,1)} %collective-permute-done), kind=kLoop, calls=%fused_computation.43 | loop fusion | bytes 524288 | tf_op jit(solution)/shard_map/squeeze | solution.py:129
  17.8 0.2 convert_reduce_fusion.4
  18.1 0.1 reshape.267
  18.2 0.6 %gather_fusion = bf16[16,32,2,128]{3,1,2,0:T(8,128)(2,1)S(1)} fusion(bf16[8,32,2,128]{3,1,2,0:T(8,128)(2,1)S(1)} %get-tuple-element.34, s32[1024]{0:T(1024)S(1)} %pad_clamp_fusion), kind=kCustom, calls=%fused_computation.clone | custom fusion | bytes 524352 | tf_op jit(solution)/shard_map/jit(_take)/gather | solution.py:128
  18.8 0.6 %gather_fusion.1 = bf16[16,32,2,128]{3,1,2,0:T(8,128)(2,1)S(1)} fusion(bf16[8,32,2,128]{3,1,2,0:T(8,128)(2,1)S(1)} %get-tuple-element.36, s32[1024]{0:T(1024)S(1)} %pad_clamp_fusion), kind=kCustom, calls=%fused_computation.1.clone | custom fusion | bytes 524352 | tf_op jit(solution)/shard_map/jit(_take)/gather | solution.py:128
  19.4 0.4 fusion.60
  19.8 0.4 fusion.59
  20.3 0.6 %gather_fusion.2 = bf16[16,32,2,128]{3,1,2,0:T(8,128)(2,1)S(1)} fusion(bf16[8,32,2,128]{3,1,2,0:T(8,128)(2,1)S(1)} %get-tuple-element.33, s32[1024]{0:T(1024)S(1)} %pad_clamp_fusion), kind=kCustom, calls=%fused_computation.2.clone | custom fusion | bytes 524352 | tf_op jit(solution)/shard_map/jit(_take)/gather | solution.py:129
  20.9 0.6 %gather_fusion.3 = bf16[16,32,2,128]{3,1,2,0:T(8,128)(2,1)S(1)} fusion(bf16[8,32,2,128]{3,1,2,0:T(8,128)(2,1)S(1)} %get-tuple-element.35, s32[1024]{0:T(1024)S(1)} %pad_clamp_fusion), kind=kCustom, calls=%fused_computation.3.clone | custom fusion | bytes 524352 | tf_op jit(solution)/shard_map/jit(_take)/gather | solution.py:129
  21.5 0.5 convert_reduce_fusion.1
  22.0 0.3 fusion.2
  22.3 0.3 fusion.1
  22.6 0.1 fusion.37
  22.8 0.1 reshape.248
  22.9 0.1 reshape.246
  23.0 0.1 select_maximum_fusion
  23.1 1.0 %reshape.321 = f32[32,1,2176]{2,1,0:T(1,128)} reshape(f32[32,17,128]{2,1,0:T(8,128)S(1)} %pad_maximum_fusion) | data formatting | bytes 557056 | tf_op jit(solution)/shard_map/reshape | solution.py:177
  24.1 6.0 %all-to-all-start.1 = ((f32[32,1,2176]{2,1,0:T(1,128)}), f32[32,1,2176]{2,1,0:T(1,128)S(1)}, u32[]{:S(2)}, u32[]{:S(2)}) async-start(f32[32,1,2176]{2,1,0:T(1,128)} %reshape.321), calls=%async_computation.1 | async-start | bytes 557056 | tf_op jit(solution)/shard_map/all_to_all | solution.py:176
  30.2 0.3 select_reduce_fusion.1
  30.5 0.1 reshape.256
  30.5 0.1 reshape.257
  30.6 0.1 convert_reduce_fusion.3
  30.7 0.1 reshape.263
  30.8 0.1 reshape.264
  30.9 0.6 %copy-done.6 = bf16[2,2,512]{2,1,0:T(2,128)(2,1)S(1)} copy-done((bf16[2,2,512]{2,1,0:T(2,128)(2,1)S(1)}, bf16[2,2,512]{2,1,0:T(2,128)(2,1)}, u32[]{:S(2)}) %copy-start.6) | copy-done | bytes 4120
  31.5 0.2 convolution_bitcast_fusion.2
  31.7 9.5 %all-to-all-done.1 = f32[32,1,2176]{2,1,0:T(1,128)S(1)} async-done(((f32[32,1,2176]{2,1,0:T(1,128)}), f32[32,1,2176]{2,1,0:T(1,128)S(1)}, u32[]{:S(2)}, u32[]{:S(2)}) %all-to-all-start.1) | async-done | bytes 278560 | tf_op jit(solution)/shard_map/all_to_all | solution.py:176
  41.2 0.7 %reduce.6 = f32[32,2176]{1,0:T(8,128)S(1)} reduce(f32[32,1,2176]{2,1,0:T(1,128)S(1)} %all-to-all-done.1, f32[]{:T(128)} %constant.98), dimensions={1}, to_apply=%all_to_all.7.reduce_sub_computation | reduce | bytes 557060 | tf_op jit(solution)/shard_map/all_to_all | solution.py:176
  42.0 0.1 fusion.58
  42.1 0.1 fusion.50
  42.2 0.1 multiply_reduce_fusion
  42.3 0.1 fusion.49
  42.4 0.1 divide_convert_fusion
  42.5 5.2 %all-gather = bf16[8,16,128]{2,1,0:T(8,128)(2,1)S(1)} all-gather(bf16[2,16,128]{2,1,0:T(8,128)(2,1)S(1)} %divide_convert_fusion), channel_id=2, replica_groups=mesh['ctx'=4,'row'=8] {'ctx'}, dimensions={0}, use_global_device_ids=true | all-gather | bytes 40960 | tf_op jit(solution)/shard_map/all_gather | solution.py:210
  47.7 0.6 %reshape.266 = bf16[2,2,4096]{2,1,0:T(2,128)(2,1)} reshape(bf16[2,2,2,16,128]{4,3,2,1,0:T(8,128)(2,1)S(1)} %bitcast.162) | data formatting | bytes 65536 | tf_op jit(solution)/shard_map/reshape | solution.py:213
  (59 shorter events, 0.9 us)
Async XLA Ops:
  0.0 13.5 %copy-start = (bf16[16,64,512]{2,1,0:T(8,128)(2,1)S(1)}, bf16[16,64,512]{2,1,0:T(8,128)(2,1)}, u32[]{:S(2)}) copy-start(bf16[16,64,512]{2,1,0:T(8,128)(2,1)} %param.18) | copy-start | bytes 3145732
  0.0 0.8 %copy-start.5 = (bf16[2,2,4096]{2,1,0:T(2,128)(2,1)S(1)}, bf16[2,2,4096]{2,1,0:T(2,128)(2,1)}, u32[]{:S(2)}) copy-start(bf16[2,2,4096]{2,1,0:T(2,128)(2,1)} %param.14) | copy-start | bytes 98308
  0.9 0.7 %copy-start.10 = (s32[2]{0:T(128)S(1)}, s32[2]{0:T(128)}, u32[]{:S(2)}) copy-start(s32[2]{0:T(128)} %param.15) | copy-start | bytes 28
  1.7 7.9 %copy-start.3 = (bf16[8,32,512]{2,1,0:T(8,128)(2,1)S(1)}, bf16[8,32,512]{2,1,0:T(8,128)(2,1)}, u32[]{:S(2)}) copy-start(bf16[8,32,512]{2,1,0:T(8,128)(2,1)} %param.16) | copy-start | bytes 786436
  2.4 15.5 %all-to-all-start = ((bf16[8,80,128]{2,1,0:T(8,128)(2,1)}), bf16[8,80,128]{2,1,0:T(8,128)(2,1)S(1)}, u32[]{:S(2)}, u32[]{:S(2)}) async-start(bf16[8,80,128]{2,1,0:T(8,128)(2,1)} %broadcast_in_dim.141), calls=%async_computation | async-start | bytes 327680 | tf_op jit(solution)/shard_map/all_to_all | solution.py:105
  9.6 1.0 %copy-start.4 = (bf16[8,32,512]{2,1,0:T(8,128)(2,1)S(1)}, bf16[8,32,512]{2,1,0:T(8,128)(2,1)}, u32[]{:S(2)}) copy-start(bf16[8,32,512]{2,1,0:T(8,128)(2,1)} %param.17) | copy-start | bytes 786436
  9.7 2.6 %copy-start.1 = (bf16[16,64,512]{2,1,0:T(8,128)(2,1)S(1)}, bf16[16,64,512]{2,1,0:T(8,128)(2,1)}, u32[]{:S(2)}) copy-start(bf16[16,64,512]{2,1,0:T(8,128)(2,1)} %param.19) | copy-start | bytes 3145732
  10.8 6.1 %collective-permute-start = (bf16[2,8,32,2,128]{4,2,3,1,0:T(8,128)(2,1)S(1)}, bf16[2,8,32,2,128]{4,2,3,1,0:T(8,128)(2,1)}, u32[]{:S(2)}, u32[]{:S(2)}) collective-permute-start(bf16[2,8,32,2,128]{4,2,3,1,0:T(8,128)(2,1)S(1)} %constant_dynamic-slice_fusion.6), channel_id=1, source_target_pairs={{0,8},{8,0},{16,24},{24,16},{1,9},{9,1},{17,25},{25,17},{2,10},{10... | collective-permute-start | bytes 786440 | tf_op jit(solution)/shard_map/ppermute | solution.py:124
  10.8 0.7 %copy-start.7 = (s32[2,32]{1,0:T(2,128)S(1)}, s32[2,32]{1,0:T(2,128)}, u32[]{:S(2)}) copy-start(s32[2,32]{1,0:T(2,128)} %param.20) | copy-start | bytes 772
  12.3 1.1 %copy-start.8 = (s32[2]{0:T(128)S(1)}, s32[2]{0:T(128)}, u32[]{:S(2)}) copy-start(s32[2]{0:T(128)} %param.21) | copy-start | bytes 28
  13.5 1.2 %copy-start.2 = (bf16[1024,4,128]{2,1,0:T(4,128)(2,1)S(1)}, bf16[1024,4,128]{2,1,0:T(4,128)(2,1)}, u32[]{:S(2)}) copy-start(bf16[1024,4,128]{2,1,0:T(4,128)(2,1)} %reshape.243) | copy-start | bytes 3145732
  15.1 1.4 %collective-permute-start.1 = (f32[2,2,2,8,130]{4,3,1,2,0:T(8,128)S(1)}, f32[2,2,2,8,130]{4,3,1,2,0:T(8,128)S(1)}, u32[]{:S(2)}, u32[]{:S(2)}) collective-permute-start(f32[2,2,2,8,130]{4,3,1,2,0:T(8,128)S(1)} %fusion.31), channel_id=1, source_target_pairs={{0,8},{8,0},{16,24},{24,16},{1,9},{9,1},{17,25},{25,17},{2,10},{10... | collective-permute-start | bytes 99848 | tf_op jit(solution)/shard_map/ppermute | solution.py:147
  24.1 6.0 %copy-start.9 = (bf16[2,2,512]{2,1,0:T(2,128)(2,1)S(1)}, bf16[2,2,512]{2,1,0:T(2,128)(2,1)}, u32[]{:S(2)}) copy-start(bf16[2,2,512]{2,1,0:T(2,128)(2,1)} %param.22) | copy-start | bytes 12292
  24.1 17.1 %all-to-all-start.1 = ((f32[32,1,2176]{2,1,0:T(1,128)}), f32[32,1,2176]{2,1,0:T(1,128)S(1)}, u32[]{:S(2)}, u32[]{:S(2)}) async-start(f32[32,1,2176]{2,1,0:T(1,128)} %reshape.321), calls=%async_computation.1 | async-start | bytes 557056 | tf_op jit(solution)/shard_map/all_to_all | solution.py:176
  30.8 0.7 %copy-start.6 = (bf16[2,2,512]{2,1,0:T(2,128)(2,1)S(1)}, bf16[2,2,512]{2,1,0:T(2,128)(2,1)}, u32[]{:S(2)}) copy-start(bf16[2,2,512]{2,1,0:T(2,128)(2,1)} %param.23) | copy-start | bytes 12292

commit v14 on v13

--- a/solution.py
+++ b/solution.py
@@ -125,8 +125,8 @@
 
 
     def prefix_block(kv):
-        row_keys = jnp.take(kv[0], every_prefix, axis=0)
-        row_values = jnp.take(kv[1], every_prefix, axis=0)
+        row_kv = jnp.take(kv, every_prefix, axis=1)
+        row_keys, row_values = row_kv[0], row_kv[1]
         scores = (
             jnp.einsum(
                 "rskgd,rtkd->rskgt", half_query, row_keys, preferred_element_type=jnp.float32

time: 48.8 us -> 47.6 us (0.975)
  starting transfers between devices: 13.9 us -> 11.4 us
  waiting for transfers between devices: 10.3 us -> 12.8 us
  local copies, waits for them, and re-layouts: 12.7 us -> 11.6 us
    all_to_all x1, waiting for transfers between devices: 0.01 us -> 2.22 us  [per_device(): lax.all_to_all(fanned, 'row', split_axis=0, concat_axis=0, tiled=True)]
    all_to_all x1, starting transfers between devices: 6.04 us -> 3.84 us  [per_device(): lax.all_to_all(outgoing.reshape(dests, 1, (chunk + pt_rows) * LANES), ('c...]
    gather x4 -> x2, local copies, waits for them, and re-layouts: 2.39 us -> 1.3 us  [prefix_block(): row_kv = jnp.take(kv, every_prefix, axis=1)]
    another operation x3, local copies, waits for them, and re-layouts: 0.2 us -> 1.23 us  [per_device(): jnp.stack([prefix_keys.reshape(prefix_count, span_len, KVH, HD), prefix_v...]
    squeeze x2 -> x0, local copies, waits for them, and re-layouts: 1.03 us -> none  [prefix_block(): row_values = jnp.take(kv[1], every_prefix, axis=0)]
    unnamed x23 -> x21, local copies, waits for them, and re-layouts: 3.66 us -> 2.91 us
    dynamic_slice x1, local copies, waits for them, and re-layouts: 0.02 us -> 0.77 us  [per_device(): own_kv = lax.dynamic_slice_in_dim(kv_both, core_bit * half_kv, half_kv, 3)]
  transfers between devices with their start and end apart: 4 -> 4, of which waited for: 2 -> 3; matrix products, arithmetic and copies ran while one was open for 13% -> 14% of each run, Pallas kernels for 0% -> 0%
where the time goes in v14:
time: 47.6 us; the launch traced here: 47.2 us
  waiting for transfers between devices  12.8 us (27%)
  local copies, waits for them, and re-layouts  11.6 us (24%)
  starting transfers between devices  11.4 us (24%)
  blocking collectives  5.19 us (11%)
  other arithmetic  3.3 us (7%)
  matrix products  2.56 us (5%)
    all_to_all x1, waiting for transfers between devices, per_device(): lax.all_to_all(outgoing.reshape(dests, 1, (chunk + pt_rows) * LANES), ('c...  9.49 us
    all_to_all x1, starting transfers between devices, per_device(): lax.all_to_all(fanned, 'row', split_axis=0, concat_axis=0, tiled=True)  6.9 us
    all_gather x1, blocking collectives, per_device(): whole = lax.all_gather(result, 'ctx', axis=0, tiled=False)  5.19 us
    all_to_all x1, starting transfers between devices, per_device(): lax.all_to_all(outgoing.reshape(dests, 1, (chunk + pt_rows) * LANES), ('c...  3.84 us
    unnamed x21, local copies, waits for them, and re-layouts  2.91 us
    all_to_all x1, waiting for transfers between devices, per_device(): lax.all_to_all(fanned, 'row', split_axis=0, concat_axis=0, tiled=True)  2.22 us
    gather x2, local copies, waits for them, and re-layouts, prefix_block(): row_kv = jnp.take(kv, every_prefix, axis=1)  1.3 us
    another operation x3, local copies, waits for them, and re-layouts, per_device(): jnp.stack([prefix_keys.reshape(prefix_count, span_len, KVH, HD), prefix_v...  1.23 us
  transfers between devices with their start and end apart: 4, of which 3 were waited for; matrix products, arithmetic and copies ran while one was open for 14% of the time, Pallas kernels for 0%

profile of v14, /device:TPU:0, one launch (start us, length us, event | category | flops | bytes accessed | tf_op | source)
XLA Modules:
  0.0 47.2 jit_solution(5641311288490839684)
XLA Ops:
  0.0 1.1 %stack_reshape.6 = bf16[1,8,32,4,128]{4,3,2,1,0:T(4,128)(2,1)S(1)} reshape(bf16[8,32,512]{2,1,0:T(8,128)(2,1)} %param.16) | data formatting | bytes 524288 | tf_op jit(solution)/shard_map/stack;reshape | solution.py:116
  1.2 0.9 %copy-done.3 = bf16[8,32,512]{2,1,0:T(8,128)(2,1)S(1)} copy-done((bf16[8,32,512]{2,1,0:T(8,128)(2,1)S(1)}, bf16[8,32,512]{2,1,0:T(8,128)(2,1)}, u32[]{:S(2)}) %copy-start.3) | copy-done | bytes 262168
  2.2 0.8 %constant_dynamic-slice_fusion.8 = (bf16[2,8,32,2,128]{4,2,3,1,0:T(8,128)(2,1)S(1)}, bf16[2,8,32,2,128]{4,2,3,1,0:T(8,128)(2,1)}) fusion(bf16[2,8,32,4,128]{4,2,3,1,0:T(8,128)(2,1)S(1)} %copy_dynamic-update-slice_fusion, s32[]{:T(128)S(6)} %select_n.76, s32[]{:T(128)S(6)} %select_n.77), kind=kLoop, calls=%fused_computation.85 | loop fusion | bytes 1048584 | tf_op jit(solution)/shard_map/dynamic_slice | solution.py:122
  3.0 0.5 collective-permute-start
  3.5 0.6 %copy-done.9 = s32[2]{0:T(128)S(1)} copy-done((s32[2]{0:T(128)S(1)}, s32[2]{0:T(128)}, u32[]{:S(2)}) %copy-start.9) | copy-done | bytes 32
  4.2 0.1 compare_select_fusion.2
  4.2 0.1 pad_maximum_fusion.1
  4.3 0.7 %broadcast_in_dim.141 = bf16[8,80,128]{2,1,0:T(8,128)(2,1)} broadcast(bf16[80,128]{1,0:T(8,128)(2,1)S(1)} %pad_maximum_fusion.1), dimensions={1,2} | broadcast | bytes 184320 | tf_op jit(solution)/shard_map/broadcast_in_dim | solution.py:104
  5.0 6.9 %all-to-all-start = ((bf16[8,80,128]{2,1,0:T(8,128)(2,1)}), bf16[8,80,128]{2,1,0:T(8,128)(2,1)S(1)}, u32[]{:S(2)}, u32[]{:S(2)}) async-start(bf16[8,80,128]{2,1,0:T(8,128)(2,1)} %broadcast_in_dim.141), calls=%async_computation | async-start | bytes 327680 | tf_op jit(solution)/shard_map/all_to_all | solution.py:105
  11.9 0.7 %copy-done.6 = s32[2,32]{1,0:T(2,128)S(1)} copy-done((s32[2,32]{1,0:T(2,128)S(1)}, s32[2,32]{1,0:T(2,128)}, u32[]{:S(2)}) %copy-start.6) | copy-done | bytes 280
  12.6 0.2 fusion.25
  12.8 0.2 compare_reduce_fusion
  13.0 0.1 add.105
  13.0 0.1 add.106
  13.1 0.1 and.29
  13.2 0.1 and.30
  13.3 0.1 add.108
  13.4 1.1 %reshape.243 = bf16[1024,4,128]{2,1,0:T(4,128)(2,1)} reshape(bf16[16,64,512]{2,1,0:T(8,128)(2,1)S(1)} %copy-done.1) | data formatting | bytes 2097152 | tf_op jit(solution)/shard_map/reshape | solution.py:70
  14.5 0.1 compare_and_fusion
  14.6 0.6 %select_reduce_fusion = (f32[2,2,4,8]{3,2,1,0:T(4,128)S(1)}, f32[2,2,4,8,1024]{4,3,2,1,0:T(8,128)S(1)}) fusion(pred[2,1024]{1,0:T(4,128)(4,1)S(1)} %compare_and_fusion, bf16[1024,512,1,1,1]{1,0,4,3,2:T(8,128)(2,1)S(1)} %bitcast.153, pred[4,4]{1,0:T(4,128)(4,1)S(1)} %iota_compare_fusion.1, bf16[2,2,4,8,128]{4,3,2,1,0:T(8,128)(2,1)S(1)} %reshape.239), kind=kOutput, calls=%fused_computation.23 | convolution fusion | flops 134676352 | bytes 1608208 | tf_op jit(solution)/shard_map/rskgw,tw->rskgt/dot_general | solution.py:78
  15.2 0.3 convert_reduce_fusion
  15.4 0.2 copy.180
  15.6 0.2 copy.179
  15.8 0.3 fusion.6
  16.1 0.1 fusion.17
  16.2 0.2 collective-permute-start.1
  16.4 1.1 %collective-permute-done.1 = f32[2,2,2,8,130]{4,3,1,2,0:T(8,128)S(1)} collective-permute-done((f32[2,2,2,8,130]{4,3,1,2,0:T(8,128)S(1)}, f32[2,2,2,8,130]{4,3,1,2,0:T(8,128)S(1)}, u32[]{:S(2)}, u32[]{:S(2)}) %collective-permute-start.1) | collective-permute-done | bytes 33312 | tf_op jit(solution)/shard_map/ppermute | solution.py:147
  17.4 0.1 fusion.39
  17.5 0.1 copy.217
  17.6 0.1 copy.219
  17.8 2.2 %all-to-all-done = bf16[8,80,128]{2,1,0:T(8,128)(2,1)S(1)} async-done(((bf16[8,80,128]{2,1,0:T(8,128)(2,1)}), bf16[8,80,128]{2,1,0:T(8,128)(2,1)S(1)}, u32[]{:S(2)}, u32[]{:S(2)}) %all-to-all-start) | async-done | bytes 163872 | tf_op jit(solution)/shard_map/all_to_all | solution.py:105
  20.0 0.2 convert_reduce_fusion.4
  20.2 0.1 reshape.267
  20.3 0.6 %gather_fusion = bf16[16,2,32,2,128]{4,2,3,1,0:T(8,128)(2,1)S(1)} fusion(bf16[2,8,32,2,128]{4,2,3,1,0:T(8,128)(2,1)S(1)} %get-tuple-element.33, s32[1024]{0:T(1024)S(1)} %pad_clamp_fusion), kind=kCustom, calls=%fused_computation.clone | custom fusion | bytes 1048640 | tf_op jit(solution)/shard_map/jit(_take)/gather | solution.py:128
  21.0 0.6 %gather_fusion.1 = bf16[16,2,32,2,128]{4,2,3,1,0:T(8,128)(2,1)S(1)} fusion(bf16[2,8,32,2,128]{4,2,3,1,0:T(8,128)(2,1)S(1)} %collective-permute-done, s32[1024]{0:T(1024)S(1)} %pad_clamp_fusion), kind=kCustom, calls=%fused_computation.1.clone | custom fusion | bytes 1048640 | tf_op jit(solution)/shard_map/jit(_take)/gather | solution.py:128
  21.6 0.2 fusion.9
  21.8 0.4 fusion.42
  22.2 0.4 fusion.41
  22.5 0.5 convert_reduce_fusion.1
  23.1 0.3 fusion.2
  23.3 0.3 fusion.1
  23.6 0.1 fusion.23
  23.8 0.1 reshape.248
  24.0 0.1 reshape.246
  24.1 0.1 select_maximum_fusion
  24.2 1.0 %reshape.299 = f32[32,1,2176]{2,1,0:T(1,128)} reshape(f32[32,17,128]{2,1,0:T(8,128)S(1)} %pad_maximum_fusion) | data formatting | bytes 557056 | tf_op jit(solution)/shard_map/reshape | solution.py:177
  25.2 3.8 %all-to-all-start.1 = ((f32[32,1,2176]{2,1,0:T(1,128)}), f32[32,1,2176]{2,1,0:T(1,128)S(1)}, u32[]{:S(2)}, u32[]{:S(2)}) async-start(f32[32,1,2176]{2,1,0:T(1,128)} %reshape.299), calls=%async_computation.1 | async-start | bytes 557056 | tf_op jit(solution)/shard_map/all_to_all | solution.py:176
  29.0 0.3 select_reduce_fusion.1
  29.3 0.1 reshape.256
  29.4 0.1 reshape.257
  29.5 0.1 convert_reduce_fusion.3
  29.6 0.1 reshape.263
  29.7 0.1 reshape.264
  29.8 0.6 %copy-done.5 = bf16[2,2,512]{2,1,0:T(2,128)(2,1)S(1)} copy-done((bf16[2,2,512]{2,1,0:T(2,128)(2,1)S(1)}, bf16[2,2,512]{2,1,0:T(2,128)(2,1)}, u32[]{:S(2)}) %copy-start.5) | copy-done | bytes 4120
  30.4 0.2 convolution_bitcast_fusion.2
  30.6 9.5 %all-to-all-done.1 = f32[32,1,2176]{2,1,0:T(1,128)S(1)} async-done(((f32[32,1,2176]{2,1,0:T(1,128)}), f32[32,1,2176]{2,1,0:T(1,128)S(1)}, u32[]{:S(2)}, u32[]{:S(2)}) %all-to-all-start.1) | async-done | bytes 278560 | tf_op jit(solution)/shard_map/all_to_all | solution.py:176
  40.1 0.7 %reduce.6 = f32[32,2176]{1,0:T(8,128)S(1)} reduce(f32[32,1,2176]{2,1,0:T(1,128)S(1)} %all-to-all-done.1, f32[]{:T(128)} %constant.98), dimensions={1}, to_apply=%all_to_all.7.reduce_sub_computation | reduce | bytes 557060 | tf_op jit(solution)/shard_map/all_to_all | solution.py:176
  40.8 0.1 fusion.40
  40.9 0.1 fusion.36
  41.1 0.1 multiply_reduce_fusion
  41.2 0.1 fusion.35
  41.3 0.1 divide_convert_fusion
  41.4 5.2 %all-gather = bf16[8,16,128]{2,1,0:T(8,128)(2,1)S(1)} all-gather(bf16[2,16,128]{2,1,0:T(8,128)(2,1)S(1)} %divide_convert_fusion), channel_id=2, replica_groups=mesh['ctx'=4,'row'=8] {'ctx'}, dimensions={0}, use_global_device_ids=true | all-gather | bytes 40960 | tf_op jit(solution)/shard_map/all_gather | solution.py:210
  46.5 0.6 %reshape.266 = bf16[2,2,4096]{2,1,0:T(2,128)(2,1)} reshape(bf16[2,2,2,16,128]{4,3,2,1,0:T(8,128)(2,1)S(1)} %bitcast.164) | data formatting | bytes 65536 | tf_op jit(solution)/shard_map/reshape | solution.py:213
  (54 shorter events, 0.8 us)
Async XLA Ops:
  0.0 14.6 %copy-start = (bf16[16,64,512]{2,1,0:T(8,128)(2,1)S(1)}, bf16[16,64,512]{2,1,0:T(8,128)(2,1)}, u32[]{:S(2)}) copy-start(bf16[16,64,512]{2,1,0:T(8,128)(2,1)} %param.18) | copy-start | bytes 3145732
  1.1 1.0 %copy-start.3 = (bf16[8,32,512]{2,1,0:T(8,128)(2,1)S(1)}, bf16[8,32,512]{2,1,0:T(8,128)(2,1)}, u32[]{:S(2)}) copy-start(bf16[8,32,512]{2,1,0:T(8,128)(2,1)} %param.17) | copy-start | bytes 786436
  2.1 11.2 %copy-start.1 = (bf16[16,64,512]{2,1,0:T(8,128)(2,1)S(1)}, bf16[16,64,512]{2,1,0:T(8,128)(2,1)}, u32[]{:S(2)}) copy-start(bf16[16,64,512]{2,1,0:T(8,128)(2,1)} %param.19) | copy-start | bytes 3145732
  2.2 1.2 %copy-start.4 = (bf16[2,2,4096]{2,1,0:T(2,128)(2,1)S(1)}, bf16[2,2,4096]{2,1,0:T(2,128)(2,1)}, u32[]{:S(2)}) copy-start(bf16[2,2,4096]{2,1,0:T(2,128)(2,1)} %param.14) | copy-start | bytes 98308
  3.0 18.0 %collective-permute-start = (bf16[2,8,32,2,128]{4,2,3,1,0:T(8,128)(2,1)}, bf16[2,8,32,2,128]{4,2,3,1,0:T(8,128)(2,1)S(1)}, u32[]{:S(2)}, u32[]{:S(2)}) collective-permute-start(bf16[2,8,32,2,128]{4,2,3,1,0:T(8,128)(2,1)} %get-tuple-element.34), channel_id=1, source_target_pairs={{0,8},{8,0},{16,24},{24,16},{1,9},{9,1},{17,25},{25,17},{2,10},{10... | collective-permute-start | bytes 786440 | tf_op jit(solution)/shard_map/ppermute | solution.py:124
  3.5 0.7 %copy-start.9 = (s32[2]{0:T(128)S(1)}, s32[2]{0:T(128)}, u32[]{:S(2)}) copy-start(s32[2]{0:T(128)} %param.15) | copy-start | bytes 28
  5.0 15.0 %all-to-all-start = ((bf16[8,80,128]{2,1,0:T(8,128)(2,1)}), bf16[8,80,128]{2,1,0:T(8,128)(2,1)S(1)}, u32[]{:S(2)}, u32[]{:S(2)}) async-start(bf16[8,80,128]{2,1,0:T(8,128)(2,1)} %broadcast_in_dim.141), calls=%async_computation | async-start | bytes 327680 | tf_op jit(solution)/shard_map/all_to_all | solution.py:105
  11.9 0.7 %copy-start.6 = (s32[2,32]{1,0:T(2,128)S(1)}, s32[2,32]{1,0:T(2,128)}, u32[]{:S(2)}) copy-start(s32[2,32]{1,0:T(2,128)} %param.20) | copy-start | bytes 772
  13.4 1.1 %copy-start.7 = (s32[2]{0:T(128)S(1)}, s32[2]{0:T(128)}, u32[]{:S(2)}) copy-start(s32[2]{0:T(128)} %param.21) | copy-start | bytes 28
  14.6 1.2 %copy-start.2 = (bf16[1024,4,128]{2,1,0:T(4,128)(2,1)S(1)}, bf16[1024,4,128]{2,1,0:T(4,128)(2,1)}, u32[]{:S(2)}) copy-start(bf16[1024,4,128]{2,1,0:T(4,128)(2,1)} %reshape.243) | copy-start | bytes 3145732
  16.2 1.3 %collective-permute-start.1 = (f32[2,2,2,8,130]{4,3,1,2,0:T(8,128)S(1)}, f32[2,2,2,8,130]{4,3,1,2,0:T(8,128)S(1)}, u32[]{:S(2)}, u32[]{:S(2)}) collective-permute-start(f32[2,2,2,8,130]{4,3,1,2,0:T(8,128)S(1)} %fusion.17), channel_id=1, source_target_pairs={{0,8},{8,0},{16,24},{24,16},{1,9},{9,1},{17,25},{25,17},{2,10},{10... | collective-permute-start | bytes 99848 | tf_op jit(solution)/shard_map/ppermute | solution.py:147
  25.2 3.9 %copy-start.8 = (bf16[2,2,512]{2,1,0:T(2,128)(2,1)S(1)}, bf16[2,2,512]{2,1,0:T(2,128)(2,1)}, u32[]{:S(2)}) copy-start(bf16[2,2,512]{2,1,0:T(2,128)(2,1)} %param.22) | copy-start | bytes 12292
  25.2 14.9 %all-to-all-start.1 = ((f32[32,1,2176]{2,1,0:T(1,128)}), f32[32,1,2176]{2,1,0:T(1,128)S(1)}, u32[]{:S(2)}, u32[]{:S(2)}) async-start(f32[32,1,2176]{2,1,0:T(1,128)} %reshape.299), calls=%async_computation.1 | async-start | bytes 557056 | tf_op jit(solution)/shard_map/all_to_all | solution.py:176
  29.7 0.7 %copy-start.5 = (bf16[2,2,512]{2,1,0:T(2,128)(2,1)S(1)}, bf16[2,2,512]{2,1,0:T(2,128)(2,1)}, u32[]{:S(2)}) copy-start(bf16[2,2,512]{2,1,0:T(2,128)(2,1)} %param.23) | copy-start | bytes 12292

commit v15 on v14

--- a/solution.py
+++ b/solution.py
@@ -113,19 +113,24 @@
     swap = [(c, c ^ 1) for c in range(ctx_count)]
     span_len = prefix_keys.shape[1]
     prefix_count = prefix_keys.shape[0]
-    kv_both = jnp.stack(
-        [
-            prefix_keys.reshape(prefix_count, span_len, KVH, HD),
-            prefix_values.reshape(prefix_count, span_len, KVH, HD),
-        ]
-    )
-    own_kv = lax.dynamic_slice_in_dim(kv_both, core_bit * half_kv, half_kv, 3)
-    given_kv = lax.dynamic_slice_in_dim(kv_both, (1 - core_bit) * half_kv, half_kv, 3)
+    lane_half = half_kv * HD
+
+    def lane_half_of(member, at):
+        return lax.dynamic_slice_in_dim(member, at * lane_half, lane_half, 2)
+
+    own_kv = jnp.stack(
+        [lane_half_of(prefix_keys, core_bit), lane_half_of(prefix_values, core_bit)]
+    )
+    given_kv = jnp.stack(
+        [lane_half_of(prefix_keys, 1 - core_bit), lane_half_of(prefix_values, 1 - core_bit)]
+    )
     partner_kv = lax.ppermute(given_kv, "ctx", swap)
 
 
     def prefix_block(kv):
-        row_kv = jnp.take(kv, every_prefix, axis=1)
+        row_kv = jnp.take(kv, every_prefix, axis=1).reshape(
+            2, total_rows, span_len, half_kv, HD
+        )
         row_keys, row_values = row_kv[0], row_kv[1]
         scores = (
             jnp.einsum(

time: 47.6 us -> 52.6 us (1.11)
  other arithmetic: 3.3 us -> 6.11 us
  waiting for transfers between devices: 12.8 us -> 10.5 us
  starting transfers between devices: 11.4 us -> 13.4 us
  local copies, waits for them, and re-layouts: 11.6 us -> 13 us
  matrix products: 2.56 us -> 3.3 us
    all_to_all x1, starting transfers between devices: 3.84 us -> 5.91 us  [per_device(): lax.all_to_all(outgoing.reshape(dests, 1, (chunk + pt_rows) * LANES), ('c...]
    all_to_all x1, waiting for transfers between devices: 2.22 us -> 0.15 us  [per_device(): lax.all_to_all(fanned, 'row', split_axis=0, concat_axis=0, tiled=True)]
    unnamed x21 -> x26, local copies, waits for them, and re-layouts: 2.91 us -> 4.14 us
    slice x1, local copies, waits for them, and re-layouts: 0.01 us -> 0.92 us  [per_device(): gathered[:, :query_rows, :]]
    reshape x1, local copies, waits for them, and re-layouts: 1.12 us -> 0.27 us  [per_device(): flat_values = pool_values.reshape(slot_count * page_len, KVH, HD)]
    dynamic_slice x1 -> x0, local copies, waits for them, and re-layouts: 0.77 us -> none  [per_device(): own_kv = lax.dynamic_slice_in_dim(kv_both, core_bit * half_kv, half_kv, 3)]
    dot_general x1, matrix products: 0.57 us -> 1.32 us  [per_device(): jnp.einsum('rskgw,tw->rskgt', wide_query, flat_keys, preferred_element_ty...]
    another operation x0 -> x2, other arithmetic: none -> 0.74 us  [the longest x1 0.72 us: per_device(): jnp.stack([lane_half_of(prefix_keys, 1 - core_bit), lane_half_of(prefix_v...]
  transfers between devices with their start and end apart: 4 -> 4, of which waited for: 3 -> 3; matrix products, arithmetic and copies ran while one was open for 14% -> 16% of each run, Pallas kernels for 0% -> 0%
where the time goes in v15:
time: 52.6 us; the launch traced here: 51.9 us
  starting transfers between devices  13.4 us (25%)
  local copies, waits for them, and re-layouts  13 us (25%)
  waiting for transfers between devices  10.5 us (20%)
  other arithmetic  6.11 us (12%)
  blocking collectives  5.19 us (10%)
  matrix products  3.3 us (6%)
    all_to_all x1, waiting for transfers between devices, per_device(): lax.all_to_all(outgoing.reshape(dests, 1, (chunk + pt_rows) * LANES), ('c...  9.48 us
    all_to_all x1, starting transfers between devices, per_device(): lax.all_to_all(fanned, 'row', split_axis=0, concat_axis=0, tiled=True)  6.84 us
    all_to_all x1, starting transfers between devices, per_device(): lax.all_to_all(outgoing.reshape(dests, 1, (chunk + pt_rows) * LANES), ('c...  5.91 us
    all_gather x1, blocking collectives, per_device(): whole = lax.all_gather(result, 'ctx', axis=0, tiled=False)  5.19 us
    unnamed x26, local copies, waits for them, and re-layouts  4.14 us
    another operation x1, local copies, waits for them, and re-layouts, per_device(): jnp.stack([lane_half_of(prefix_keys, core_bit), lane_half_of(prefix_value...  1.92 us
    dot_general x1, matrix products, per_device(): jnp.einsum('rskgw,tw->rskgt', wide_query, flat_keys, preferred_element_ty...  1.32 us
    gather x2, local copies, waits for them, and re-layouts, prefix_block(): jnp.take(kv, every_prefix, axis=1)  1.16 us
  transfers between devices with their start and end apart: 4, of which 3 were waited for; matrix products, arithmetic and copies ran while one was open for 16% of the time, Pallas kernels for 0%

profile of v15, /device:TPU:0, one launch (start us, length us, event | category | flops | bytes accessed | tf_op | source)
XLA Modules:
  0.0 51.9 jit_solution(12280184218224628384)
XLA Ops:
  0.0 1.9 %dynamic-slice_bitcast_fusion.2 = (bf16[1,8,32,256]{3,2,1,0:T(8,128)(2,1)S(1)}, bf16[1,8,32,256]{3,2,1,0:T(8,128)(2,1)S(1)}, bf16[1,8,32,256]{3,2,1,0:T(8,128)(2,1)S(1)}, bf16[1,8,32,256]{3,2,1,0:T(8,128)(2,1)}) fusion(bf16[8,32,512]{2,1,0:T(8,128)(2,1)} %param.17, s32[]{:T(128)S(6)} %select_n.82, s32[]{:T(128)S(6)} %select_n.84, bf16[8,32,512]{2,1,0:T(8,128)(2,1)} %param.16), kind=kLoop, calls=%fused_computation.42 | loop fusion | bytes 1048584 | tf_op jit(solution)/shard_map/stack | solution.py:121
  1.9 0.7 %pad_maximum_fusion.2 = bf16[2,8,32,256]{3,2,1,0:T(8,128)(2,1)} fusion(bf16[1,8,32,256]{3,2,1,0:T(8,128)(2,1)S(1)} %get-tuple-element.40, bf16[1,8,32,256]{3,2,1,0:T(8,128)(2,1)S(1)} %get-tuple-element.58), kind=kLoop, calls=%fused_computation.24 | loop fusion | flops 131072 | bytes 524288 | tf_op jit(solution)/shard_map/stack | solution.py:124
  2.6 0.5 collective-permute-start
  3.1 0.6 %copy-done.12 = s32[2]{0:T(128)S(1)} copy-done((s32[2]{0:T(128)S(1)}, s32[2]{0:T(128)}, u32[]{:S(2)}) %copy-start.12) | copy-done | bytes 32
  3.8 0.1 compare_select_fusion.2
  3.9 0.4 copy-done.3
  4.4 0.7 %broadcast_in_dim.141 = bf16[8,80,128]{2,1,0:T(8,128)(2,1)} broadcast(bf16[80,128]{1,0:T(8,128)(2,1)S(1)} %pad_maximum_fusion.3), dimensions={1,2} | broadcast | bytes 184320 | tf_op jit(solution)/shard_map/broadcast_in_dim | solution.py:104
  5.0 6.8 %all-to-all-start = ((bf16[8,80,128]{2,1,0:T(8,128)(2,1)}), bf16[8,80,128]{2,1,0:T(8,128)(2,1)}, u32[]{:S(2)}, u32[]{:S(2)}) async-start(bf16[8,80,128]{2,1,0:T(8,128)(2,1)} %broadcast_in_dim.141), calls=%async_computation | async-start | bytes 327680 | tf_op jit(solution)/shard_map/all_to_all | solution.py:105
  11.9 0.7 %copy-done.9 = s32[2,32]{1,0:T(2,128)S(1)} copy-done((s32[2,32]{1,0:T(2,128)S(1)}, s32[2,32]{1,0:T(2,128)}, u32[]{:S(2)}) %copy-start.9) | copy-done | bytes 280
  12.6 0.2 fusion.27
  12.7 0.2 compare_reduce_fusion
  12.9 0.6 %iota_compare_fusion.1 = pred[4,4]{1,0:T(4,128)(4,1)} fusion(), kind=kLoop, calls=%fused_computation.103 | loop fusion | flops 16 | bytes 16 | tf_op jit(solution)/shard_map/eq | solution.py:71
  13.6 0.1 add.113
  13.7 0.1 and.30
  13.9 0.3 reshape.253
  14.2 0.7 %compare_and_fusion = pred[2,1024]{1,0:T(4,128)(4,1)S(1)} fusion(pred[2,1024]{1,0:T(4,128)(4,1)S(1)} %and.30, s32[2,1024]{1,0:T(2,128)S(1)} %add.113, s32[2]{0:T(128)} %param.21, s32[1024]{0:T(1024)S(1)} %add.115), kind=kLoop, calls=%fused_computation.75 | loop fusion | flops 6144 | bytes 16392 | tf_op jit(solution)/shard_map/and | solution.py:67
  14.9 0.6 %copy-done.10 = pred[4,4]{1,0:T(4,128)(4,1)S(1)} copy-done((pred[4,4]{1,0:T(4,128)(4,1)S(1)}, pred[4,4]{1,0:T(4,128)(4,1)}, u32[]{:S(2)}) %copy-start.10) | copy-done | bytes 40
  15.5 1.3 %select_reduce_fusion = (f32[2,2,4,8]{3,2,1,0:T(4,128)S(1)}, f32[2,2,4,8,1024]{4,3,2,1,0:T(8,128)S(1)}) fusion(pred[2,1024]{1,0:T(4,128)(4,1)S(1)} %compare_and_fusion, bf16[1024,512,1,1,1]{1,0,4,3,2:T(8,128)(2,1)S(1)} %bitcast.153, pred[4,4]{1,0:T(4,128)(4,1)S(1)} %copy-done.10, bf16[2,2,4,8,128]{4,3,2,1,0:T(8,128)(2,1)} %copy-done.3), kind=kOutput, calls=%fused_computation.21 | convolution fusion | flops 134676352 | bytes 1608208 | tf_op jit(solution)/shard_map/rskgw,tw->rskgt/dot_general | solution.py:78
  16.9 0.3 convert_reduce_fusion
  17.1 0.2 copy.182
  17.3 0.2 copy.181
  17.5 0.3 fusion.6
  17.8 0.1 fusion.19
  17.9 0.5 copy-done.5
  18.4 0.2 collective-permute-start.1
  18.6 0.1 copy-done.2
  18.7 0.9 %collective-permute-done.1 = f32[2,2,2,8,130]{4,3,1,2,0:T(8,128)S(1)} collective-permute-done((f32[2,2,2,8,130]{4,3,1,2,0:T(8,128)S(1)}, f32[2,2,2,8,130]{4,3,1,2,0:T(8,128)S(1)}, u32[]{:S(2)}, u32[]{:S(2)}) %collective-permute-start.1) | collective-permute-done | bytes 33312 | tf_op jit(solution)/shard_map/ppermute | solution.py:152
  19.7 0.1 copy.227
  19.8 0.1 copy.229
  19.9 0.2 all-to-all-done
  20.1 0.9 %convert_reduce_fusion.4 = s32[8,2]{1,0:T(8,128)S(1)} fusion(bf16[8,80,128]{2,1,0:T(8,128)(2,1)} %all-to-all-done), kind=kLoop, calls=%fused_computation.76 | loop fusion | flops 16 | bytes 96 | tf_op jit(solution)/shard_map/convert_element_type | solution.py:111
  21.0 0.1 reshape.277
  21.1 0.6 %gather_fusion = bf16[16,2,32,256]{3,2,1,0:T(8,128)(2,1)S(1)} fusion(bf16[2,8,32,256]{3,2,1,0:T(8,128)(2,1)S(1)} %pad_maximum_fusion.1, s32[1024]{0:T(1024)S(1)} %pad_clamp_fusion), kind=kCustom, calls=%fused_computation.clone | custom fusion | bytes 1048640 | tf_op jit(solution)/shard_map/jit(_take)/gather | solution.py:131
  21.7 0.6 %gather_fusion.1 = bf16[16,2,32,256]{3,2,1,0:T(8,128)(2,1)S(1)} fusion(bf16[2,8,32,256]{3,2,1,0:T(8,128)(2,1)S(1)} %collective-permute-done, s32[1024]{0:T(1024)S(1)} %pad_clamp_fusion), kind=kCustom, calls=%fused_computation.1.clone | custom fusion | bytes 1048640 | tf_op jit(solution)/shard_map/jit(_take)/gather | solution.py:131
  22.3 0.2 select_bitcast_fusion.1
  22.7 0.9 %slice.78 = bf16[8,64,128]{2,1,0:T(8,128)(2,1)S(1)} slice(bf16[8,80,128]{2,1,0:T(8,128)(2,1)} %all-to-all-done), slice={[0:8], [0:64], [0:128]} | slice | bytes 262144 | tf_op jit(solution)/shard_map/slice | solution.py:107
  23.6 0.4 fusion.46
  24.0 0.4 fusion.45
  24.5 0.3 convert_reduce_fusion.2
  24.8 0.3 convert_reduce_fusion.1
  25.2 0.3 fusion.2
  25.5 0.3 fusion.1
  25.8 0.5 %copy-done.6 = f32[4,2,2,8,128]{4,3,2,0,1:T(8,128)S(1)} copy-done((f32[4,2,2,8,128]{4,3,2,0,1:T(8,128)S(1)}, f32[4,2,2,8,128]{4,3,2,0,1:T(8,128)}, u32[]{:S(2)}) %copy-start.6) | copy-done | bytes 65560
  26.3 0.1 fusion.25
  26.5 0.1 reshape.258
  26.6 0.1 reshape.256
  26.7 0.1 select_maximum_fusion
  26.8 1.0 %reshape.309 = f32[32,1,2176]{2,1,0:T(1,128)} reshape(f32[32,17,128]{2,1,0:T(8,128)S(1)} %pad_maximum_fusion) | data formatting | bytes 557056 | tf_op jit(solution)/shard_map/reshape | solution.py:182
  27.8 5.9 %all-to-all-start.1 = ((f32[32,1,2176]{2,1,0:T(1,128)}), f32[32,1,2176]{2,1,0:T(1,128)S(1)}, u32[]{:S(2)}, u32[]{:S(2)}) async-start(f32[32,1,2176]{2,1,0:T(1,128)} %reshape.309), calls=%async_computation.1 | async-start | bytes 557056 | tf_op jit(solution)/shard_map/all_to_all | solution.py:181
  33.7 0.3 select_reduce_fusion.1
  34.0 0.1 reshape.266
  34.1 0.1 reshape.267
  34.2 0.1 convert_reduce_fusion.3
  34.3 0.1 reshape.273
  34.4 0.1 reshape.274
  34.5 0.6 %copy-done.8 = bf16[2,2,512]{2,1,0:T(2,128)(2,1)S(1)} copy-done((bf16[2,2,512]{2,1,0:T(2,128)(2,1)S(1)}, bf16[2,2,512]{2,1,0:T(2,128)(2,1)}, u32[]{:S(2)}) %copy-start.8) | copy-done | bytes 4120
  35.1 0.2 convolution_bitcast_fusion.2
  35.3 9.5 %all-to-all-done.1 = f32[32,1,2176]{2,1,0:T(1,128)S(1)} async-done(((f32[32,1,2176]{2,1,0:T(1,128)}), f32[32,1,2176]{2,1,0:T(1,128)S(1)}, u32[]{:S(2)}, u32[]{:S(2)}) %all-to-all-start.1) | async-done | bytes 278560 | tf_op jit(solution)/shard_map/all_to_all | solution.py:181
  44.8 0.7 %reduce.6 = f32[32,2176]{1,0:T(8,128)S(1)} reduce(f32[32,1,2176]{2,1,0:T(1,128)S(1)} %all-to-all-done.1, f32[]{:T(128)} %constant.102), dimensions={1}, to_apply=%all_to_all.7.reduce_sub_computation | reduce | bytes 557060 | tf_op jit(solution)/shard_map/all_to_all | solution.py:181
  45.8 0.1 multiply_reduce_fusion
  45.9 0.1 fusion.37
  46.0 0.1 divide_convert_fusion
  46.1 5.2 %all-gather = bf16[8,16,128]{2,1,0:T(8,128)(2,1)S(1)} all-gather(bf16[2,16,128]{2,1,0:T(8,128)(2,1)S(1)} %divide_convert_fusion), channel_id=2, replica_groups=mesh['ctx'=4,'row'=8] {'ctx'}, dimensions={0}, use_global_device_ids=true | all-gather | bytes 40960 | tf_op jit(solution)/shard_map/all_gather | solution.py:215
  51.3 0.6 %reshape.276 = bf16[2,2,4096]{2,1,0:T(2,128)(2,1)} reshape(bf16[2,2,2,16,128]{4,3,2,1,0:T(8,128)(2,1)S(1)} %bitcast.168) | data formatting | bytes 65536 | tf_op jit(solution)/shard_map/reshape | solution.py:218
  (65 shorter events, 1.4 us)
Async XLA Ops:
  0.0 14.9 %copy-start = (bf16[16,64,512]{2,1,0:T(8,128)(2,1)S(1)}, bf16[16,64,512]{2,1,0:T(8,128)(2,1)}, u32[]{:S(2)}) copy-start(bf16[16,64,512]{2,1,0:T(8,128)(2,1)} %param.18) | copy-start | bytes 3145732
  0.0 13.9 %copy-start.1 = (bf16[16,64,512]{2,1,0:T(8,128)(2,1)S(1)}, bf16[16,64,512]{2,1,0:T(8,128)(2,1)}, u32[]{:S(2)}) copy-start(bf16[16,64,512]{2,1,0:T(8,128)(2,1)} %param.19) | copy-start | bytes 3145732
  1.9 1.2 %copy-start.7 = (bf16[2,2,4096]{2,1,0:T(2,128)(2,1)S(1)}, bf16[2,2,4096]{2,1,0:T(2,128)(2,1)}, u32[]{:S(2)}) copy-start(bf16[2,2,4096]{2,1,0:T(2,128)(2,1)} %param.14) | copy-start | bytes 98308
  2.6 19.1 %collective-permute-start = (bf16[2,8,32,256]{3,2,1,0:T(8,128)(2,1)}, bf16[2,8,32,256]{3,2,1,0:T(8,128)(2,1)S(1)}, u32[]{:S(2)}, u32[]{:S(2)}) collective-permute-start(bf16[2,8,32,256]{3,2,1,0:T(8,128)(2,1)} %pad_maximum_fusion.2), channel_id=1, source_target_pairs={{0,8},{8,0},{16,24},{24,16},{1,9},{9,1},{17,25},{25,17},{2,10},{10... | collective-permute-start | bytes 786440 | tf_op jit(solution)/shard_map/ppermute | solution.py:127
  3.1 0.7 %copy-start.12 = (s32[2]{0:T(128)S(1)}, s32[2]{0:T(128)}, u32[]{:S(2)}) copy-start(s32[2]{0:T(128)} %param.15) | copy-start | bytes 28
  3.8 0.6 %copy-start.3 = (bf16[2,2,4,8,128]{4,3,2,1,0:T(8,128)(2,1)}, bf16[2,2,4,8,128]{4,3,2,1,0:T(8,128)(2,1)S(1)}, u32[]{:S(2)}) copy-start(bf16[2,2,4,8,128]{4,3,2,1,0:T(8,128)(2,1)S(1)} %reshape.249) | copy-start | bytes 98308
  5.0 15.0 %all-to-all-start = ((bf16[8,80,128]{2,1,0:T(8,128)(2,1)}), bf16[8,80,128]{2,1,0:T(8,128)(2,1)}, u32[]{:S(2)}, u32[]{:S(2)}) async-start(bf16[8,80,128]{2,1,0:T(8,128)(2,1)} %broadcast_in_dim.141), calls=%async_computation | async-start | bytes 327680 | tf_op jit(solution)/shard_map/all_to_all | solution.py:105
  11.9 0.7 %copy-start.9 = (s32[2,32]{1,0:T(2,128)S(1)}, s32[2,32]{1,0:T(2,128)}, u32[]{:S(2)}) copy-start(s32[2,32]{1,0:T(2,128)} %param.20) | copy-start | bytes 772
  14.9 0.6 %copy-start.10 = (pred[4,4]{1,0:T(4,128)(4,1)S(1)}, pred[4,4]{1,0:T(4,128)(4,1)}, u32[]{:S(2)}) copy-start(pred[4,4]{1,0:T(4,128)(4,1)} %iota_compare_fusion.1) | copy-start | bytes 52
  17.8 0.6 %copy-start.5 = (f32[4,2,2,8,128]{4,3,2,0,1:T(8,128)}, f32[4,2,2,8,128]{4,3,2,0,1:T(8,128)S(1)}, u32[]{:S(2)}) copy-start(f32[4,2,2,8,128]{4,3,2,0,1:T(8,128)S(1)} %fusion.6) | copy-start | bytes 196612
  17.8 0.9 %copy-start.2 = (bf16[1,8,32,256]{3,2,1,0:T(8,128)(2,1)S(1)}, bf16[1,8,32,256]{3,2,1,0:T(8,128)(2,1)}, u32[]{:S(2)}) copy-start(bf16[1,8,32,256]{3,2,1,0:T(8,128)(2,1)} %get-tuple-element.59) | copy-start | bytes 393220
  18.4 1.3 %collective-permute-start.1 = (f32[2,2,2,8,130]{4,3,1,2,0:T(8,128)S(1)}, f32[2,2,2,8,130]{4,3,1,2,0:T(8,128)S(1)}, u32[]{:S(2)}, u32[]{:S(2)}) collective-permute-start(f32[2,2,2,8,130]{4,3,1,2,0:T(8,128)S(1)} %fusion.19), channel_id=1, source_target_pairs={{0,8},{8,0},{16,24},{24,16},{1,9},{9,1},{17,25},{25,17},{2,10},{10... | collective-permute-start | bytes 99848 | tf_op jit(solution)/shard_map/ppermute | solution.py:152
  25.5 0.8 %copy-start.6 = (f32[4,2,2,8,128]{4,3,2,0,1:T(8,128)S(1)}, f32[4,2,2,8,128]{4,3,2,0,1:T(8,128)}, u32[]{:S(2)}) copy-start(f32[4,2,2,8,128]{4,3,2,0,1:T(8,128)} %copy-done.5) | copy-start | bytes 196612
  27.8 5.9 %copy-start.4 = (bf16[2,2,4,8,128]{4,3,2,1,0:T(8,128)(2,1)S(1)}, bf16[2,2,4,8,128]{4,3,2,1,0:T(8,128)(2,1)}, u32[]{:S(2)}) copy-start(bf16[2,2,4,8,128]{4,3,2,1,0:T(8,128)(2,1)} %copy-done.3) | copy-start | bytes 98308
  27.8 5.9 %copy-start.11 = (bf16[2,2,512]{2,1,0:T(2,128)(2,1)S(1)}, bf16[2,2,512]{2,1,0:T(2,128)(2,1)}, u32[]{:S(2)}) copy-start(bf16[2,2,512]{2,1,0:T(2,128)(2,1)} %param.22) | copy-start | bytes 12292
  27.8 17.0 %all-to-all-start.1 = ((f32[32,1,2176]{2,1,0:T(1,128)}), f32[32,1,2176]{2,1,0:T(1,128)S(1)}, u32[]{:S(2)}, u32[]{:S(2)}) async-start(f32[32,1,2176]{2,1,0:T(1,128)} %reshape.309), calls=%async_computation.1 | async-start | bytes 557056 | tf_op jit(solution)/shard_map/all_to_all | solution.py:181
  34.4 0.7 %copy-start.8 = (bf16[2,2,512]{2,1,0:T(2,128)(2,1)S(1)}, bf16[2,2,512]{2,1,0:T(2,128)(2,1)}, u32[]{:S(2)}) copy-start(bf16[2,2,512]{2,1,0:T(2,128)(2,1)} %param.23) | copy-start | bytes 12292

commit v16 on v14

--- a/solution.py
+++ b/solution.py
@@ -165,8 +165,7 @@
     dests = ctx_count * row_count
 
     def by_dest(member, tail=()):
-        shaped = member.reshape((row_count, ctx_count, chunk) + tail)
-        return jnp.swapaxes(shaped, 0, 1).reshape((dests, chunk) + tail)
+        return member.reshape((dests, chunk) + tail)
 
     pt = jnp.concatenate([by_dest(peak_all), by_dest(total_all)], axis=-1)
     pt = jnp.pad(pt, ((0, 0), (0, pt_rows * LANES - 2 * chunk)))
@@ -175,7 +174,7 @@
     )
     incoming = lax.all_to_all(
         outgoing.reshape(dests, 1, (chunk + pt_rows) * LANES),
-        ("ctx", "row"),
+        ("row", "ctx"),
         split_axis=0,
         concat_axis=0,
         tiled=True,
@@ -185,8 +184,8 @@
     pairs = ctx_count // 2
 
     def by_half(member, tail=()):
-        shaped = member.reshape((pairs, 2, row_count, chunk) + tail)
-        return jnp.swapaxes(shaped, 0, 1).reshape((2, pairs * row_count, chunk) + tail)
+        shaped = member.reshape((row_count, pairs, 2, chunk) + tail)
+        return jnp.moveaxis(shaped, 2, 0).reshape((2, row_count * pairs, chunk) + tail)
 
     got_peak = by_half(got_pt[:, :chunk])
     got_total = by_half(got_pt[:, chunk : 2 * chunk])

time: 47.6 us -> 47.6 us (level)
  no operation moved by 1% of the time
where the time goes in v16:
time: 47.6 us; the launch traced here: 47.1 us
  waiting for transfers between devices  12.8 us (27%)
  local copies, waits for them, and re-layouts  11.6 us (24%)
  starting transfers between devices  11.4 us (24%)
  blocking collectives  5.18 us (11%)
  other arithmetic  3.31 us (7%)
  matrix products  2.56 us (5%)
    all_to_all x1, waiting for transfers between devices, per_device(): lax.all_to_all(outgoing.reshape(dests, 1, (chunk + pt_rows) * LANES), ('r...  9.51 us
    all_to_all x1, starting transfers between devices, per_device(): lax.all_to_all(fanned, 'row', split_axis=0, concat_axis=0, tiled=True)  6.9 us
    all_gather x1, blocking collectives, per_device(): whole = lax.all_gather(result, 'ctx', axis=0, tiled=False)  5.18 us
    all_to_all x1, starting transfers between devices, per_device(): lax.all_to_all(outgoing.reshape(dests, 1, (chunk + pt_rows) * LANES), ('r...  3.84 us
    unnamed x21, local copies, waits for them, and re-layouts  2.91 us
    all_to_all x1, waiting for transfers between devices, per_device(): lax.all_to_all(fanned, 'row', split_axis=0, concat_axis=0, tiled=True)  2.22 us
    gather x2, local copies, waits for them, and re-layouts, prefix_block(): row_kv = jnp.take(kv, every_prefix, axis=1)  1.3 us
    another operation x3, local copies, waits for them, and re-layouts, per_device(): jnp.stack([prefix_keys.reshape(prefix_count, span_len, KVH, HD), prefix_v...  1.23 us
  transfers between devices with their start and end apart: 4, of which 3 were waited for; matrix products, arithmetic and copies ran while one was open for 14% of the time, Pallas kernels for 0%

profile of v16, /device:TPU:0, one launch (start us, length us, event | category | flops | bytes accessed | tf_op | source)
XLA Modules:
  0.0 47.1 jit_solution(2411790009275315972)
XLA Ops:
  0.0 1.1 %stack_reshape.6 = bf16[1,8,32,4,128]{4,3,2,1,0:T(4,128)(2,1)S(1)} reshape(bf16[8,32,512]{2,1,0:T(8,128)(2,1)} %param.16) | data formatting | bytes 524288 | tf_op jit(solution)/shard_map/stack;reshape | solution.py:116
  1.2 0.9 %copy-done.3 = bf16[8,32,512]{2,1,0:T(8,128)(2,1)S(1)} copy-done((bf16[8,32,512]{2,1,0:T(8,128)(2,1)S(1)}, bf16[8,32,512]{2,1,0:T(8,128)(2,1)}, u32[]{:S(2)}) %copy-start.3) | copy-done | bytes 262168
  2.2 0.8 %constant_dynamic-slice_fusion.8 = (bf16[2,8,32,2,128]{4,2,3,1,0:T(8,128)(2,1)S(1)}, bf16[2,8,32,2,128]{4,2,3,1,0:T(8,128)(2,1)}) fusion(bf16[2,8,32,4,128]{4,2,3,1,0:T(8,128)(2,1)S(1)} %copy_dynamic-update-slice_fusion, s32[]{:T(128)S(6)} %select_n.76, s32[]{:T(128)S(6)} %select_n.77), kind=kLoop, calls=%fused_computation.83 | loop fusion | bytes 1048584 | tf_op jit(solution)/shard_map/dynamic_slice | solution.py:122
  3.0 0.5 collective-permute-start
  3.5 0.6 %copy-done.9 = s32[2]{0:T(128)S(1)} copy-done((s32[2]{0:T(128)S(1)}, s32[2]{0:T(128)}, u32[]{:S(2)}) %copy-start.9) | copy-done | bytes 32
  4.2 0.1 compare_select_fusion.2
  4.2 0.1 pad_maximum_fusion.1
  4.3 0.7 %broadcast_in_dim.141 = bf16[8,80,128]{2,1,0:T(8,128)(2,1)} broadcast(bf16[80,128]{1,0:T(8,128)(2,1)S(1)} %pad_maximum_fusion.1), dimensions={1,2} | broadcast | bytes 184320 | tf_op jit(solution)/shard_map/broadcast_in_dim | solution.py:104
  5.0 6.9 %all-to-all-start = ((bf16[8,80,128]{2,1,0:T(8,128)(2,1)}), bf16[8,80,128]{2,1,0:T(8,128)(2,1)S(1)}, u32[]{:S(2)}, u32[]{:S(2)}) async-start(bf16[8,80,128]{2,1,0:T(8,128)(2,1)} %broadcast_in_dim.141), calls=%async_computation | async-start | bytes 327680 | tf_op jit(solution)/shard_map/all_to_all | solution.py:105
  11.9 0.7 %copy-done.6 = s32[2,32]{1,0:T(2,128)S(1)} copy-done((s32[2,32]{1,0:T(2,128)S(1)}, s32[2,32]{1,0:T(2,128)}, u32[]{:S(2)}) %copy-start.6) | copy-done | bytes 280
  12.6 0.2 fusion.25
  12.8 0.2 compare_reduce_fusion
  13.0 0.1 add.105
  13.0 0.1 add.106
  13.1 0.1 and.29
  13.2 0.1 and.30
  13.3 0.1 add.108
  13.4 1.1 %reshape.234 = bf16[1024,4,128]{2,1,0:T(4,128)(2,1)} reshape(bf16[16,64,512]{2,1,0:T(8,128)(2,1)S(1)} %copy-done.1) | data formatting | bytes 2097152 | tf_op jit(solution)/shard_map/reshape | solution.py:70
  14.5 0.1 compare_and_fusion
  14.6 0.6 %select_reduce_fusion = (f32[2,2,4,8]{3,2,1,0:T(4,128)S(1)}, f32[2,2,4,8,1024]{4,3,2,1,0:T(8,128)S(1)}) fusion(pred[2,1024]{1,0:T(4,128)(4,1)S(1)} %compare_and_fusion, bf16[1024,512,1,1,1]{1,0,4,3,2:T(8,128)(2,1)S(1)} %bitcast.141, pred[4,4]{1,0:T(4,128)(4,1)S(1)} %iota_compare_fusion.1, bf16[2,2,4,8,128]{4,3,2,1,0:T(8,128)(2,1)S(1)} %reshape.230), kind=kOutput, calls=%fused_computation.23 | convolution fusion | flops 134676352 | bytes 1608208 | tf_op jit(solution)/shard_map/rskgw,tw->rskgt/dot_general | solution.py:78
  15.2 0.3 convert_reduce_fusion
  15.4 0.2 copy.169
  15.6 0.2 copy.168
  15.8 0.3 fusion.6
  16.1 0.1 fusion.17
  16.2 0.2 collective-permute-start.1
  16.4 1.1 %collective-permute-done.1 = f32[2,2,2,8,130]{4,3,1,2,0:T(8,128)S(1)} collective-permute-done((f32[2,2,2,8,130]{4,3,1,2,0:T(8,128)S(1)}, f32[2,2,2,8,130]{4,3,1,2,0:T(8,128)S(1)}, u32[]{:S(2)}, u32[]{:S(2)}) %collective-permute-start.1) | collective-permute-done | bytes 33312 | tf_op jit(solution)/shard_map/ppermute | solution.py:147
  17.4 0.1 fusion.39
  17.5 0.1 copy.203
  17.6 0.1 copy.205
  17.8 2.2 %all-to-all-done = bf16[8,80,128]{2,1,0:T(8,128)(2,1)S(1)} async-done(((bf16[8,80,128]{2,1,0:T(8,128)(2,1)}), bf16[8,80,128]{2,1,0:T(8,128)(2,1)S(1)}, u32[]{:S(2)}, u32[]{:S(2)}) %all-to-all-start) | async-done | bytes 163872 | tf_op jit(solution)/shard_map/all_to_all | solution.py:105
  20.0 0.2 convert_reduce_fusion.4
  20.2 0.1 reshape.255
  20.3 0.6 %gather_fusion = bf16[16,2,32,2,128]{4,2,3,1,0:T(8,128)(2,1)S(1)} fusion(bf16[2,8,32,2,128]{4,2,3,1,0:T(8,128)(2,1)S(1)} %get-tuple-element.35, s32[1024]{0:T(1024)S(1)} %pad_clamp_fusion), kind=kCustom, calls=%fused_computation.clone | custom fusion | bytes 1048640 | tf_op jit(solution)/shard_map/jit(_take)/gather | solution.py:128
  21.0 0.6 %gather_fusion.1 = bf16[16,2,32,2,128]{4,2,3,1,0:T(8,128)(2,1)S(1)} fusion(bf16[2,8,32,2,128]{4,2,3,1,0:T(8,128)(2,1)S(1)} %collective-permute-done, s32[1024]{0:T(1024)S(1)} %pad_clamp_fusion), kind=kCustom, calls=%fused_computation.1.clone | custom fusion | bytes 1048640 | tf_op jit(solution)/shard_map/jit(_take)/gather | solution.py:128
  21.6 0.2 fusion.9
  21.8 0.4 fusion.42
  22.2 0.4 fusion.41
  22.5 0.5 convert_reduce_fusion.1
  23.1 0.3 fusion.2
  23.3 0.3 fusion.1
  23.6 0.1 fusion.23
  23.8 0.1 reshape.236
  23.9 0.1 reshape.237
  24.0 0.1 select_maximum_fusion
  24.1 1.0 %reshape.287 = f32[32,1,2176]{2,1,0:T(1,128)} reshape(f32[32,17,128]{2,1,0:T(8,128)S(1)} %pad_maximum_fusion) | data formatting | bytes 557056 | tf_op jit(solution)/shard_map/reshape | solution.py:176
  25.1 3.8 %all-to-all-start.1 = ((f32[32,1,2176]{2,1,0:T(1,128)}), f32[32,1,2176]{2,1,0:T(1,128)S(1)}, u32[]{:S(2)}, u32[]{:S(2)}) async-start(f32[32,1,2176]{2,1,0:T(1,128)} %reshape.287), calls=%async_computation.1 | async-start | bytes 557056 | tf_op jit(solution)/shard_map/all_to_all | solution.py:175
  29.0 0.3 select_reduce_fusion.1
  29.3 0.1 reshape.244
  29.3 0.1 reshape.245
  29.4 0.1 convert_reduce_fusion.3
  29.5 0.1 reshape.251
  29.6 0.1 reshape.252
  29.7 0.6 %copy-done.5 = bf16[2,2,512]{2,1,0:T(2,128)(2,1)S(1)} copy-done((bf16[2,2,512]{2,1,0:T(2,128)(2,1)S(1)}, bf16[2,2,512]{2,1,0:T(2,128)(2,1)}, u32[]{:S(2)}) %copy-start.5) | copy-done | bytes 4120
  30.3 0.2 convolution_bitcast_fusion.2
  30.5 9.5 %all-to-all-done.1 = f32[32,1,2176]{2,1,0:T(1,128)S(1)} async-done(((f32[32,1,2176]{2,1,0:T(1,128)}), f32[32,1,2176]{2,1,0:T(1,128)S(1)}, u32[]{:S(2)}, u32[]{:S(2)}) %all-to-all-start.1) | async-done | bytes 278560 | tf_op jit(solution)/shard_map/all_to_all | solution.py:175
  40.0 0.7 %reduce.6 = f32[32,2176]{1,0:T(8,128)S(1)} reduce(f32[32,1,2176]{2,1,0:T(1,128)S(1)} %all-to-all-done.1, f32[]{:T(128)} %constant.98), dimensions={1}, to_apply=%all_to_all.7.reduce_sub_computation | reduce | bytes 557060 | tf_op jit(solution)/shard_map/all_to_all | solution.py:175
  40.8 0.1 fusion.40
  40.9 0.1 fusion.36
  41.0 0.1 fusion.35
  41.1 0.1 multiply_reduce_fusion
  41.2 0.1 divide_convert_fusion
  41.3 5.2 %all-gather = bf16[8,16,128]{2,1,0:T(8,128)(2,1)S(1)} all-gather(bf16[2,16,128]{2,1,0:T(8,128)(2,1)S(1)} %divide_convert_fusion), channel_id=2, replica_groups=mesh['ctx'=4,'row'=8] {'ctx'}, dimensions={0}, use_global_device_ids=true | all-gather | bytes 40960 | tf_op jit(solution)/shard_map/all_gather | solution.py:209
  46.5 0.6 %reshape.254 = bf16[2,2,4096]{2,1,0:T(2,128)(2,1)} reshape(bf16[2,2,2,16,128]{4,3,2,1,0:T(8,128)(2,1)S(1)} %bitcast.152) | data formatting | bytes 65536 | tf_op jit(solution)/shard_map/reshape | solution.py:212
  (50 shorter events, 0.7 us)
Async XLA Ops:
  0.0 14.6 %copy-start = (bf16[16,64,512]{2,1,0:T(8,128)(2,1)S(1)}, bf16[16,64,512]{2,1,0:T(8,128)(2,1)}, u32[]{:S(2)}) copy-start(bf16[16,64,512]{2,1,0:T(8,128)(2,1)} %param.18) | copy-start | bytes 3145732
  1.1 1.0 %copy-start.3 = (bf16[8,32,512]{2,1,0:T(8,128)(2,1)S(1)}, bf16[8,32,512]{2,1,0:T(8,128)(2,1)}, u32[]{:S(2)}) copy-start(bf16[8,32,512]{2,1,0:T(8,128)(2,1)} %param.17) | copy-start | bytes 786436
  2.1 11.2 %copy-start.1 = (bf16[16,64,512]{2,1,0:T(8,128)(2,1)S(1)}, bf16[16,64,512]{2,1,0:T(8,128)(2,1)}, u32[]{:S(2)}) copy-start(bf16[16,64,512]{2,1,0:T(8,128)(2,1)} %param.19) | copy-start | bytes 3145732
  2.2 1.2 %copy-start.4 = (bf16[2,2,4096]{2,1,0:T(2,128)(2,1)S(1)}, bf16[2,2,4096]{2,1,0:T(2,128)(2,1)}, u32[]{:S(2)}) copy-start(bf16[2,2,4096]{2,1,0:T(2,128)(2,1)} %param.14) | copy-start | bytes 98308
  3.0 18.0 %collective-permute-start = (bf16[2,8,32,2,128]{4,2,3,1,0:T(8,128)(2,1)}, bf16[2,8,32,2,128]{4,2,3,1,0:T(8,128)(2,1)S(1)}, u32[]{:S(2)}, u32[]{:S(2)}) collective-permute-start(bf16[2,8,32,2,128]{4,2,3,1,0:T(8,128)(2,1)} %get-tuple-element.36), channel_id=1, source_target_pairs={{0,8},{8,0},{16,24},{24,16},{1,9},{9,1},{17,25},{25,17},{2,10},{10... | collective-permute-start | bytes 786440 | tf_op jit(solution)/shard_map/ppermute | solution.py:124
  3.5 0.7 %copy-start.9 = (s32[2]{0:T(128)S(1)}, s32[2]{0:T(128)}, u32[]{:S(2)}) copy-start(s32[2]{0:T(128)} %param.15) | copy-start | bytes 28
  5.0 15.0 %all-to-all-start = ((bf16[8,80,128]{2,1,0:T(8,128)(2,1)}), bf16[8,80,128]{2,1,0:T(8,128)(2,1)S(1)}, u32[]{:S(2)}, u32[]{:S(2)}) async-start(bf16[8,80,128]{2,1,0:T(8,128)(2,1)} %broadcast_in_dim.141), calls=%async_computation | async-start | bytes 327680 | tf_op jit(solution)/shard_map/all_to_all | solution.py:105
  11.9 0.7 %copy-start.6 = (s32[2,32]{1,0:T(2,128)S(1)}, s32[2,32]{1,0:T(2,128)}, u32[]{:S(2)}) copy-start(s32[2,32]{1,0:T(2,128)} %param.20) | copy-start | bytes 772
  13.4 1.1 %copy-start.7 = (s32[2]{0:T(128)S(1)}, s32[2]{0:T(128)}, u32[]{:S(2)}) copy-start(s32[2]{0:T(128)} %param.21) | copy-start | bytes 28
  14.6 1.2 %copy-start.2 = (bf16[1024,4,128]{2,1,0:T(4,128)(2,1)S(1)}, bf16[1024,4,128]{2,1,0:T(4,128)(2,1)}, u32[]{:S(2)}) copy-start(bf16[1024,4,128]{2,1,0:T(4,128)(2,1)} %reshape.234) | copy-start | bytes 3145732
  16.2 1.3 %collective-permute-start.1 = (f32[2,2,2,8,130]{4,3,1,2,0:T(8,128)S(1)}, f32[2,2,2,8,130]{4,3,1,2,0:T(8,128)S(1)}, u32[]{:S(2)}, u32[]{:S(2)}) collective-permute-start(f32[2,2,2,8,130]{4,3,1,2,0:T(8,128)S(1)} %fusion.17), channel_id=1, source_target_pairs={{0,8},{8,0},{16,24},{24,16},{1,9},{9,1},{17,25},{25,17},{2,10},{10... | collective-permute-start | bytes 99848 | tf_op jit(solution)/shard_map/ppermute | solution.py:147
  25.1 3.9 %copy-start.8 = (bf16[2,2,512]{2,1,0:T(2,128)(2,1)S(1)}, bf16[2,2,512]{2,1,0:T(2,128)(2,1)}, u32[]{:S(2)}) copy-start(bf16[2,2,512]{2,1,0:T(2,128)(2,1)} %param.22) | copy-start | bytes 12292
  25.1 14.9 %all-to-all-start.1 = ((f32[32,1,2176]{2,1,0:T(1,128)}), f32[32,1,2176]{2,1,0:T(1,128)S(1)}, u32[]{:S(2)}, u32[]{:S(2)}) async-start(f32[32,1,2176]{2,1,0:T(1,128)} %reshape.287), calls=%async_computation.1 | async-start | bytes 557056 | tf_op jit(solution)/shard_map/all_to_all | solution.py:175
  29.6 0.7 %copy-start.5 = (bf16[2,2,512]{2,1,0:T(2,128)(2,1)S(1)}, bf16[2,2,512]{2,1,0:T(2,128)(2,1)}, u32[]{:S(2)}) copy-start(bf16[2,2,512]{2,1,0:T(2,128)(2,1)} %param.23) | copy-start | bytes 12292

commit v17 on v16

--- a/solution.py
+++ b/solution.py
@@ -111,6 +111,9 @@
     every_prefix = every_prefix.astype(jnp.int32)
 
     swap = [(c, c ^ 1) for c in range(ctx_count)]
+    prefix_keys, prefix_values, _ = lax.optimization_barrier(
+        (prefix_keys, prefix_values, suffix_stats[0])
+    )
     span_len = prefix_keys.shape[1]
     prefix_count = prefix_keys.shape[0]
     kv_both = jnp.stack(

time: 47.6 us -> 55 us (1.16)
  local copies, waits for them, and re-layouts: 11.6 us -> 15.5 us
  starting transfers between devices: 11.4 us -> 14.7 us
  waiting for transfers between devices: 12.8 us -> 10.2 us
  other arithmetic: 3.31 us -> 4.81 us
  matrix products: 2.56 us -> 3.5 us
    all_to_all x1, starting transfers between devices: 3.84 us -> 6.96 us  [per_device(): lax.all_to_all(outgoing.reshape(dests, 1, (chunk + pt_rows) * LANES), ('r...]
    unnamed x21 -> x31, local copies, waits for them, and re-layouts: 2.91 us -> 5.25 us
    all_to_all x1, waiting for transfers between devices: 2.22 us -> 0.01 us  [per_device(): lax.all_to_all(fanned, 'row', split_axis=0, concat_axis=0, tiled=True)]
    another operation x3, local copies, waits for them, and re-layouts: 1.23 us -> 0.2 us  [per_device(): jnp.stack([prefix_keys.reshape(prefix_count, span_len, KVH, HD), prefix_v...]
    gather x2, local copies, waits for them, and re-layouts: 1.3 us -> 2.25 us  [prefix_block(): row_kv = jnp.take(kv, every_prefix, axis=1)]
    dot_general x4, matrix products: 1 us -> 1.94 us  [block_stats(): jnp.einsum(einsum_form, weights, values, preferred_element_type=jnp.float32)]
    slice x1, local copies, waits for them, and re-layouts: 0.01 us -> 0.92 us  [per_device(): gathered[:, :query_rows, :]]
    reshape x1, local copies, waits for them, and re-layouts: 1.12 us -> 0.27 us  [per_device(): flat_values = pool_values.reshape(slot_count * page_len, KVH, HD)]
  transfers between devices with their start and end apart: 4 -> 4, of which waited for: 3 -> 2; matrix products, arithmetic and copies ran while one was open for 14% -> 16% of each run, Pallas kernels for 0% -> 0%
where the time goes in v17:
time: 55 us; the launch traced here: 54.3 us
  local copies, waits for them, and re-layouts  15.5 us (28%)
  starting transfers between devices  14.7 us (27%)
  waiting for transfers between devices  10.2 us (19%)
  blocking collectives  5.19 us (9%)
  other arithmetic  4.81 us (9%)
  matrix products  3.5 us (6%)
    all_to_all x1, waiting for transfers between devices, per_device(): lax.all_to_all(outgoing.reshape(dests, 1, (chunk + pt_rows) * LANES), ('r...  9.5 us
    all_to_all x1, starting transfers between devices, per_device(): lax.all_to_all(fanned, 'row', split_axis=0, concat_axis=0, tiled=True)  7.25 us
    all_to_all x1, starting transfers between devices, per_device(): lax.all_to_all(outgoing.reshape(dests, 1, (chunk + pt_rows) * LANES), ('r...  6.96 us
    unnamed x31, local copies, waits for them, and re-layouts  5.25 us
    all_gather x1, blocking collectives, per_device(): whole = lax.all_gather(result, 'ctx', axis=0, tiled=False)  5.19 us
    gather x2, local copies, waits for them, and re-layouts, prefix_block(): row_kv = jnp.take(kv, every_prefix, axis=1)  2.25 us
    dot_general x4, matrix products, block_stats(): jnp.einsum(einsum_form, weights, values, preferred_element_type=jnp.float32)  1.94 us
    reduce_sum x4, other arithmetic, block_stats(): block_total = jnp.sum(weights.astype(jnp.float32), axis=-1)  1.59 us
  transfers between devices with their start and end apart: 4, of which 2 were waited for; matrix products, arithmetic and copies ran while one was open for 16% of the time, Pallas kernels for 0%

profile of v17, /device:TPU:0, one launch (start us, length us, event | category | flops | bytes accessed | tf_op | source)
XLA Modules:
  0.0 54.3 jit_solution(4054280051965836877)
XLA Ops:
  0.0 0.8 %copy-done.13 = s32[2]{0:T(128)S(1)} copy-done((s32[2]{0:T(128)S(1)}, s32[2]{0:T(128)}, u32[]{:S(2)}) %copy-start.13) | copy-done | bytes 32
  1.0 0.7 %broadcast_in_dim.151 = bf16[8,80,128]{2,1,0:T(8,128)(2,1)} broadcast(bf16[80,128]{1,0:T(8,128)(2,1)S(1)} %pad_maximum_fusion.1), dimensions={1,2} | broadcast | bytes 184320 | tf_op jit(solution)/shard_map/broadcast_in_dim | solution.py:104
  1.7 7.3 %all-to-all-start = ((bf16[8,80,128]{2,1,0:T(8,128)(2,1)}), bf16[8,80,128]{2,1,0:T(8,128)(2,1)}, u32[]{:S(2)}, u32[]{:S(2)}) async-start(bf16[8,80,128]{2,1,0:T(8,128)(2,1)} %broadcast_in_dim.151), calls=%async_computation | async-start | bytes 327680 | tf_op jit(solution)/shard_map/all_to_all | solution.py:105
  9.0 0.7 %copy-done.10 = s32[2,32]{1,0:T(2,128)S(1)} copy-done((s32[2,32]{1,0:T(2,128)S(1)}, s32[2,32]{1,0:T(2,128)}, u32[]{:S(2)}) %copy-start.10) | copy-done | bytes 280
  9.6 0.2 compare_reduce_fusion
  9.8 0.2 fusion.25
  10.1 0.1 and.29
  10.4 0.6 %copy-done.11 = s32[2]{0:T(128)S(1)} copy-done((s32[2]{0:T(128)S(1)}, s32[2]{0:T(128)}, u32[]{:S(2)}) %copy-start.11) | copy-done | bytes 32
  11.1 0.6 %select_reduce_fusion = (f32[2,2,4,8]{3,2,1,0:T(4,128)S(1)}, f32[2,2,4,8,1024]{4,3,2,1,0:T(8,128)S(1)}) fusion(pred[2,1024]{1,0:T(4,128)(4,1)S(1)} %compare_and_fusion, bf16[1024,512,1,1,1]{1,0,4,3,2:T(8,128)(2,1)S(1)} %bitcast.117, pred[4,4]{1,0:T(4,128)(4,1)S(1)} %iota_compare_fusion.1, bf16[2,2,4,8,128]{4,3,2,1,0:T(8,128)(2,1)S(1)} %broadcast_in_dim.147), kind=kOutput, calls=%fused_computation.23 | convolution fusion | flops 134676352 | bytes 1608208 | tf_op jit(solution)/shard_map/rskgw,tw->rskgt/dot_general | solution.py:78
  11.7 0.4 copy-done.2
  12.2 0.9 %copy-done.3 = bf16[8,32,512]{2,1,0:T(8,128)(2,1)S(1)} copy-done((bf16[8,32,512]{2,1,0:T(8,128)(2,1)S(1)}, bf16[8,32,512]{2,1,0:T(8,128)(2,1)}, u32[]{:S(2)}) %copy-start.3) | copy-done | bytes 262168
  13.2 0.7 %constant_dynamic-slice_fusion.6 = (bf16[2,8,32,2,128]{4,2,3,1,0:T(8,128)(2,1)S(1)}, bf16[2,8,32,2,128]{4,2,3,1,0:T(8,128)(2,1)}) fusion(bf16[2,8,32,4,128]{4,2,3,1,0:T(8,128)(2,1)S(1)} %copy_dynamic-update-slice_fusion, s32[]{:T(128)S(6)} %select_n.80, s32[]{:T(128)S(6)} %select_n.81), kind=kLoop, calls=%fused_computation.88 | loop fusion | bytes 1048584 | tf_op jit(solution)/shard_map/dynamic_slice | solution.py:125
  14.0 0.9 %convert_reduce_fusion = (f32[2,2,4,8]{3,2,1,0:T(4,128)S(1)}, bf16[2,2,4,8,1024]{4,3,2,1,0:T(8,128)(2,1)}) fusion(f32[2,2,4,8,1024]{4,3,2,1,0:T(8,128)S(1)} %get-tuple-element.49, f32[2,2,4,8]{3,2,1,0:T(4,128)S(1)} %get-tuple-element.48, pred[2,1024]{1,0:T(4,128)(4,1)S(1)} %compare_and_fusion), kind=kLoop, calls=%fused_computation.21 | loop fusion | flops 655232 | bytes 789504 | tf_op jit(solution)/shard_map/reduce_sum | solution.py:22
  14.8 0.2 copy.216
  15.0 0.2 copy.217
  15.2 0.3 reshape.231
  15.4 1.2 %fusion.6 = f32[4,2,2,8,128]{4,3,2,0,1:T(8,128)S(1)} fusion(bf16[1024,4,128,1,1]{2,1,0,4,3:T(4,128)(2,1)S(1)} %bitcast.120, bf16[2,2,4,8,1024]{4,3,2,1,0:T(8,128)(2,1)} %get-tuple-element.35), kind=kOutput, calls=%fused_computation.15 | convolution fusion | flops 33554432 | bytes 1376256 | tf_op jit(solution)/shard_map/rskgt,tkd->rskgd/dot_general | solution.py:23
  16.8 0.5 copy-done.6
  17.3 0.5 collective-permute-start.1
  17.8 0.1 copy.258
  17.9 0.1 copy.257
  18.0 0.7 %collective-permute-done.1 = f32[2,2,2,8,130]{4,3,1,2,0:T(8,128)S(1)} collective-permute-done((f32[2,2,2,8,130]{4,3,1,2,0:T(8,128)S(1)}, f32[2,2,2,8,130]{4,3,1,2,0:T(8,128)S(1)}, u32[]{:S(2)}, u32[]{:S(2)}) %collective-permute-start.1) | collective-permute-done | bytes 33312 | tf_op jit(solution)/shard_map/ppermute | solution.py:150
  18.8 0.1 copy.218
  18.9 0.1 copy.231
  19.0 0.1 copy.232
  19.1 0.1 copy.219
  19.2 0.9 %convert_reduce_fusion.4 = s32[8,2]{1,0:T(8,128)S(1)} fusion(bf16[8,80,128]{2,1,0:T(8,128)(2,1)} %all-to-all-done), kind=kLoop, calls=%fused_computation.78 | loop fusion | flops 16 | bytes 96 | tf_op jit(solution)/shard_map/convert_element_type | solution.py:111
  20.3 0.6 %gather_fusion = bf16[16,2,32,2,128]{4,2,3,1,0:T(8,128)(2,1)S(1)} fusion(bf16[2,8,32,2,128]{4,2,3,1,0:T(8,128)(2,1)S(1)} %get-tuple-element.40, s32[1024]{0:T(1024)S(1)} %pad_clamp_fusion), kind=kCustom, calls=%fused_computation.clone | custom fusion | bytes 1048640 | tf_op jit(solution)/shard_map/jit(_take)/gather | solution.py:131
  21.0 1.6 %gather_fusion.1 = bf16[16,2,32,2,128]{4,2,3,1,0:T(8,128)(2,1)S(1)} fusion(bf16[2,8,32,2,128]{4,2,3,1,0:T(8,128)(2,1)} %collective-permute-done, s32[1024]{0:T(1024)S(1)} %pad_clamp_fusion), kind=kCustom, calls=%fused_computation.1.clone | custom fusion | bytes 1048640 | tf_op jit(solution)/shard_map/jit(_take)/gather | solution.py:131
  22.6 0.2 fusion.9
  22.7 0.9 %slice.74 = bf16[8,64,128]{2,1,0:T(8,128)(2,1)S(1)} slice(bf16[8,80,128]{2,1,0:T(8,128)(2,1)} %all-to-all-done), slice={[0:8], [0:64], [0:128]} | slice | bytes 262144 | tf_op jit(solution)/shard_map/slice | solution.py:107
  23.7 0.4 fusion.35
  24.1 0.3 convert_reduce_fusion.2
  24.5 0.4 fusion.34
  24.9 0.3 convert_reduce_fusion.1
  25.3 0.1 copy.209
  25.4 0.3 fusion.2
  25.7 0.1 copy.211
  25.8 0.1 multiply_add_fusion
  25.9 0.2 dynamic_update_slice.10
  26.1 0.2 dynamic_update_slice.11
  26.3 0.1 copy.220
  26.4 0.1 copy.222
  26.5 0.1 copy.225
  26.6 0.1 copy.221
  26.7 0.3 fusion.1
  27.0 0.6 %copy-done.7 = f32[4,2,2,8,128]{4,3,2,0,1:T(8,128)S(1)} copy-done((f32[4,2,2,8,128]{4,3,2,0,1:T(8,128)S(1)}, f32[4,2,2,8,128]{4,3,2,0,1:T(8,128)}, u32[]{:S(2)}) %copy-start.7) | copy-done | bytes 65560
  27.6 0.1 fusion.23
  27.7 0.1 copy.233
  27.8 0.1 reshape.234
  27.9 0.1 copy.227
  28.0 0.1 reshape.233
  28.2 1.0 %reshape.284 = f32[32,1,2176]{2,1,0:T(1,128)} reshape(f32[32,17,128]{2,1,0:T(8,128)S(1)} %pad_maximum_fusion) | data formatting | bytes 557056 | tf_op jit(solution)/shard_map/reshape | solution.py:179
  29.2 7.0 %all-to-all-start.1 = ((f32[32,1,2176]{2,1,0:T(1,128)}), f32[32,1,2176]{2,1,0:T(1,128)S(1)}, u32[]{:S(2)}, u32[]{:S(2)}) async-start(f32[32,1,2176]{2,1,0:T(1,128)} %reshape.284), calls=%async_computation.1 | async-start | bytes 557056 | tf_op jit(solution)/shard_map/all_to_all | solution.py:178
  36.2 0.3 select_reduce_fusion.1
  36.6 0.1 reshape.242
  36.6 0.1 convert_reduce_fusion.3
  36.9 0.6 %copy-done.9 = bf16[2,2,512]{2,1,0:T(2,128)(2,1)S(1)} copy-done((bf16[2,2,512]{2,1,0:T(2,128)(2,1)S(1)}, bf16[2,2,512]{2,1,0:T(2,128)(2,1)}, u32[]{:S(2)}) %copy-start.9) | copy-done | bytes 4120
  37.5 0.2 convolution_bitcast_fusion.2
  37.8 9.5 %all-to-all-done.1 = f32[32,1,2176]{2,1,0:T(1,128)S(1)} async-done(((f32[32,1,2176]{2,1,0:T(1,128)}), f32[32,1,2176]{2,1,0:T(1,128)S(1)}, u32[]{:S(2)}, u32[]{:S(2)}) %all-to-all-start.1) | async-done | bytes 278560 | tf_op jit(solution)/shard_map/all_to_all | solution.py:178
  47.2 0.7 %reduce.6 = f32[32,2176]{1,0:T(8,128)S(1)} reduce(f32[32,1,2176]{2,1,0:T(1,128)S(1)} %all-to-all-done.1, f32[]{:T(128)} %constant.98), dimensions={1}, to_apply=%all_to_all.7.reduce_sub_computation | reduce | bytes 557060 | tf_op jit(solution)/shard_map/all_to_all | solution.py:178
  48.2 0.1 multiply_reduce_fusion
  48.5 5.2 %all-gather = bf16[8,16,128]{2,1,0:T(8,128)(2,1)S(1)} all-gather(bf16[2,16,128]{2,1,0:T(8,128)(2,1)S(1)} %divide_convert_fusion), channel_id=2, replica_groups=mesh['ctx'=4,'row'=8] {'ctx'}, dimensions={0}, use_global_device_ids=true | all-gather | bytes 40960 | tf_op jit(solution)/shard_map/all_gather | solution.py:212
  53.7 0.6 %reshape.251 = bf16[2,2,4096]{2,1,0:T(2,128)(2,1)} reshape(bf16[2,2,2,16,128]{4,3,2,1,0:T(8,128)(2,1)S(1)} %bitcast.128) | data formatting | bytes 65536 | tf_op jit(solution)/shard_map/reshape | solution.py:215
  (75 shorter events, 2.4 us)
Async XLA Ops:
  0.0 11.1 %copy-start = (bf16[16,64,512]{2,1,0:T(8,128)(2,1)S(1)}, bf16[16,64,512]{2,1,0:T(8,128)(2,1)}, u32[]{:S(2)}) copy-start(bf16[16,64,512]{2,1,0:T(8,128)(2,1)} %param.18) | copy-start | bytes 3145732
  0.0 0.9 %copy-start.8 = (bf16[2,2,4096]{2,1,0:T(2,128)(2,1)S(1)}, bf16[2,2,4096]{2,1,0:T(2,128)(2,1)}, u32[]{:S(2)}) copy-start(bf16[2,2,4096]{2,1,0:T(2,128)(2,1)} %param.14) | copy-start | bytes 98308
  0.0 0.8 %copy-start.13 = (s32[2]{0:T(128)S(1)}, s32[2]{0:T(128)}, u32[]{:S(2)}) copy-start(s32[2]{0:T(128)} %param.15) | copy-start | bytes 28
  0.9 10.2 %copy-start.4 = (bf16[2,2,4,8,128]{4,3,2,1,0:T(8,128)(2,1)}, bf16[2,2,4,8,128]{4,3,2,1,0:T(8,128)(2,1)S(1)}, u32[]{:S(2)}) copy-start(bf16[2,2,4,8,128]{4,3,2,1,0:T(8,128)(2,1)S(1)} %broadcast_in_dim.147) | copy-start | bytes 98308
  1.7 17.5 %all-to-all-start = ((bf16[8,80,128]{2,1,0:T(8,128)(2,1)}), bf16[8,80,128]{2,1,0:T(8,128)(2,1)}, u32[]{:S(2)}, u32[]{:S(2)}) async-start(bf16[8,80,128]{2,1,0:T(8,128)(2,1)} %broadcast_in_dim.151), calls=%async_computation | async-start | bytes 327680 | tf_op jit(solution)/shard_map/all_to_all | solution.py:105
  9.0 0.7 %copy-start.10 = (s32[2,32]{1,0:T(2,128)S(1)}, s32[2,32]{1,0:T(2,128)}, u32[]{:S(2)}) copy-start(s32[2,32]{1,0:T(2,128)} %param.20) | copy-start | bytes 772
  10.3 0.7 %copy-start.11 = (s32[2]{0:T(128)S(1)}, s32[2]{0:T(128)}, u32[]{:S(2)}) copy-start(s32[2]{0:T(128)} %param.21) | copy-start | bytes 28
  11.1 1.0 %copy-start.2 = (bf16[8,32,512]{2,1,0:T(8,128)(2,1)S(1)}, bf16[8,32,512]{2,1,0:T(8,128)(2,1)}, u32[]{:S(2)}) copy-start(bf16[8,32,512]{2,1,0:T(8,128)(2,1)} %param.16) | copy-start | bytes 786436
  12.1 1.0 %copy-start.3 = (bf16[8,32,512]{2,1,0:T(8,128)(2,1)S(1)}, bf16[8,32,512]{2,1,0:T(8,128)(2,1)}, u32[]{:S(2)}) copy-start(bf16[8,32,512]{2,1,0:T(8,128)(2,1)} %param.17) | copy-start | bytes 786436
  13.2 2.0 %copy-start.1 = (bf16[16,64,512]{2,1,0:T(8,128)(2,1)S(1)}, bf16[16,64,512]{2,1,0:T(8,128)(2,1)}, u32[]{:S(2)}) copy-start(bf16[16,64,512]{2,1,0:T(8,128)(2,1)} %param.19) | copy-start | bytes 3145732
  14.0 7.0 %collective-permute-start = (bf16[2,8,32,2,128]{4,2,3,1,0:T(8,128)(2,1)}, bf16[2,8,32,2,128]{4,2,3,1,0:T(8,128)(2,1)}, u32[]{:S(2)}, u32[]{:S(2)}) collective-permute-start(bf16[2,8,32,2,128]{4,2,3,1,0:T(8,128)(2,1)} %get-tuple-element.41), channel_id=1, source_target_pairs={{0,8},{8,0},{16,24},{24,16},{1,9},{9,1},{17,25},{25,17},{2,10},{10... | collective-permute-start | bytes 786440 | tf_op jit(solution)/shard_map/ppermute | solution.py:127
  16.7 0.6 %copy-start.6 = (f32[4,2,2,8,128]{4,3,2,0,1:T(8,128)}, f32[4,2,2,8,128]{4,3,2,0,1:T(8,128)S(1)}, u32[]{:S(2)}) copy-start(f32[4,2,2,8,128]{4,3,2,0,1:T(8,128)S(1)} %fusion.6) | copy-start | bytes 196612
  17.3 1.4 %collective-permute-start.1 = (f32[2,2,2,8,130]{4,3,1,2,0:T(8,128)S(1)}, f32[2,2,2,8,130]{4,3,1,2,0:T(8,128)S(1)}, u32[]{:S(2)}, u32[]{:S(2)}) collective-permute-start(f32[2,2,2,8,130]{4,3,1,2,0:T(8,128)S(1)} %fusion.17), channel_id=1, source_target_pairs={{0,8},{8,0},{16,24},{24,16},{1,9},{9,1},{17,25},{25,17},{2,10},{10... | collective-permute-start | bytes 99848 | tf_op jit(solution)/shard_map/ppermute | solution.py:150
  26.7 0.8 %copy-start.7 = (f32[4,2,2,8,128]{4,3,2,0,1:T(8,128)S(1)}, f32[4,2,2,8,128]{4,3,2,0,1:T(8,128)}, u32[]{:S(2)}) copy-start(f32[4,2,2,8,128]{4,3,2,0,1:T(8,128)} %copy-done.6) | copy-start | bytes 196612
  29.2 7.0 %copy-start.5 = (bf16[2,2,4,8,128]{4,3,2,1,0:T(8,128)(2,1)S(1)}, bf16[2,2,4,8,128]{4,3,2,1,0:T(8,128)(2,1)}, u32[]{:S(2)}) copy-start(bf16[2,2,4,8,128]{4,3,2,1,0:T(8,128)(2,1)} %copy-done.4) | copy-start | bytes 98308
  29.2 7.0 %copy-start.12 = (bf16[2,2,512]{2,1,0:T(2,128)(2,1)S(1)}, bf16[2,2,512]{2,1,0:T(2,128)(2,1)}, u32[]{:S(2)}) copy-start(bf16[2,2,512]{2,1,0:T(2,128)(2,1)} %param.22) | copy-start | bytes 12292
  29.2 18.1 %all-to-all-start.1 = ((f32[32,1,2176]{2,1,0:T(1,128)}), f32[32,1,2176]{2,1,0:T(1,128)S(1)}, u32[]{:S(2)}, u32[]{:S(2)}) async-start(f32[32,1,2176]{2,1,0:T(1,128)} %reshape.284), calls=%async_computation.1 | async-start | bytes 557056 | tf_op jit(solution)/shard_map/all_to_all | solution.py:178
  36.8 0.7 %copy-start.9 = (bf16[2,2,512]{2,1,0:T(2,128)(2,1)S(1)}, bf16[2,2,512]{2,1,0:T(2,128)(2,1)}, u32[]{:S(2)}) copy-start(bf16[2,2,512]{2,1,0:T(2,128)(2,1)} %param.23) | copy-start | bytes 12292

commit v18 on v16

--- a/solution.py
+++ b/solution.py
@@ -149,15 +149,19 @@
     suffix_kept = tuple(head_half(member, core_bit) for member in suffix_stats)
     suffix_half = combine_pair(suffix_kept, suffix_partner)
 
-    row_start = row_index * rows_dev
-    own_prefix = tuple(
-        lax.dynamic_slice_in_dim(member, row_start, rows_dev, 0) for member in prefix_stats
-    )
-    own_merged = combine_pair(own_prefix, suffix_half)
-    peak_all, total_all, sum_all = tuple(
-        lax.dynamic_update_slice_in_dim(whole_arr, piece_arr, row_start, 0)
-        for whole_arr, piece_arr in zip(prefix_stats, own_merged)
-    )
+    own_row = (jnp.arange(total_rows, dtype=jnp.int32) // rows_dev) == row_index
+
+    def over_rows(member, empty):
+        tiled = jnp.tile(member, (row_count,) + (1,) * (member.ndim - 1))
+        mask = own_row.reshape((total_rows,) + (1,) * (member.ndim - 1))
+        return jnp.where(mask, tiled, empty)
+
+    suffix_rows = (
+        over_rows(suffix_half[0], MASKED_SCORE),
+        over_rows(suffix_half[1], 0.0),
+        over_rows(suffix_half[2], 0.0),
+    )
+    peak_all, total_all, sum_all = combine_pair(prefix_stats, suffix_rows)
 
     half_units = rows_dev * step_count * half_heads
     chunk = half_units // ctx_count

time: 47.6 us -> 53.6 us (1.13)
  local copies, waits for them, and re-layouts: 11.6 us -> 16.6 us
  starting transfers between devices: 11.4 us -> 10.5 us
  other arithmetic: 3.31 us -> 4.16 us
  waiting for transfers between devices: 12.8 us -> 13.6 us
    unnamed x21 -> x39, local copies, waits for them, and re-layouts: 2.91 us -> 6.61 us
    exp x0 -> x6, local copies, waits for them, and re-layouts: none -> 1.54 us  [the longest x3 0.77 us: combine_pair(): right_factor = jnp.exp(later[0] - highest)]
    all_to_all x1, waiting for transfers between devices: 2.22 us -> 3.48 us  [per_device(): lax.all_to_all(fanned, 'row', split_axis=0, concat_axis=0, tiled=True)]
    ppermute x1, waiting for transfers between devices: 1.08 us -> 0.01 us  [per_device(): lax.ppermute(head_half(suffix_packed, 1 - core_bit), 'ctx', swap)]
    another operation x3, local copies, waits for them, and re-layouts: 1.23 us -> 0.2 us  [per_device(): jnp.stack([prefix_keys.reshape(prefix_count, span_len, KVH, HD), prefix_v...]
    all_to_all x1, starting transfers between devices: 3.84 us -> 2.98 us  [per_device(): lax.all_to_all(outgoing.reshape(dests, 1, (chunk + pt_rows) * LANES), ('r...]
    dynamic_slice x1, local copies, waits for them, and re-layouts: 0.77 us -> 0.04 us  [per_device(): own_kv = lax.dynamic_slice_in_dim(kv_both, core_bit * half_kv, half_kv, 3)]
    broadcast_in_dim x0 -> x2, local copies, waits for them, and re-layouts: none -> 0.72 us  [over_rows(): return jnp.where(mask, tiled, empty)]
  transfers between devices with their start and end apart: 4 -> 4, of which waited for: 3 -> 2; matrix products, arithmetic and copies ran while one was open for 14% -> 11% of each run, Pallas kernels for 0% -> 0%
where the time goes in v18:
time: 53.6 us; the launch traced here: 53.1 us
  local copies, waits for them, and re-layouts  16.6 us (31%)
  waiting for transfers between devices  13.6 us (25%)
  starting transfers between devices  10.5 us (20%)
  blocking collectives  5.19 us (10%)
  other arithmetic  4.16 us (8%)
  matrix products  2.56 us (5%)
    all_to_all x1, waiting for transfers between devices, per_device(): lax.all_to_all(outgoing.reshape(dests, 1, (chunk + pt_rows) * LANES), ('r...  10.1 us
    all_to_all x1, starting transfers between devices, per_device(): lax.all_to_all(fanned, 'row', split_axis=0, concat_axis=0, tiled=True)  6.8 us
    unnamed x39, local copies, waits for them, and re-layouts  6.61 us
    all_gather x1, blocking collectives, per_device(): whole = lax.all_gather(result, 'ctx', axis=0, tiled=False)  5.19 us
    all_to_all x1, waiting for transfers between devices, per_device(): lax.all_to_all(fanned, 'row', split_axis=0, concat_axis=0, tiled=True)  3.48 us
    all_to_all x1, starting transfers between devices, per_device(): lax.all_to_all(outgoing.reshape(dests, 1, (chunk + pt_rows) * LANES), ('r...  2.98 us
    reshape x1, local copies, waits for them, and re-layouts, per_device(): flat_values = pool_values.reshape(slot_count * page_len, KVH, HD)  1.35 us
    gather x2, local copies, waits for them, and re-layouts, prefix_block(): row_kv = jnp.take(kv, every_prefix, axis=1)  1.3 us
  transfers between devices with their start and end apart: 4, of which 2 were waited for; matrix products, arithmetic and copies ran while one was open for 11% of the time, Pallas kernels for 0%

profile of v18, /device:TPU:0, one launch (start us, length us, event | category | flops | bytes accessed | tf_op | source)
XLA Modules:
  0.0 53.1 jit_solution(16563677457096026774)
XLA Ops:
  0.0 0.8 %copy-done.14 = s32[2,32]{1,0:T(2,128)S(1)} copy-done((s32[2,32]{1,0:T(2,128)S(1)}, s32[2,32]{1,0:T(2,128)}, u32[]{:S(2)}) %copy-start.14) | copy-done | bytes 280
  0.8 0.2 compare_reduce_fusion
  1.0 0.2 fusion.25
  1.2 1.3 %reshape.311 = bf16[1024,4,128]{2,1,0:T(4,128)(2,1)S(1)} reshape(bf16[16,64,512]{2,1,0:T(8,128)(2,1)} %param.19) | data formatting | bytes 2097152 | tf_op jit(solution)/shard_map/reshape | solution.py:70
  2.6 0.1 and.52
  2.9 0.5 copy-done.7
  3.5 0.6 %copy-done.15 = s32[2]{0:T(128)S(1)} copy-done((s32[2]{0:T(128)S(1)}, s32[2]{0:T(128)}, u32[]{:S(2)}) %copy-start.15) | copy-done | bytes 32
  4.2 0.6 %select_reduce_fusion = (f32[2,2,4,8]{3,2,1,0:T(4,128)S(1)}, f32[2,2,4,8,1024]{4,3,2,1,0:T(8,128)S(1)}) fusion(pred[2,1024]{1,0:T(4,128)(4,1)S(1)} %compare_and_fusion, bf16[1024,512,1,1,1]{1,0,4,3,2:T(8,128)(2,1)S(1)} %bitcast.141, pred[4,4]{1,0:T(4,128)(4,1)S(1)} %iota_compare_fusion.1, bf16[2,2,4,8,128]{4,3,2,1,0:T(8,128)(2,1)S(1)} %reshape.307), kind=kOutput, calls=%fused_computation.25 | convolution fusion | flops 134676352 | bytes 1608208 | tf_op jit(solution)/shard_map/rskgw,tw->rskgt/dot_general | solution.py:78
  4.8 0.3 convert_reduce_fusion
  5.0 0.2 copy.195
  5.2 0.2 copy.196
  5.3 0.3 fusion.8
  5.7 0.5 copy-done.5
  6.2 0.5 collective-permute-start.1
  6.7 0.7 %copy-done.18 = s32[2]{0:T(128)S(1)} copy-done((s32[2]{0:T(128)S(1)}, s32[2]{0:T(128)}, u32[]{:S(2)}) %copy-start.18) | copy-done | bytes 32
  7.5 0.7 %broadcast_in_dim.179 = bf16[8,80,128]{2,1,0:T(8,128)(2,1)} broadcast(bf16[80,128]{1,0:T(8,128)(2,1)S(1)} %pad_maximum_fusion.1), dimensions={1,2} | broadcast | bytes 184320 | tf_op jit(solution)/shard_map/broadcast_in_dim | solution.py:104
  8.2 6.8 %all-to-all-start = ((bf16[8,80,128]{2,1,0:T(8,128)(2,1)}), bf16[8,80,128]{2,1,0:T(8,128)(2,1)S(1)}, u32[]{:S(2)}, u32[]{:S(2)}) async-start(bf16[8,80,128]{2,1,0:T(8,128)(2,1)} %broadcast_in_dim.179), calls=%async_computation | async-start | bytes 327680 | tf_op jit(solution)/shard_map/all_to_all | solution.py:105
  15.1 0.9 %copy-done.4 = bf16[8,32,512]{2,1,0:T(8,128)(2,1)S(1)} copy-done((bf16[8,32,512]{2,1,0:T(8,128)(2,1)S(1)}, bf16[8,32,512]{2,1,0:T(8,128)(2,1)}, u32[]{:S(2)}) %copy-start.4) | copy-done | bytes 262168
  16.2 0.3 collective-permute-start
  16.5 0.5 %iota_compare_fusion.2 = pred[2,2]{1,0:T(4,128)(4,1)} fusion(), kind=kLoop, calls=%fused_computation.102 | loop fusion | flops 4 | bytes 4 | tf_op jit(solution)/shard_map/le | solution.py:89
  17.2 0.6 %broadcast_in_dim.195 = pred[32]{0:T(512)(128)(4,1)} reshape(pred[16,2]{1,0:T(8,128)(4,1)S(1)} %broadcast_in_dim.194) | data formatting | bytes 64 | tf_op jit(solution)/shard_map/jit(_where)/broadcast_in_dim | solution.py:157
  17.9 0.1 copy.214
  18.0 0.1 copy.197
  18.2 0.1 tile.38
  18.3 0.1 tile.36
  18.5 0.6 %copy.207 = f32[2,2,2,8]{3,1,0,2:T(2,128)} copy(f32[2,2,2,8]{3,2,1,0:T(2,128)S(1)} %get-tuple-element.28) | data formatting | bytes 512 | tf_op jit(solution)/shard_map/exp | solution.py:30
  19.1 0.6 %copy.206 = f32[2,2,2,8]{3,1,0,2:T(2,128)} copy(f32[2,2,2,8]{3,2,1,0:T(2,128)S(1)} %get-tuple-element.27) | data formatting | bytes 512 | tf_op jit(solution)/shard_map/exp | solution.py:29
  19.7 3.5 %all-to-all-done = bf16[8,80,128]{2,1,0:T(8,128)(2,1)S(1)} async-done(((bf16[8,80,128]{2,1,0:T(8,128)(2,1)}), bf16[8,80,128]{2,1,0:T(8,128)(2,1)S(1)}, u32[]{:S(2)}, u32[]{:S(2)}) %all-to-all-start) | async-done | bytes 163872 | tf_op jit(solution)/shard_map/all_to_all | solution.py:105
  23.1 0.2 convert_reduce_fusion.4
  23.5 0.6 %gather_fusion = bf16[16,2,32,2,128]{4,2,3,1,0:T(8,128)(2,1)S(1)} fusion(bf16[2,8,32,2,128]{4,2,3,1,0:T(8,128)(2,1)S(1)} %get-tuple-element.32, s32[1024]{0:T(1024)S(1)} %pad_clamp_fusion), kind=kCustom, calls=%fused_computation.clone | custom fusion | bytes 1048640 | tf_op jit(solution)/shard_map/jit(_take)/gather | solution.py:128
  24.2 0.6 %gather_fusion.1 = bf16[16,2,32,2,128]{4,2,3,1,0:T(8,128)(2,1)S(1)} fusion(bf16[2,8,32,2,128]{4,2,3,1,0:T(8,128)(2,1)S(1)} %collective-permute-done, s32[1024]{0:T(1024)S(1)} %pad_clamp_fusion), kind=kCustom, calls=%fused_computation.1.clone | custom fusion | bytes 1048640 | tf_op jit(solution)/shard_map/jit(_take)/gather | solution.py:128
  24.8 0.2 fusion.11
  25.0 0.7 %copy-done.2 = bf16[8,80,128]{2,1,0:T(8,128)(2,1)S(1)} copy-done((bf16[8,80,128]{2,1,0:T(8,128)(2,1)S(1)}, bf16[8,80,128]{2,1,0:T(8,128)(2,1)}, u32[]{:S(2)}) %copy-start.2) | copy-done | bytes 163864
  25.7 0.4 fusion.41
  26.2 0.4 fusion.40
  26.7 0.3 convert_reduce_fusion.1
  27.0 0.1 reduce_sum.72
  27.1 0.1 reduce_max.53
  27.2 0.1 reduce_max.52
  27.3 0.3 convert_reduce_fusion.2
  27.6 0.1 reduce_sum.70
  27.7 0.6 %copy-done.12 = pred[16]{0:T(512)(128)(4,1)S(1)} copy-done((pred[16]{0:T(512)(128)(4,1)S(1)}, pred[16]{0:T(512)(128)(4,1)}, u32[]{:S(2)}) %copy-start.12) | copy-done | bytes 40
  28.3 0.1 copy.205
  28.4 0.1 copy.202
  28.5 0.3 fusion.2
  28.7 0.1 copy.204
  28.9 0.1 copy.200
  28.9 0.6 %copy-done.6 = f32[4,2,2,8,128]{4,3,2,1,0:T(8,128)S(1)} copy-done((f32[4,2,2,8,128]{4,3,2,1,0:T(8,128)S(1)}, f32[4,2,2,8,128]{4,3,2,1,0:T(8,128)}, u32[]{:S(2)}) %copy-start.6) | copy-done | bytes 65560
  29.6 0.2 fusion.12
  29.7 0.3 fusion.6
  30.1 0.6 %copy-done.10 = pred[32]{0:T(512)(128)(4,1)S(1)} copy-done((pred[32]{0:T(512)(128)(4,1)S(1)}, pred[32]{0:T(512)(128)(4,1)}, u32[]{:S(2)}) %copy-start.10) | copy-done | bytes 56
  30.7 0.1 multiply_add_fusion
  30.9 1.0 %reshape.362 = f32[32,1,2176]{2,1,0:T(1,128)} reshape(f32[32,17,128]{2,1,0:T(8,128)S(1)} %pad_maximum_fusion) | data formatting | bytes 557056 | tf_op jit(solution)/shard_map/reshape | solution.py:180
  31.9 3.0 %all-to-all-start.1 = ((f32[32,1,2176]{2,1,0:T(1,128)}), f32[32,1,2176]{2,1,0:T(1,128)S(1)}, u32[]{:S(2)}, u32[]{:S(2)}) async-start(f32[32,1,2176]{2,1,0:T(1,128)} %reshape.362), calls=%async_computation.1 | async-start | bytes 557056 | tf_op jit(solution)/shard_map/all_to_all | solution.py:179
  34.9 0.3 select_reduce_fusion.1
  35.3 0.1 reshape.320
  35.4 0.1 convert_reduce_fusion.3
  35.5 0.2 convolution_bitcast_fusion.2
  35.8 0.1 reshape.327
  35.9 10.1 %all-to-all-done.1 = f32[32,1,2176]{2,1,0:T(1,128)S(1)} async-done(((f32[32,1,2176]{2,1,0:T(1,128)}), f32[32,1,2176]{2,1,0:T(1,128)S(1)}, u32[]{:S(2)}, u32[]{:S(2)}) %all-to-all-start.1) | async-done | bytes 278560 | tf_op jit(solution)/shard_map/all_to_all | solution.py:179
  46.0 0.7 %reduce.6 = f32[32,2176]{1,0:T(8,128)S(1)} reduce(f32[32,1,2176]{2,1,0:T(1,128)S(1)} %all-to-all-done.1, f32[]{:T(128)} %constant.113), dimensions={1}, to_apply=%all_to_all.7.reduce_sub_computation | reduce | bytes 557060 | tf_op jit(solution)/shard_map/all_to_all | solution.py:179
  47.0 0.1 multiply_reduce_fusion
  47.3 5.2 %all-gather = bf16[8,16,128]{2,1,0:T(8,128)(2,1)S(1)} all-gather(bf16[2,16,128]{2,1,0:T(8,128)(2,1)S(1)} %divide_convert_fusion), channel_id=2, replica_groups=mesh['ctx'=4,'row'=8] {'ctx'}, dimensions={0}, use_global_device_ids=true | all-gather | bytes 40960 | tf_op jit(solution)/shard_map/all_gather | solution.py:213
  52.5 0.6 %reshape.329 = bf16[2,2,4096]{2,1,0:T(2,128)(2,1)} reshape(bf16[2,2,2,16,128]{4,3,2,1,0:T(8,128)(2,1)S(1)} %bitcast.153) | data formatting | bytes 65536 | tf_op jit(solution)/shard_map/reshape | solution.py:216
  (92 shorter events, 2.5 us)
Async XLA Ops:
  0.0 4.2 %copy-start = (bf16[16,64,512]{2,1,0:T(8,128)(2,1)S(1)}, bf16[16,64,512]{2,1,0:T(8,128)(2,1)}, u32[]{:S(2)}) copy-start(bf16[16,64,512]{2,1,0:T(8,128)(2,1)} %param.18) | copy-start | bytes 3145732
  0.0 0.8 %copy-start.14 = (s32[2,32]{1,0:T(2,128)S(1)}, s32[2,32]{1,0:T(2,128)}, u32[]{:S(2)}) copy-start(s32[2,32]{1,0:T(2,128)} %param.20) | copy-start | bytes 772
  2.7 0.8 %copy-start.7 = (bf16[2,2,4096]{2,1,0:T(2,128)(2,1)S(1)}, bf16[2,2,4096]{2,1,0:T(2,128)(2,1)}, u32[]{:S(2)}) copy-start(bf16[2,2,4096]{2,1,0:T(2,128)(2,1)} %param.14) | copy-start | bytes 98308
  3.4 0.7 %copy-start.15 = (s32[2]{0:T(128)S(1)}, s32[2]{0:T(128)}, u32[]{:S(2)}) copy-start(s32[2]{0:T(128)} %param.21) | copy-start | bytes 28
  5.6 0.6 %copy-start.5 = (f32[4,2,2,8,128]{4,3,2,1,0:T(8,128)}, f32[4,2,2,8,128]{4,3,2,1,0:T(8,128)S(1)}, u32[]{:S(2)}) copy-start(f32[4,2,2,8,128]{4,3,2,1,0:T(8,128)S(1)} %fusion.8) | copy-start | bytes 196612
  6.2 11.6 %collective-permute-start.1 = (f32[2,2,2,8,130]{4,3,1,0,2:T(8,128)S(1)}, f32[2,2,2,8,130]{4,3,1,0,2:T(8,128)S(1)}, u32[]{:S(2)}, u32[]{:S(2)}) collective-permute-start(f32[2,2,2,8,130]{4,3,1,0,2:T(8,128)S(1)} %fusion.20), channel_id=1, source_target_pairs={{0,8},{8,0},{16,24},{24,16},{1,9},{9,1},{17,25},{25,17},{2,10},{10... | collective-permute-start | bytes 99848 | tf_op jit(solution)/shard_map/ppermute | solution.py:147
  6.7 0.7 %copy-start.18 = (s32[2]{0:T(128)S(1)}, s32[2]{0:T(128)}, u32[]{:S(2)}) copy-start(s32[2]{0:T(128)} %param.15) | copy-start | bytes 28
  7.5 7.5 %copy-start.3 = (bf16[8,32,512]{2,1,0:T(8,128)(2,1)S(1)}, bf16[8,32,512]{2,1,0:T(8,128)(2,1)}, u32[]{:S(2)}) copy-start(bf16[8,32,512]{2,1,0:T(8,128)(2,1)} %param.16) | copy-start | bytes 786436
  8.2 14.9 %all-to-all-start = ((bf16[8,80,128]{2,1,0:T(8,128)(2,1)}), bf16[8,80,128]{2,1,0:T(8,128)(2,1)S(1)}, u32[]{:S(2)}, u32[]{:S(2)}) async-start(bf16[8,80,128]{2,1,0:T(8,128)(2,1)} %broadcast_in_dim.179), calls=%async_computation | async-start | bytes 327680 | tf_op jit(solution)/shard_map/all_to_all | solution.py:105
  15.1 1.0 %copy-start.4 = (bf16[8,32,512]{2,1,0:T(8,128)(2,1)S(1)}, bf16[8,32,512]{2,1,0:T(8,128)(2,1)}, u32[]{:S(2)}) copy-start(bf16[8,32,512]{2,1,0:T(8,128)(2,1)} %param.17) | copy-start | bytes 786436
  16.2 7.9 %collective-permute-start = (bf16[2,8,32,2,128]{4,2,3,1,0:T(8,128)(2,1)S(1)}, bf16[2,8,32,2,128]{4,2,3,1,0:T(8,128)(2,1)S(1)}, u32[]{:S(2)}, u32[]{:S(2)}) collective-permute-start(bf16[2,8,32,2,128]{4,2,3,1,0:T(8,128)(2,1)S(1)} %get-tuple-element.33), channel_id=1, source_target_pairs={{0,8},{8,0},{16,24},{24,16},{1,9},{9,1},{17,25},{25,17},{2,10},{10... | collective-permute-start | bytes 786440 | tf_op jit(solution)/shard_map/ppermute | solution.py:124
  16.5 0.6 %copy-start.11 = (pred[16]{0:T(512)(128)(4,1)}, pred[16]{0:T(512)(128)(4,1)S(1)}, u32[]{:S(2)}) copy-start(pred[16]{0:T(512)(128)(4,1)S(1)} %fusion.35) | copy-start | bytes 52
  23.1 1.0 %copy-start.1 = (bf16[8,80,128]{2,1,0:T(8,128)(2,1)}, bf16[8,80,128]{2,1,0:T(8,128)(2,1)S(1)}, u32[]{:S(2)}) copy-start(bf16[8,80,128]{2,1,0:T(8,128)(2,1)S(1)} %all-to-all-done) | copy-start | bytes 491524
  24.8 0.9 %copy-start.2 = (bf16[8,80,128]{2,1,0:T(8,128)(2,1)S(1)}, bf16[8,80,128]{2,1,0:T(8,128)(2,1)}, u32[]{:S(2)}) copy-start(bf16[8,80,128]{2,1,0:T(8,128)(2,1)} %copy-done.1) | copy-start | bytes 491524
  27.6 0.7 %copy-start.12 = (pred[16]{0:T(512)(128)(4,1)S(1)}, pred[16]{0:T(512)(128)(4,1)}, u32[]{:S(2)}) copy-start(pred[16]{0:T(512)(128)(4,1)} %copy-done.11) | copy-start | bytes 52
  28.7 0.8 %copy-start.6 = (f32[4,2,2,8,128]{4,3,2,1,0:T(8,128)S(1)}, f32[4,2,2,8,128]{4,3,2,1,0:T(8,128)}, u32[]{:S(2)}) copy-start(f32[4,2,2,8,128]{4,3,2,1,0:T(8,128)} %copy-done.5) | copy-start | bytes 196612
  28.8 0.7 %copy-start.8 = (f32[2,2,2,8]{3,1,0,2:T(2,128)S(1)}, f32[2,2,2,8]{3,1,0,2:T(2,128)}, u32[]{:S(2)}) copy-start(f32[2,2,2,8]{3,1,0,2:T(2,128)} %copy.207) | copy-start | bytes 772
  28.8 0.7 %copy-start.9 = (f32[2,2,2,8]{3,1,0,2:T(2,128)S(1)}, f32[2,2,2,8]{3,1,0,2:T(2,128)}, u32[]{:S(2)}) copy-start(f32[2,2,2,8]{3,1,0,2:T(2,128)} %copy.206) | copy-start | bytes 772
  30.0 0.6 %copy-start.10 = (pred[32]{0:T(512)(128)(4,1)S(1)}, pred[32]{0:T(512)(128)(4,1)}, u32[]{:S(2)}) copy-start(pred[32]{0:T(512)(128)(4,1)} %broadcast_in_dim.195) | copy-start | bytes 100
  31.9 3.0 %copy-start.16 = (pred[2,2]{1,0:T(4,128)(4,1)S(1)}, pred[2,2]{1,0:T(4,128)(4,1)}, u32[]{:S(2)}) copy-start(pred[2,2]{1,0:T(4,128)(4,1)} %iota_compare_fusion.2) | copy-start | bytes 16
  31.9 3.0 %copy-start.17 = (bf16[2,2,512]{2,1,0:T(2,128)(2,1)S(1)}, bf16[2,2,512]{2,1,0:T(2,128)(2,1)}, u32[]{:S(2)}) copy-start(bf16[2,2,512]{2,1,0:T(2,128)(2,1)} %param.22) | copy-start | bytes 12292
  31.9 3.6 %copy-start.13 = (bf16[2,2,512]{2,1,0:T(2,128)(2,1)S(1)}, bf16[2,2,512]{2,1,0:T(2,128)(2,1)}, u32[]{:S(2)}) copy-start(bf16[2,2,512]{2,1,0:T(2,128)(2,1)} %param.23) | copy-start | bytes 12292
  31.9 14.1 %all-to-all-start.1 = ((f32[32,1,2176]{2,1,0:T(1,128)}), f32[32,1,2176]{2,1,0:T(1,128)S(1)}, u32[]{:S(2)}, u32[]{:S(2)}) async-start(f32[32,1,2176]{2,1,0:T(1,128)} %reshape.362), calls=%async_computation.1 | async-start | bytes 557056 | tf_op jit(solution)/shard_map/all_to_all | solution.py:179

commit v19 on v16

--- a/solution.py
+++ b/solution.py
@@ -124,17 +124,23 @@
     partner_kv = lax.ppermute(given_kv, "ctx", swap)
 
 
+    chosen = (
+        every_prefix[:, None] == jnp.arange(prefix_count, dtype=jnp.int32)[None, :]
+    ).reshape(total_rows, 1, 1, 1, prefix_count, 1)
+
     def prefix_block(kv):
-        row_kv = jnp.take(kv, every_prefix, axis=1)
-        row_keys, row_values = row_kv[0], row_kv[1]
-        scores = (
-            jnp.einsum(
-                "rskgd,rtkd->rskgt", half_query, row_keys, preferred_element_type=jnp.float32
-            )
-            * score_scale
+        every_scores = jnp.einsum(
+            "rskgd,ptkd->rskgpt", half_query, kv[0], preferred_element_type=jnp.float32
         )
-        always = jnp.ones((1, 1, 1, 1, span_len), dtype=bool)
-        return block_stats(scores, always, row_values, "rskgt,rtkd->rskgd")
+        scores = jnp.sum(jnp.where(chosen, every_scores, 0.0), axis=4) * score_scale
+        block_peak = jnp.max(scores, axis=-1)
+        weights = jnp.exp(scores - block_peak[..., None]).astype(jnp.bfloat16)
+        block_total = jnp.sum(weights.astype(jnp.float32), axis=-1)
+        spread = jnp.where(chosen, weights[..., None, :], jnp.zeros((), jnp.bfloat16))
+        block_sum = jnp.einsum(
+            "rskgpt,ptkd->rskgd", spread, kv[1], preferred_element_type=jnp.float32
+        )
+        return (block_peak, block_total, block_sum)
 
     prefix_stats = combine_pair(prefix_block(own_kv), prefix_block(partner_kv))
 

time: 47.6 us -> 49.8 us (1.046)
  starting transfers between devices: 11.4 us -> 14.4 us
  local copies, waits for them, and re-layouts: 11.6 us -> 8.77 us
  matrix products: 2.56 us -> 5.17 us
  waiting for transfers between devices: 12.8 us -> 11.2 us
  other arithmetic: 3.31 us -> 4.32 us
    dot_general x2 -> x4, matrix products: 0.71 us -> 3.85 us  [the longest x2 2.02 us: prefix_block(): jnp.einsum('rskgpt,ptkd->rskgd', spread, kv[1], preferred_element_type=jn...]
    all_to_all x1, starting transfers between devices: 3.84 us -> 6.63 us  [per_device(): lax.all_to_all(outgoing.reshape(dests, 1, (chunk + pt_rows) * LANES), ('r...]
    unnamed x21, local copies, waits for them, and re-layouts: 2.91 us -> 0.65 us
    all_to_all x1, waiting for transfers between devices: 2.22 us -> 0.39 us  [per_device(): lax.all_to_all(fanned, 'row', split_axis=0, concat_axis=0, tiled=True)]
    gather x2 -> x0, local copies, waits for them, and re-layouts: 1.3 us -> none  [prefix_block(): row_kv = jnp.take(kv, every_prefix, axis=1)]
    reshape x1, local copies, waits for them, and re-layouts: 0.03 us -> 0.89 us  [per_device(): own_query = queries.reshape(rows_dev, step_count, KVH, groups, HD)]
    reshape x1, local copies, waits for them, and re-layouts: 1.12 us -> 0.27 us  [per_device(): flat_values = pool_values.reshape(slot_count * page_len, KVH, HD)]
    convert_element_type x1, other arithmetic: 0.01 us -> 0.66 us  [per_device(): prefix_id.astype(jnp.bfloat16)[:, None]]
  transfers between devices with their start and end apart: 4 -> 4, of which waited for: 3 -> 3; matrix products, arithmetic and copies ran while one was open for 14% -> 15% of each run, Pallas kernels for 0% -> 0%
where the time goes in v19:
time: 49.8 us; the launch traced here: 49.5 us
  starting transfers between devices  14.4 us (29%)
  waiting for transfers between devices  11.2 us (22%)
  local copies, waits for them, and re-layouts  8.77 us (18%)
  blocking collectives  5.18 us (10%)
  matrix products  5.17 us (10%)
  other arithmetic  4.32 us (9%)
    all_to_all x1, waiting for transfers between devices, per_device(): lax.all_to_all(outgoing.reshape(dests, 1, (chunk + pt_rows) * LANES), ('r...  10.1 us
    all_to_all x1, starting transfers between devices, per_device(): lax.all_to_all(fanned, 'row', split_axis=0, concat_axis=0, tiled=True)  7.25 us
    all_to_all x1, starting transfers between devices, per_device(): lax.all_to_all(outgoing.reshape(dests, 1, (chunk + pt_rows) * LANES), ('r...  6.63 us
    all_gather x1, blocking collectives, per_device(): whole = lax.all_gather(result, 'ctx', axis=0, tiled=False)  5.18 us
    dot_general x2, matrix products, prefix_block(): jnp.einsum('rskgpt,ptkd->rskgd', spread, kv[1], preferred_element_type=jn...  2.02 us
    dot_general x2, matrix products, prefix_block(): jnp.einsum('rskgd,ptkd->rskgpt', half_query, kv[0], preferred_element_typ...  1.82 us
    another operation x3, local copies, waits for them, and re-layouts, per_device(): jnp.stack([prefix_keys.reshape(prefix_count, span_len, KVH, HD), prefix_v...  1.14 us
  transfers between devices with their start and end apart: 4, of which 3 were waited for; matrix products, arithmetic and copies ran while one was open for 15% of the time, Pallas kernels for 0%

profile of v19, /device:TPU:0, one launch (start us, length us, event | category | flops | bytes accessed | tf_op | source)
XLA Modules:
  0.0 49.5 jit_solution(286432153888737342)
XLA Ops:
  0.0 0.9 %reshape.263 = bf16[2,2,4,8,128]{4,3,2,1,0:T(8,128)(2,1)S(1)} reshape(bf16[2,2,4096]{2,1,0:T(2,128)(2,1)} %param.12) | data formatting | bytes 65536 | tf_op jit(solution)/shard_map/reshape | solution.py:56
  0.9 0.7 %convert_element_type.52 = bf16[2]{0:T(256)(128)(2,1)S(1)} convert(s32[2]{0:T(128)} %param.13) | non-fusion elementwise | flops 2 | bytes 12 | tf_op jit(solution)/shard_map/convert_element_type | solution.py:101
  1.6 0.1 compare_select_fusion.1
  1.7 0.7 %broadcast_in_dim.159 = bf16[8,80,128]{2,1,0:T(8,128)(2,1)} broadcast(bf16[80,128]{1,0:T(8,128)(2,1)S(1)} %pad_maximum_fusion.1), dimensions={1,2} | broadcast | bytes 184320 | tf_op jit(solution)/shard_map/broadcast_in_dim | solution.py:104
  2.4 7.3 %all-to-all-start = ((bf16[8,80,128]{2,1,0:T(8,128)(2,1)}), bf16[8,80,128]{2,1,0:T(8,128)(2,1)S(1)}, u32[]{:S(2)}, u32[]{:S(2)}) async-start(bf16[8,80,128]{2,1,0:T(8,128)(2,1)} %broadcast_in_dim.159), calls=%async_computation | async-start | bytes 327680 | tf_op jit(solution)/shard_map/all_to_all | solution.py:105
  9.7 1.0 %stack_reshape.6 = bf16[1,8,32,4,128]{4,3,2,1,0:T(4,128)(2,1)S(1)} reshape(bf16[8,32,512]{2,1,0:T(8,128)(2,1)} %param.14) | data formatting | bytes 524288 | tf_op jit(solution)/shard_map/stack;reshape | solution.py:116
  10.9 0.7 %constant_dynamic-slice_fusion.4 = bf16[2,8,32,2,128]{4,2,1,3,0:T(8,128)(2,1)} fusion(bf16[2,8,32,4,128]{4,2,1,3,0:T(8,128)(2,1)S(1)} %copy_dynamic-update-slice_fusion, s32[]{:T(128)S(6)} %select_n.80), kind=kLoop, calls=%fused_computation.88 | loop fusion | bytes 524292 | tf_op jit(solution)/shard_map/dynamic_slice | solution.py:123
  11.7 0.2 fusion.31
  11.8 0.2 compare_reduce_fusion
  12.1 0.1 add.103
  12.3 0.1 and.26
  12.5 0.3 reshape.267
  12.7 0.4 copy-done.7
  13.2 0.6 %select_reduce_fusion = (f32[2,2,4,8]{3,2,1,0:T(4,128)S(1)}, f32[2,2,4,8,1024]{4,3,2,1,0:T(8,128)S(1)}) fusion(pred[2,1024]{1,0:T(4,128)(4,1)S(1)} %compare_and_fusion, bf16[1024,512,1,1,1]{1,0,4,3,2:T(8,128)(2,1)S(1)} %bitcast.135, pred[4,4]{1,0:T(4,128)(4,1)S(1)} %iota_compare_fusion.2, bf16[2,2,4,8,128]{4,3,2,1,0:T(8,128)(2,1)S(1)} %reshape.263), kind=kOutput, calls=%fused_computation.21 | convolution fusion | flops 134676352 | bytes 1608208 | tf_op jit(solution)/shard_map/rskgw,tw->rskgt/dot_general | solution.py:78
  13.8 0.3 convert_reduce_fusion
  14.0 0.3 fusion.6
  14.4 0.2 copy.173
  14.5 0.2 copy.172
  14.7 0.1 fusion.23
  14.8 0.6 %collective-permute-start.1 = (f32[2,2,2,8,130]{4,0,3,1,2:T(2,128)S(1)}, f32[2,2,2,8,130]{4,0,3,1,2:T(2,128)S(1)}, u32[]{:S(2)}, u32[]{:S(2)}) collective-permute-start(f32[2,2,2,8,130]{4,0,3,1,2:T(2,128)S(1)} %fusion.23), channel_id=1, source_target_pairs={{0,8},{8,0},{16,24},{24,16},{1,9},{9,1},{17,25},{25,17},{2,10},{10... | collective-permute-start | bytes 99848 | tf_op jit(solution)/shard_map/ppermute | solution.py:153
  15.4 0.1 copy.212
  15.5 0.1 copy.213
  15.6 0.7 %collective-permute-done.1 = f32[2,2,2,8,130]{4,0,3,1,2:T(2,128)S(1)} collective-permute-done((f32[2,2,2,8,130]{4,0,3,1,2:T(2,128)S(1)}, f32[2,2,2,8,130]{4,0,3,1,2:T(2,128)S(1)}, u32[]{:S(2)}, u32[]{:S(2)}) %collective-permute-start.1) | collective-permute-done | bytes 33312 | tf_op jit(solution)/shard_map/ppermute | solution.py:153
  16.3 0.1 fusion.43
  16.4 0.1 copy.174
  16.5 0.1 copy.175
  16.6 0.1 copy.181
  16.7 0.1 copy.182
  16.8 0.4 all-to-all-done
  17.2 0.2 convert_reduce_fusion.4
  17.4 0.1 reshape.288
  17.6 0.5 fusion.1
  18.0 0.1 multiply_reduce_fusion.2
  18.2 0.3 convert_reduce_fusion.2
  18.5 1.4 %fusion = f32[16,2,2,8,32]{4,0,3,1,2:T(8,128)S(1)} fusion(pred[16,8]{0,1:T(8,128)(4,1)S(1)} %iota_compare_fusion.1, bf16[2,8,32,2,128]{4,2,1,3,0:T(8,128)(2,1)} %collective-permute-done, bf16[16,2,2,8,128,1]{4,3,2,1,0,5:T(8,128)(2,1)S(1)} %bitcast.146), kind=kOutput, calls=%fused_computation.1 | convolution fusion | flops 33800192 | bytes 327808 | tf_op jit(solution)/shard_map/rskgd,ptkd->rskgpt/dot_general | solution.py:132
  19.8 0.1 multiply_reduce_fusion.1
  20.0 0.3 convert_reduce_fusion.1
  20.3 0.6 %fusion.4 = f32[16,2,2,8,128]{4,0,3,1,2:T(8,128)S(1)} fusion(pred[16,8]{0,1:T(8,128)(4,1)S(1)} %iota_compare_fusion.1, bf16[16,2,2,8,32]{4,0,3,1,2:T(8,128)(2,1)S(1)} %get-tuple-element.36, bf16[2,8,32,4,128]{4,2,1,3,0:T(8,128)(2,1)S(1)} %copy-done.3, s32[]{:T(128)S(6)} %add.118, s32[]{:T(128)S(6)} %select_n.78, f32[16,2,2,8]{0,3,1,2:T(8,128)S(1)} %get-tuple-element.32), kind=kOutput, calls=%fused_computation.9 | convolution fusion | flops 33751040 | bytes 541704 | tf_op jit(solution)/shard_map/rskgpt,ptkd->rskgd/dot_general | solution.py:140
  20.9 0.1 multiply_add_fusion
  21.0 1.4 %fusion.3 = f32[16,2,2,8,128]{4,0,3,1,2:T(8,128)S(1)} fusion(f32[16,2,2,8,128]{4,0,3,1,2:T(8,128)S(1)} %fusion.4, pred[16,8]{0,1:T(8,128)(4,1)S(1)} %iota_compare_fusion.1, bf16[16,2,2,8,32]{4,0,3,1,2:T(8,128)(2,1)S(1)} %get-tuple-element.38, bf16[2,8,32,2,128]{4,2,1,3,0:T(8,128)(2,1)} %collective-permute-done, f32[16,2,2,8]{0,3,1,2:T(8,128)S(1)} %get-tuple-element.33), kind=kOutput, calls=%fused_computation.7 | convolution fusion | flops 33816576 | bytes 690304 | tf_op jit(solution)/shard_map/rskgpt,ptkd->rskgd/dot_general | solution.py:140
  22.4 0.3 fusion.29
  22.6 0.1 copy.178
  22.7 0.2 dynamic_update_slice.10
  23.0 0.1 copy.179
  23.1 0.1 reshape.269
  23.2 0.2 dynamic_update_slice.11
  23.4 0.1 copy.183
  23.4 0.1 reshape.270
  23.5 0.1 select_maximum_fusion
  23.7 1.0 %reshape.302 = f32[32,1,2176]{2,1,0:T(1,128)} reshape(f32[32,17,128]{2,1,0:T(8,128)S(1)} %pad_maximum_fusion) | data formatting | bytes 557056 | tf_op jit(solution)/shard_map/reshape | solution.py:182
  24.6 6.6 %all-to-all-start.1 = ((f32[32,1,2176]{2,1,0:T(1,128)}), f32[32,1,2176]{2,1,0:T(1,128)S(1)}, u32[]{:S(2)}, u32[]{:S(2)}) async-start(f32[32,1,2176]{2,1,0:T(1,128)} %reshape.302), calls=%async_computation.1 | async-start | bytes 557056 | tf_op jit(solution)/shard_map/all_to_all | solution.py:181
  31.3 0.3 select_reduce_fusion.1
  31.6 0.1 reshape.277
  31.7 0.1 reshape.278
  31.7 0.1 convert_reduce_fusion.3
  31.9 0.1 reshape.284
  32.0 0.1 reshape.285
  32.0 0.2 convolution_bitcast_fusion.2
  32.3 10.1 %all-to-all-done.1 = f32[32,1,2176]{2,1,0:T(1,128)S(1)} async-done(((f32[32,1,2176]{2,1,0:T(1,128)}), f32[32,1,2176]{2,1,0:T(1,128)S(1)}, u32[]{:S(2)}, u32[]{:S(2)}) %all-to-all-start.1) | async-done | bytes 278560 | tf_op jit(solution)/shard_map/all_to_all | solution.py:181
  42.4 0.7 %reduce.6 = f32[32,2176]{1,0:T(8,128)S(1)} reduce(f32[32,1,2176]{2,1,0:T(1,128)S(1)} %all-to-all-done.1, f32[]{:T(128)} %constant.88), dimensions={1}, to_apply=%all_to_all.7.reduce_sub_computation | reduce | bytes 557060 | tf_op jit(solution)/shard_map/all_to_all | solution.py:181
  43.4 0.1 multiply_reduce_fusion
  43.6 0.1 divide_convert_fusion
  43.6 5.2 %all-gather = bf16[8,16,128]{2,1,0:T(8,128)(2,1)S(1)} all-gather(bf16[2,16,128]{2,1,0:T(8,128)(2,1)S(1)} %divide_convert_fusion), channel_id=2, replica_groups=mesh['ctx'=4,'row'=8] {'ctx'}, dimensions={0}, use_global_device_ids=true | all-gather | bytes 40960 | tf_op jit(solution)/shard_map/all_gather | solution.py:215
  48.8 0.6 %reshape.287 = bf16[2,2,4096]{2,1,0:T(2,128)(2,1)} reshape(bf16[2,2,2,16,128]{4,3,2,1,0:T(8,128)(2,1)S(1)} %bitcast.144) | data formatting | bytes 65536 | tf_op jit(solution)/shard_map/reshape | solution.py:218
  (53 shorter events, 1.1 us)
Async XLA Ops:
  0.0 13.2 %copy-start = (bf16[16,64,512]{2,1,0:T(8,128)(2,1)S(1)}, bf16[16,64,512]{2,1,0:T(8,128)(2,1)}, u32[]{:S(2)}) copy-start(bf16[16,64,512]{2,1,0:T(8,128)(2,1)} %param.16) | copy-start | bytes 3145732
  0.0 10.8 %copy-start.4 = (bf16[8,32,512]{2,1,0:T(8,128)(2,1)S(1)}, bf16[8,32,512]{2,1,0:T(8,128)(2,1)}, u32[]{:S(2)}) copy-start(bf16[8,32,512]{2,1,0:T(8,128)(2,1)} %param.15) | copy-start | bytes 786436
  2.4 14.8 %all-to-all-start = ((bf16[8,80,128]{2,1,0:T(8,128)(2,1)}), bf16[8,80,128]{2,1,0:T(8,128)(2,1)S(1)}, u32[]{:S(2)}, u32[]{:S(2)}) async-start(bf16[8,80,128]{2,1,0:T(8,128)(2,1)} %broadcast_in_dim.159), calls=%async_computation | async-start | bytes 327680 | tf_op jit(solution)/shard_map/all_to_all | solution.py:105
  10.7 1.0 %copy-start.6 = (s32[2,32]{1,0:T(2,128)S(1)}, s32[2,32]{1,0:T(2,128)}, u32[]{:S(2)}) copy-start(s32[2,32]{1,0:T(2,128)} %param.18) | copy-start | bytes 772
  10.7 1.8 %copy-start.1 = (bf16[16,64,512]{2,1,0:T(8,128)(2,1)S(1)}, bf16[16,64,512]{2,1,0:T(8,128)(2,1)}, u32[]{:S(2)}) copy-start(bf16[16,64,512]{2,1,0:T(8,128)(2,1)} %param.17) | copy-start | bytes 3145732
  10.9 1.5 %copy-start.2 = (bf16[2,8,32,4,128]{4,2,1,3,0:T(8,128)(2,1)}, bf16[2,8,32,4,128]{4,2,1,3,0:T(8,128)(2,1)S(1)}, u32[]{:S(2)}) copy-start(bf16[2,8,32,4,128]{4,2,1,3,0:T(8,128)(2,1)S(1)} %copy_dynamic-update-slice_fusion) | copy-start | bytes 1572868
  11.6 6.8 %collective-permute-start = (bf16[2,8,32,2,128]{4,2,1,3,0:T(8,128)(2,1)}, bf16[2,8,32,2,128]{4,2,1,3,0:T(8,128)(2,1)}, u32[]{:S(2)}, u32[]{:S(2)}) collective-permute-start(bf16[2,8,32,2,128]{4,2,1,3,0:T(8,128)(2,1)} %constant_dynamic-slice_fusion.4), channel_id=1, source_target_pairs={{0,8},{8,0},{16,24},{24,16},{1,9},{9,1},{17,25},{25,17},{2,10},{10... | collective-permute-start | bytes 786440 | tf_op jit(solution)/shard_map/ppermute | solution.py:124
  12.5 0.7 %copy-start.7 = (s32[2]{0:T(128)S(1)}, s32[2]{0:T(128)}, u32[]{:S(2)}) copy-start(s32[2]{0:T(128)} %param.19) | copy-start | bytes 28
  14.0 3.5 %copy-start.3 = (bf16[2,8,32,4,128]{4,2,1,3,0:T(8,128)(2,1)S(1)}, bf16[2,8,32,4,128]{4,2,1,3,0:T(8,128)(2,1)}, u32[]{:S(2)}) copy-start(bf16[2,8,32,4,128]{4,2,1,3,0:T(8,128)(2,1)} %copy-done.2) | copy-start | bytes 1572868
  14.8 1.5 %collective-permute-start.1 = (f32[2,2,2,8,130]{4,0,3,1,2:T(2,128)S(1)}, f32[2,2,2,8,130]{4,0,3,1,2:T(2,128)S(1)}, u32[]{:S(2)}, u32[]{:S(2)}) collective-permute-start(f32[2,2,2,8,130]{4,0,3,1,2:T(2,128)S(1)} %fusion.23), channel_id=1, source_target_pairs={{0,8},{8,0},{16,24},{24,16},{1,9},{9,1},{17,25},{25,17},{2,10},{10... | collective-permute-start | bytes 99848 | tf_op jit(solution)/shard_map/ppermute | solution.py:153
  23.2 8.1 %copy-start.8 = (bf16[2,2,512]{2,1,0:T(2,128)(2,1)S(1)}, bf16[2,2,512]{2,1,0:T(2,128)(2,1)}, u32[]{:S(2)}) copy-start(bf16[2,2,512]{2,1,0:T(2,128)(2,1)} %param.20) | copy-start | bytes 12292
  23.6 8.4 %copy-start.5 = (bf16[2,2,512]{2,1,0:T(2,128)(2,1)S(1)}, bf16[2,2,512]{2,1,0:T(2,128)(2,1)}, u32[]{:S(2)}) copy-start(bf16[2,2,512]{2,1,0:T(2,128)(2,1)} %param.21) | copy-start | bytes 12292
  24.6 17.7 %all-to-all-start.1 = ((f32[32,1,2176]{2,1,0:T(1,128)}), f32[32,1,2176]{2,1,0:T(1,128)S(1)}, u32[]{:S(2)}, u32[]{:S(2)}) async-start(f32[32,1,2176]{2,1,0:T(1,128)} %reshape.302), calls=%async_computation.1 | async-start | bytes 557056 | tf_op jit(solution)/shard_map/all_to_all | solution.py:181

commit v20 on v16

--- a/solution.py
+++ b/solution.py
@@ -124,19 +124,26 @@
     partner_kv = lax.ppermute(given_kv, "ctx", swap)
 
 
-    def prefix_block(kv):
-        row_kv = jnp.take(kv, every_prefix, axis=1)
-        row_keys, row_values = row_kv[0], row_kv[1]
-        scores = (
-            jnp.einsum(
-                "rskgd,rtkd->rskgt", half_query, row_keys, preferred_element_type=jnp.float32
-            )
-            * score_scale
+    kv_pair = jnp.concatenate([own_kv, partner_kv], axis=2)
+    row_kv = jnp.take(kv_pair, every_prefix, axis=1).reshape(
+        2, total_rows, 2, span_len, half_kv, HD
+    )
+    pair_scores = (
+        jnp.einsum(
+            "rskgd,rbtkd->rskgbt", half_query, row_kv[0], preferred_element_type=jnp.float32
         )
-        always = jnp.ones((1, 1, 1, 1, span_len), dtype=bool)
-        return block_stats(scores, always, row_values, "rskgt,rtkd->rskgd")
-
-    prefix_stats = combine_pair(prefix_block(own_kv), prefix_block(partner_kv))
+        * score_scale
+    )
+    pair_peak = jnp.max(pair_scores, axis=-1)
+    pair_weights = jnp.exp(pair_scores - pair_peak[..., None]).astype(jnp.bfloat16)
+    pair_total = jnp.sum(pair_weights.astype(jnp.float32), axis=-1)
+    pair_sum = jnp.einsum(
+        "rskgbt,rbtkd->rskgbd", pair_weights, row_kv[1], preferred_element_type=jnp.float32
+    )
+    prefix_stats = combine_pair(
+        (pair_peak[..., 0], pair_total[..., 0], pair_sum[..., 0, :]),
+        (pair_peak[..., 1], pair_total[..., 1], pair_sum[..., 1, :]),
+    )
 
     def head_half(member, at):
         return lax.dynamic_slice_in_dim(member, at * half_kv, half_kv, 2)

time: 47.6 us -> 51.1 us (1.074)
  starting transfers between devices: 11.4 us -> 14.3 us
  waiting for transfers between devices: 12.8 us -> 11 us
  other arithmetic: 3.31 us -> 4.57 us
  local copies, waits for them, and re-layouts: 11.6 us -> 12.6 us
    all_to_all x1, starting transfers between devices: 3.84 us -> 6.51 us  [per_device(): lax.all_to_all(outgoing.reshape(dests, 1, (chunk + pt_rows) * LANES), ('r...]
    all_to_all x1, waiting for transfers between devices: 2.22 us -> 0.49 us  [per_device(): lax.all_to_all(fanned, 'row', split_axis=0, concat_axis=0, tiled=True)]
    concatenate x0 -> x1, other arithmetic: none -> 1.01 us  [per_device(): kv_pair = jnp.concatenate([own_kv, partner_kv], axis=2)]
    unnamed x21 -> x27, local copies, waits for them, and re-layouts: 2.91 us -> 3.67 us
    dynamic_slice x1, local copies, waits for them, and re-layouts: 0.77 us -> 0.04 us  [per_device(): own_kv = lax.dynamic_slice_in_dim(kv_both, core_bit * half_kv, half_kv, 3)]
    gather x2 -> x1, local copies, waits for them, and re-layouts: 1.3 us -> 0.75 us  [per_device(): jnp.take(kv_pair, every_prefix, axis=1)]
    dot_general x2, matrix products: 0.71 us -> 1.24 us  [the longest x1 0.91 us: per_device(): jnp.einsum('rskgd,rbtkd->rskgbt', half_query, row_kv[0], preferred_elemen...]
    dynamic_update_slice x3 -> x5, local copies, waits for them, and re-layouts: 0.05 us -> 0.59 us  [per_device(): lax.dynamic_update_slice_in_dim(whole_arr, piece_arr, row_start, 0)]
where the time goes in v20:
time: 51.1 us; the launch traced here: 50.6 us
  starting transfers between devices  14.3 us (28%)
  local copies, waits for them, and re-layouts  12.6 us (25%)
  waiting for transfers between devices  11 us (22%)
  blocking collectives  5.18 us (10%)
  other arithmetic  4.57 us (9%)
  matrix products  2.56 us (5%)
    all_to_all x1, waiting for transfers between devices, per_device(): lax.all_to_all(outgoing.reshape(dests, 1, (chunk + pt_rows) * LANES), ('r...  9.51 us
    all_to_all x1, starting transfers between devices, per_device(): lax.all_to_all(fanned, 'row', split_axis=0, concat_axis=0, tiled=True)  7.25 us
    all_to_all x1, starting transfers between devices, per_device(): lax.all_to_all(outgoing.reshape(dests, 1, (chunk + pt_rows) * LANES), ('r...  6.51 us
    all_gather x1, blocking collectives, per_device(): whole = lax.all_gather(result, 'ctx', axis=0, tiled=False)  5.18 us
    unnamed x27, local copies, waits for them, and re-layouts  3.67 us
    another operation x3, local copies, waits for them, and re-layouts, per_device(): jnp.stack([prefix_keys.reshape(prefix_count, span_len, KVH, HD), prefix_v...  1.23 us
    reshape x1, local copies, waits for them, and re-layouts, per_device(): flat_values = pool_values.reshape(slot_count * page_len, KVH, HD)  1.12 us
  transfers between devices with their start and end apart: 4, of which 3 were waited for; matrix products, arithmetic and copies ran while one was open for 14% of the time, Pallas kernels for 0%

profile of v20, /device:TPU:0, one launch (start us, length us, event | category | flops | bytes accessed | tf_op | source)
XLA Modules:
  0.0 50.6 jit_solution(12740560464071468074)
XLA Ops:
  0.0 1.1 %stack_reshape.6 = bf16[1,8,32,4,128]{4,3,2,1,0:T(4,128)(2,1)S(1)} reshape(bf16[8,32,512]{2,1,0:T(8,128)(2,1)} %param.14) | data formatting | bytes 524288 | tf_op jit(solution)/shard_map/stack;reshape | solution.py:116
  1.2 0.9 %copy-done.3 = bf16[8,32,512]{2,1,0:T(8,128)(2,1)S(1)} copy-done((bf16[8,32,512]{2,1,0:T(8,128)(2,1)S(1)}, bf16[8,32,512]{2,1,0:T(8,128)(2,1)}, u32[]{:S(2)}) %copy-start.3) | copy-done | bytes 262168
  2.3 0.5 %collective-permute-start = (bf16[2,8,32,2,128]{4,2,3,1,0:T(8,128)(2,1)S(1)}, bf16[2,8,32,2,128]{4,2,3,1,0:T(8,128)(2,1)}, u32[]{:S(2)}, u32[]{:S(2)}) collective-permute-start(bf16[2,8,32,2,128]{4,2,3,1,0:T(8,128)(2,1)S(1)} %get-tuple-element.34), channel_id=1, source_target_pairs={{0,8},{8,0},{16,24},{24,16},{1,9},{9,1},{17,25},{25,17},{2,10},{10... | collective-permute-start | bytes 786440 | tf_op jit(solution)/shard_map/ppermute | solution.py:124
  2.8 0.3 copy-done.4
  3.1 0.6 %copy-done.9 = s32[2]{0:T(128)S(1)} copy-done((s32[2]{0:T(128)S(1)}, s32[2]{0:T(128)}, u32[]{:S(2)}) %copy-start.9) | copy-done | bytes 32
  3.9 0.7 %broadcast_in_dim.121 = bf16[8,80,128]{2,1,0:T(8,128)(2,1)} broadcast(bf16[80,128]{1,0:T(8,128)(2,1)S(1)} %pad_maximum_fusion.2), dimensions={1,2} | broadcast | bytes 184320 | tf_op jit(solution)/shard_map/broadcast_in_dim | solution.py:104
  4.6 7.3 %all-to-all-start = ((bf16[8,80,128]{2,1,0:T(8,128)(2,1)}), bf16[8,80,128]{2,1,0:T(8,128)(2,1)S(1)}, u32[]{:S(2)}, u32[]{:S(2)}) async-start(bf16[8,80,128]{2,1,0:T(8,128)(2,1)} %broadcast_in_dim.121), calls=%async_computation | async-start | bytes 327680 | tf_op jit(solution)/shard_map/all_to_all | solution.py:105
  11.9 0.7 %copy-done.6 = s32[2,32]{1,0:T(2,128)S(1)} copy-done((s32[2,32]{1,0:T(2,128)S(1)}, s32[2,32]{1,0:T(2,128)}, u32[]{:S(2)}) %copy-start.6) | copy-done | bytes 280
  12.5 0.2 fusion.21
  12.7 0.2 compare_reduce_fusion
  13.2 0.1 and.34
  13.3 1.1 %reshape.247 = bf16[1024,4,128]{2,1,0:T(4,128)(2,1)} reshape(bf16[16,64,512]{2,1,0:T(8,128)(2,1)S(1)} %copy-done.1) | data formatting | bytes 2097152 | tf_op jit(solution)/shard_map/reshape | solution.py:70
  14.5 0.6 %select_reduce_fusion = (f32[2,2,4,8]{3,2,1,0:T(4,128)S(1)}, f32[2,2,4,8,1024]{4,3,2,1,0:T(8,128)S(1)}) fusion(pred[2,1024]{1,0:T(4,128)(4,1)S(1)} %compare_and_fusion, bf16[1024,512,1,1,1]{1,0,4,3,2:T(8,128)(2,1)S(1)} %bitcast.153, pred[4,4]{1,0:T(4,128)(4,1)S(1)} %iota_compare_fusion.1, bf16[2,2,4,8,128]{4,3,2,1,0:T(8,128)(2,1)S(1)} %reshape.243), kind=kOutput, calls=%fused_computation.15 | convolution fusion | flops 134676352 | bytes 1608208 | tf_op jit(solution)/shard_map/rskgw,tw->rskgt/dot_general | solution.py:78
  15.1 0.3 convert_reduce_fusion.1
  15.4 0.2 copy.208
  15.5 0.2 copy.207
  15.8 0.3 fusion.2
  16.0 0.1 fusion.13
  16.2 0.1 copy.252
  16.3 0.1 copy.255
  16.4 1.0 %collective-permute-done.1 = f32[2,2,2,8,130]{4,3,1,2,0:T(8,128)S(1)} collective-permute-done((f32[2,2,2,8,130]{4,3,1,2,0:T(8,128)S(1)}, f32[2,2,2,8,130]{4,3,1,2,0:T(8,128)S(1)}, u32[]{:S(2)}, u32[]{:S(2)}) %collective-permute-start.1) | collective-permute-done | bytes 33312 | tf_op jit(solution)/shard_map/ppermute | solution.py:154
  17.5 0.1 copy.209
  17.6 0.1 copy.210
  17.7 0.1 copy.222
  17.8 0.1 copy.223
  17.9 1.0 %pad_maximum_fusion = bf16[2,8,64,2,128]{4,2,3,1,0:T(8,128)(2,1)S(1)} fusion(bf16[2,8,32,2,128]{4,2,3,1,0:T(8,128)(2,1)} %collective-permute-done, bf16[2,8,32,2,128]{4,2,3,1,0:T(8,128)(2,1)S(1)} %get-tuple-element.33), kind=kLoop, calls=%fused_computation.11 | loop fusion | flops 1048576 | bytes 1048576 | tf_op jit(solution)/shard_map/concatenate | solution.py:127
  18.9 0.5 all-to-all-done
  19.4 0.2 convert_reduce_fusion.3
  19.8 0.7 %gather_fusion = bf16[16,2,64,2,128]{4,2,3,1,0:T(8,128)(2,1)S(1)} fusion(bf16[2,8,64,2,128]{4,2,3,1,0:T(8,128)(2,1)S(1)} %pad_maximum_fusion, s32[1024]{0:T(1024)S(1)} %pad_clamp_fusion), kind=kCustom, calls=%fused_computation | custom fusion | bytes 2097216 | tf_op jit(solution)/shard_map/jit(_take)/gather | solution.py:128
  20.6 0.2 select_bitcast_fusion
  20.9 0.9 %fusion.42 = (f32[16,2,2,8,2]{3,1,4,2,0:T(2,128)S(1)}, f32[16,2,2,8,2,32]{5,3,1,4,2,0:T(8,128)S(1)}) fusion(bf16[16,2,32,2,128,1]{4,2,5,1,3,0:T(8,128)(2,1)S(1)} %bitcast.154, bf16[16,2,2,8,128,1]{4,3,2,1,0,5:T(8,128)(2,1)S(1)} %bitcast.158), kind=kOutput, calls=%fused_computation.109 | convolution fusion | flops 8453120 | bytes 790528 | tf_op jit(solution)/shard_map/rskgd,rbtkd->rskgbt/dot_general | solution.py:132
  22.0 0.1 copy.200
  22.1 0.1 copy.202
  22.2 0.5 convert_reduce_fusion
  22.7 0.3 convolution_bitcast_fusion
  23.2 0.1 multiply_add_fusion
  23.3 0.1 copy.211
  23.4 0.1 copy.212
  23.5 0.1 copy.213
  23.6 0.1 copy.216
  23.7 0.2 fusion.5
  23.9 0.1 fusion.19
  24.0 0.2 dynamic_update_slice.10
  24.3 0.1 copy.218
  24.4 0.1 reshape.249
  24.5 0.2 dynamic_update_slice.11
  24.6 0.1 copy.224
  24.7 0.1 reshape.250
  24.9 1.0 %reshape.286 = f32[32,1,2176]{2,1,0:T(1,128)} reshape(f32[32,17,128]{2,1,0:T(8,128)S(1)} %pad_maximum_fusion.1) | data formatting | bytes 557056 | tf_op jit(solution)/shard_map/reshape | solution.py:183
  25.9 6.5 %all-to-all-start.1 = ((f32[32,1,2176]{2,1,0:T(1,128)}), f32[32,1,2176]{2,1,0:T(1,128)S(1)}, u32[]{:S(2)}, u32[]{:S(2)}) async-start(f32[32,1,2176]{2,1,0:T(1,128)} %reshape.286), calls=%async_computation.1 | async-start | bytes 557056 | tf_op jit(solution)/shard_map/all_to_all | solution.py:182
  32.4 0.3 select_reduce_fusion.1
  32.7 0.1 reshape.257
  32.8 0.1 reshape.258
  32.9 0.1 convert_reduce_fusion.2
  33.0 0.1 reshape.264
  33.1 0.1 reshape.265
  33.2 0.6 %copy-done.5 = bf16[2,2,512]{2,1,0:T(2,128)(2,1)S(1)} copy-done((bf16[2,2,512]{2,1,0:T(2,128)(2,1)S(1)}, bf16[2,2,512]{2,1,0:T(2,128)(2,1)}, u32[]{:S(2)}) %copy-start.5) | copy-done | bytes 4120
  33.8 0.2 convolution_bitcast_fusion.1
  34.0 9.5 %all-to-all-done.1 = f32[32,1,2176]{2,1,0:T(1,128)S(1)} async-done(((f32[32,1,2176]{2,1,0:T(1,128)}), f32[32,1,2176]{2,1,0:T(1,128)S(1)}, u32[]{:S(2)}, u32[]{:S(2)}) %all-to-all-start.1) | async-done | bytes 278560 | tf_op jit(solution)/shard_map/all_to_all | solution.py:182
  43.5 0.7 %reduce.7 = f32[32,2176]{1,0:T(8,128)S(1)} reduce(f32[32,1,2176]{2,1,0:T(1,128)S(1)} %all-to-all-done.1, f32[]{:T(128)} %constant.102), dimensions={1}, to_apply=%all_to_all.7.reduce_sub_computation | reduce | bytes 557060 | tf_op jit(solution)/shard_map/all_to_all | solution.py:182
  44.6 0.1 multiply_reduce_fusion
  44.7 0.1 divide_convert_fusion
  44.8 5.2 %all-gather = bf16[8,16,128]{2,1,0:T(8,128)(2,1)S(1)} all-gather(bf16[2,16,128]{2,1,0:T(8,128)(2,1)S(1)} %divide_convert_fusion), channel_id=2, replica_groups=mesh['ctx'=4,'row'=8] {'ctx'}, dimensions={0}, use_global_device_ids=true | all-gather | bytes 40960 | tf_op jit(solution)/shard_map/all_gather | solution.py:216
  50.0 0.6 %reshape.267 = bf16[2,2,4096]{2,1,0:T(2,128)(2,1)} reshape(bf16[2,2,2,16,128]{4,3,2,1,0:T(8,128)(2,1)S(1)} %bitcast.165) | data formatting | bytes 65536 | tf_op jit(solution)/shard_map/reshape | solution.py:219
  (71 shorter events, 2.2 us)
Async XLA Ops:
  0.0 14.5 %copy-start = (bf16[16,64,512]{2,1,0:T(8,128)(2,1)S(1)}, bf16[16,64,512]{2,1,0:T(8,128)(2,1)}, u32[]{:S(2)}) copy-start(bf16[16,64,512]{2,1,0:T(8,128)(2,1)} %param.16) | copy-start | bytes 3145732
  1.1 1.0 %copy-start.3 = (bf16[8,32,512]{2,1,0:T(8,128)(2,1)S(1)}, bf16[8,32,512]{2,1,0:T(8,128)(2,1)}, u32[]{:S(2)}) copy-start(bf16[8,32,512]{2,1,0:T(8,128)(2,1)} %param.15) | copy-start | bytes 786436
  2.1 11.2 %copy-start.1 = (bf16[16,64,512]{2,1,0:T(8,128)(2,1)S(1)}, bf16[16,64,512]{2,1,0:T(8,128)(2,1)}, u32[]{:S(2)}) copy-start(bf16[16,64,512]{2,1,0:T(8,128)(2,1)} %param.17) | copy-start | bytes 3145732
  2.2 0.8 %copy-start.4 = (bf16[2,2,4096]{2,1,0:T(2,128)(2,1)S(1)}, bf16[2,2,4096]{2,1,0:T(2,128)(2,1)}, u32[]{:S(2)}) copy-start(bf16[2,2,4096]{2,1,0:T(2,128)(2,1)} %param.12) | copy-start | bytes 98308
  2.3 15.6 %collective-permute-start = (bf16[2,8,32,2,128]{4,2,3,1,0:T(8,128)(2,1)S(1)}, bf16[2,8,32,2,128]{4,2,3,1,0:T(8,128)(2,1)}, u32[]{:S(2)}, u32[]{:S(2)}) collective-permute-start(bf16[2,8,32,2,128]{4,2,3,1,0:T(8,128)(2,1)S(1)} %get-tuple-element.34), channel_id=1, source_target_pairs={{0,8},{8,0},{16,24},{24,16},{1,9},{9,1},{17,25},{25,17},{2,10},{10... | collective-permute-start | bytes 786440 | tf_op jit(solution)/shard_map/ppermute | solution.py:124
  3.1 0.7 %copy-start.9 = (s32[2]{0:T(128)S(1)}, s32[2]{0:T(128)}, u32[]{:S(2)}) copy-start(s32[2]{0:T(128)} %param.13) | copy-start | bytes 28
  4.6 14.8 %all-to-all-start = ((bf16[8,80,128]{2,1,0:T(8,128)(2,1)}), bf16[8,80,128]{2,1,0:T(8,128)(2,1)S(1)}, u32[]{:S(2)}, u32[]{:S(2)}) async-start(bf16[8,80,128]{2,1,0:T(8,128)(2,1)} %broadcast_in_dim.121), calls=%async_computation | async-start | bytes 327680 | tf_op jit(solution)/shard_map/all_to_all | solution.py:105
  11.9 0.7 %copy-start.6 = (s32[2,32]{1,0:T(2,128)S(1)}, s32[2,32]{1,0:T(2,128)}, u32[]{:S(2)}) copy-start(s32[2,32]{1,0:T(2,128)} %param.18) | copy-start | bytes 772
  13.3 1.1 %copy-start.7 = (s32[2]{0:T(128)S(1)}, s32[2]{0:T(128)}, u32[]{:S(2)}) copy-start(s32[2]{0:T(128)} %param.19) | copy-start | bytes 28
  14.5 1.2 %copy-start.2 = (bf16[1024,4,128]{2,1,0:T(4,128)(2,1)S(1)}, bf16[1024,4,128]{2,1,0:T(4,128)(2,1)}, u32[]{:S(2)}) copy-start(bf16[1024,4,128]{2,1,0:T(4,128)(2,1)} %reshape.247) | copy-start | bytes 3145732
  16.1 1.3 %collective-permute-start.1 = (f32[2,2,2,8,130]{4,3,1,2,0:T(8,128)S(1)}, f32[2,2,2,8,130]{4,3,1,2,0:T(8,128)S(1)}, u32[]{:S(2)}, u32[]{:S(2)}) collective-permute-start(f32[2,2,2,8,130]{4,3,1,2,0:T(8,128)S(1)} %fusion.13), channel_id=1, source_target_pairs={{0,8},{8,0},{16,24},{24,16},{1,9},{9,1},{17,25},{25,17},{2,10},{10... | collective-permute-start | bytes 99848 | tf_op jit(solution)/shard_map/ppermute | solution.py:154
  25.9 6.5 %copy-start.8 = (bf16[2,2,512]{2,1,0:T(2,128)(2,1)S(1)}, bf16[2,2,512]{2,1,0:T(2,128)(2,1)}, u32[]{:S(2)}) copy-start(bf16[2,2,512]{2,1,0:T(2,128)(2,1)} %param.20) | copy-start | bytes 12292
  25.9 17.6 %all-to-all-start.1 = ((f32[32,1,2176]{2,1,0:T(1,128)}), f32[32,1,2176]{2,1,0:T(1,128)S(1)}, u32[]{:S(2)}, u32[]{:S(2)}) async-start(f32[32,1,2176]{2,1,0:T(1,128)} %reshape.286), calls=%async_computation.1 | async-start | bytes 557056 | tf_op jit(solution)/shard_map/all_to_all | solution.py:182
  33.1 0.7 %copy-start.5 = (bf16[2,2,512]{2,1,0:T(2,128)(2,1)S(1)}, bf16[2,2,512]{2,1,0:T(2,128)(2,1)}, u32[]{:S(2)}) copy-start(bf16[2,2,512]{2,1,0:T(2,128)(2,1)} %param.21) | copy-start | bytes 12292

commit v21 on v16

--- a/solution.py
+++ b/solution.py
@@ -179,17 +179,17 @@
         concat_axis=0,
         tiled=True,
     )
-    incoming = incoming.reshape(dests, chunk + pt_rows, LANES)
-    got_pt = incoming[:, chunk:, :].reshape(dests, pt_rows * LANES)
+    incoming = incoming.reshape(dests, (chunk + pt_rows) * LANES)
+    got_pt = incoming[:, chunk * HD : chunk * HD + 2 * chunk]
     pairs = ctx_count // 2
 
-    def by_half(member, tail=()):
-        shaped = member.reshape((row_count, pairs, 2, chunk) + tail)
-        return jnp.moveaxis(shaped, 2, 0).reshape((2, row_count * pairs, chunk) + tail)
+    def by_half(member):
+        shaped = member.reshape((row_count, pairs, 2) + member.shape[1:])
+        return jnp.moveaxis(shaped, 2, 0).reshape((2, row_count * pairs) + member.shape[1:])
 
     got_peak = by_half(got_pt[:, :chunk])
     got_total = by_half(got_pt[:, chunk : 2 * chunk])
-    got_sum = by_half(incoming[:, :chunk, :], (HD,))
+    got_sum = by_half(incoming[:, : chunk * HD])
 
     def fresh_chunk(member, tail=()):
         shaped = member.reshape((rows_dev, step_count, 2, half_heads) + tail)
@@ -204,7 +204,9 @@
     factor = jnp.exp(got_peak - top[:, None])
     fresh_factor = jnp.exp(fresh_peak - top)
     denom = jnp.sum(factor * got_total, axis=1) + fresh_factor * fresh_total
-    numer = jnp.sum(factor[..., None] * got_sum, axis=1) + fresh_factor[..., None] * fresh_sum
+    spread_factor = jnp.repeat(factor, HD, axis=2)
+    numer = jnp.sum(spread_factor * got_sum, axis=1).reshape(2, chunk, HD)
+    numer = numer + fresh_factor[..., None] * fresh_sum
     result = (numer / denom[..., None]).astype(jnp.bfloat16)
     whole = lax.all_gather(result, "ctx", axis=0, tiled=False)
     whole = jnp.swapaxes(whole, 0, 1).reshape(2, rows_dev, step_count, half_heads, HD)

time: 47.6 us -> 47.3 us (level)
  other arithmetic: 3.31 us -> 2.69 us
    all_to_all x1 -> x0, other arithmetic: 0.65 us -> none  [per_device(): lax.all_to_all(outgoing.reshape(dests, 1, (chunk + pt_rows) * LANES), ('r...]
    unnamed x21 -> x23, local copies, waits for them, and re-layouts: 2.91 us -> 2.93 us
where the time goes in v21:
time: 47.3 us; the launch traced here: 46.9 us
  waiting for transfers between devices  12.8 us (27%)
  local copies, waits for them, and re-layouts  11.9 us (25%)
  starting transfers between devices  11.4 us (24%)
  blocking collectives  5.18 us (11%)
  other arithmetic  2.69 us (6%)
  matrix products  2.56 us (5%)
    all_to_all x1, waiting for transfers between devices, per_device(): lax.all_to_all(outgoing.reshape(dests, 1, (chunk + pt_rows) * LANES), ('r...  9.51 us
    all_to_all x1, starting transfers between devices, per_device(): lax.all_to_all(fanned, 'row', split_axis=0, concat_axis=0, tiled=True)  6.9 us
    all_gather x1, blocking collectives, per_device(): whole = lax.all_gather(result, 'ctx', axis=0, tiled=False)  5.18 us
    all_to_all x1, starting transfers between devices, per_device(): lax.all_to_all(outgoing.reshape(dests, 1, (chunk + pt_rows) * LANES), ('r...  3.84 us
    unnamed x23, local copies, waits for them, and re-layouts  2.93 us
    all_to_all x1, waiting for transfers between devices, per_device(): lax.all_to_all(fanned, 'row', split_axis=0, concat_axis=0, tiled=True)  2.22 us
    gather x2, local copies, waits for them, and re-layouts, prefix_block(): row_kv = jnp.take(kv, every_prefix, axis=1)  1.3 us
    another operation x3, local copies, waits for them, and re-layouts, per_device(): jnp.stack([prefix_keys.reshape(prefix_count, span_len, KVH, HD), prefix_v...  1.23 us
  transfers between devices with their start and end apart: 4, of which 3 were waited for; matrix products, arithmetic and copies ran while one was open for 14% of the time, Pallas kernels for 0%

profile of v21, /device:TPU:0, one launch (start us, length us, event | category | flops | bytes accessed | tf_op | source)
XLA Modules:
  0.0 46.9 jit_solution(16009743946842239331)
XLA Ops:
  0.0 1.1 %stack_reshape.6 = bf16[1,8,32,4,128]{4,3,2,1,0:T(4,128)(2,1)S(1)} reshape(bf16[8,32,512]{2,1,0:T(8,128)(2,1)} %param.16) | data formatting | bytes 524288 | tf_op jit(solution)/shard_map/stack;reshape | solution.py:116
  1.2 0.9 %copy-done.3 = bf16[8,32,512]{2,1,0:T(8,128)(2,1)S(1)} copy-done((bf16[8,32,512]{2,1,0:T(8,128)(2,1)S(1)}, bf16[8,32,512]{2,1,0:T(8,128)(2,1)}, u32[]{:S(2)}) %copy-start.3) | copy-done | bytes 262168
  2.2 0.8 %constant_dynamic-slice_fusion.8 = (bf16[2,8,32,2,128]{4,2,3,1,0:T(8,128)(2,1)S(1)}, bf16[2,8,32,2,128]{4,2,3,1,0:T(8,128)(2,1)}) fusion(bf16[2,8,32,4,128]{4,2,3,1,0:T(8,128)(2,1)S(1)} %copy_dynamic-update-slice_fusion, s32[]{:T(128)S(6)} %select_n.76, s32[]{:T(128)S(6)} %select_n.77), kind=kLoop, calls=%fused_computation.87 | loop fusion | bytes 1048584 | tf_op jit(solution)/shard_map/dynamic_slice | solution.py:122
  3.0 0.5 collective-permute-start
  3.5 0.6 %copy-done.9 = s32[2]{0:T(128)S(1)} copy-done((s32[2]{0:T(128)S(1)}, s32[2]{0:T(128)}, u32[]{:S(2)}) %copy-start.9) | copy-done | bytes 32
  4.2 0.1 compare_select_fusion.2
  4.2 0.1 pad_maximum_fusion.1
  4.3 0.7 %broadcast_in_dim.145 = bf16[8,80,128]{2,1,0:T(8,128)(2,1)} broadcast(bf16[80,128]{1,0:T(8,128)(2,1)S(1)} %pad_maximum_fusion.1), dimensions={1,2} | broadcast | bytes 184320 | tf_op jit(solution)/shard_map/broadcast_in_dim | solution.py:104
  5.0 6.9 %all-to-all-start = ((bf16[8,80,128]{2,1,0:T(8,128)(2,1)}), bf16[8,80,128]{2,1,0:T(8,128)(2,1)S(1)}, u32[]{:S(2)}, u32[]{:S(2)}) async-start(bf16[8,80,128]{2,1,0:T(8,128)(2,1)} %broadcast_in_dim.145), calls=%async_computation | async-start | bytes 327680 | tf_op jit(solution)/shard_map/all_to_all | solution.py:105
  11.9 0.7 %copy-done.6 = s32[2,32]{1,0:T(2,128)S(1)} copy-done((s32[2,32]{1,0:T(2,128)S(1)}, s32[2,32]{1,0:T(2,128)}, u32[]{:S(2)}) %copy-start.6) | copy-done | bytes 280
  12.6 0.2 fusion.26
  12.8 0.2 compare_reduce_fusion
  13.0 0.1 add.106
  13.1 0.1 and.29
  13.2 0.1 and.30
  13.4 1.1 %reshape.233 = bf16[1024,4,128]{2,1,0:T(4,128)(2,1)} reshape(bf16[16,64,512]{2,1,0:T(8,128)(2,1)S(1)} %copy-done.1) | data formatting | bytes 2097152 | tf_op jit(solution)/shard_map/reshape | solution.py:70
  14.5 0.1 compare_and_fusion
  14.6 0.6 %select_reduce_fusion = (f32[2,2,4,8]{3,2,1,0:T(4,128)S(1)}, f32[2,2,4,8,1024]{4,3,2,1,0:T(8,128)S(1)}) fusion(pred[2,1024]{1,0:T(4,128)(4,1)S(1)} %compare_and_fusion, bf16[1024,512,1,1,1]{1,0,4,3,2:T(8,128)(2,1)S(1)} %bitcast.160, pred[4,4]{1,0:T(4,128)(4,1)S(1)} %iota_compare_fusion.1, bf16[2,2,4,8,128]{4,3,2,1,0:T(8,128)(2,1)S(1)} %reshape.229), kind=kOutput, calls=%fused_computation.23 | convolution fusion | flops 134676352 | bytes 1608208 | tf_op jit(solution)/shard_map/rskgw,tw->rskgt/dot_general | solution.py:78
  15.2 0.3 convert_reduce_fusion
  15.4 0.2 copy.169
  15.6 0.2 copy.168
  15.8 0.3 fusion.6
  16.1 0.1 fusion.18
  16.2 0.2 collective-permute-start.1
  16.4 1.1 %collective-permute-done.1 = f32[2,2,2,8,130]{4,3,1,2,0:T(8,128)S(1)} collective-permute-done((f32[2,2,2,8,130]{4,3,1,2,0:T(8,128)S(1)}, f32[2,2,2,8,130]{4,3,1,2,0:T(8,128)S(1)}, u32[]{:S(2)}, u32[]{:S(2)}) %collective-permute-start.1) | collective-permute-done | bytes 33312 | tf_op jit(solution)/shard_map/ppermute | solution.py:147
  17.4 0.1 fusion.43
  17.5 0.1 copy.203
  17.6 0.1 copy.205
  17.8 2.2 %all-to-all-done = bf16[8,80,128]{2,1,0:T(8,128)(2,1)S(1)} async-done(((bf16[8,80,128]{2,1,0:T(8,128)(2,1)}), bf16[8,80,128]{2,1,0:T(8,128)(2,1)S(1)}, u32[]{:S(2)}, u32[]{:S(2)}) %all-to-all-start) | async-done | bytes 163872 | tf_op jit(solution)/shard_map/all_to_all | solution.py:105
  20.0 0.2 convert_reduce_fusion.4
  20.2 0.1 reshape.254
  20.3 0.6 %gather_fusion = bf16[16,2,32,2,128]{4,2,3,1,0:T(8,128)(2,1)S(1)} fusion(bf16[2,8,32,2,128]{4,2,3,1,0:T(8,128)(2,1)S(1)} %get-tuple-element.33, s32[1024]{0:T(1024)S(1)} %pad_clamp_fusion), kind=kCustom, calls=%fused_computation.clone | custom fusion | bytes 1048640 | tf_op jit(solution)/shard_map/jit(_take)/gather | solution.py:128
  21.0 0.6 %gather_fusion.1 = bf16[16,2,32,2,128]{4,2,3,1,0:T(8,128)(2,1)S(1)} fusion(bf16[2,8,32,2,128]{4,2,3,1,0:T(8,128)(2,1)S(1)} %collective-permute-done, s32[1024]{0:T(1024)S(1)} %pad_clamp_fusion), kind=kCustom, calls=%fused_computation.1.clone | custom fusion | bytes 1048640 | tf_op jit(solution)/shard_map/jit(_take)/gather | solution.py:128
  21.6 0.2 fusion.9
  21.8 0.4 fusion.45
  22.2 0.4 fusion.44
  22.5 0.5 convert_reduce_fusion.1
  23.1 0.3 fusion.2
  23.3 0.3 fusion.1
  23.6 0.1 fusion.24
  23.8 0.1 reshape.235
  23.9 0.1 reshape.236
  24.0 0.1 select_maximum_fusion
  24.1 1.0 %reshape.286 = f32[32,1,2176]{2,1,0:T(1,128)} reshape(f32[32,17,128]{2,1,0:T(8,128)S(1)} %pad_maximum_fusion) | data formatting | bytes 557056 | tf_op jit(solution)/shard_map/reshape | solution.py:176
  25.1 3.8 %all-to-all-start.1 = ((f32[32,1,2176]{2,1,0:T(1,128)}), f32[32,1,2176]{2,1,0:T(1,128)S(1)}, u32[]{:S(2)}, u32[]{:S(2)}) async-start(f32[32,1,2176]{2,1,0:T(1,128)} %reshape.286), calls=%async_computation.1 | async-start | bytes 557056 | tf_op jit(solution)/shard_map/all_to_all | solution.py:175
  29.0 0.3 select_reduce_fusion.1
  29.3 0.1 reshape.243
  29.3 0.1 reshape.244
  29.4 0.1 convert_reduce_fusion.3
  29.5 0.1 reshape.250
  29.6 0.1 reshape.251
  29.7 0.6 %copy-done.5 = bf16[2,2,512]{2,1,0:T(2,128)(2,1)S(1)} copy-done((bf16[2,2,512]{2,1,0:T(2,128)(2,1)S(1)}, bf16[2,2,512]{2,1,0:T(2,128)(2,1)}, u32[]{:S(2)}) %copy-start.5) | copy-done | bytes 4120
  30.3 0.2 convolution_bitcast_fusion.2
  30.5 9.5 %all-to-all-done.1 = f32[32,1,2176]{2,1,0:T(1,128)S(1)} async-done(((f32[32,1,2176]{2,1,0:T(1,128)}), f32[32,1,2176]{2,1,0:T(1,128)S(1)}, u32[]{:S(2)}, u32[]{:S(2)}) %all-to-all-start.1) | async-done | bytes 278560 | tf_op jit(solution)/shard_map/all_to_all | solution.py:175
  40.1 0.1 fusion.42
  40.2 0.1 fusion.39
  40.3 0.1 broadcast_in_dim.158
  40.5 0.1 broadcast_in_dim.159
  40.6 0.1 reshape.245
  40.8 0.1 fusion.38
  40.8 0.1 fusion.10
  41.0 0.1 fusion.28
  41.1 5.2 %all-gather = bf16[8,16,128]{2,1,0:T(8,128)(2,1)S(1)} all-gather(bf16[2,16,128]{2,1,0:T(8,128)(2,1)S(1)} %fusion.28), channel_id=2, replica_groups=mesh['ctx'=4,'row'=8] {'ctx'}, dimensions={0}, use_global_device_ids=true | all-gather | bytes 40960 | tf_op jit(solution)/shard_map/all_gather | solution.py:211
  46.3 0.6 %reshape.253 = bf16[2,2,4096]{2,1,0:T(2,128)(2,1)} reshape(bf16[2,2,2,16,128]{4,3,2,1,0:T(8,128)(2,1)S(1)} %bitcast.172) | data formatting | bytes 65536 | tf_op jit(solution)/shard_map/reshape | solution.py:214
  (53 shorter events, 0.8 us)
Async XLA Ops:
  0.0 14.6 %copy-start = (bf16[16,64,512]{2,1,0:T(8,128)(2,1)S(1)}, bf16[16,64,512]{2,1,0:T(8,128)(2,1)}, u32[]{:S(2)}) copy-start(bf16[16,64,512]{2,1,0:T(8,128)(2,1)} %param.18) | copy-start | bytes 3145732
  1.1 1.0 %copy-start.3 = (bf16[8,32,512]{2,1,0:T(8,128)(2,1)S(1)}, bf16[8,32,512]{2,1,0:T(8,128)(2,1)}, u32[]{:S(2)}) copy-start(bf16[8,32,512]{2,1,0:T(8,128)(2,1)} %param.17) | copy-start | bytes 786436
  2.1 11.2 %copy-start.1 = (bf16[16,64,512]{2,1,0:T(8,128)(2,1)S(1)}, bf16[16,64,512]{2,1,0:T(8,128)(2,1)}, u32[]{:S(2)}) copy-start(bf16[16,64,512]{2,1,0:T(8,128)(2,1)} %param.19) | copy-start | bytes 3145732
  2.2 1.2 %copy-start.4 = (bf16[2,2,4096]{2,1,0:T(2,128)(2,1)S(1)}, bf16[2,2,4096]{2,1,0:T(2,128)(2,1)}, u32[]{:S(2)}) copy-start(bf16[2,2,4096]{2,1,0:T(2,128)(2,1)} %param.14) | copy-start | bytes 98308
  3.0 18.0 %collective-permute-start = (bf16[2,8,32,2,128]{4,2,3,1,0:T(8,128)(2,1)}, bf16[2,8,32,2,128]{4,2,3,1,0:T(8,128)(2,1)S(1)}, u32[]{:S(2)}, u32[]{:S(2)}) collective-permute-start(bf16[2,8,32,2,128]{4,2,3,1,0:T(8,128)(2,1)} %get-tuple-element.34), channel_id=1, source_target_pairs={{0,8},{8,0},{16,24},{24,16},{1,9},{9,1},{17,25},{25,17},{2,10},{10... | collective-permute-start | bytes 786440 | tf_op jit(solution)/shard_map/ppermute | solution.py:124
  3.5 0.7 %copy-start.9 = (s32[2]{0:T(128)S(1)}, s32[2]{0:T(128)}, u32[]{:S(2)}) copy-start(s32[2]{0:T(128)} %param.15) | copy-start | bytes 28
  5.0 15.0 %all-to-all-start = ((bf16[8,80,128]{2,1,0:T(8,128)(2,1)}), bf16[8,80,128]{2,1,0:T(8,128)(2,1)S(1)}, u32[]{:S(2)}, u32[]{:S(2)}) async-start(bf16[8,80,128]{2,1,0:T(8,128)(2,1)} %broadcast_in_dim.145), calls=%async_computation | async-start | bytes 327680 | tf_op jit(solution)/shard_map/all_to_all | solution.py:105
  11.9 0.7 %copy-start.6 = (s32[2,32]{1,0:T(2,128)S(1)}, s32[2,32]{1,0:T(2,128)}, u32[]{:S(2)}) copy-start(s32[2,32]{1,0:T(2,128)} %param.20) | copy-start | bytes 772
  13.4 1.1 %copy-start.7 = (s32[2]{0:T(128)S(1)}, s32[2]{0:T(128)}, u32[]{:S(2)}) copy-start(s32[2]{0:T(128)} %param.21) | copy-start | bytes 28
  14.6 1.2 %copy-start.2 = (bf16[1024,4,128]{2,1,0:T(4,128)(2,1)S(1)}, bf16[1024,4,128]{2,1,0:T(4,128)(2,1)}, u32[]{:S(2)}) copy-start(bf16[1024,4,128]{2,1,0:T(4,128)(2,1)} %reshape.233) | copy-start | bytes 3145732
  16.2 1.3 %collective-permute-start.1 = (f32[2,2,2,8,130]{4,3,1,2,0:T(8,128)S(1)}, f32[2,2,2,8,130]{4,3,1,2,0:T(8,128)S(1)}, u32[]{:S(2)}, u32[]{:S(2)}) collective-permute-start(f32[2,2,2,8,130]{4,3,1,2,0:T(8,128)S(1)} %fusion.18), channel_id=1, source_target_pairs={{0,8},{8,0},{16,24},{24,16},{1,9},{9,1},{17,25},{25,17},{2,10},{10... | collective-permute-start | bytes 99848 | tf_op jit(solution)/shard_map/ppermute | solution.py:147
  25.1 3.9 %copy-start.8 = (bf16[2,2,512]{2,1,0:T(2,128)(2,1)S(1)}, bf16[2,2,512]{2,1,0:T(2,128)(2,1)}, u32[]{:S(2)}) copy-start(bf16[2,2,512]{2,1,0:T(2,128)(2,1)} %param.22) | copy-start | bytes 12292
  25.1 14.9 %all-to-all-start.1 = ((f32[32,1,2176]{2,1,0:T(1,128)}), f32[32,1,2176]{2,1,0:T(1,128)S(1)}, u32[]{:S(2)}, u32[]{:S(2)}) async-start(f32[32,1,2176]{2,1,0:T(1,128)} %reshape.286), calls=%async_computation.1 | async-start | bytes 557056 | tf_op jit(solution)/shard_map/all_to_all | solution.py:175
  29.6 0.7 %copy-start.5 = (bf16[2,2,512]{2,1,0:T(2,128)(2,1)S(1)}, bf16[2,2,512]{2,1,0:T(2,128)(2,1)}, u32[]{:S(2)}) copy-start(bf16[2,2,512]{2,1,0:T(2,128)(2,1)} %param.23) | copy-start | bytes 12292

commit v22 on v21

--- a/solution.py
+++ b/solution.py
@@ -154,23 +154,22 @@
         lax.dynamic_slice_in_dim(member, row_start, rows_dev, 0) for member in prefix_stats
     )
     own_merged = combine_pair(own_prefix, suffix_half)
-    peak_all, total_all, sum_all = tuple(
-        lax.dynamic_update_slice_in_dim(whole_arr, piece_arr, row_start, 0)
-        for whole_arr, piece_arr in zip(prefix_stats, own_merged)
-    )
 
     half_units = rows_dev * step_count * half_heads
     chunk = half_units // ctx_count
     pt_rows = -(-2 * chunk // LANES)
     dests = ctx_count * row_count
 
-    def by_dest(member, tail=()):
-        return member.reshape((dests, chunk) + tail)
-
-    pt = jnp.concatenate([by_dest(peak_all), by_dest(total_all)], axis=-1)
-    pt = jnp.pad(pt, ((0, 0), (0, pt_rows * LANES - 2 * chunk)))
-    outgoing = jnp.concatenate(
-        [by_dest(sum_all, (HD,)), pt.reshape(dests, pt_rows, LANES)], axis=1
+    def pack(peak, total, sums):
+        count = peak.size // chunk
+        pt = jnp.concatenate([peak.reshape(count, chunk), total.reshape(count, chunk)], axis=-1)
+        pt = jnp.pad(pt, ((0, 0), (0, pt_rows * LANES - 2 * chunk)))
+        return jnp.concatenate(
+            [sums.reshape(count, chunk, HD), pt.reshape(count, pt_rows, LANES)], axis=1
+        )
+
+    outgoing = lax.dynamic_update_slice_in_dim(
+        pack(*prefix_stats), pack(*own_merged), row_index * ctx_count, 0
     )
     incoming = lax.all_to_all(
         outgoing.reshape(dests, 1, (chunk + pt_rows) * LANES),

time: 47.3 us -> 49.6 us (1.049)
  starting transfers between devices: 11.4 us -> 13.8 us
  waiting for transfers between devices: 12.8 us -> 11 us
  local copies, waits for them, and re-layouts: 11.9 us -> 13.4 us
    all_to_all x1, waiting for transfers between devices: 2.22 us -> 0.01 us  [per_device(): lax.all_to_all(fanned, 'row', split_axis=0, concat_axis=0, tiled=True)]
    all_to_all x1, starting transfers between devices: 3.84 us -> 6.04 us  [per_device(): lax.all_to_all(outgoing.reshape(dests, 1, (chunk + pt_rows) * LANES), ('r...]
    unnamed x23 -> x31, local copies, waits for them, and re-layouts: 2.93 us -> 4.24 us
    another operation x3, local copies, waits for them, and re-layouts: 1.23 us -> 0.2 us  [per_device(): jnp.stack([prefix_keys.reshape(prefix_count, span_len, KVH, HD), prefix_v...]
    reshape x1, local copies, waits for them, and re-layouts: 0.03 us -> 0.88 us  [per_device(): own_query = queries.reshape(rows_dev, step_count, KVH, groups, HD)]
    all_to_all x1, waiting for transfers between devices: 9.51 us -> 10.1 us  [per_device(): lax.all_to_all(outgoing.reshape(dests, 1, (chunk + pt_rows) * LANES), ('r...]
  transfers between devices with their start and end apart: 4 -> 4, of which waited for: 3 -> 2; matrix products, arithmetic and copies ran while one was open for 14% -> 14% of each run, Pallas kernels for 0% -> 0%
where the time goes in v22:
time: 49.6 us; the launch traced here: 49.2 us
  starting transfers between devices  13.8 us (28%)
  local copies, waits for them, and re-layouts  13.4 us (27%)
  waiting for transfers between devices  11 us (22%)
  blocking collectives  5.19 us (10%)
  other arithmetic  2.78 us (6%)
  matrix products  2.54 us (5%)
    all_to_all x1, waiting for transfers between devices, per_device(): lax.all_to_all(outgoing.reshape(dests, 1, (chunk + pt_rows) * LANES), ('r...  10.1 us
    all_to_all x1, starting transfers between devices, per_device(): lax.all_to_all(fanned, 'row', split_axis=0, concat_axis=0, tiled=True)  7.25 us
    all_to_all x1, starting transfers between devices, per_device(): lax.all_to_all(outgoing.reshape(dests, 1, (chunk + pt_rows) * LANES), ('r...  6.04 us
    all_gather x1, blocking collectives, per_device(): whole = lax.all_gather(result, 'ctx', axis=0, tiled=False)  5.19 us
    unnamed x31, local copies, waits for them, and re-layouts  4.24 us
    gather x2, local copies, waits for them, and re-layouts, prefix_block(): row_kv = jnp.take(kv, every_prefix, axis=1)  1.3 us
    reshape x1, local copies, waits for them, and re-layouts, per_device(): flat_values = pool_values.reshape(slot_count * page_len, KVH, HD)  1.12 us
  transfers between devices with their start and end apart: 4, of which 2 were waited for; matrix products, arithmetic and copies ran while one was open for 14% of the time, Pallas kernels for 0%

profile of v22, /device:TPU:0, one launch (start us, length us, event | category | flops | bytes accessed | tf_op | source)
XLA Modules:
  0.0 49.2 jit_solution(11829657760474528169)
XLA Ops:
  0.0 0.9 %reshape.243 = bf16[2,2,4,8,128]{4,3,2,1,0:T(8,128)(2,1)S(1)} reshape(bf16[2,2,4096]{2,1,0:T(2,128)(2,1)} %param.14) | data formatting | bytes 65536 | tf_op jit(solution)/shard_map/reshape | solution.py:56
  0.9 0.6 %copy-done.13 = s32[2]{0:T(128)S(1)} copy-done((s32[2]{0:T(128)S(1)}, s32[2]{0:T(128)}, u32[]{:S(2)}) %copy-start.13) | copy-done | bytes 32
  1.6 0.1 compare_select_fusion.2
  1.6 0.1 pad_maximum_fusion.1
  1.7 0.7 %broadcast_in_dim.145 = bf16[8,80,128]{2,1,0:T(8,128)(2,1)} broadcast(bf16[80,128]{1,0:T(8,128)(2,1)S(1)} %pad_maximum_fusion.1), dimensions={1,2} | broadcast | bytes 184320 | tf_op jit(solution)/shard_map/broadcast_in_dim | solution.py:104
  2.4 7.3 %all-to-all-start = ((bf16[8,80,128]{2,1,0:T(8,128)(2,1)}), bf16[8,80,128]{2,1,0:T(8,128)(2,1)S(1)}, u32[]{:S(2)}, u32[]{:S(2)}) async-start(bf16[8,80,128]{2,1,0:T(8,128)(2,1)} %broadcast_in_dim.145), calls=%async_computation | async-start | bytes 327680 | tf_op jit(solution)/shard_map/all_to_all | solution.py:105
  9.8 0.9 %copy-done.6 = bf16[8,32,512]{2,1,0:T(8,128)(2,1)S(1)} copy-done((bf16[8,32,512]{2,1,0:T(8,128)(2,1)S(1)}, bf16[8,32,512]{2,1,0:T(8,128)(2,1)}, u32[]{:S(2)}) %copy-start.6) | copy-done | bytes 262168
  10.8 0.8 %constant_dynamic-slice_fusion.11 = (bf16[2,8,32,2,128]{4,2,3,1,0:T(8,128)(2,1)S(1)}, bf16[2,8,32,2,128]{4,2,3,1,0:T(8,128)(2,1)}) fusion(bf16[2,8,32,4,128]{4,2,3,1,0:T(8,128)(2,1)S(1)} %copy_dynamic-update-slice_fusion, s32[]{:T(128)S(6)} %select_n.76, s32[]{:T(128)S(6)} %select_n.77), kind=kLoop, calls=%fused_computation.88 | loop fusion | bytes 1048584 | tf_op jit(solution)/shard_map/dynamic_slice | solution.py:122
  11.6 0.7 %copy-done.10 = s32[2,32]{1,0:T(2,128)S(1)} copy-done((s32[2,32]{1,0:T(2,128)S(1)}, s32[2,32]{1,0:T(2,128)}, u32[]{:S(2)}) %copy-start.10) | copy-done | bytes 280
  12.3 0.2 compare_reduce_fusion
  12.5 0.2 fusion.25
  12.7 0.1 and.30
  12.9 0.1 add.112
  13.1 1.1 %reshape.249 = bf16[1024,4,128]{2,1,0:T(4,128)(2,1)} reshape(bf16[16,64,512]{2,1,0:T(8,128)(2,1)S(1)} %copy-done.1) | data formatting | bytes 2097152 | tf_op jit(solution)/shard_map/reshape | solution.py:70
  14.2 0.1 compare_and_fusion
  14.3 0.6 %select_reduce_fusion = (f32[2,2,4,8]{3,2,1,0:T(4,128)S(1)}, f32[2,2,4,8,1024]{4,3,2,1,0:T(8,128)S(1)}) fusion(pred[2,1024]{1,0:T(4,128)(4,1)S(1)} %compare_and_fusion, bf16[1024,512,1,1,1]{1,0,4,3,2:T(8,128)(2,1)S(1)} %bitcast.160, pred[4,4]{1,0:T(4,128)(4,1)S(1)} %iota_compare_fusion.2, bf16[2,2,4,8,128]{4,3,2,1,0:T(8,128)(2,1)S(1)} %reshape.243), kind=kOutput, calls=%fused_computation.23 | convolution fusion | flops 134676352 | bytes 1608208 | tf_op jit(solution)/shard_map/rskgw,tw->rskgt/dot_general | solution.py:78
  14.9 0.3 convert_reduce_fusion
  15.1 0.2 copy.186
  15.3 0.2 copy.187
  15.5 0.3 fusion.6
  15.8 0.1 fusion.18
  15.9 0.5 %copy-done.7 = f32[4,2,2,8,128]{4,3,2,0,1:T(8,128)} copy-done((f32[4,2,2,8,128]{4,3,2,0,1:T(8,128)}, f32[4,2,2,8,128]{4,3,2,0,1:T(8,128)S(1)}, u32[]{:S(2)}) %copy-start.7) | copy-done | bytes 65560
  16.4 0.5 %collective-permute-start.1 = (f32[2,2,2,8,130]{4,3,1,2,0:T(8,128)S(1)}, f32[2,2,2,8,130]{4,3,1,2,0:T(8,128)S(1)}, u32[]{:S(2)}, u32[]{:S(2)}) collective-permute-start(f32[2,2,2,8,130]{4,3,1,2,0:T(8,128)S(1)} %fusion.18), channel_id=1, source_target_pairs={{0,8},{8,0},{16,24},{24,16},{1,9},{9,1},{17,25},{25,17},{2,10},{10... | collective-permute-start | bytes 99848 | tf_op jit(solution)/shard_map/ppermute | solution.py:147
  16.9 0.9 %collective-permute-done.1 = f32[2,2,2,8,130]{4,3,1,2,0:T(8,128)S(1)} collective-permute-done((f32[2,2,2,8,130]{4,3,1,2,0:T(8,128)S(1)}, f32[2,2,2,8,130]{4,3,1,2,0:T(8,128)S(1)}, u32[]{:S(2)}, u32[]{:S(2)}) %collective-permute-start.1) | collective-permute-done | bytes 33312 | tf_op jit(solution)/shard_map/ppermute | solution.py:147
  17.9 0.1 copy.223
  18.0 0.1 copy.221
  18.2 0.2 convert_reduce_fusion.4
  18.4 0.1 reshape.270
  18.5 0.6 %gather_fusion = bf16[16,2,32,2,128]{4,2,3,1,0:T(8,128)(2,1)S(1)} fusion(bf16[2,8,32,2,128]{4,2,3,1,0:T(8,128)(2,1)S(1)} %get-tuple-element.34, s32[1024]{0:T(1024)S(1)} %pad_clamp_fusion), kind=kCustom, calls=%fused_computation.clone | custom fusion | bytes 1048640 | tf_op jit(solution)/shard_map/jit(_take)/gather | solution.py:128
  19.2 0.6 %gather_fusion.1 = bf16[16,2,32,2,128]{4,2,3,1,0:T(8,128)(2,1)S(1)} fusion(bf16[2,8,32,2,128]{4,2,3,1,0:T(8,128)(2,1)S(1)} %collective-permute-done, s32[1024]{0:T(1024)S(1)} %pad_clamp_fusion), kind=kCustom, calls=%fused_computation.1.clone | custom fusion | bytes 1048640 | tf_op jit(solution)/shard_map/jit(_take)/gather | solution.py:128
  19.8 0.2 fusion.9
  20.0 0.7 %copy-done.4 = bf16[8,80,128]{2,1,0:T(8,128)(2,1)S(1)} copy-done((bf16[8,80,128]{2,1,0:T(8,128)(2,1)S(1)}, bf16[8,80,128]{2,1,0:T(8,128)(2,1)}, u32[]{:S(2)}) %copy-start.4) | copy-done | bytes 163864
  20.8 0.4 fusion.47
  21.1 0.4 fusion.48
  21.6 0.5 convert_reduce_fusion.1
  22.0 0.1 reduce_sum.72
  22.1 0.1 reduce_max.52
  22.2 0.1 reduce_sum.70
  22.3 0.1 reduce_max.51
  22.5 0.3 fusion.2
  22.7 0.3 fusion.1
  23.1 0.1 reshape.252
  23.2 0.1 reshape.251
  23.2 0.6 %copy-done.8 = f32[4,2,2,8,128]{4,3,2,0,1:T(8,128)S(1)} copy-done((f32[4,2,2,8,128]{4,3,2,0,1:T(8,128)S(1)}, f32[4,2,2,8,128]{4,3,2,0,1:T(8,128)}, u32[]{:S(2)}) %copy-start.8) | copy-done | bytes 65560
  23.8 0.1 fusion.23
  24.0 0.1 select_maximum_fusion
  24.2 1.0 %reshape.302 = f32[32,1,2176]{2,1,0:T(1,128)} reshape(f32[32,17,128]{2,1,0:T(8,128)S(1)} %maximum_dynamic-update-slice_fusion) | data formatting | bytes 557056 | tf_op jit(solution)/shard_map/reshape | solution.py:175
  25.2 6.0 %all-to-all-start.1 = ((f32[32,1,2176]{2,1,0:T(1,128)}), f32[32,1,2176]{2,1,0:T(1,128)S(1)}, u32[]{:S(2)}, u32[]{:S(2)}) async-start(f32[32,1,2176]{2,1,0:T(1,128)} %reshape.302), calls=%async_computation.1 | async-start | bytes 557056 | tf_op jit(solution)/shard_map/all_to_all | solution.py:174
  31.2 0.3 select_reduce_fusion.1
  31.5 0.1 reshape.259
  31.6 0.1 reshape.260
  31.7 0.1 convert_reduce_fusion.3
  31.8 0.2 convolution_bitcast_fusion.2
  32.0 0.1 reshape.266
  32.1 0.1 reshape.267
  32.2 10.1 %all-to-all-done.1 = f32[32,1,2176]{2,1,0:T(1,128)S(1)} async-done(((f32[32,1,2176]{2,1,0:T(1,128)}), f32[32,1,2176]{2,1,0:T(1,128)S(1)}, u32[]{:S(2)}, u32[]{:S(2)}) %all-to-all-start.1) | async-done | bytes 278560 | tf_op jit(solution)/shard_map/all_to_all | solution.py:174
  42.6 0.1 broadcast_in_dim.158
  42.7 0.1 broadcast_in_dim.159
  42.8 0.1 reshape.261
  43.0 0.1 fusion.10
  43.2 0.1 fusion.40
  43.3 0.1 fusion.27
  43.3 5.2 %all-gather = bf16[8,16,128]{2,1,0:T(8,128)(2,1)S(1)} all-gather(bf16[2,16,128]{2,1,0:T(8,128)(2,1)S(1)} %fusion.27), channel_id=2, replica_groups=mesh['ctx'=4,'row'=8] {'ctx'}, dimensions={0}, use_global_device_ids=true | all-gather | bytes 40960 | tf_op jit(solution)/shard_map/all_gather | solution.py:210
  48.5 0.6 %reshape.269 = bf16[2,2,4096]{2,1,0:T(2,128)(2,1)} reshape(bf16[2,2,2,16,128]{4,3,2,1,0:T(8,128)(2,1)S(1)} %bitcast.172) | data formatting | bytes 65536 | tf_op jit(solution)/shard_map/reshape | solution.py:213
  (74 shorter events, 1.3 us)
Async XLA Ops:
  0.0 14.3 %copy-start = (bf16[16,64,512]{2,1,0:T(8,128)(2,1)S(1)}, bf16[16,64,512]{2,1,0:T(8,128)(2,1)}, u32[]{:S(2)}) copy-start(bf16[16,64,512]{2,1,0:T(8,128)(2,1)} %param.18) | copy-start | bytes 3145732
  0.9 0.7 %copy-start.13 = (s32[2]{0:T(128)S(1)}, s32[2]{0:T(128)}, u32[]{:S(2)}) copy-start(s32[2]{0:T(128)} %param.15) | copy-start | bytes 28
  1.7 7.9 %copy-start.5 = (bf16[8,32,512]{2,1,0:T(8,128)(2,1)S(1)}, bf16[8,32,512]{2,1,0:T(8,128)(2,1)}, u32[]{:S(2)}) copy-start(bf16[8,32,512]{2,1,0:T(8,128)(2,1)} %param.16) | copy-start | bytes 786436
  2.4 15.7 %all-to-all-start = ((bf16[8,80,128]{2,1,0:T(8,128)(2,1)}), bf16[8,80,128]{2,1,0:T(8,128)(2,1)S(1)}, u32[]{:S(2)}, u32[]{:S(2)}) async-start(bf16[8,80,128]{2,1,0:T(8,128)(2,1)} %broadcast_in_dim.145), calls=%async_computation | async-start | bytes 327680 | tf_op jit(solution)/shard_map/all_to_all | solution.py:105
  9.7 1.0 %copy-start.6 = (bf16[8,32,512]{2,1,0:T(8,128)(2,1)S(1)}, bf16[8,32,512]{2,1,0:T(8,128)(2,1)}, u32[]{:S(2)}) copy-start(bf16[8,32,512]{2,1,0:T(8,128)(2,1)} %param.17) | copy-start | bytes 786436
  10.7 2.4 %copy-start.1 = (bf16[16,64,512]{2,1,0:T(8,128)(2,1)S(1)}, bf16[16,64,512]{2,1,0:T(8,128)(2,1)}, u32[]{:S(2)}) copy-start(bf16[16,64,512]{2,1,0:T(8,128)(2,1)} %param.19) | copy-start | bytes 3145732
  11.6 7.5 %collective-permute-start = (bf16[2,8,32,2,128]{4,2,3,1,0:T(8,128)(2,1)}, bf16[2,8,32,2,128]{4,2,3,1,0:T(8,128)(2,1)S(1)}, u32[]{:S(2)}, u32[]{:S(2)}) collective-permute-start(bf16[2,8,32,2,128]{4,2,3,1,0:T(8,128)(2,1)} %get-tuple-element.35), channel_id=1, source_target_pairs={{0,8},{8,0},{16,24},{24,16},{1,9},{9,1},{17,25},{25,17},{2,10},{10... | collective-permute-start | bytes 786440 | tf_op jit(solution)/shard_map/ppermute | solution.py:124
  11.6 0.7 %copy-start.10 = (s32[2,32]{1,0:T(2,128)S(1)}, s32[2,32]{1,0:T(2,128)}, u32[]{:S(2)}) copy-start(s32[2,32]{1,0:T(2,128)} %param.20) | copy-start | bytes 772
  13.1 1.1 %copy-start.11 = (s32[2]{0:T(128)S(1)}, s32[2]{0:T(128)}, u32[]{:S(2)}) copy-start(s32[2]{0:T(128)} %param.21) | copy-start | bytes 28
  14.3 1.2 %copy-start.2 = (bf16[1024,4,128]{2,1,0:T(4,128)(2,1)S(1)}, bf16[1024,4,128]{2,1,0:T(4,128)(2,1)}, u32[]{:S(2)}) copy-start(bf16[1024,4,128]{2,1,0:T(4,128)(2,1)} %reshape.249) | copy-start | bytes 3145732
  15.8 0.6 %copy-start.7 = (f32[4,2,2,8,128]{4,3,2,0,1:T(8,128)}, f32[4,2,2,8,128]{4,3,2,0,1:T(8,128)S(1)}, u32[]{:S(2)}) copy-start(f32[4,2,2,8,128]{4,3,2,0,1:T(8,128)S(1)} %fusion.6) | copy-start | bytes 196612
  16.4 1.4 %collective-permute-start.1 = (f32[2,2,2,8,130]{4,3,1,2,0:T(8,128)S(1)}, f32[2,2,2,8,130]{4,3,1,2,0:T(8,128)S(1)}, u32[]{:S(2)}, u32[]{:S(2)}) collective-permute-start(f32[2,2,2,8,130]{4,3,1,2,0:T(8,128)S(1)} %fusion.18), channel_id=1, source_target_pairs={{0,8},{8,0},{16,24},{24,16},{1,9},{9,1},{17,25},{25,17},{2,10},{10... | collective-permute-start | bytes 99848 | tf_op jit(solution)/shard_map/ppermute | solution.py:147
  18.1 1.0 %copy-start.3 = (bf16[8,80,128]{2,1,0:T(8,128)(2,1)}, bf16[8,80,128]{2,1,0:T(8,128)(2,1)S(1)}, u32[]{:S(2)}) copy-start(bf16[8,80,128]{2,1,0:T(8,128)(2,1)S(1)} %all-to-all-done) | copy-start | bytes 491524
  19.8 0.9 %copy-start.4 = (bf16[8,80,128]{2,1,0:T(8,128)(2,1)S(1)}, bf16[8,80,128]{2,1,0:T(8,128)(2,1)}, u32[]{:S(2)}) copy-start(bf16[8,80,128]{2,1,0:T(8,128)(2,1)} %copy-done.3) | copy-start | bytes 491524
  23.0 0.8 %copy-start.8 = (f32[4,2,2,8,128]{4,3,2,0,1:T(8,128)S(1)}, f32[4,2,2,8,128]{4,3,2,0,1:T(8,128)}, u32[]{:S(2)}) copy-start(f32[4,2,2,8,128]{4,3,2,0,1:T(8,128)} %copy-done.7) | copy-start | bytes 196612
  25.2 6.1 %copy-start.12 = (bf16[2,2,512]{2,1,0:T(2,128)(2,1)S(1)}, bf16[2,2,512]{2,1,0:T(2,128)(2,1)}, u32[]{:S(2)}) copy-start(bf16[2,2,512]{2,1,0:T(2,128)(2,1)} %param.22) | copy-start | bytes 12292
  25.2 6.6 %copy-start.9 = (bf16[2,2,512]{2,1,0:T(2,128)(2,1)S(1)}, bf16[2,2,512]{2,1,0:T(2,128)(2,1)}, u32[]{:S(2)}) copy-start(bf16[2,2,512]{2,1,0:T(2,128)(2,1)} %param.23) | copy-start | bytes 12292
  25.2 17.1 %all-to-all-start.1 = ((f32[32,1,2176]{2,1,0:T(1,128)}), f32[32,1,2176]{2,1,0:T(1,128)S(1)}, u32[]{:S(2)}, u32[]{:S(2)}) async-start(f32[32,1,2176]{2,1,0:T(1,128)} %reshape.302), calls=%async_computation.1 | async-start | bytes 557056 | tf_op jit(solution)/shard_map/all_to_all | solution.py:174
